TPU v7x, 256 devices: a whole 4x4x8 slice. The times are simulated.
256 devices in a mesh: segment: 4 (over x_hi, core), dp: 64 (over y, x_lo, z).
Axes of the slice: x: 4 (x_hi: 2, x_lo: 2; x = x_hi * 2 + x_lo), y: 4, z: 8, core: 2. Of those that a mesh axis runs over, the one named last changes fastest.
Arguments:
- inputs: bfloat16 [8192, 4096], P('dp'), may hold values from -6 to 6
- cotangent: bfloat16 [8192, 4096], P('dp'), may hold values from -0.125 to 0.125
- blocks: bfloat16 [4, 32, 8, 128, 128], P('segment'), may hold values from -0.1875 to 0.1875
- block_cols: int32 [4, 32, 8], P('segment'), may hold values from 0 to 31, as said below
Outputs:
- grad_blocks: bfloat16 [4, 32768, 128], P('segment', 'dp')
Inputs may be any that keep to these rules, and one draw needn't show every extreme that they name: In each layer, a row of block_cols names 8 different input blocks, and every input block is named exactly 8 times.
All inputs are finite; a program needn't handle non-finite values.
Results may differ from a plain program's by a relative error of at most 0.008.
Values may be sent and summed in bfloat16 or wider, within the bound.
No kernel may reach another device: no remote copies, remote signals or barrier semaphores. Data moves between devices by JAX's collectives and lax.ppermute only.
A program may use at most 128 MiB of HBM per device.

v0:
```python
import jax
import jax.numpy as jnp
from jax import lax
from jax.sharding import PartitionSpec as P

MICRO = 4


def from_behind(block, axis, distance):
    devices = range(lax.axis_size(axis))
    route = [(i - distance, i) for i in devices if i - distance in devices]
    return lax.ppermute(block, axis, route)


def body(inputs, cotangent, blocks, block_cols):
    segments = lax.axis_size("segment")
    segment_index = lax.axis_index("segment")
    groups = lax.axis_size("dp")
    weight = blocks[0]
    col_table = block_cols[0]
    num_blocks, per_block, edge_size = (weight.shape[0], weight.shape[1], weight.shape[2])
    layer_width = inputs.shape[1]
    all_rows = inputs.shape[0]
    micro_rows = all_rows // MICRO
    tick_count = MICRO + segments - 1
    flat_cols = col_table.reshape(-1)
    pair_order = jnp.argsort(flat_cols, stable=True)
    source_block = (pair_order // per_block).reshape(num_blocks, per_block)
    sorted_weight = weight.reshape(num_blocks * per_block, edge_size, edge_size)[
        pair_order
    ].reshape(num_blocks, per_block, edge_size, edge_size)

    def picked_of(hidden, row_count):
        return hidden.reshape(row_count, num_blocks, edge_size)[:, flat_cols, :].reshape(
            row_count, num_blocks, per_block, edge_size
        )

    stash_x = jnp.zeros((MICRO, micro_rows, layer_width), jnp.bfloat16)
    stash_z = jnp.zeros((MICRO, micro_rows, layer_width), jnp.float32)
    arrived = jnp.zeros((micro_rows, layer_width), jnp.bfloat16)
    for step_now in range(tick_count):
        batch_index = step_now - segment_index
        active = (batch_index >= 0) & (batch_index < MICRO)
        position = jnp.clip(batch_index, 0, MICRO - 1)
        leading = lax.dynamic_slice_in_dim(inputs, position * micro_rows, micro_rows, 0)
        current = jnp.where(segment_index == 0, leading, arrived)
        preact = jnp.einsum(
            "rjka,jkab->rjb",
            picked_of(current, micro_rows),
            weight,
            preferred_element_type=jnp.float32,
        ).reshape(micro_rows, layer_width)
        result = (current.astype(jnp.float32) + jax.nn.silu(preact)).astype(jnp.bfloat16)
        old_x = lax.dynamic_index_in_dim(stash_x, position, 0, False)
        stash_x = lax.dynamic_update_index_in_dim(
            stash_x, jnp.where(active, current, old_x), position, 0
        )
        old_z = lax.dynamic_index_in_dim(stash_z, position, 0, False)
        stash_z = lax.dynamic_update_index_in_dim(
            stash_z, jnp.where(active, preact, old_z), position, 0
        )
        if step_now + 1 < tick_count:
            arrived = from_behind(result, "segment", 1)
    stash_g = jnp.zeros((MICRO, micro_rows, layer_width), jnp.bfloat16)
    incoming = jnp.zeros((micro_rows, layer_width), jnp.bfloat16)
    for step_now in range(tick_count):
        batch_index = step_now - (segments - 1 - segment_index)
        active = (batch_index >= 0) & (batch_index < MICRO)
        position = jnp.clip(batch_index, 0, MICRO - 1)
        from_cot = lax.dynamic_slice_in_dim(cotangent, position * micro_rows, micro_rows, 0)
        upstream = jnp.where(segment_index == segments - 1, from_cot, incoming)
        preact = lax.dynamic_index_in_dim(stash_z, position, 0, False)
        sigmoid_z = jax.nn.sigmoid(preact)
        grad_pre = (
            upstream.astype(jnp.float32) * sigmoid_z * (1.0 + preact * (1.0 - sigmoid_z))
        ).astype(jnp.bfloat16)
        old_g = lax.dynamic_index_in_dim(stash_g, position, 0, False)
        stash_g = lax.dynamic_update_index_in_dim(
            stash_g, jnp.where(active, grad_pre, old_g), position, 0
        )
        spread = grad_pre.reshape(micro_rows, num_blocks, edge_size)[:, source_block, :]
        back_sum = jnp.einsum(
            "rckb,ckab->rca", spread, sorted_weight, preferred_element_type=jnp.float32
        )
        passed = (upstream.astype(jnp.float32) + back_sum.reshape(micro_rows, layer_width)).astype(
            jnp.bfloat16
        )
        if step_now + 1 < tick_count:
            incoming = from_behind(passed, "segment", -1)
    all_inputs = stash_x.reshape(all_rows, layer_width)
    all_grads = stash_g.reshape(all_rows, layer_width)
    picked_all = picked_of(all_inputs, all_rows).reshape(
        all_rows, num_blocks * per_block * edge_size
    )
    grad_view = all_grads.reshape(all_rows, num_blocks, edge_size)
    share_rows = num_blocks * per_block * edge_size // groups
    picked_cols = picked_all.reshape(
        all_rows, lax.axis_size("dp") * share_rows // edge_size, edge_size
    )
    pair_ids = jnp.arange(lax.axis_size("dp") * share_rows // edge_size, dtype=jnp.int32)
    chosen = grad_view[:, pair_ids // per_block, :]
    own_share = lax.psum_scatter(
        jnp.einsum("rpa,rpb->pab", picked_cols, chosen, preferred_element_type=jnp.float32).reshape(
            lax.axis_size("dp") * share_rows, edge_size
        ),
        "dp",
        scatter_dimension=0,
        tiled=True,
    )
    summed = own_share.astype(jnp.bfloat16)
    return summed[None]


def solution(mesh):
    return jax.shard_map(
        body,
        mesh=mesh,
        in_specs=(
            P("dp", None),
            P("dp", None),
            P("segment", None, None, None, None),
            P("segment", None, None),
        ),
        out_specs=P("segment", "dp", None),
        check_vma=False,
    )
```

profile of v0, /device:TPU:0, one launch (start us, length us, event | category | flops | bytes accessed | tf_op | source)
XLA Modules:
  0.0 669.9 jit_solution(127607280823348803)
XLA Ops:
  8.4 2.2 gather_fusion
  10.6 5.5 bitcast_select_fusion
  19.1 3.2 sort.17
  25.1 12.1 %gather_fusion.8 = bf16[256,128,128]{2,1,0:T(8,128)(2,1)} fusion(bf16[256,128,128]{2,1,0:T(8,128)(2,1)} %bitcast.540, s32[1024]{0:T(1024)S(1)} %pad_clamp_fusion.2), kind=kCustom, calls=%fused_computation.8 | custom fusion | bytes 16778240 | tf_op jit(solution)/shard_map/gather | solution.py:29
  41.2 5.4 fusion.13
  49.8 3.3 collective-permute-start.1
  58.3 5.4 fusion.11
  67.0 4.5 collective-permute-start.2
  74.5 2.2 gather_fusion.3
  76.7 5.4 fusion.9
  85.4 7.5 %collective-permute-start.3 = (bf16[32,4096]{1,0:T(8,128)(2,1)S(1)}, bf16[32,4096]{1,0:T(8,128)(2,1)S(1)}, u32[]{:S(2)}, u32[]{:S(2)}) collective-permute-start(bf16[32,4096]{1,0:T(8,128)(2,1)S(1)} %fusion.95), channel_id=1, source_target_pairs={{0,64},{64,128},{128,192},{1,65},{65,129},{129,193},{2,66},{66,130... | collective-permute-start | bytes 786440 | tf_op jit(solution)/shard_map/ppermute | solution.py:12
  98.0 5.4 fusion.7
  106.7 8.0 %collective-permute-start.4 = (bf16[32,4096]{1,0:T(8,128)(2,1)S(1)}, bf16[32,4096]{1,0:T(8,128)(2,1)S(1)}, u32[]{:S(2)}, u32[]{:S(2)}) collective-permute-start(bf16[32,4096]{1,0:T(8,128)(2,1)S(1)} %fusion.96), channel_id=1, source_target_pairs={{0,64},{64,128},{128,192},{1,65},{65,129},{129,193},{2,66},{66,130... | collective-permute-start | bytes 786440 | tf_op jit(solution)/shard_map/ppermute | solution.py:12
  119.8 5.4 fusion.5
  128.4 8.4 %collective-permute-start.5 = (bf16[32,4096]{1,0:T(8,128)(2,1)S(1)}, bf16[32,4096]{1,0:T(8,128)(2,1)S(1)}, u32[]{:S(2)}, u32[]{:S(2)}) collective-permute-start(bf16[32,4096]{1,0:T(8,128)(2,1)S(1)} %fusion.97), channel_id=1, source_target_pairs={{0,64},{64,128},{128,192},{1,65},{65,129},{129,193},{2,66},{66,130... | collective-permute-start | bytes 786440 | tf_op jit(solution)/shard_map/ppermute | solution.py:12
  140.8 5.4 fusion.17
  151.7 8.7 %gather_fusion.6 = bf16[256,128,128]{2,1,0:T(8,128)(2,1)} fusion(bf16[128,32,128]{2,0,1:T(8,128)(2,1)S(1)} %copy.53, s32[1024]{0:T(1024)S(1)} %pad_clamp_fusion.3), kind=kCustom, calls=%fused_computation.6 | custom fusion | bytes 16778240 | tf_op jit(solution)/shard_map/gather | solution.py:34
  162.5 6.9 %convolution_bitcast_fusion.5 = f32[32,4,8,128]{3,2,1,0:T(8,128)S(1)} fusion(bf16[32,8,128,128]{3,2,1,0:T(8,128)(2,1)} %bitcast.541, bf16[32,32,8,128]{3,0,2,1:T(8,128)(2,1)} %bitcast.558), kind=kOutput, calls=%fused_computation.39 | convolution fusion | flops 268435456 | bytes 11010048 | tf_op jit(solution)/shard_map/rckb,ckab->rca/dot_general | solution.py:82
  170.9 7.7 %collective-permute-done.6 = bf16[32,4096]{1,0:T(8,128)(2,1)S(1)} collective-permute-done((bf16[32,4096]{1,0:T(8,128)(2,1)S(1)}, bf16[32,4096]{1,0:T(8,128)(2,1)S(1)}, u32[]{:S(2)}, u32[]{:S(2)}) %collective-permute-start.6) | collective-permute-done | bytes 262176 | tf_op jit(solution)/shard_map/ppermute | solution.py:12
  181.5 6.9 %convolution_bitcast_fusion.4 = f32[32,4,8,128]{3,2,1,0:T(8,128)S(1)} fusion(bf16[32,8,128,128]{3,2,1,0:T(8,128)(2,1)} %bitcast.542, bf16[32,32,8,128]{3,0,2,1:T(8,128)(2,1)} %bitcast.559), kind=kOutput, calls=%fused_computation.38 | convolution fusion | flops 268435456 | bytes 11010048 | tf_op jit(solution)/shard_map/rckb,ckab->rca/dot_general | solution.py:82
  189.9 8.6 %collective-permute-done.7 = bf16[32,4096]{1,0:T(8,128)(2,1)S(1)} collective-permute-done((bf16[32,4096]{1,0:T(8,128)(2,1)S(1)}, bf16[32,4096]{1,0:T(8,128)(2,1)S(1)}, u32[]{:S(2)}, u32[]{:S(2)}) %collective-permute-start.7) | collective-permute-done | bytes 262176 | tf_op jit(solution)/shard_map/ppermute | solution.py:12
  201.4 6.9 %convolution_bitcast_fusion.3 = f32[32,4,8,128]{3,2,1,0:T(8,128)S(1)} fusion(bf16[32,8,128,128]{3,2,1,0:T(8,128)(2,1)} %bitcast.543, bf16[32,32,8,128]{3,0,2,1:T(8,128)(2,1)} %bitcast.560), kind=kOutput, calls=%fused_computation.37 | convolution fusion | flops 268435456 | bytes 11010048 | tf_op jit(solution)/shard_map/rckb,ckab->rca/dot_general | solution.py:82
  209.9 7.6 %collective-permute-done.8 = bf16[32,4096]{1,0:T(8,128)(2,1)S(1)} collective-permute-done((bf16[32,4096]{1,0:T(8,128)(2,1)S(1)}, bf16[32,4096]{1,0:T(8,128)(2,1)S(1)}, u32[]{:S(2)}, u32[]{:S(2)}) %collective-permute-start.8) | collective-permute-done | bytes 262176 | tf_op jit(solution)/shard_map/ppermute | solution.py:12
  220.5 6.9 %convolution_bitcast_fusion.2 = f32[32,4,8,128]{3,2,1,0:T(8,128)S(1)} fusion(bf16[32,8,128,128]{3,2,1,0:T(8,128)(2,1)} %bitcast.544, bf16[32,32,8,128]{3,0,2,1:T(8,128)(2,1)} %bitcast.561), kind=kOutput, calls=%fused_computation.36 | convolution fusion | flops 268435456 | bytes 11010048 | tf_op jit(solution)/shard_map/rckb,ckab->rca/dot_general | solution.py:82
  228.8 7.9 %collective-permute-done.9 = bf16[32,4096]{1,0:T(8,128)(2,1)S(1)} collective-permute-done((bf16[32,4096]{1,0:T(8,128)(2,1)S(1)}, bf16[32,4096]{1,0:T(8,128)(2,1)S(1)}, u32[]{:S(2)}, u32[]{:S(2)}) %collective-permute-start.9) | collective-permute-done | bytes 262176 | tf_op jit(solution)/shard_map/ppermute | solution.py:12
  239.6 6.9 %convolution_bitcast_fusion.1 = f32[32,4,8,128]{3,2,1,0:T(8,128)S(1)} fusion(bf16[32,8,128,128]{3,2,1,0:T(8,128)(2,1)} %bitcast.545, bf16[32,32,8,128]{3,0,2,1:T(8,128)(2,1)} %bitcast.562), kind=kOutput, calls=%fused_computation.35 | convolution fusion | flops 268435456 | bytes 11010048 | tf_op jit(solution)/shard_map/rckb,ckab->rca/dot_general | solution.py:82
  247.9 7.9 %collective-permute-done.10 = bf16[32,4096]{1,0:T(8,128)(2,1)S(1)} collective-permute-done((bf16[32,4096]{1,0:T(8,128)(2,1)S(1)}, bf16[32,4096]{1,0:T(8,128)(2,1)S(1)}, u32[]{:S(2)}, u32[]{:S(2)}) %collective-permute-start.10) | collective-permute-done | bytes 262176 | tf_op jit(solution)/shard_map/ppermute | solution.py:12
  258.7 6.9 %convolution_bitcast_fusion = f32[32,4,8,128]{3,2,1,0:T(8,128)S(1)} fusion(bf16[32,8,128,128]{3,2,1,0:T(8,128)(2,1)} %bitcast.546, bf16[32,32,8,128]{3,0,2,1:T(8,128)(2,1)} %bitcast.557), kind=kOutput, calls=%fused_computation.34 | convolution fusion | flops 268435456 | bytes 11010048 | tf_op jit(solution)/shard_map/rckb,ckab->rca/dot_general | solution.py:82
  267.3 7.6 %collective-permute-done.11 = bf16[32,4096]{1,0:T(8,128)(2,1)S(1)} collective-permute-done((bf16[32,4096]{1,0:T(8,128)(2,1)S(1)}, bf16[32,4096]{1,0:T(8,128)(2,1)S(1)}, u32[]{:S(2)}, u32[]{:S(2)}) %collective-permute-start.11) | collective-permute-done | bytes 262176 | tf_op jit(solution)/shard_map/ppermute | solution.py:12
  275.8 8.7 %gather_fusion.15 = bf16[256,128,128]{2,1,0:T(8,128)(2,1)} fusion(bf16[128,32,128]{2,0,1:T(8,128)(2,1)S(1)} %copy.75, s32[1024]{0:T(1024)S(1)} %pad_clamp_fusion), kind=kCustom, calls=%fused_computation.15 | custom fusion | bytes 16778240 | tf_op jit(solution)/shard_map/gather | solution.py:101
  284.5 14.4 %fusion = f32[256,128,128]{2,1,0:T(8,128)} fusion(bf16[256,128,128]{2,1,0:T(8,128)(2,1)} %gather_fusion.15, bf16[256,128,128]{2,1,0:T(8,128)(2,1)} %gather_fusion.6), kind=kOutput, calls=%fused_computation.16 | convolution fusion | flops 1073741824 | bytes 33554432 | tf_op jit(solution)/shard_map/rpa,rpb->pab/dot_general | solution.py:103
  298.9 362.1 %reduce-scatter.2.cloned.1.call-done = f32[512,128]{1,0:T(8,128)} async-done(((f32[32768,128]{1,0:T(8,128)}), f32[512,128]{1,0:T(8,128)}) %reduce-scatter.2.cloned.1.call-update) | async-done | bytes 262160 | tf_op jit(solution)/shard_map/reduce_scatter | solution.py:102
  (181 shorter events, 83.5 us)
Async XLA Ops:
  6.5 654.5 %reduce-scatter.2.cloned.1.call-start = ((), (), s32[]{:S(2)}) async-start(), calls=%async_computation.1 | async-start | bytes 17039360 | tf_op jit(solution)/shard_map/reduce_scatter | solution.py:102
  10.6 5.5 copy-start.8
  17.0 20.2 %collective-permute-start = (bf16[32,4096]{1,0:T(8,128)(2,1)}, bf16[32,4096]{1,0:T(8,128)(2,1)}, u32[]{:S(2)}, u32[]{:S(2)}) collective-permute-start(bf16[32,4096]{1,0:T(8,128)(2,1)} %fusion.92), channel_id=1, source_target_pairs={{0,64},{64,128},{128,192},{1,65},{65,129},{129,193},{2,66},{66,130... | collective-permute-start | bytes 786440 | tf_op jit(solution)/shard_map/ppermute | solution.py:12
  41.2 5.4 copy-start.11
  49.8 4.5 collective-permute-start.1
  58.3 5.4 copy-start.13
  67.0 5.7 collective-permute-start.2
  76.7 5.4 copy-start.15
  85.4 8.6 %collective-permute-start.3 = (bf16[32,4096]{1,0:T(8,128)(2,1)S(1)}, bf16[32,4096]{1,0:T(8,128)(2,1)S(1)}, u32[]{:S(2)}, u32[]{:S(2)}) collective-permute-start(bf16[32,4096]{1,0:T(8,128)(2,1)S(1)} %fusion.95), channel_id=1, source_target_pairs={{0,64},{64,128},{128,192},{1,65},{65,129},{129,193},{2,66},{66,130... | collective-permute-start | bytes 786440 | tf_op jit(solution)/shard_map/ppermute | solution.py:12
  98.0 5.4 copy-start.17
  106.7 9.1 %collective-permute-start.4 = (bf16[32,4096]{1,0:T(8,128)(2,1)S(1)}, bf16[32,4096]{1,0:T(8,128)(2,1)S(1)}, u32[]{:S(2)}, u32[]{:S(2)}) collective-permute-start(bf16[32,4096]{1,0:T(8,128)(2,1)S(1)} %fusion.96), channel_id=1, source_target_pairs={{0,64},{64,128},{128,192},{1,65},{65,129},{129,193},{2,66},{66,130... | collective-permute-start | bytes 786440 | tf_op jit(solution)/shard_map/ppermute | solution.py:12
  119.8 5.4 copy-start.19
  128.4 9.3 %copy-start.9 = (bf16[128,4096]{1,0:T(8,128)(2,1)S(1)}, bf16[128,4096]{1,0:T(8,128)(2,1)}, u32[]{:S(2)}) copy-start(bf16[128,4096]{1,0:T(8,128)(2,1)} %param.4) | copy-start | bytes 3145732
  128.4 9.3 %collective-permute-start.5 = (bf16[32,4096]{1,0:T(8,128)(2,1)S(1)}, bf16[32,4096]{1,0:T(8,128)(2,1)S(1)}, u32[]{:S(2)}, u32[]{:S(2)}) collective-permute-start(bf16[32,4096]{1,0:T(8,128)(2,1)S(1)} %fusion.97), channel_id=1, source_target_pairs={{0,64},{64,128},{128,192},{1,65},{65,129},{129,193},{2,66},{66,130... | collective-permute-start | bytes 786440 | tf_op jit(solution)/shard_map/ppermute | solution.py:12
  162.5 6.9 %copy-start.2 = (bf16[128,4096]{1,0:T(8,128)(2,1)S(1)}, bf16[128,4096]{1,0:T(8,128)(2,1)}, u32[]{:S(2)}) copy-start(bf16[128,4096]{1,0:T(8,128)(2,1)} %param.5) | copy-start | bytes 3145732
  162.5 8.3 %copy-start.1 = (bf16[4,32,4096]{2,1,0:T(8,128)(2,1)S(1)}, bf16[4,32,4096]{2,1,0:T(8,128)(2,1)}, u32[]{:S(2)}) copy-start(bf16[4,32,4096]{2,1,0:T(8,128)(2,1)} %copy-done) | copy-start | bytes 3145732
  169.5 9.1 %collective-permute-start.6 = (bf16[32,4096]{1,0:T(8,128)(2,1)S(1)}, bf16[32,4096]{1,0:T(8,128)(2,1)S(1)}, u32[]{:S(2)}, u32[]{:S(2)}) collective-permute-start(bf16[32,4096]{1,0:T(8,128)(2,1)S(1)} %fusion.22), channel_id=1, source_target_pairs={{64,0},{128,64},{192,128},{65,1},{129,65},{193,129},{66,2},{130,66... | collective-permute-start | bytes 786440 | tf_op jit(solution)/shard_map/ppermute | solution.py:12
  181.5 6.9 %copy-start.3 = (bf16[128,4096]{1,0:T(8,128)(2,1)S(1)}, bf16[128,4096]{1,0:T(8,128)(2,1)}, u32[]{:S(2)}) copy-start(bf16[128,4096]{1,0:T(8,128)(2,1)} %param.5) | copy-start | bytes 3145732
  181.5 6.9 %copy-start.24 = (bf16[32,4096]{1,0:T(8,128)(2,1)S(1)}, bf16[32,4096]{1,0:T(8,128)(2,1)}, u32[]{:S(2)}) copy-start(bf16[32,4096]{1,0:T(8,128)(2,1)} %copy-done.23) | copy-start | bytes 786436
  188.5 9.9 %collective-permute-start.7 = (bf16[32,4096]{1,0:T(8,128)(2,1)S(1)}, bf16[32,4096]{1,0:T(8,128)(2,1)S(1)}, u32[]{:S(2)}, u32[]{:S(2)}) collective-permute-start(bf16[32,4096]{1,0:T(8,128)(2,1)S(1)} %fusion.25), channel_id=1, source_target_pairs={{64,0},{128,64},{192,128},{65,1},{129,65},{193,129},{66,2},{130,66... | collective-permute-start | bytes 786440 | tf_op jit(solution)/shard_map/ppermute | solution.py:12
  201.4 6.9 %copy-start.4 = (bf16[128,4096]{1,0:T(8,128)(2,1)S(1)}, bf16[128,4096]{1,0:T(8,128)(2,1)}, u32[]{:S(2)}) copy-start(bf16[128,4096]{1,0:T(8,128)(2,1)} %param.5) | copy-start | bytes 3145732
  201.4 6.9 %copy-start.26 = (bf16[32,4096]{1,0:T(8,128)(2,1)S(1)}, bf16[32,4096]{1,0:T(8,128)(2,1)}, u32[]{:S(2)}) copy-start(bf16[32,4096]{1,0:T(8,128)(2,1)} %copy-done.25) | copy-start | bytes 786436
  208.4 9.2 %collective-permute-start.8 = (bf16[32,4096]{1,0:T(8,128)(2,1)S(1)}, bf16[32,4096]{1,0:T(8,128)(2,1)S(1)}, u32[]{:S(2)}, u32[]{:S(2)}) collective-permute-start(bf16[32,4096]{1,0:T(8,128)(2,1)S(1)} %fusion.28), channel_id=1, source_target_pairs={{64,0},{128,64},{192,128},{65,1},{129,65},{193,129},{66,2},{130,66... | collective-permute-start | bytes 786440 | tf_op jit(solution)/shard_map/ppermute | solution.py:12
  220.5 6.9 %copy-start.5 = (bf16[128,4096]{1,0:T(8,128)(2,1)S(1)}, bf16[128,4096]{1,0:T(8,128)(2,1)}, u32[]{:S(2)}) copy-start(bf16[128,4096]{1,0:T(8,128)(2,1)} %param.5) | copy-start | bytes 3145732
  220.5 6.9 %copy-start.28 = (bf16[32,4096]{1,0:T(8,128)(2,1)S(1)}, bf16[32,4096]{1,0:T(8,128)(2,1)}, u32[]{:S(2)}) copy-start(bf16[32,4096]{1,0:T(8,128)(2,1)} %copy-done.27) | copy-start | bytes 786436
  227.5 9.2 %collective-permute-start.9 = (bf16[32,4096]{1,0:T(8,128)(2,1)S(1)}, bf16[32,4096]{1,0:T(8,128)(2,1)S(1)}, u32[]{:S(2)}, u32[]{:S(2)}) collective-permute-start(bf16[32,4096]{1,0:T(8,128)(2,1)S(1)} %fusion.31), channel_id=1, source_target_pairs={{64,0},{128,64},{192,128},{65,1},{129,65},{193,129},{66,2},{130,66... | collective-permute-start | bytes 786440 | tf_op jit(solution)/shard_map/ppermute | solution.py:12
  239.6 6.9 %copy-start.6 = (bf16[128,4096]{1,0:T(8,128)(2,1)S(1)}, bf16[128,4096]{1,0:T(8,128)(2,1)}, u32[]{:S(2)}) copy-start(bf16[128,4096]{1,0:T(8,128)(2,1)} %param.5) | copy-start | bytes 3145732
  239.6 6.9 %copy-start.30 = (bf16[32,4096]{1,0:T(8,128)(2,1)S(1)}, bf16[32,4096]{1,0:T(8,128)(2,1)}, u32[]{:S(2)}) copy-start(bf16[32,4096]{1,0:T(8,128)(2,1)} %copy-done.29) | copy-start | bytes 786436
  246.6 9.2 %collective-permute-start.10 = (bf16[32,4096]{1,0:T(8,128)(2,1)S(1)}, bf16[32,4096]{1,0:T(8,128)(2,1)S(1)}, u32[]{:S(2)}, u32[]{:S(2)}) collective-permute-start(bf16[32,4096]{1,0:T(8,128)(2,1)S(1)} %fusion.34), channel_id=1, source_target_pairs={{64,0},{128,64},{192,128},{65,1},{129,65},{193,129},{66,2},{130,66... | collective-permute-start | bytes 786440 | tf_op jit(solution)/shard_map/ppermute | solution.py:12
  258.7 6.9 %copy-start.7 = (bf16[128,4096]{1,0:T(8,128)(2,1)S(1)}, bf16[128,4096]{1,0:T(8,128)(2,1)}, u32[]{:S(2)}) copy-start(bf16[128,4096]{1,0:T(8,128)(2,1)} %param.5) | copy-start | bytes 3145732
  258.7 6.9 %copy-start.22 = (bf16[32,4096]{1,0:T(8,128)(2,1)S(1)}, bf16[32,4096]{1,0:T(8,128)(2,1)}, u32[]{:S(2)}) copy-start(bf16[32,4096]{1,0:T(8,128)(2,1)} %copy-done.21) | copy-start | bytes 786436
  265.7 9.2 %collective-permute-start.11 = (bf16[32,4096]{1,0:T(8,128)(2,1)S(1)}, bf16[32,4096]{1,0:T(8,128)(2,1)S(1)}, u32[]{:S(2)}, u32[]{:S(2)}) collective-permute-start(bf16[32,4096]{1,0:T(8,128)(2,1)S(1)} %fusion.37), channel_id=1, source_target_pairs={{64,0},{128,64},{192,128},{65,1},{129,65},{193,129},{66,2},{130,66... | collective-permute-start | bytes 786440 | tf_op jit(solution)/shard_map/ppermute | solution.py:12
  (12 other events, 8.9 us)
Sparse Core Ops, SparseCore 0:
  299.0 361.9 reduce-scatter.1
where the time goes:
time: 679 us; the launch traced here: 670 us
  waiting for transfers between devices  411 us (61%)
  matrix products  93.7 us (14%)
  local copies, waits for them, and re-layouts  88.3 us (13%)
  starting transfers between devices  41.8 us (6%)
  other arithmetic  20.1 us (3%)
  between operations  14.7 us (2%)
    reduce_scatter x1, waiting for transfers between devices, body(): lax.psum_scatter(jnp.einsum('rpa,rpb->pab', picked_cols, chosen, preferre...  362 us
    ppermute x12, waiting for transfers between devices, from_behind(): return lax.ppermute(block, axis, route)  49.1 us
    ppermute x12, starting transfers between devices, from_behind(): return lax.ppermute(block, axis, route)  41.8 us
    dot_general x6, matrix products, body(): jnp.einsum('rckb,ckab->rca', spread, sorted_weight, preferred_element_typ...  41.3 us
    dot_general x7, matrix products, body(): jnp.einsum('rjka,jkab->rjb', picked_of(current, micro_rows), weight, pref...  38 us
    gather x8, local copies, waits for them, and re-layouts, picked_of(): hidden.reshape(row_count, num_blocks, edge_size)[:, flat_cols, :]  23.9 us
    dot_general x1, matrix products, body(): jnp.einsum('rpa,rpb->pab', picked_cols, chosen, preferred_element_type=jn...  14.4 us
  transfers between devices with their start and end apart: 13, of which 9 were waited for; matrix products, arithmetic and copies ran while one was open for 3% of the time, Pallas kernels for 0%

commit v1 on v0

--- a/solution.py
+++ b/solution.py
@@ -1,9 +1,12 @@
 import jax
+import numpy as np
 import jax.numpy as jnp
 from jax import lax
-from jax.sharding import PartitionSpec as P
+from jax.sharding import Mesh, PartitionSpec as P
 
-MICRO = 4
+MICRO = 1
+DP_AXES = ("y", "xlo", "z")
+DP_SIZES = (4, 2, 8)
 
 
 def from_behind(block, axis, distance):
@@ -15,7 +18,7 @@
 def body(inputs, cotangent, blocks, block_cols):
     segments = lax.axis_size("segment")
     segment_index = lax.axis_index("segment")
-    groups = lax.axis_size("dp")
+    groups = DP_SIZES[0] * DP_SIZES[1] * DP_SIZES[2]
     weight = blocks[0]
     col_table = block_cols[0]
     num_blocks, per_block, edge_size = (weight.shape[0], weight.shape[1], weight.shape[2])
@@ -89,38 +92,34 @@
             incoming = from_behind(passed, "segment", -1)
     all_inputs = stash_x.reshape(all_rows, layer_width)
     all_grads = stash_g.reshape(all_rows, layer_width)
-    picked_all = picked_of(all_inputs, all_rows).reshape(
-        all_rows, num_blocks * per_block * edge_size
-    )
+    share_pairs = num_blocks * per_block // groups
+    ny, nx, nz = DP_SIZES
+    order = np.arange(num_blocks * per_block).reshape(ny, nx, nz, share_pairs)
+    order = order.transpose(2, 0, 1, 3).reshape(-1)
+    picked_cols = all_inputs.reshape(all_rows, num_blocks, edge_size)[:, flat_cols[order], :]
     grad_view = all_grads.reshape(all_rows, num_blocks, edge_size)
-    share_rows = num_blocks * per_block * edge_size // groups
-    picked_cols = picked_all.reshape(
-        all_rows, lax.axis_size("dp") * share_rows // edge_size, edge_size
-    )
-    pair_ids = jnp.arange(lax.axis_size("dp") * share_rows // edge_size, dtype=jnp.int32)
-    chosen = grad_view[:, pair_ids // per_block, :]
-    own_share = lax.psum_scatter(
-        jnp.einsum("rpa,rpb->pab", picked_cols, chosen, preferred_element_type=jnp.float32).reshape(
-            lax.axis_size("dp") * share_rows, edge_size
-        ),
-        "dp",
-        scatter_dimension=0,
-        tiled=True,
-    )
+    chosen = grad_view[:, order // per_block, :]
+    partial = jnp.einsum(
+        "rpa,rpb->pab", picked_cols, chosen, preferred_element_type=jnp.float32
+    ).reshape(num_blocks * per_block * edge_size, edge_size)
+    for axis in ("z", "y", "xlo"):
+        partial = lax.psum_scatter(partial, axis, scatter_dimension=0, tiled=True)
+    own_share = partial
     summed = own_share.astype(jnp.bfloat16)
     return summed[None]
 
 
 def solution(mesh):
+    fine = Mesh(mesh.devices.reshape(mesh.shape["segment"], *DP_SIZES), ("segment",) + DP_AXES)
     return jax.shard_map(
         body,
-        mesh=mesh,
+        mesh=fine,
         in_specs=(
-            P("dp", None),
-            P("dp", None),
+            P(DP_AXES, None),
+            P(DP_AXES, None),
             P("segment", None, None, None, None),
             P("segment", None, None),
         ),
-        out_specs=P("segment", "dp", None),
+        out_specs=P("segment", DP_AXES, None),
         check_vma=False,
     )

time: 679 us -> 549 us (0.81)
  the two profiles are of different devices: /device:TPU:0 before, /device:TPU:2 now
where the time goes in v1:
time: 549 us; the launch traced here: 541 us
  waiting for transfers between devices  274 us (50%)
  local copies, waits for them, and re-layouts  108 us (20%)
  matrix products  77.1 us (14%)
  starting transfers between devices  37.2 us (7%)
  other arithmetic  30.7 us (6%)
  between operations  13.7 us (2%)
    reduce_scatter x3, waiting for transfers between devices, body(): partial = lax.psum_scatter(partial, axis, scatter_dimension=0, tiled=True)  243 us
    dot_general x4, matrix products, body(): jnp.einsum('rjka,jkab->rjb', picked_of(current, micro_rows), weight, pref...  38.3 us
    ppermute x6, starting transfers between devices, from_behind(): return lax.ppermute(block, axis, route)  37.1 us
    gather x4, local copies, waits for them, and re-layouts, picked_of(): hidden.reshape(row_count, num_blocks, edge_size)[:, flat_cols, :]  34.5 us
    ppermute x6, waiting for transfers between devices, from_behind(): return lax.ppermute(block, axis, route)  31.2 us
    gather x3, local copies, waits for them, and re-layouts, body(): grad_pre.reshape(micro_rows, num_blocks, edge_size)[:, source_block, :]  26.3 us
    dot_general x3, matrix products, body(): jnp.einsum('rckb,ckab->rca', spread, sorted_weight, preferred_element_typ...  24.4 us
    dot_general x1, matrix products, body(): jnp.einsum('rpa,rpb->pab', picked_cols, chosen, preferred_element_type=jn...  14.4 us
  transfers between devices with their start and end apart: 9, of which 8 were waited for; matrix products, arithmetic and copies ran while one was open for 5% of the time, Pallas kernels for 0%

profile of v1, /device:TPU:2, one launch (start us, length us, event | category | flops | bytes accessed | tf_op | source)
XLA Modules:
  0.0 541.0 jit_solution(4803397822225986093)
XLA Ops:
  9.8 8.6 %gather_fusion = bf16[256,128,128]{2,1,0:T(8,128)(2,1)} fusion(bf16[128,32,128]{2,0,1:T(8,128)(2,1)S(1)} %copy.55, s32[1024]{0:T(1024)S(1)} %pad_clamp_fusion.5), kind=kCustom, calls=%fused_computation | custom fusion | bytes 16778240 | tf_op jit(solution)/shard_map/gather | solution.py:37
  18.5 9.5 %fusion.9 = f32[32,128,128,1]{1,2,3,0:T(8,128)} fusion(bf16[128,32,8,128]{3,0,2,1:T(8,128)(2,1)} %bitcast.175, bf16[1,32,8,128,128]{4,3,2,1,0:T(8,128)(2,1)} %param.10), kind=kOutput, calls=%fused_computation.20 | convolution fusion | flops 1073741824 | bytes 18874368 | tf_op jit(solution)/shard_map/rjka,jkab->rjb/dot_general | solution.py:50
  28.0 2.2 fusion.32
  35.0 8.6 %gather_fusion.1 = bf16[256,128,128]{2,1,0:T(8,128)(2,1)} fusion(bf16[128,32,128]{2,0,1:T(8,128)(2,1)S(1)} %copy.58, s32[1024]{0:T(1024)S(1)} %pad_clamp_fusion.5), kind=kCustom, calls=%fused_computation.1 | custom fusion | bytes 16778240 | tf_op jit(solution)/shard_map/gather | solution.py:37
  43.7 9.5 %fusion.7 = f32[32,128,128,1]{1,2,3,0:T(8,128)} fusion(bf16[128,32,8,128]{3,0,2,1:T(8,128)(2,1)} %bitcast.176, bf16[1,32,8,128,128]{4,3,2,1,0:T(8,128)(2,1)} %param.10), kind=kOutput, calls=%fused_computation.18 | convolution fusion | flops 1073741824 | bytes 18874368 | tf_op jit(solution)/shard_map/rjka,jkab->rjb/dot_general | solution.py:50
  53.2 2.1 fusion.33
  55.3 14.4 %collective-permute-start.1 = (bf16[128,4096]{0,1:T(8,128)(2,1)S(1)}, bf16[128,4096]{0,1:T(8,128)(2,1)S(1)}, u32[]{:S(2)}, u32[]{:S(2)}) collective-permute-start(bf16[128,4096]{0,1:T(8,128)(2,1)S(1)} %fusion.33), channel_id=1, source_target_pairs={{0,64},{64,128},{128,192},{1,65},{65,129},{129,193},{2,66},{66,130... | collective-permute-start | bytes 3145736 | tf_op jit(solution)/shard_map/ppermute | solution.py:15
  74.1 8.6 %gather_fusion.2 = bf16[256,128,128]{2,1,0:T(8,128)(2,1)} fusion(bf16[128,32,128]{2,0,1:T(8,128)(2,1)S(1)} %copy.61, s32[1024]{0:T(1024)S(1)} %pad_clamp_fusion.5), kind=kCustom, calls=%fused_computation.2 | custom fusion | bytes 16778240 | tf_op jit(solution)/shard_map/gather | solution.py:37
  82.7 9.6 %fusion.5 = f32[32,128,128,1]{1,2,3,0:T(8,128)} fusion(bf16[128,32,8,128]{3,0,2,1:T(8,128)(2,1)} %bitcast.177, bf16[1,32,8,128,128]{4,3,2,1,0:T(8,128)(2,1)} %param.10), kind=kOutput, calls=%fused_computation.16 | convolution fusion | flops 1073741824 | bytes 18874368 | tf_op jit(solution)/shard_map/rjka,jkab->rjb/dot_general | solution.py:50
  92.3 3.2 fusion.34
  95.5 16.5 %collective-permute-start.2 = (bf16[128,4096]{0,1:T(8,128)(2,1)}, bf16[128,4096]{0,1:T(8,128)(2,1)}, u32[]{:S(2)}, u32[]{:S(2)}) collective-permute-start(bf16[128,4096]{0,1:T(8,128)(2,1)} %fusion.34), channel_id=1, source_target_pairs={{0,64},{64,128},{128,192},{1,65},{65,129},{129,193},{2,66},{66,130... | collective-permute-start | bytes 3145736 | tf_op jit(solution)/shard_map/ppermute | solution.py:15
  112.2 3.2 sort.17
  117.2 12.0 %gather_fusion.5 = bf16[256,128,128]{2,1,0:T(8,128)(2,1)} fusion(bf16[256,128,128]{2,1,0:T(8,128)(2,1)} %bitcast.166, s32[1024]{0:T(1024)S(1)} %pad_clamp_fusion.2), kind=kCustom, calls=%fused_computation.5 | custom fusion | bytes 16778240 | tf_op jit(solution)/shard_map/gather | solution.py:32
  132.5 8.6 %gather_fusion.6 = bf16[256,128,128]{2,1,0:T(8,128)(2,1)} fusion(bf16[128,32,128]{2,0,1:T(8,128)(2,1)S(1)} %copy.67, s32[1024]{0:T(1024)S(1)} %pad_clamp_fusion.5), kind=kCustom, calls=%fused_computation.6 | custom fusion | bytes 16778240 | tf_op jit(solution)/shard_map/gather | solution.py:37
  141.2 9.7 %fusion.3 = f32[32,128,128,1]{1,2,3,0:T(8,128)} fusion(bf16[128,32,8,128]{3,0,2,1:T(8,128)(2,1)} %bitcast.174, bf16[1,32,8,128,128]{4,3,2,1,0:T(8,128)(2,1)} %param.10), kind=kOutput, calls=%fused_computation.14 | convolution fusion | flops 1073741824 | bytes 18874368 | tf_op jit(solution)/shard_map/rjka,jkab->rjb/dot_general | solution.py:50
  150.8 5.8 %fusion.12 = (bf16[128,4096]{0,1:T(8,128)(2,1)}, f32[128,4096]{0,1:T(8,128)}) fusion(bf16[128,4096]{0,1:T(8,128)(2,1)S(1)} %copy.74, pred[]{:T(512)S(6)} %eq.5, f32[32,128,128,1]{1,2,3,0:T(8,128)S(1)} %copy-done.2, pred[]{:T(512)S(6)} %and.33, f32[32,128,128,1]{1,2,3,0:T(8,128)} %fusion.7, pred[]{:T(512)S(6)} %and.32, f32[32,128,128,1]{1,2,3,0:T(8,128)} %fusion.5, ...), kind=kLoop, calls=%fused_computation.29 | loop fusion | flops 7864320 | bytes 12582917 | tf_op jit(solution)/shard_map/convert_element_type | solution.py:79
  158.3 9.0 %gather_fusion.7 = bf16[256,128,128]{2,1,0:T(8,128)(2,1)} fusion(bf16[128,32,128]{2,0,1:T(8,128)(2,1)S(1)} %copy.69, s32[1024]{0:T(1024)S(1)} %pad_clamp_fusion.1), kind=kCustom, calls=%fused_computation.7 | custom fusion | bytes 16778240 | tf_op jit(solution)/shard_map/gather | solution.py:84
  167.3 8.1 %fusion.35 = f32[32,128,128,1]{2,1,3,0:T(8,128)S(1)} fusion(bf16[32,8,128,128]{3,2,1,0:T(8,128)(2,1)} %bitcast.167, bf16[128,32,8,128]{3,0,2,1:T(8,128)(2,1)} %bitcast.172), kind=kOutput, calls=%fused_computation.89 | convolution fusion | flops 1073741824 | bytes 18874368 | tf_op jit(solution)/shard_map/rckb,ckab->rca/dot_general | solution.py:85
  177.2 7.0 %collective-permute-done.3 = bf16[128,4096]{0,1:T(8,128)(2,1)S(1)} collective-permute-done((bf16[128,4096]{0,1:T(8,128)(2,1)S(1)}, bf16[128,4096]{0,1:T(8,128)(2,1)S(1)}, u32[]{:S(2)}, u32[]{:S(2)}) %collective-permute-start.3) | collective-permute-done | bytes 1048608 | tf_op jit(solution)/shard_map/ppermute | solution.py:15
  187.8 8.6 %gather_fusion.8 = bf16[256,128,128]{2,1,0:T(8,128)(2,1)} fusion(bf16[128,32,128]{2,0,1:T(8,128)(2,1)S(1)} %copy.71, s32[1024]{0:T(1024)S(1)} %pad_clamp_fusion.1), kind=kCustom, calls=%fused_computation.8 | custom fusion | bytes 16778240 | tf_op jit(solution)/shard_map/gather | solution.py:84
  196.4 8.1 %fusion.36 = f32[32,128,128,1]{2,1,3,0:T(8,128)S(1)} fusion(bf16[32,8,128,128]{3,2,1,0:T(8,128)(2,1)} %bitcast.168, bf16[128,32,8,128]{3,0,2,1:T(8,128)(2,1)} %bitcast.173), kind=kOutput, calls=%fused_computation.90 | convolution fusion | flops 1073741824 | bytes 18874368 | tf_op jit(solution)/shard_map/rckb,ckab->rca/dot_general | solution.py:85
  206.4 16.3 %collective-permute-done.4 = bf16[128,4096]{0,1:T(8,128)(2,1)S(1)} collective-permute-done((bf16[128,4096]{0,1:T(8,128)(2,1)S(1)}, bf16[128,4096]{0,1:T(8,128)(2,1)S(1)}, u32[]{:S(2)}, u32[]{:S(2)}) %collective-permute-start.4) | collective-permute-done | bytes 1048608 | tf_op jit(solution)/shard_map/ppermute | solution.py:15
  226.5 8.6 %gather_fusion.9 = bf16[256,128,128]{2,1,0:T(8,128)(2,1)} fusion(bf16[128,32,128]{2,0,1:T(8,128)(2,1)S(1)} %copy.73, s32[1024]{0:T(1024)S(1)} %pad_clamp_fusion.1), kind=kCustom, calls=%fused_computation.9 | custom fusion | bytes 16778240 | tf_op jit(solution)/shard_map/gather | solution.py:84
  235.1 8.2 %fusion.37 = f32[32,128,128,1]{2,1,3,0:T(8,128)S(1)} fusion(bf16[32,8,128,128]{3,2,1,0:T(8,128)(2,1)} %bitcast.169, bf16[128,32,8,128]{3,0,2,1:T(8,128)(2,1)} %bitcast.171), kind=kOutput, calls=%fused_computation.91 | convolution fusion | flops 1073741824 | bytes 18874368 | tf_op jit(solution)/shard_map/rckb,ckab->rca/dot_general | solution.py:85
  249.8 8.6 %gather_fusion.4 = bf16[256,128,128]{2,1,0:T(8,128)(2,1)} fusion(bf16[128,32,128]{2,0,1:T(8,128)(2,1)S(1)} %copy.65, s32[1024]{0:T(1024)S(1)} %pad_clamp_fusion.3), kind=kCustom, calls=%fused_computation.4 | custom fusion | bytes 16778240 | tf_op jit(solution)/shard_map/gather | solution.py:99
  258.4 4.3 collective-permute-done.5
  262.7 3.5 select_select_fusion
  266.9 8.6 %gather_fusion.10 = bf16[256,128,128]{2,1,0:T(8,128)(2,1)} fusion(bf16[128,32,128]{2,0,1:T(8,128)(2,1)S(1)} %copy.75, s32[1024]{0:T(1024)S(1)} %pad_clamp_fusion), kind=kCustom, calls=%fused_computation.10 | custom fusion | bytes 16778240 | tf_op jit(solution)/shard_map/gather | solution.py:101
  275.5 14.4 %fusion = f32[256,128,128]{2,1,0:T(8,128)} fusion(bf16[256,128,128]{2,1,0:T(8,128)(2,1)} %gather_fusion.10, bf16[256,128,128]{2,1,0:T(8,128)(2,1)} %gather_fusion.4), kind=kOutput, calls=%fused_computation.11 | convolution fusion | flops 1073741824 | bytes 33554432 | tf_op jit(solution)/shard_map/rpa,rpb->pab/dot_general | solution.py:102
  290.0 188.3 %reduce-scatter.4.cloned.1.call-done = f32[4096,128]{1,0:T(8,128)} async-done(((f32[32768,128]{1,0:T(8,128)}), f32[4096,128]{1,0:T(8,128)}) %reduce-scatter.4.cloned.1.call-update) | async-done | bytes 2097168 | tf_op jit(solution)/shard_map/reduce_scatter | solution.py:106
  478.3 33.4 %reduce-scatter.6.cloned.1.call-done = f32[1024,128]{1,0:T(8,128)} async-done(((f32[4096,128]{1,0:T(8,128)}), f32[1024,128]{1,0:T(8,128)}) %reduce-scatter.6.cloned.1.call-update) | async-done | bytes 524304 | tf_op jit(solution)/shard_map/reduce_scatter | solution.py:106
  511.8 20.9 %reduce-scatter.8.cloned.1.call-done = f32[512,128]{1,0:T(8,128)} async-done(((f32[1024,128]{1,0:T(8,128)}), f32[512,128]{1,0:T(8,128)}) %reduce-scatter.8.cloned.1.call-update) | async-done | bytes 262160 | tf_op jit(solution)/shard_map/reduce_scatter | solution.py:106
  (67 shorter events, 39.0 us)
Async XLA Ops:
  6.5 471.7 %reduce-scatter.4.cloned.1.call-start = ((), (), s32[]{:S(2)}) async-start(), calls=%async_computation.3 | async-start | bytes 18874368 | tf_op jit(solution)/shard_map/reduce_scatter | solution.py:106
  30.2 4.0 collective-permute-start
  55.3 16.0 %collective-permute-start.1 = (bf16[128,4096]{0,1:T(8,128)(2,1)S(1)}, bf16[128,4096]{0,1:T(8,128)(2,1)S(1)}, u32[]{:S(2)}, u32[]{:S(2)}) collective-permute-start(bf16[128,4096]{0,1:T(8,128)(2,1)S(1)} %fusion.33), channel_id=1, source_target_pairs={{0,64},{64,128},{128,192},{1,65},{65,129},{129,193},{2,66},{66,130... | collective-permute-start | bytes 3145736 | tf_op jit(solution)/shard_map/ppermute | solution.py:15
  82.7 9.6 %copy-start.3 = (bf16[128,4096]{0,1:T(8,128)(2,1)S(1)}, bf16[128,4096]{0,1:T(8,128)(2,1)}, u32[]{:S(2)}) copy-start(bf16[128,4096]{0,1:T(8,128)(2,1)} %broadcast_select_fusion.4) | copy-start | bytes 3145732
  95.5 33.7 %collective-permute-start.2 = (bf16[128,4096]{0,1:T(8,128)(2,1)}, bf16[128,4096]{0,1:T(8,128)(2,1)}, u32[]{:S(2)}, u32[]{:S(2)}) collective-permute-start(bf16[128,4096]{0,1:T(8,128)(2,1)} %fusion.34), channel_id=1, source_target_pairs={{0,64},{64,128},{128,192},{1,65},{65,129},{129,193},{2,66},{66,130... | collective-permute-start | bytes 3145736 | tf_op jit(solution)/shard_map/ppermute | solution.py:15
  141.2 9.7 %copy-start.2 = (f32[32,128,128,1]{1,2,3,0:T(8,128)S(1)}, f32[32,128,128,1]{1,2,3,0:T(8,128)}, u32[]{:S(2)}) copy-start(f32[32,128,128,1]{1,2,3,0:T(8,128)} %fusion.9) | copy-start | bytes 6291460
  175.4 8.7 %copy-start = (f32[128,4096]{0,1:T(8,128)S(1)}, f32[128,4096]{0,1:T(8,128)}, u32[]{:S(2)}) copy-start(f32[128,4096]{0,1:T(8,128)} %get-tuple-element.10) | copy-start | bytes 6291460
  175.7 8.4 %collective-permute-start.3 = (bf16[128,4096]{0,1:T(8,128)(2,1)S(1)}, bf16[128,4096]{0,1:T(8,128)(2,1)S(1)}, u32[]{:S(2)}, u32[]{:S(2)}) collective-permute-start(bf16[128,4096]{0,1:T(8,128)(2,1)S(1)} %fusion.13), channel_id=1, source_target_pairs={{64,0},{128,64},{192,128},{65,1},{129,65},{193,129},{66,2},{130,66... | collective-permute-start | bytes 3145736 | tf_op jit(solution)/shard_map/ppermute | solution.py:15
  204.5 18.2 %copy-start.1 = (f32[128,4096]{0,1:T(8,128)S(1)}, f32[128,4096]{0,1:T(8,128)}, u32[]{:S(2)}) copy-start(f32[128,4096]{0,1:T(8,128)} %get-tuple-element.10) | copy-start | bytes 6291460
  205.0 17.8 %collective-permute-start.4 = (bf16[128,4096]{0,1:T(8,128)(2,1)S(1)}, bf16[128,4096]{0,1:T(8,128)(2,1)S(1)}, u32[]{:S(2)}, u32[]{:S(2)}) collective-permute-start(bf16[128,4096]{0,1:T(8,128)(2,1)S(1)} %fusion.16), channel_id=1, source_target_pairs={{64,0},{128,64},{192,128},{65,1},{129,65},{193,129},{66,2},{130,66... | collective-permute-start | bytes 3145736 | tf_op jit(solution)/shard_map/ppermute | solution.py:15
  222.7 2.0 copy-start.4
  235.1 8.2 %copy-start.5 = (bf16[128,4096]{0,1:T(8,128)(2,1)S(1)}, bf16[128,4096]{0,1:T(8,128)(2,1)}, u32[]{:S(2)}) copy-start(bf16[128,4096]{0,1:T(8,128)(2,1)} %copy-done.4) | copy-start | bytes 3145732
  243.3 2.8 copy-start.7
  243.3 4.8 copy-start.6
  244.8 18.0 %collective-permute-start.5 = (bf16[128,4096]{0,1:T(8,128)(2,1)}, bf16[128,4096]{0,1:T(8,128)(2,1)}, u32[]{:S(2)}, u32[]{:S(2)}) collective-permute-start(bf16[128,4096]{0,1:T(8,128)(2,1)} %fusion.19), channel_id=1, source_target_pairs={{64,0},{128,64},{192,128},{65,1},{129,65},{193,129},{66,2},{130,66... | collective-permute-start | bytes 3145736 | tf_op jit(solution)/shard_map/ppermute | solution.py:15
  289.9 221.8 %reduce-scatter.6.cloned.1.call-start = ((), (), s32[]{:S(2)}) async-start(), calls=%async_computation.4 | async-start | bytes 2621440 | tf_op jit(solution)/shard_map/reduce_scatter | solution.py:106
  478.3 54.4 %reduce-scatter.8.cloned.1.call-start = ((), (), s32[]{:S(2)}) async-start(), calls=%async_computation.5 | async-start | bytes 786432 | tf_op jit(solution)/shard_map/reduce_scatter | solution.py:106
Sparse Core Ops, SparseCore 0:
  290.1 188.1 reduce-scatter.3
  480.8 30.9 reduce-scatter.5
  514.4 18.1 reduce-scatter.7

commit v2 on v1

--- a/solution.py
+++ b/solution.py
@@ -92,19 +92,23 @@
             incoming = from_behind(passed, "segment", -1)
     all_inputs = stash_x.reshape(all_rows, layer_width)
     all_grads = stash_g.reshape(all_rows, layer_width)
-    share_pairs = num_blocks * per_block // groups
     ny, nx, nz = DP_SIZES
-    order = np.arange(num_blocks * per_block).reshape(ny, nx, nz, share_pairs)
-    order = order.transpose(2, 0, 1, 3).reshape(-1)
-    picked_cols = all_inputs.reshape(all_rows, num_blocks, edge_size)[:, flat_cols[order], :]
-    grad_view = all_grads.reshape(all_rows, num_blocks, edge_size)
-    chosen = grad_view[:, order // per_block, :]
+    members = ny * nx
+    group_pairs = num_blocks * per_block // members
+    group_j = num_blocks // members
+    member = lax.axis_index("y") * nx + lax.axis_index("xlo")
+    grads_here = all_grads.reshape(all_rows, members, group_j * edge_size)
+    grads_group = lax.all_to_all(
+        grads_here, ("y", "xlo"), split_axis=1, concat_axis=0, tiled=True
+    ).reshape(members * all_rows, group_j, edge_size)
+    inputs_group = lax.all_gather(all_inputs, ("y", "xlo"), axis=0, tiled=True)
+    cols_here = lax.dynamic_slice_in_dim(flat_cols, member * group_pairs, group_pairs)
+    picked_cols = inputs_group.reshape(members * all_rows, num_blocks, edge_size)[:, cols_here, :]
+    chosen = grads_group[:, np.arange(group_pairs) // per_block, :]
     partial = jnp.einsum(
         "rpa,rpb->pab", picked_cols, chosen, preferred_element_type=jnp.float32
-    ).reshape(num_blocks * per_block * edge_size, edge_size)
-    for axis in ("z", "y", "xlo"):
-        partial = lax.psum_scatter(partial, axis, scatter_dimension=0, tiled=True)
-    own_share = partial
+    ).reshape(group_pairs * edge_size, edge_size)
+    own_share = lax.psum_scatter(partial, "z", scatter_dimension=0, tiled=True)
     summed = own_share.astype(jnp.bfloat16)
     return summed[None]
 

time: 549 us -> 461 us (0.84)
  waiting for transfers between devices: 274 us -> 182 us
  starting transfers between devices: 37.2 us -> 43.2 us
    reduce_scatter x3 -> x1, waiting for transfers between devices: 243 us -> 83.1 us  [body(): own_share = lax.psum_scatter(partial, 'z', scatter_dimension=0, tiled=True)]
    ppermute x6, waiting for transfers between devices: 31.2 us -> 88.9 us  [from_behind(): return lax.ppermute(block, axis, route)]
    reshape x0 -> x3, local copies, waits for them, and re-layouts: none -> 13.4 us  [the longest x1 12 us: body(): inputs_group.reshape(members * all_rows, num_blocks, edge_size)]
    all_to_all x0 -> x1, waiting for transfers between devices: none -> 10.2 us  [body(): lax.all_to_all(grads_here, ('y', 'xlo'), split_axis=1, concat_axis=0, til...]
    all_to_all x0 -> x1, starting transfers between devices: none -> 6.05 us  [body(): lax.all_to_all(grads_here, ('y', 'xlo'), split_axis=1, concat_axis=0, til...]
    gather x3 -> x2, local copies, waits for them, and re-layouts: 19.2 us -> 13.4 us  [the longest x1 8.41 us: body(): inputs_group.reshape(members * all_rows, num_blocks, edge_size)]
  transfers between devices with their start and end apart: 9 -> 9, of which waited for: 8 -> 7; matrix products, arithmetic and copies ran while one was open for 5% -> 23% of each run, Pallas kernels for 0% -> 0%
where the time goes in v2:
time: 461 us; the launch traced here: 455 us
  waiting for transfers between devices  182 us (39%)
  local copies, waits for them, and re-layouts  113 us (25%)
  matrix products  72.4 us (16%)
  starting transfers between devices  43.2 us (9%)
  other arithmetic  29.8 us (6%)
  between operations  14.3 us (3%)
    ppermute x6, waiting for transfers between devices, from_behind(): return lax.ppermute(block, axis, route)  88.9 us
    reduce_scatter x1, waiting for transfers between devices, body(): own_share = lax.psum_scatter(partial, 'z', scatter_dimension=0, tiled=True)  83.1 us
    dot_general x4, matrix products, body(): jnp.einsum('rjka,jkab->rjb', picked_of(current, micro_rows), weight, pref...  38.3 us
    ppermute x6, starting transfers between devices, from_behind(): return lax.ppermute(block, axis, route)  37.2 us
    gather x4, local copies, waits for them, and re-layouts, picked_of(): hidden.reshape(row_count, num_blocks, edge_size)[:, flat_cols, :]  34.5 us
    gather x3, local copies, waits for them, and re-layouts, body(): grad_pre.reshape(micro_rows, num_blocks, edge_size)[:, source_block, :]  26.1 us
    dot_general x3, matrix products, body(): jnp.einsum('rckb,ckab->rca', spread, sorted_weight, preferred_element_typ...  24.5 us
    gather x1, local copies, waits for them, and re-layouts, body(): weight.reshape(num_blocks * per_block, edge_size, edge_size)[pair_order]  12 us
  transfers between devices with their start and end apart: 9, of which 7 were waited for; matrix products, arithmetic and copies ran while one was open for 23% of the time, Pallas kernels for 0%

profile of v2, /device:TPU:2, one launch (start us, length us, event | category | flops | bytes accessed | tf_op | source)
XLA Modules:
  0.0 454.7 jit_solution(7587409888216989268)
XLA Ops:
  9.1 8.6 %gather_fusion = bf16[256,128,128]{2,1,0:T(8,128)(2,1)} fusion(bf16[128,32,128]{2,0,1:T(8,128)(2,1)S(1)} %copy.80, s32[1024]{0:T(1024)S(1)} %pad_clamp_fusion.4), kind=kCustom, calls=%fused_computation | custom fusion | bytes 16778240 | tf_op jit(solution)/shard_map/gather | solution.py:37
  17.8 9.6 %fusion.9 = f32[32,128,128,1]{1,2,3,0:T(8,128)} fusion(bf16[128,32,8,128]{3,0,2,1:T(8,128)(2,1)} %bitcast.179, bf16[1,32,8,128,128]{4,3,2,1,0:T(8,128)(2,1)} %param.8), kind=kOutput, calls=%fused_computation.19 | convolution fusion | flops 1073741824 | bytes 18874368 | tf_op jit(solution)/shard_map/rjka,jkab->rjb/dot_general | solution.py:50
  27.3 2.2 fusion.32
  34.3 8.6 %gather_fusion.1 = bf16[256,128,128]{2,1,0:T(8,128)(2,1)} fusion(bf16[128,32,128]{2,0,1:T(8,128)(2,1)S(1)} %copy.83, s32[1024]{0:T(1024)S(1)} %pad_clamp_fusion.4), kind=kCustom, calls=%fused_computation.1 | custom fusion | bytes 16778240 | tf_op jit(solution)/shard_map/gather | solution.py:37
  43.0 9.5 %fusion.7 = f32[32,128,128,1]{1,2,3,0:T(8,128)} fusion(bf16[128,32,8,128]{3,0,2,1:T(8,128)(2,1)} %bitcast.180, bf16[1,32,8,128,128]{4,3,2,1,0:T(8,128)(2,1)} %param.8), kind=kOutput, calls=%fused_computation.17 | convolution fusion | flops 1073741824 | bytes 18874368 | tf_op jit(solution)/shard_map/rjka,jkab->rjb/dot_general | solution.py:50
  54.6 14.4 %collective-permute-start.1 = (bf16[128,4096]{0,1:T(8,128)(2,1)S(1)}, bf16[128,4096]{0,1:T(8,128)(2,1)S(1)}, u32[]{:S(2)}, u32[]{:S(2)}) collective-permute-start(bf16[128,4096]{0,1:T(8,128)(2,1)S(1)} %fusion.33), channel_id=1, source_target_pairs={{0,64},{64,128},{128,192},{1,65},{65,129},{129,193},{2,66},{66,130... | collective-permute-start | bytes 3145736 | tf_op jit(solution)/shard_map/ppermute | solution.py:15
  73.4 8.6 %gather_fusion.2 = bf16[256,128,128]{2,1,0:T(8,128)(2,1)} fusion(bf16[128,32,128]{2,0,1:T(8,128)(2,1)S(1)} %copy.86, s32[1024]{0:T(1024)S(1)} %pad_clamp_fusion.4), kind=kCustom, calls=%fused_computation.2 | custom fusion | bytes 16778240 | tf_op jit(solution)/shard_map/gather | solution.py:37
  82.0 9.6 %fusion.5 = f32[32,128,128,1]{1,2,3,0:T(8,128)} fusion(bf16[128,32,8,128]{3,0,2,1:T(8,128)(2,1)} %bitcast.181, bf16[1,32,8,128,128]{4,3,2,1,0:T(8,128)(2,1)} %param.8), kind=kOutput, calls=%fused_computation.15 | convolution fusion | flops 1073741824 | bytes 18874368 | tf_op jit(solution)/shard_map/rjka,jkab->rjb/dot_general | solution.py:50
  91.7 3.1 fusion.34
  94.8 16.5 %collective-permute-start.2 = (bf16[128,4096]{0,1:T(8,128)(2,1)}, bf16[128,4096]{0,1:T(8,128)(2,1)}, u32[]{:S(2)}, u32[]{:S(2)}) collective-permute-start(bf16[128,4096]{0,1:T(8,128)(2,1)} %fusion.34), channel_id=1, source_target_pairs={{0,64},{64,128},{128,192},{1,65},{65,129},{129,193},{2,66},{66,130... | collective-permute-start | bytes 3145736 | tf_op jit(solution)/shard_map/ppermute | solution.py:15
  113.0 3.2 sort.17
  116.4 12.0 %gather_fusion.4 = bf16[256,128,128]{2,1,0:T(8,128)(2,1)} fusion(bf16[256,128,128]{2,1,0:T(8,128)(2,1)} %bitcast.171, s32[1024]{0:T(1024)S(1)} %pad_clamp_fusion.2), kind=kCustom, calls=%fused_computation.4 | custom fusion | bytes 16778240 | tf_op jit(solution)/shard_map/gather | solution.py:32
  131.6 8.6 %gather_fusion.5 = bf16[256,128,128]{2,1,0:T(8,128)(2,1)} fusion(bf16[128,32,128]{2,0,1:T(8,128)(2,1)S(1)} %copy.92, s32[1024]{0:T(1024)S(1)} %pad_clamp_fusion.4), kind=kCustom, calls=%fused_computation.5 | custom fusion | bytes 16778240 | tf_op jit(solution)/shard_map/gather | solution.py:37
  140.3 9.6 %fusion.3 = f32[32,128,128,1]{1,2,3,0:T(8,128)} fusion(bf16[128,32,8,128]{3,0,2,1:T(8,128)(2,1)} %bitcast.178, bf16[1,32,8,128,128]{4,3,2,1,0:T(8,128)(2,1)} %param.8), kind=kOutput, calls=%fused_computation.13 | convolution fusion | flops 1073741824 | bytes 18874368 | tf_op jit(solution)/shard_map/rjka,jkab->rjb/dot_general | solution.py:50
  149.9 5.7 %fusion.12 = (bf16[128,4096]{0,1:T(8,128)(2,1)}, f32[128,4096]{0,1:T(8,128)}) fusion(bf16[128,4096]{0,1:T(8,128)(2,1)S(1)} %copy.99, pred[]{:T(512)S(6)} %eq.5, f32[32,128,128,1]{1,2,3,0:T(8,128)S(1)} %copy-done.3, pred[]{:T(512)S(6)} %and.35, f32[32,128,128,1]{1,2,3,0:T(8,128)} %fusion.7, pred[]{:T(512)S(6)} %and.34, f32[32,128,128,1]{1,2,3,0:T(8,128)} %fusion.5, ...), kind=kLoop, calls=%fused_computation.28 | loop fusion | flops 7864320 | bytes 12582917 | tf_op jit(solution)/shard_map/convert_element_type | solution.py:79
  157.3 8.8 %gather_fusion.6 = bf16[256,128,128]{2,1,0:T(8,128)(2,1)} fusion(bf16[128,32,128]{2,0,1:T(8,128)(2,1)S(1)} %copy.94, s32[1024]{0:T(1024)S(1)} %pad_clamp_fusion.1), kind=kCustom, calls=%fused_computation.6 | custom fusion | bytes 16778240 | tf_op jit(solution)/shard_map/gather | solution.py:84
  166.1 8.1 %fusion.35 = f32[32,128,128,1]{2,1,3,0:T(8,128)S(1)} fusion(bf16[32,8,128,128]{3,2,1,0:T(8,128)(2,1)} %bitcast.172, bf16[128,32,8,128]{3,0,2,1:T(8,128)(2,1)} %bitcast.176), kind=kOutput, calls=%fused_computation.87 | convolution fusion | flops 1073741824 | bytes 18874368 | tf_op jit(solution)/shard_map/rckb,ckab->rca/dot_general | solution.py:85
  175.9 7.2 %collective-permute-done.3 = bf16[128,4096]{0,1:T(8,128)(2,1)S(1)} collective-permute-done((bf16[128,4096]{0,1:T(8,128)(2,1)S(1)}, bf16[128,4096]{0,1:T(8,128)(2,1)S(1)}, u32[]{:S(2)}, u32[]{:S(2)}) %collective-permute-start.3) | collective-permute-done | bytes 1048608 | tf_op jit(solution)/shard_map/ppermute | solution.py:15
  186.6 8.6 %gather_fusion.7 = bf16[256,128,128]{2,1,0:T(8,128)(2,1)} fusion(bf16[128,32,128]{2,0,1:T(8,128)(2,1)S(1)} %copy.96, s32[1024]{0:T(1024)S(1)} %pad_clamp_fusion.1), kind=kCustom, calls=%fused_computation.7 | custom fusion | bytes 16778240 | tf_op jit(solution)/shard_map/gather | solution.py:84
  195.3 8.2 %fusion.36 = f32[32,128,128,1]{2,1,3,0:T(8,128)S(1)} fusion(bf16[32,8,128,128]{3,2,1,0:T(8,128)(2,1)} %bitcast.173, bf16[128,32,8,128]{3,0,2,1:T(8,128)(2,1)} %bitcast.177), kind=kOutput, calls=%fused_computation.88 | convolution fusion | flops 1073741824 | bytes 18874368 | tf_op jit(solution)/shard_map/rckb,ckab->rca/dot_general | solution.py:85
  205.3 39.1 %collective-permute-done.4 = bf16[128,4096]{0,1:T(8,128)(2,1)S(1)} collective-permute-done((bf16[128,4096]{0,1:T(8,128)(2,1)S(1)}, bf16[128,4096]{0,1:T(8,128)(2,1)S(1)}, u32[]{:S(2)}, u32[]{:S(2)}) %collective-permute-start.4) | collective-permute-done | bytes 1048608 | tf_op jit(solution)/shard_map/ppermute | solution.py:15
  246.4 8.6 %gather_fusion.8 = bf16[256,128,128]{2,1,0:T(8,128)(2,1)} fusion(bf16[128,32,128]{2,0,1:T(8,128)(2,1)S(1)} %copy.98, s32[1024]{0:T(1024)S(1)} %pad_clamp_fusion.1), kind=kCustom, calls=%fused_computation.8 | custom fusion | bytes 16778240 | tf_op jit(solution)/shard_map/gather | solution.py:84
  255.0 8.2 %fusion.37 = f32[32,128,128,1]{2,1,3,0:T(8,128)S(1)} fusion(bf16[32,8,128,128]{3,2,1,0:T(8,128)(2,1)} %bitcast.174, bf16[128,32,8,128]{3,0,2,1:T(8,128)(2,1)} %bitcast.175), kind=kOutput, calls=%fused_computation.89 | convolution fusion | flops 1073741824 | bytes 18874368 | tf_op jit(solution)/shard_map/rckb,ckab->rca/dot_general | solution.py:85
  265.9 39.1 %collective-permute-done.5 = bf16[128,4096]{0,1:T(8,128)(2,1)} collective-permute-done((bf16[128,4096]{0,1:T(8,128)(2,1)}, bf16[128,4096]{0,1:T(8,128)(2,1)}, u32[]{:S(2)}, u32[]{:S(2)}) %collective-permute-start.5) | collective-permute-done | bytes 1048608 | tf_op jit(solution)/shard_map/ppermute | solution.py:15
  305.0 4.1 select_select_fusion
  309.1 6.1 %all-to-all-start = ((bf16[128,8,512]{0,2,1:T(8,128)(2,1)}), bf16[128,8,512]{0,2,1:T(8,128)(2,1)S(1)}, u32[]{:S(2)}, u32[]{:S(2)}) async-start(bf16[128,8,512]{0,2,1:T(8,128)(2,1)} %bitcast.188), calls=%async_computation | async-start | bytes 2097152 | tf_op jit(solution)/shard_map/all_to_all | solution.py:101
  315.2 10.2 %all-to-all-done = bf16[128,8,512]{0,2,1:T(8,128)(2,1)S(1)} async-done(((bf16[128,8,512]{0,2,1:T(8,128)(2,1)}), bf16[128,8,512]{0,2,1:T(8,128)(2,1)S(1)}, u32[]{:S(2)}, u32[]{:S(2)}) %all-to-all-start) | async-done | bytes 1048608 | tf_op jit(solution)/shard_map/all_to_all | solution.py:101
  327.6 5.0 %gather_fusion.9 = bf16[32,1024,128]{2,1,0:T(8,128)(2,1)} fusion(bf16[1024,4,128]{2,0,1:T(8,128)(2,1)S(1)} %copy.101, s32[1024]{0:T(1024)S(1)} %pad_clamp_fusion), kind=kCustom, calls=%fused_computation.9 | custom fusion | bytes 16777344 | tf_op jit(solution)/shard_map/gather | solution.py:107
  332.7 12.0 %copy.90 = bf16[1024,32,128]{2,0,1:T(8,128)(2,1)} copy(bf16[1024,32,128]{0,2,1:T(8,128)(2,1)} %bitcast.185) | data formatting | bytes 16777216 | tf_op jit(solution)/shard_map/reshape | solution.py:106
  344.6 8.4 %gather_fusion.3 = bf16[32,1024,128]{2,1,0:T(8,128)(2,1)} fusion(bf16[1024,32,128]{2,0,1:T(8,128)(2,1)} %copy.90, s32[1024]{0:T(1024)S(1)} %pad_clamp_fusion.3), kind=kCustom, calls=%fused_computation.3 | custom fusion | bytes 16777344 | tf_op jit(solution)/shard_map/gather | solution.py:106
  353.0 9.6 %fusion = f32[32,128,128]{2,1,0:T(8,128)} fusion(bf16[32,1024,128]{2,1,0:T(8,128)(2,1)} %gather_fusion.9, bf16[32,1024,128]{2,1,0:T(8,128)(2,1)} %gather_fusion.3), kind=kOutput, calls=%fused_computation.10 | convolution fusion | flops 1073741824 | bytes 18874368 | tf_op jit(solution)/shard_map/rpa,rpb->pab/dot_general | solution.py:108
  362.6 83.1 %reduce-scatter.2.cloned.1.call-done = f32[512,128]{1,0:T(8,128)} async-done(((f32[4096,128]{1,0:T(8,128)}), f32[512,128]{1,0:T(8,128)}) %reduce-scatter.2.cloned.1.call-update) | async-done | bytes 262160 | tf_op jit(solution)/shard_map/reduce_scatter | solution.py:111
  (70 shorter events, 35.9 us)
Async XLA Ops:
  6.5 326.1 %all-gather.2.cloned.1.call-start = ((), (), s32[]{:S(2)}) async-start(), calls=%async_computation.2 | async-start | bytes 9437184 | tf_op jit(solution)/shard_map/all_gather | solution.py:104
  8.2 0.8 copy-start.8
  29.5 4.0 collective-permute-start
  54.6 16.0 %collective-permute-start.1 = (bf16[128,4096]{0,1:T(8,128)(2,1)S(1)}, bf16[128,4096]{0,1:T(8,128)(2,1)S(1)}, u32[]{:S(2)}, u32[]{:S(2)}) collective-permute-start(bf16[128,4096]{0,1:T(8,128)(2,1)S(1)} %fusion.33), channel_id=1, source_target_pairs={{0,64},{64,128},{128,192},{1,65},{65,129},{129,193},{2,66},{66,130... | collective-permute-start | bytes 3145736 | tf_op jit(solution)/shard_map/ppermute | solution.py:15
  82.0 9.6 %copy-start.4 = (bf16[128,4096]{0,1:T(8,128)(2,1)S(1)}, bf16[128,4096]{0,1:T(8,128)(2,1)}, u32[]{:S(2)}) copy-start(bf16[128,4096]{0,1:T(8,128)(2,1)} %broadcast_select_fusion.4) | copy-start | bytes 3145732
  94.8 33.7 %collective-permute-start.2 = (bf16[128,4096]{0,1:T(8,128)(2,1)}, bf16[128,4096]{0,1:T(8,128)(2,1)}, u32[]{:S(2)}, u32[]{:S(2)}) collective-permute-start(bf16[128,4096]{0,1:T(8,128)(2,1)} %fusion.34), channel_id=1, source_target_pairs={{0,64},{64,128},{128,192},{1,65},{65,129},{129,193},{2,66},{66,130... | collective-permute-start | bytes 3145736 | tf_op jit(solution)/shard_map/ppermute | solution.py:15
  140.3 9.6 %copy-start.3 = (f32[32,128,128,1]{1,2,3,0:T(8,128)S(1)}, f32[32,128,128,1]{1,2,3,0:T(8,128)}, u32[]{:S(2)}) copy-start(f32[32,128,128,1]{1,2,3,0:T(8,128)} %fusion.9) | copy-start | bytes 6291460
  174.2 8.9 %copy-start = (f32[128,4096]{0,1:T(8,128)S(1)}, f32[128,4096]{0,1:T(8,128)}, u32[]{:S(2)}) copy-start(f32[128,4096]{0,1:T(8,128)} %get-tuple-element.10) | copy-start | bytes 6291460
  174.5 8.6 %collective-permute-start.3 = (bf16[128,4096]{0,1:T(8,128)(2,1)S(1)}, bf16[128,4096]{0,1:T(8,128)(2,1)S(1)}, u32[]{:S(2)}, u32[]{:S(2)}) collective-permute-start(bf16[128,4096]{0,1:T(8,128)(2,1)S(1)} %fusion.13), channel_id=1, source_target_pairs={{64,0},{128,64},{192,128},{65,1},{129,65},{193,129},{66,2},{130,66... | collective-permute-start | bytes 3145736 | tf_op jit(solution)/shard_map/ppermute | solution.py:15
  183.1 20.4 %copy-start.5 = (bf16[128,4096]{0,1:T(8,128)(2,1)}, bf16[128,4096]{0,1:T(8,128)(2,1)S(1)}, u32[]{:S(2)}) copy-start(bf16[128,4096]{0,1:T(8,128)(2,1)S(1)} %collective-permute-done.3) | copy-start | bytes 3145732
  203.5 41.0 %copy-start.1 = (f32[128,4096]{0,1:T(8,128)S(1)}, f32[128,4096]{0,1:T(8,128)}, u32[]{:S(2)}) copy-start(f32[128,4096]{0,1:T(8,128)} %get-tuple-element.10) | copy-start | bytes 6291460
  203.9 40.6 %collective-permute-start.4 = (bf16[128,4096]{0,1:T(8,128)(2,1)S(1)}, bf16[128,4096]{0,1:T(8,128)(2,1)S(1)}, u32[]{:S(2)}, u32[]{:S(2)}) collective-permute-start(bf16[128,4096]{0,1:T(8,128)(2,1)S(1)} %fusion.16), channel_id=1, source_target_pairs={{64,0},{128,64},{192,128},{65,1},{129,65},{193,129},{66,2},{130,66... | collective-permute-start | bytes 3145736 | tf_op jit(solution)/shard_map/ppermute | solution.py:15
  244.5 1.0 copy-start.6
  255.0 8.2 %copy-start.7 = (bf16[128,4096]{0,1:T(8,128)(2,1)S(1)}, bf16[128,4096]{0,1:T(8,128)(2,1)}, u32[]{:S(2)}) copy-start(bf16[128,4096]{0,1:T(8,128)(2,1)} %copy-done.6) | copy-start | bytes 3145732
  263.2 41.8 %copy-start.2 = (f32[128,4096]{0,1:T(8,128)S(1)}, f32[128,4096]{0,1:T(8,128)}, u32[]{:S(2)}) copy-start(f32[128,4096]{0,1:T(8,128)} %get-tuple-element.10) | copy-start | bytes 6291460
  264.5 40.5 %collective-permute-start.5 = (bf16[128,4096]{0,1:T(8,128)(2,1)}, bf16[128,4096]{0,1:T(8,128)(2,1)}, u32[]{:S(2)}, u32[]{:S(2)}) collective-permute-start(bf16[128,4096]{0,1:T(8,128)(2,1)} %fusion.19), channel_id=1, source_target_pairs={{64,0},{128,64},{192,128},{65,1},{129,65},{193,129},{66,2},{130,66... | collective-permute-start | bytes 3145736 | tf_op jit(solution)/shard_map/ppermute | solution.py:15
  309.1 6.1 %copy-start.9 = (s32[32]{0:T(128)S(1)}, s32[32]{0:T(128)}, u32[]{:S(2)}) copy-start(s32[32]{0:T(128)} %constant.142) | copy-start | bytes 388
  309.1 16.4 %all-to-all-start = ((bf16[128,8,512]{0,2,1:T(8,128)(2,1)}), bf16[128,8,512]{0,2,1:T(8,128)(2,1)S(1)}, u32[]{:S(2)}, u32[]{:S(2)}) async-start(bf16[128,8,512]{0,2,1:T(8,128)(2,1)} %bitcast.188), calls=%async_computation | async-start | bytes 2097152 | tf_op jit(solution)/shard_map/all_to_all | solution.py:101
  315.1 130.6 %reduce-scatter.2.cloned.1.call-start = ((), (), s32[]{:S(2)}) async-start(), calls=%async_computation.3 | async-start | bytes 2359296 | tf_op jit(solution)/shard_map/reduce_scatter | solution.py:111
Sparse Core Ops, SparseCore 0:
  140.4 175.9 all-gather.1
  362.8 82.9 reduce-scatter.1

commit v3 on v2

v3 whole, which is shorter than its diff:
```python
import functools

import jax
import jax.numpy as jnp
import numpy as np
from jax import lax
from jax.experimental import pallas as pl
from jax.experimental.pallas import tpu as pltpu
from jax.sharding import Mesh, PartitionSpec as P

DP_AXES = ("y", "xlo", "z")
DP_SIZES = (4, 2, 8)
JB = 4


def from_behind(block, axis, distance):
    devices = range(lax.axis_size(axis))
    route = [(i - distance, i) for i in devices if i - distance in devices]
    return lax.ppermute(block, axis, route)


def forward_kernel(cols_ref, h_ref, w_ref, z_ref, out_ref):
    edge = w_ref.shape[-1]
    per_block = w_ref.shape[1]
    step = pl.program_id(0)
    for jj in range(w_ref.shape[0]):
        j = step * w_ref.shape[0] + jj
        acc = None
        for k in range(per_block):
            c = cols_ref[j * per_block + k]
            x = h_ref[:, pl.ds(pl.multiple_of(c * edge, edge), edge)]
            part = jnp.dot(x, w_ref[jj, k], preferred_element_type=jnp.float32)
            acc = part if acc is None else acc + part
        z_ref[:, jj * edge:(jj + 1) * edge] = acc
        own = h_ref[:, pl.ds(pl.multiple_of(j * edge, edge), edge)].astype(jnp.float32)
        out_ref[:, jj * edge:(jj + 1) * edge] = (own + acc * jax.nn.sigmoid(acc)).astype(out_ref.dtype)


def backward_kernel(cols_ref, up_ref, z_ref, w_ref, g_ref, new_ref, back_ref):
    edge = w_ref.shape[-1]
    per_block = w_ref.shape[1]
    step = pl.program_id(0)

    @pl.when(step == 0)
    def _():
        back_ref[...] = jnp.zeros_like(back_ref)

    for jj in range(w_ref.shape[0]):
        j = step * w_ref.shape[0] + jj
        z = z_ref[:, jj * edge:(jj + 1) * edge]
        u = up_ref[:, pl.ds(pl.multiple_of(j * edge, edge), edge)].astype(jnp.float32)
        s = jax.nn.sigmoid(z)
        g = (u * s * (1.0 + z * (1.0 - s))).astype(jnp.bfloat16)
        g_ref[:, jj * edge:(jj + 1) * edge] = g
        for k in range(per_block):
            c = cols_ref[j * per_block + k]
            contrib = lax.dot_general(
                g, w_ref[jj, k], (((1,), (1,)), ((), ())), preferred_element_type=jnp.float32
            )
            at = pl.ds(pl.multiple_of(c * edge, edge), edge)
            back_ref[:, at] = back_ref[:, at] + contrib

    @pl.when(step == pl.num_programs(0) - 1)
    def _():
        new_ref[...] = (up_ref[...].astype(jnp.float32) + back_ref[...]).astype(new_ref.dtype)


def layer_forward(cols, hidden, weight):
    rows, width = hidden.shape
    num_blocks, per_block, edge, _ = weight.shape
    grid = pltpu.PrefetchScalarGridSpec(
        num_scalar_prefetch=1,
        grid=(num_blocks // JB,),
        in_specs=[
            pl.BlockSpec((rows, width), lambda i, c: (0, 0)),
            pl.BlockSpec((JB, per_block, edge, edge), lambda i, c: (i, 0, 0, 0)),
        ],
        out_specs=[
            pl.BlockSpec((rows, JB * edge), lambda i, c: (0, i)),
            pl.BlockSpec((rows, JB * edge), lambda i, c: (0, i)),
        ],
    )
    flops = 2 * rows * num_blocks * per_block * edge * edge
    return pl.pallas_call(
        forward_kernel,
        grid_spec=grid,
        out_shape=[
            jax.ShapeDtypeStruct((rows, width), jnp.float32),
            jax.ShapeDtypeStruct((rows, width), hidden.dtype),
        ],
        compiler_params=pltpu.CompilerParams(dimension_semantics=("arbitrary",)),
        cost_estimate=pl.CostEstimate(
            flops=flops, transcendentals=rows * width, bytes_accessed=weight.size * 2 + rows * width * 8
        ),
    )(cols, hidden, weight)


def layer_backward(cols, upstream, preact, weight):
    rows, width = upstream.shape
    num_blocks, per_block, edge, _ = weight.shape
    grid = pltpu.PrefetchScalarGridSpec(
        num_scalar_prefetch=1,
        grid=(num_blocks // JB,),
        in_specs=[
            pl.BlockSpec((rows, width), lambda i, c: (0, 0)),
            pl.BlockSpec((rows, JB * edge), lambda i, c: (0, i)),
            pl.BlockSpec((JB, per_block, edge, edge), lambda i, c: (i, 0, 0, 0)),
        ],
        out_specs=[
            pl.BlockSpec((rows, JB * edge), lambda i, c: (0, i)),
            pl.BlockSpec((rows, width), lambda i, c: (0, 0)),
        ],
        scratch_shapes=[pltpu.VMEM((rows, width), jnp.float32)],
    )
    flops = 2 * rows * num_blocks * per_block * edge * edge
    return pl.pallas_call(
        backward_kernel,
        grid_spec=grid,
        out_shape=[
            jax.ShapeDtypeStruct((rows, width), jnp.bfloat16),
            jax.ShapeDtypeStruct((rows, width), upstream.dtype),
        ],
        compiler_params=pltpu.CompilerParams(dimension_semantics=("arbitrary",)),
        cost_estimate=pl.CostEstimate(
            flops=flops, transcendentals=rows * width, bytes_accessed=weight.size * 2 + rows * width * 10
        ),
    )(cols, upstream, preact, weight)


def body(inputs, cotangent, blocks, block_cols):
    segments = lax.axis_size("segment")
    segment_index = lax.axis_index("segment")
    weight = blocks[0]
    num_blocks, per_block, edge_size = (weight.shape[0], weight.shape[1], weight.shape[2])
    all_rows, layer_width = inputs.shape
    flat_cols = block_cols[0].reshape(-1)

    stash_x = jnp.zeros((all_rows, layer_width), jnp.bfloat16)
    stash_z = jnp.zeros((all_rows, layer_width), jnp.float32)
    arrived = jnp.zeros((all_rows, layer_width), jnp.bfloat16)
    for step_now in range(segments):
        active = segment_index == step_now
        current = jnp.where(segment_index == 0, inputs, arrived)
        preact, result = layer_forward(flat_cols, current, weight)
        stash_x = jnp.where(active, current, stash_x)
        stash_z = jnp.where(active, preact, stash_z)
        if step_now + 1 < segments:
            arrived = from_behind(result, "segment", 1)
    stash_g = jnp.zeros((all_rows, layer_width), jnp.bfloat16)
    incoming = jnp.zeros((all_rows, layer_width), jnp.bfloat16)
    for step_now in range(segments):
        active = segment_index == segments - 1 - step_now
        upstream = jnp.where(segment_index == segments - 1, cotangent, incoming)
        grad_pre, passed = layer_backward(flat_cols, upstream, stash_z, weight)
        stash_g = jnp.where(active, grad_pre, stash_g)
        if step_now + 1 < segments:
            incoming = from_behind(passed, "segment", -1)
    all_inputs = stash_x
    all_grads = stash_g
    ny, nx, nz = DP_SIZES
    members = ny * nx
    group_pairs = num_blocks * per_block // members
    group_j = num_blocks // members
    member = lax.axis_index("y") * nx + lax.axis_index("xlo")
    grads_here = all_grads.reshape(all_rows, members, group_j * edge_size)
    grads_group = lax.all_to_all(
        grads_here, ("y", "xlo"), split_axis=1, concat_axis=0, tiled=True
    ).reshape(members * all_rows, group_j, edge_size)
    inputs_group = lax.all_gather(all_inputs, ("y", "xlo"), axis=0, tiled=True)
    cols_here = lax.dynamic_slice_in_dim(flat_cols, member * group_pairs, group_pairs)
    picked_cols = inputs_group.reshape(members * all_rows, num_blocks, edge_size)[:, cols_here, :]
    chosen = grads_group[:, np.arange(group_pairs) // per_block, :]
    partial = jnp.einsum(
        "rpa,rpb->pab", picked_cols, chosen, preferred_element_type=jnp.float32
    ).reshape(group_pairs * edge_size, edge_size)
    own_share = lax.psum_scatter(partial, "z", scatter_dimension=0, tiled=True)
    summed = own_share.astype(jnp.bfloat16)
    return summed[None]


def solution(mesh):
    fine = Mesh(mesh.devices.reshape(mesh.shape["segment"], *DP_SIZES), ("segment",) + DP_AXES)
    return jax.shard_map(
        body,
        mesh=fine,
        in_specs=(
            P(DP_AXES, None),
            P(DP_AXES, None),
            P("segment", None, None, None, None),
            P("segment", None, None),
        ),
        out_specs=P("segment", DP_AXES, None),
        check_vma=False,
    )
```

time: 461 us -> 404 us (0.88)
  Pallas kernels: 0 us -> 90.2 us
  local copies, waits for them, and re-layouts: 113 us -> 27.2 us
  matrix products: 72.4 us -> 9.58 us
  waiting for transfers between devices: 182 us -> 205 us
  other arithmetic: 29.8 us -> 15.6 us
    pallas_call x0 -> x8, Pallas kernels: none -> 90.2 us  [the longest x4 50 us: layer_backward(): pl.pallas_call(backward_kernel, grid_spec=grid, out_shape=[jax.ShapeDtype...]
    gather x8 -> x0, local copies, waits for them, and re-layouts: 72.7 us -> none  [the longest x4 34.5 us: picked_of(): hidden.reshape(row_count, num_blocks, edge_size)[:, flat_cols, :]]
    dot_general x7 -> x0, matrix products: 62.8 us -> none  [the longest x4 38.3 us: body(): jnp.einsum('rjka,jkab->rjb', picked_of(current, micro_rows), weight, pref...]
    convert_element_type x9 -> x0, other arithmetic: 17.9 us -> none  [the longest x3 8.52 us: body(): grad_pre = (upstream.astype(jnp.float32) * sigmoid_z * (1.0 + preact * (1...]
    ppermute x6, waiting for transfers between devices: 88.9 us -> 105 us  [from_behind(): return lax.ppermute(block, axis, route)]
    reshape x8 -> x1, local copies, waits for them, and re-layouts: 8.76 us -> 1.37 us  [body(): grads_here = all_grads.reshape(all_rows, members, group_j * edge_size)]
    all_to_all x1, waiting for transfers between devices: 10.2 us -> 17.2 us  [body(): lax.all_to_all(grads_here, ('y', 'xlo'), split_axis=1, concat_axis=0, til...]
    select_n x8 -> x10, other arithmetic: 6.94 us -> 13.9 us  [the longest x3 4.54 us: body(): current = jnp.where(segment_index == 0, inputs, arrived)]
  transfers between devices with their start and end apart: 9 -> 9, of which waited for: 7 -> 8; matrix products, arithmetic and copies ran while one was open for 23% -> 4% of each run, Pallas kernels for 0% -> 15%
where the time goes in v3:
time: 404 us; the launch traced here: 402 us
  waiting for transfers between devices  205 us (51%)
  Pallas kernels  90.2 us (22%)
  starting transfers between devices  40.8 us (10%)
  local copies, waits for them, and re-layouts  27.2 us (7%)
  other arithmetic  15.6 us (4%)
  between operations  13.5 us (3%)
  matrix products  9.58 us (2%)
    ppermute x6, waiting for transfers between devices, from_behind(): return lax.ppermute(block, axis, route)  105 us
    reduce_scatter x1, waiting for transfers between devices, body(): own_share = lax.psum_scatter(partial, 'z', scatter_dimension=0, tiled=True)  82.7 us
    pallas_call x4, Pallas kernels, layer_backward(): pl.pallas_call(backward_kernel, grid_spec=grid, out_shape=[jax.ShapeDtype...  50 us
    pallas_call x4, Pallas kernels, layer_forward(): pl.pallas_call(forward_kernel, grid_spec=grid, out_shape=[jax.ShapeDtypeS...  40.1 us
    ppermute x6, starting transfers between devices, from_behind(): return lax.ppermute(block, axis, route)  34.9 us
    all_to_all x1, waiting for transfers between devices, body(): lax.all_to_all(grads_here, ('y', 'xlo'), split_axis=1, concat_axis=0, til...  17.2 us
    dot_general x1, matrix products, body(): jnp.einsum('rpa,rpb->pab', picked_cols, chosen, preferred_element_type=jn...  9.58 us
    reshape x1, local copies, waits for them, and re-layouts, body(): inputs_group.reshape(members * all_rows, num_blocks, edge_size)  9 us
  transfers between devices with their start and end apart: 9, of which 8 were waited for; matrix products, arithmetic and copies ran while one was open for 4% of the time, Pallas kernels for 15%

profile of v3, /device:TPU:2, one launch (start us, length us, event | category | flops | bytes accessed | tf_op | source)
XLA Modules:
  0.0 402.3 jit_solution(16390164822331527445)
XLA Ops:
  8.0 2.3 broadcast_select_fusion.3.h_ref
  10.4 10.0 %shard_map.64 = (f32[128,4096]{1,0:T(8,128)}, bf16[128,4096]{1,0:T(8,128)(2,1)}) custom-call(s32[256]{0:T(256)} %reshape_squeeze.3.cols_ref, bf16[128,4096]{1,0:T(8,128)(2,1)} %broadcast_select_fusion.3.h_ref, bf16[32,8,128,128]{3,2,1,0:T(8,128)(2,1)} %bitcast.23), custom_call_target="tpu_custom_call" | custom-call | flops 1073741824 | bytes 12582912 | tf_op jit(solution)/shard_map/pallas_call | solution.py:84
  20.4 1.3 collective-permute-start
  21.7 2.4 collective-permute-done
  25.3 10.0 %shard_map.65 = (f32[128,4096]{1,0:T(8,128)}, bf16[128,4096]{1,0:T(8,128)(2,1)}) custom-call(s32[256]{0:T(256)} %reshape_squeeze.3.cols_ref, bf16[128,4096]{1,0:T(8,128)(2,1)} %broadcast_select_fusion.2.h_ref, bf16[32,8,128,128]{3,2,1,0:T(8,128)(2,1)} %bitcast.24), custom_call_target="tpu_custom_call" | custom-call | flops 1073741824 | bytes 12582912 | tf_op jit(solution)/shard_map/pallas_call | solution.py:84
  35.3 13.3 %collective-permute-start.1 = (bf16[128,4096]{1,0:T(8,128)(2,1)}, bf16[128,4096]{1,0:T(8,128)(2,1)S(1)}, u32[]{:S(2)}, u32[]{:S(2)}) collective-permute-start(bf16[128,4096]{1,0:T(8,128)(2,1)} %get-tuple-element.20), channel_id=1, source_target_pairs={{0,64},{64,128},{128,192},{1,65},{65,129},{129,193},{2,66},{66,130... | collective-permute-start | bytes 3145736 | tf_op jit(solution)/shard_map/ppermute | solution.py:19
  48.6 2.4 collective-permute-done.1
  52.1 10.2 %shard_map.66 = (f32[128,4096]{1,0:T(8,128)}, bf16[128,4096]{1,0:T(8,128)(2,1)}) custom-call(s32[256]{0:T(256)} %reshape_squeeze.3.cols_ref, bf16[128,4096]{1,0:T(8,128)(2,1)} %broadcast_select_fusion.1.h_ref, bf16[32,8,128,128]{3,2,1,0:T(8,128)(2,1)} %bitcast.25), custom_call_target="tpu_custom_call" | custom-call | flops 1073741824 | bytes 12582912 | tf_op jit(solution)/shard_map/pallas_call | solution.py:84
  62.2 16.3 %collective-permute-start.2 = (bf16[128,4096]{1,0:T(8,128)(2,1)}, bf16[128,4096]{1,0:T(8,128)(2,1)}, u32[]{:S(2)}, u32[]{:S(2)}) collective-permute-start(bf16[128,4096]{1,0:T(8,128)(2,1)} %get-tuple-element.21), channel_id=1, source_target_pairs={{0,64},{64,128},{128,192},{1,65},{65,129},{129,193},{2,66},{66,130... | collective-permute-start | bytes 3145736 | tf_op jit(solution)/shard_map/ppermute | solution.py:19
  78.5 1.6 collective-permute-done.2
  80.2 1.6 select_select_fusion.2
  82.8 10.0 %shard_map.67 = (f32[128,4096]{1,0:T(8,128)}, bf16[128,4096]{1,0:T(8,128)(2,1)}) custom-call(s32[256]{0:T(256)} %reshape_squeeze.3.cols_ref, bf16[128,4096]{1,0:T(8,128)(2,1)} %get-tuple-element.34.h_ref, bf16[32,8,128,128]{3,2,1,0:T(8,128)(2,1)} %bitcast.26), custom_call_target="tpu_custom_call" | custom-call | flops 1073741824 | bytes 12582912 | tf_op jit(solution)/shard_map/pallas_call | solution.py:84
  92.8 2.0 select_select_fusion.z_ref
  94.8 12.5 %shard_map.68 = (bf16[128,4096]{1,0:T(8,128)(2,1)}, bf16[128,4096]{1,0:T(8,128)(2,1)}) custom-call(s32[256]{0:T(256)} %reshape_squeeze.3.cols_ref, bf16[128,4096]{1,0:T(8,128)(2,1)} %broadcast_select_fusion.7.up_ref, f32[128,4096]{1,0:T(8,128)} %select_select_fusion.z_ref, bf16[32,8,128,128]{3,2,1,0:T(8,128)(2,1)} %bitcast.27), custom_call_target="tpu_custom_call" | custom-call | flops 1073741824 | bytes 13631488 | tf_op jit(solution)/shard_map/pallas_call | solution.py:116
  107.3 1.3 collective-permute-start.3
  108.5 19.2 %collective-permute-done.3 = bf16[128,4096]{1,0:T(8,128)(2,1)S(1)} collective-permute-done((bf16[128,4096]{1,0:T(8,128)(2,1)}, bf16[128,4096]{1,0:T(8,128)(2,1)S(1)}, u32[]{:S(2)}, u32[]{:S(2)}) %collective-permute-start.3) | collective-permute-done | bytes 1048608 | tf_op jit(solution)/shard_map/ppermute | solution.py:19
  128.8 12.5 %shard_map.69 = (bf16[128,4096]{1,0:T(8,128)(2,1)}, bf16[128,4096]{1,0:T(8,128)(2,1)}) custom-call(s32[256]{0:T(256)} %reshape_squeeze.3.cols_ref, bf16[128,4096]{1,0:T(8,128)(2,1)} %broadcast_select_fusion.6.up_ref, f32[128,4096]{1,0:T(8,128)} %select_select_fusion.z_ref, bf16[32,8,128,128]{3,2,1,0:T(8,128)(2,1)} %bitcast.28), custom_call_target="tpu_custom_call" | custom-call | flops 1073741824 | bytes 13631488 | tf_op jit(solution)/shard_map/pallas_call | solution.py:116
  142.6 40.5 %collective-permute-done.4 = bf16[128,4096]{1,0:T(8,128)(2,1)S(1)} collective-permute-done((bf16[128,4096]{1,0:T(8,128)(2,1)}, bf16[128,4096]{1,0:T(8,128)(2,1)S(1)}, u32[]{:S(2)}, u32[]{:S(2)}) %collective-permute-start.4) | collective-permute-done | bytes 1048608 | tf_op jit(solution)/shard_map/ppermute | solution.py:19
  184.1 12.5 %shard_map.70 = (bf16[128,4096]{1,0:T(8,128)(2,1)}, bf16[128,4096]{1,0:T(8,128)(2,1)}) custom-call(s32[256]{0:T(256)} %reshape_squeeze.3.cols_ref, bf16[128,4096]{1,0:T(8,128)(2,1)} %broadcast_select_fusion.5.up_ref, f32[128,4096]{1,0:T(8,128)} %select_select_fusion.z_ref, bf16[32,8,128,128]{3,2,1,0:T(8,128)(2,1)} %bitcast.29), custom_call_target="tpu_custom_call" | custom-call | flops 1073741824 | bytes 13631488 | tf_op jit(solution)/shard_map/pallas_call | solution.py:116
  196.6 1.4 collective-permute-start.5
  198.0 39.4 %collective-permute-done.5 = bf16[128,4096]{1,0:T(8,128)(2,1)S(1)} collective-permute-done((bf16[128,4096]{1,0:T(8,128)(2,1)}, bf16[128,4096]{1,0:T(8,128)(2,1)S(1)}, u32[]{:S(2)}, u32[]{:S(2)}) %collective-permute-start.5) | collective-permute-done | bytes 1048608 | tf_op jit(solution)/shard_map/ppermute | solution.py:19
  238.5 12.6 %shard_map.71 = (bf16[128,4096]{1,0:T(8,128)(2,1)}, bf16[128,4096]{1,0:T(8,128)(2,1)}) custom-call(s32[256]{0:T(256)} %reshape_squeeze.3.cols_ref, bf16[128,4096]{1,0:T(8,128)(2,1)} %broadcast_select_fusion.4.up_ref, f32[128,4096]{1,0:T(8,128)} %select_select_fusion.z_ref, bf16[32,8,128,128]{3,2,1,0:T(8,128)(2,1)} %bitcast.30), custom_call_target="tpu_custom_call" | custom-call | flops 1073741824 | bytes 13631488 | tf_op jit(solution)/shard_map/pallas_call | solution.py:116
  251.2 1.4 select_select_fusion.1
  252.6 1.4 copy.19
  254.0 5.9 %all-to-all-start = ((bf16[128,8,512]{0,2,1:T(8,128)(2,1)}), bf16[128,8,512]{0,2,1:T(8,128)(2,1)S(1)}, u32[]{:S(2)}, u32[]{:S(2)}) async-start(bf16[128,8,512]{0,2,1:T(8,128)(2,1)} %bitcast.2), calls=%async_computation | async-start | bytes 2097152 | tf_op jit(solution)/shard_map/all_to_all | solution.py:166
  260.0 17.2 %all-to-all-done = bf16[128,8,512]{0,2,1:T(8,128)(2,1)S(1)} async-done(((bf16[128,8,512]{0,2,1:T(8,128)(2,1)}), bf16[128,8,512]{0,2,1:T(8,128)(2,1)S(1)}, u32[]{:S(2)}, u32[]{:S(2)}) %all-to-all-start) | async-done | bytes 1048608 | tf_op jit(solution)/shard_map/all_to_all | solution.py:166
  279.0 5.0 %gather_fusion.1 = bf16[32,1024,128]{2,1,0:T(8,128)(2,1)} fusion(bf16[1024,4,128]{2,0,1:T(8,128)(2,1)S(1)} %copy.16, s32[1024]{0:T(1024)S(1)} %pad_clamp_fusion), kind=kCustom, calls=%fused_computation.1 | custom fusion | bytes 16777344 | tf_op jit(solution)/shard_map/gather | solution.py:172
  284.0 9.0 %copy_bitcast_fusion = bf16[1024,32,128]{2,0,1:T(8,128)(2,1)} fusion(bf16[1024,4096]{1,0:T(8,128)(2,1)} %all-gather.2.cloned.1.call-done), kind=kLoop, calls=%fused_computation.2 | loop fusion | bytes 16777216 | tf_op jit(solution)/shard_map/reshape | solution.py:171
  293.0 8.5 %gather_fusion = bf16[32,1024,128]{2,1,0:T(8,128)(2,1)} fusion(bf16[1024,32,128]{2,0,1:T(8,128)(2,1)} %copy_bitcast_fusion, s32[1024]{0:T(1024)S(1)} %pad_clamp_fusion.1), kind=kCustom, calls=%fused_computation | custom fusion | bytes 16777344 | tf_op jit(solution)/shard_map/gather | solution.py:171
  301.5 9.6 %fusion = f32[32,128,128]{2,1,0:T(8,128)} fusion(bf16[32,1024,128]{2,1,0:T(8,128)(2,1)} %gather_fusion.1, bf16[32,1024,128]{2,1,0:T(8,128)(2,1)} %gather_fusion), kind=kOutput, calls=%fused_computation.3 | convolution fusion | flops 1073741824 | bytes 18874368 | tf_op jit(solution)/shard_map/rpa,rpb->pab/dot_general | solution.py:173
  311.1 82.7 %reduce-scatter.2.cloned.1.call-done = f32[512,128]{1,0:T(8,128)} async-done(((f32[4096,128]{1,0:T(8,128)}), f32[512,128]{1,0:T(8,128)}) %reduce-scatter.2.cloned.1.call-update) | async-done | bytes 262160 | tf_op jit(solution)/shard_map/reduce_scatter | solution.py:176
  393.8 1.6 convert_bitcast_fusion
  (36 shorter events, 11.4 us)
Async XLA Ops:
  6.5 17.6 %copy-start.1 = (bf16[128,4096]{1,0:T(8,128)(2,1)S(1)}, bf16[128,4096]{1,0:T(8,128)(2,1)}, u32[]{:S(2)}) copy-start(bf16[128,4096]{1,0:T(8,128)(2,1)} %param.6) | copy-start | bytes 3145732
  6.5 277.5 %all-gather.2.cloned.1.call-start = ((), (), s32[]{:S(2)}) async-start(), calls=%async_computation.2 | async-start | bytes 9437184 | tf_op jit(solution)/shard_map/all_gather | solution.py:169
  20.4 3.8 collective-permute-start
  35.3 44.9 %copy-start.2 = (bf16[128,4096]{1,0:T(8,128)(2,1)S(1)}, bf16[128,4096]{1,0:T(8,128)(2,1)}, u32[]{:S(2)}) copy-start(bf16[128,4096]{1,0:T(8,128)(2,1)} %broadcast_select_fusion.2.h_ref) | copy-start | bytes 3145732
  35.3 15.7 %collective-permute-start.1 = (bf16[128,4096]{1,0:T(8,128)(2,1)}, bf16[128,4096]{1,0:T(8,128)(2,1)S(1)}, u32[]{:S(2)}, u32[]{:S(2)}) collective-permute-start(bf16[128,4096]{1,0:T(8,128)(2,1)} %get-tuple-element.20), channel_id=1, source_target_pairs={{0,64},{64,128},{128,192},{1,65},{65,129},{129,193},{2,66},{66,130... | collective-permute-start | bytes 3145736 | tf_op jit(solution)/shard_map/ppermute | solution.py:19
  52.1 29.7 %copy-start = (bf16[128,4096]{1,0:T(8,128)(2,1)S(1)}, bf16[128,4096]{1,0:T(8,128)(2,1)}, u32[]{:S(2)}) copy-start(bf16[128,4096]{1,0:T(8,128)(2,1)} %param.7) | copy-start | bytes 3145732
  62.2 18.0 %collective-permute-start.2 = (bf16[128,4096]{1,0:T(8,128)(2,1)}, bf16[128,4096]{1,0:T(8,128)(2,1)}, u32[]{:S(2)}, u32[]{:S(2)}) collective-permute-start(bf16[128,4096]{1,0:T(8,128)(2,1)} %get-tuple-element.21), channel_id=1, source_target_pairs={{0,64},{64,128},{128,192},{1,65},{65,129},{129,193},{2,66},{66,130... | collective-permute-start | bytes 3145736 | tf_op jit(solution)/shard_map/ppermute | solution.py:19
  81.8 11.0 %copy-start.3 = (f32[128,4096]{1,0:T(8,128)S(1)}, f32[128,4096]{1,0:T(8,128)}, u32[]{:S(2)}) copy-start(f32[128,4096]{1,0:T(8,128)} %get-tuple-element.25) | copy-start | bytes 6291460
  107.3 20.4 %collective-permute-start.3 = (bf16[128,4096]{1,0:T(8,128)(2,1)}, bf16[128,4096]{1,0:T(8,128)(2,1)S(1)}, u32[]{:S(2)}, u32[]{:S(2)}) collective-permute-start(bf16[128,4096]{1,0:T(8,128)(2,1)} %get-tuple-element.26), channel_id=1, source_target_pairs={{64,0},{128,64},{192,128},{65,1},{129,65},{193,129},{66,2},{130,66... | collective-permute-start | bytes 3145736 | tf_op jit(solution)/shard_map/ppermute | solution.py:19
  141.3 41.8 %collective-permute-start.4 = (bf16[128,4096]{1,0:T(8,128)(2,1)}, bf16[128,4096]{1,0:T(8,128)(2,1)S(1)}, u32[]{:S(2)}, u32[]{:S(2)}) collective-permute-start(bf16[128,4096]{1,0:T(8,128)(2,1)} %get-tuple-element.27), channel_id=1, source_target_pairs={{64,0},{128,64},{192,128},{65,1},{129,65},{193,129},{66,2},{130,66... | collective-permute-start | bytes 3145736 | tf_op jit(solution)/shard_map/ppermute | solution.py:19
  196.6 54.6 %copy-start.4 = (bf16[128,4096]{1,0:T(8,128)(2,1)S(1)}, bf16[128,4096]{1,0:T(8,128)(2,1)}, u32[]{:S(2)}) copy-start(bf16[128,4096]{1,0:T(8,128)(2,1)} %get-tuple-element.32) | copy-start | bytes 3145732
  196.6 54.6 %copy-start.5 = (bf16[128,4096]{1,0:T(8,128)(2,1)S(1)}, bf16[128,4096]{1,0:T(8,128)(2,1)}, u32[]{:S(2)}) copy-start(bf16[128,4096]{1,0:T(8,128)(2,1)} %get-tuple-element.31) | copy-start | bytes 3145732
  196.6 40.8 %collective-permute-start.5 = (bf16[128,4096]{1,0:T(8,128)(2,1)}, bf16[128,4096]{1,0:T(8,128)(2,1)S(1)}, u32[]{:S(2)}, u32[]{:S(2)}) collective-permute-start(bf16[128,4096]{1,0:T(8,128)(2,1)} %get-tuple-element.28), channel_id=1, source_target_pairs={{64,0},{128,64},{192,128},{65,1},{129,65},{193,129},{66,2},{130,66... | collective-permute-start | bytes 3145736 | tf_op jit(solution)/shard_map/ppermute | solution.py:19
  238.5 21.3 %copy-start.6 = (s32[256]{0:T(256)S(1)}, s32[256]{0:T(256)}, u32[]{:S(2)}) copy-start(s32[256]{0:T(256)} %reshape_squeeze.3.cols_ref) | copy-start | bytes 3076
  238.5 21.4 %copy-start.7 = (s32[32]{0:T(128)S(1)}, s32[32]{0:T(128)}, u32[]{:S(2)}) copy-start(s32[32]{0:T(128)} %constant.44) | copy-start | bytes 388
  254.0 23.2 %all-to-all-start = ((bf16[128,8,512]{0,2,1:T(8,128)(2,1)}), bf16[128,8,512]{0,2,1:T(8,128)(2,1)S(1)}, u32[]{:S(2)}, u32[]{:S(2)}) async-start(bf16[128,8,512]{0,2,1:T(8,128)(2,1)} %bitcast.2), calls=%async_computation | async-start | bytes 2097152 | tf_op jit(solution)/shard_map/all_to_all | solution.py:166
  259.8 133.9 %reduce-scatter.2.cloned.1.call-start = ((), (), s32[]{:S(2)}) async-start(), calls=%async_computation.3 | async-start | bytes 2359296 | tf_op jit(solution)/shard_map/reduce_scatter | solution.py:176
Sparse Core Ops, SparseCore 0:
  81.9 194.9 all-gather.1
  311.2 82.5 reduce-scatter.1

commit v4 on v3

--- a/solution.py
+++ b/solution.py
@@ -11,6 +11,7 @@
 DP_AXES = ("y", "xlo", "z")
 DP_SIZES = (4, 2, 8)
 JB = 4
+PER_BLOCK = 8
 
 
 def from_behind(block, axis, distance):
@@ -125,6 +126,68 @@
             flops=flops, transcendentals=rows * width, bytes_accessed=weight.size * 2 + rows * width * 10
         ),
     )(cols, upstream, preact, weight)
+
+
+def grad_kernel(cols_ref, h_ref, g_ref, out_ref):
+    edge = out_ref.shape[-1]
+    per_step = out_ref.shape[0]
+    step = pl.program_id(0)
+    for qq in range(per_step):
+        q = step * per_step + qq
+        c = cols_ref[q]
+        x = h_ref[:, pl.ds(pl.multiple_of(c * edge, edge), edge)]
+        j = q // PER_BLOCK
+        g = g_ref[:, pl.ds(pl.multiple_of(j * edge, edge), edge)]
+        out_ref[qq] = lax.dot_general(
+            x, g, (((0,), (0,)), ((), ())), preferred_element_type=jnp.float32
+        )
+
+
+def group_grads(cols, inputs_group, grads_group, pairs, per_step):
+    rows, width = inputs_group.shape
+    edge = 128
+    grid = pltpu.PrefetchScalarGridSpec(
+        num_scalar_prefetch=1,
+        grid=(pairs // per_step,),
+        in_specs=[
+            pl.BlockSpec((rows, width), lambda i, c: (0, 0)),
+            pl.BlockSpec(grads_group.shape, lambda i, c: (0, 0)),
+        ],
+        out_specs=pl.BlockSpec((per_step, edge, edge), lambda i, c: (i, 0, 0)),
+    )
+    return pl.pallas_call(
+        grad_kernel,
+        grid_spec=grid,
+        out_shape=jax.ShapeDtypeStruct((pairs, edge, edge), jnp.float32),
+        compiler_params=pltpu.CompilerParams(
+            dimension_semantics=("arbitrary",), vmem_limit_bytes=48 * 1024 * 1024
+        ),
+        cost_estimate=pl.CostEstimate(
+            flops=2 * rows * pairs * edge * edge,
+            transcendentals=0,
+            bytes_accessed=inputs_group.size * 2 + grads_group.size * 2 + pairs * edge * edge * 4,
+        ),
+    )(cols, inputs_group, grads_group)
+
+
+def ring_reduce_scatter(chunks, axis, n):
+    i = lax.axis_index(axis)
+    half = chunks.shape[1] // 2
+    east, west = chunks[:, :half], chunks[:, half:]
+    cw = [(k, (k + 1) % n) for k in range(n)]
+    ccw = [(k, (k - 1) % n) for k in range(n)]
+    got_e = got_w = None
+    for s in range(n - 1):
+        send_e = lax.dynamic_index_in_dim(east, (i - s - 1) % n, 0, False)
+        send_w = lax.dynamic_index_in_dim(west, (i + s + 1) % n, 0, False)
+        if got_e is not None:
+            send_e = got_e + send_e
+            send_w = got_w + send_w
+        got_e = lax.ppermute(send_e, axis, cw)
+        got_w = lax.ppermute(send_w, axis, ccw)
+    own_e = lax.dynamic_index_in_dim(east, i, 0, False)
+    own_w = lax.dynamic_index_in_dim(west, i, 0, False)
+    return jnp.concatenate([got_e + own_e, got_w + own_w], 0)
 
 
 def body(inputs, cotangent, blocks, block_cols):
@@ -168,12 +231,10 @@
     ).reshape(members * all_rows, group_j, edge_size)
     inputs_group = lax.all_gather(all_inputs, ("y", "xlo"), axis=0, tiled=True)
     cols_here = lax.dynamic_slice_in_dim(flat_cols, member * group_pairs, group_pairs)
-    picked_cols = inputs_group.reshape(members * all_rows, num_blocks, edge_size)[:, cols_here, :]
-    chosen = grads_group[:, np.arange(group_pairs) // per_block, :]
-    partial = jnp.einsum(
-        "rpa,rpb->pab", picked_cols, chosen, preferred_element_type=jnp.float32
-    ).reshape(group_pairs * edge_size, edge_size)
-    own_share = lax.psum_scatter(partial, "z", scatter_dimension=0, tiled=True)
+    grads_flat = grads_group.reshape(members * all_rows, group_j * edge_size)
+    partial = group_grads(cols_here, inputs_group, grads_flat, group_pairs, group_pairs // nz)
+    partial = partial.reshape(nz, group_pairs // nz * edge_size, edge_size)
+    own_share = ring_reduce_scatter(partial, "z", nz)
     summed = own_share.astype(jnp.bfloat16)
     return summed[None]
 

time: 404 us -> 384 us (0.950)
  the two profiles are of different devices: /device:TPU:2 before, /device:TPU:100 now
where the time goes in v4:
time: 384 us; the launch traced here: 383 us
  waiting for transfers between devices  202 us (53%)
  Pallas kernels  99.3 us (26%)
  starting transfers between devices  49.7 us (13%)
  other arithmetic  15.3 us (4%)
  between operations  13.6 us (4%)
    ppermute x6, waiting for transfers between devices, from_behind(): return lax.ppermute(block, axis, route)  158 us
    pallas_call x4, Pallas kernels, layer_backward(): pl.pallas_call(backward_kernel, grid_spec=grid, out_shape=[jax.ShapeDtype...  50.2 us
    pallas_call x4, Pallas kernels, layer_forward(): pl.pallas_call(forward_kernel, grid_spec=grid, out_shape=[jax.ShapeDtypeS...  40.4 us
    ppermute x7, starting transfers between devices, ring_reduce_scatter(): got_e = lax.ppermute(send_e, axis, cw)  25.5 us
    all_to_all x1, waiting for transfers between devices, body(): lax.all_to_all(grads_here, ('y', 'xlo'), split_axis=1, concat_axis=0, til...  21.4 us
    ppermute x6, starting transfers between devices, from_behind(): return lax.ppermute(block, axis, route)  18.5 us
    ppermute x7, waiting for transfers between devices, ring_reduce_scatter(): got_e = lax.ppermute(send_e, axis, cw)  17.6 us
    pallas_call x1, Pallas kernels, group_grads(): pl.pallas_call(grad_kernel, grid_spec=grid, out_shape=jax.ShapeDtypeStruc...  8.71 us
  transfers between devices with their start and end apart: 22, of which 20 were waited for; matrix products, arithmetic and copies ran while one was open for 2% of the time, Pallas kernels for 16%

profile of v4, /device:TPU:100, one launch (start us, length us, event | category | flops | bytes accessed | tf_op | source)
XLA Modules:
  0.0 382.6 jit_solution(12982324321437236779)
XLA Ops:
  9.0 10.1 %shard_map.46 = (f32[128,4096]{1,0:T(8,128)}, bf16[128,4096]{1,0:T(8,128)(2,1)}) custom-call(s32[256]{0:T(256)} %reshape_squeeze.3.cols_ref, bf16[128,4096]{1,0:T(8,128)(2,1)} %broadcast_select_fusion.3.h_ref, bf16[32,8,128,128]{3,2,1,0:T(8,128)(2,1)} %bitcast.57), custom_call_target="tpu_custom_call" | custom-call | flops 1073741824 | bytes 12582912 | tf_op jit(solution)/shard_map/pallas_call | solution.py:85
  21.1 15.9 %collective-permute-done = bf16[128,4096]{1,0:T(8,128)(2,1)S(1)} collective-permute-done((bf16[128,4096]{1,0:T(8,128)(2,1)}, bf16[128,4096]{1,0:T(8,128)(2,1)S(1)}, u32[]{:S(2)}, u32[]{:S(2)}) %collective-permute-start) | collective-permute-done | bytes 1048608 | tf_op jit(solution)/shard_map/ppermute | solution.py:20
  38.1 10.0 %shard_map.47 = (f32[128,4096]{1,0:T(8,128)}, bf16[128,4096]{1,0:T(8,128)(2,1)}) custom-call(s32[256]{0:T(256)} %reshape_squeeze.3.cols_ref, bf16[128,4096]{1,0:T(8,128)(2,1)} %broadcast_select_fusion.2.h_ref, bf16[32,8,128,128]{3,2,1,0:T(8,128)(2,1)} %bitcast.58), custom_call_target="tpu_custom_call" | custom-call | flops 1073741824 | bytes 12582912 | tf_op jit(solution)/shard_map/pallas_call | solution.py:85
  50.0 15.9 %collective-permute-done.1 = bf16[128,4096]{1,0:T(8,128)(2,1)S(1)} collective-permute-done((bf16[128,4096]{1,0:T(8,128)(2,1)}, bf16[128,4096]{1,0:T(8,128)(2,1)S(1)}, u32[]{:S(2)}, u32[]{:S(2)}) %collective-permute-start.1) | collective-permute-done | bytes 1048608 | tf_op jit(solution)/shard_map/ppermute | solution.py:20
  67.0 10.2 %shard_map.48 = (f32[128,4096]{1,0:T(8,128)}, bf16[128,4096]{1,0:T(8,128)(2,1)}) custom-call(s32[256]{0:T(256)} %reshape_squeeze.3.cols_ref, bf16[128,4096]{1,0:T(8,128)(2,1)} %broadcast_select_fusion.1.h_ref, bf16[32,8,128,128]{3,2,1,0:T(8,128)(2,1)} %bitcast.59), custom_call_target="tpu_custom_call" | custom-call | flops 1073741824 | bytes 12582912 | tf_op jit(solution)/shard_map/pallas_call | solution.py:85
  79.1 16.0 %collective-permute-done.2 = bf16[128,4096]{1,0:T(8,128)(2,1)} collective-permute-done((bf16[128,4096]{1,0:T(8,128)(2,1)}, bf16[128,4096]{1,0:T(8,128)(2,1)}, u32[]{:S(2)}, u32[]{:S(2)}) %collective-permute-start.2) | collective-permute-done | bytes 1048608 | tf_op jit(solution)/shard_map/ppermute | solution.py:20
  95.1 3.1 select_select_fusion.2
  99.3 10.1 %shard_map.49 = (f32[128,4096]{1,0:T(8,128)}, bf16[128,4096]{1,0:T(8,128)(2,1)}) custom-call(s32[256]{0:T(256)} %reshape_squeeze.3.cols_ref, bf16[128,4096]{1,0:T(8,128)(2,1)} %get-tuple-element.34.h_ref, bf16[32,8,128,128]{3,2,1,0:T(8,128)(2,1)} %bitcast.60), custom_call_target="tpu_custom_call" | custom-call | flops 1073741824 | bytes 12582912 | tf_op jit(solution)/shard_map/pallas_call | solution.py:85
  109.4 3.5 select_select_fusion.z_ref
  112.9 12.5 %shard_map.50 = (bf16[128,4096]{1,0:T(8,128)(2,1)}, bf16[128,4096]{1,0:T(8,128)(2,1)}) custom-call(s32[256]{0:T(256)} %reshape_squeeze.3.cols_ref, bf16[128,4096]{1,0:T(8,128)(2,1)} %broadcast_select_fusion.7.up_ref, f32[128,4096]{1,0:T(8,128)} %select_select_fusion.z_ref, bf16[32,8,128,128]{3,2,1,0:T(8,128)(2,1)} %bitcast.61), custom_call_target="tpu_custom_call" | custom-call | flops 1073741824 | bytes 13631488 | tf_op jit(solution)/shard_map/pallas_call | solution.py:117
  127.4 35.0 %collective-permute-done.3 = bf16[128,4096]{1,0:T(8,128)(2,1)S(1)} collective-permute-done((bf16[128,4096]{1,0:T(8,128)(2,1)}, bf16[128,4096]{1,0:T(8,128)(2,1)S(1)}, u32[]{:S(2)}, u32[]{:S(2)}) %collective-permute-start.3) | collective-permute-done | bytes 1048608 | tf_op jit(solution)/shard_map/ppermute | solution.py:20
  163.5 12.5 %shard_map.51 = (bf16[128,4096]{1,0:T(8,128)(2,1)}, bf16[128,4096]{1,0:T(8,128)(2,1)}) custom-call(s32[256]{0:T(256)} %reshape_squeeze.3.cols_ref, bf16[128,4096]{1,0:T(8,128)(2,1)} %broadcast_select_fusion.6.up_ref, f32[128,4096]{1,0:T(8,128)} %select_select_fusion.z_ref, bf16[32,8,128,128]{3,2,1,0:T(8,128)(2,1)} %bitcast.62), custom_call_target="tpu_custom_call" | custom-call | flops 1073741824 | bytes 13631488 | tf_op jit(solution)/shard_map/pallas_call | solution.py:117
  176.0 5.2 %collective-permute-start.4 = (bf16[128,4096]{1,0:T(8,128)(2,1)}, bf16[128,4096]{1,0:T(8,128)(2,1)S(1)}, u32[]{:S(2)}, u32[]{:S(2)}) collective-permute-start(bf16[128,4096]{1,0:T(8,128)(2,1)} %get-tuple-element.27), channel_id=1, source_target_pairs={{64,0},{128,64},{192,128},{65,1},{129,65},{193,129},{66,2},{130,66... | collective-permute-start | bytes 3145736 | tf_op jit(solution)/shard_map/ppermute | solution.py:20
  181.3 35.0 %collective-permute-done.4 = bf16[128,4096]{1,0:T(8,128)(2,1)S(1)} collective-permute-done((bf16[128,4096]{1,0:T(8,128)(2,1)}, bf16[128,4096]{1,0:T(8,128)(2,1)S(1)}, u32[]{:S(2)}, u32[]{:S(2)}) %collective-permute-start.4) | collective-permute-done | bytes 1048608 | tf_op jit(solution)/shard_map/ppermute | solution.py:20
  217.4 12.5 %shard_map.52 = (bf16[128,4096]{1,0:T(8,128)(2,1)}, bf16[128,4096]{1,0:T(8,128)(2,1)}) custom-call(s32[256]{0:T(256)} %reshape_squeeze.3.cols_ref, bf16[128,4096]{1,0:T(8,128)(2,1)} %broadcast_select_fusion.5.up_ref, f32[128,4096]{1,0:T(8,128)} %select_select_fusion.z_ref, bf16[32,8,128,128]{3,2,1,0:T(8,128)(2,1)} %bitcast.63), custom_call_target="tpu_custom_call" | custom-call | flops 1073741824 | bytes 13631488 | tf_op jit(solution)/shard_map/pallas_call | solution.py:117
  229.9 5.6 %collective-permute-start.5 = (bf16[128,4096]{1,0:T(8,128)(2,1)}, bf16[128,4096]{1,0:T(8,128)(2,1)S(1)}, u32[]{:S(2)}, u32[]{:S(2)}) collective-permute-start(bf16[128,4096]{1,0:T(8,128)(2,1)} %get-tuple-element.28), channel_id=1, source_target_pairs={{64,0},{128,64},{192,128},{65,1},{129,65},{193,129},{66,2},{130,66... | collective-permute-start | bytes 3145736 | tf_op jit(solution)/shard_map/ppermute | solution.py:20
  235.5 40.1 %collective-permute-done.5 = bf16[128,4096]{1,0:T(8,128)(2,1)S(1)} collective-permute-done((bf16[128,4096]{1,0:T(8,128)(2,1)}, bf16[128,4096]{1,0:T(8,128)(2,1)S(1)}, u32[]{:S(2)}, u32[]{:S(2)}) %collective-permute-start.5) | collective-permute-done | bytes 1048608 | tf_op jit(solution)/shard_map/ppermute | solution.py:20
  276.7 12.7 %shard_map.53 = (bf16[128,4096]{1,0:T(8,128)(2,1)}, bf16[128,4096]{1,0:T(8,128)(2,1)}) custom-call(s32[256]{0:T(256)} %reshape_squeeze.3.cols_ref, bf16[128,4096]{1,0:T(8,128)(2,1)} %broadcast_select_fusion.4.up_ref, f32[128,4096]{1,0:T(8,128)} %select_select_fusion.z_ref, bf16[32,8,128,128]{3,2,1,0:T(8,128)(2,1)} %bitcast.64), custom_call_target="tpu_custom_call" | custom-call | flops 1073741824 | bytes 13631488 | tf_op jit(solution)/shard_map/pallas_call | solution.py:117
  290.7 5.1 %all-to-all-start = ((bf16[128,8,512]{2,0,1:T(8,128)(2,1)}), bf16[128,8,512]{2,0,1:T(8,128)(2,1)S(1)}, u32[]{:S(2)}, u32[]{:S(2)}) async-start(bf16[128,8,512]{2,0,1:T(8,128)(2,1)} %bitcast.54), calls=%async_computation | async-start | bytes 2097152 | tf_op jit(solution)/shard_map/all_to_all | solution.py:229
  295.9 21.4 %all-to-all-done = bf16[128,8,512]{2,0,1:T(8,128)(2,1)S(1)} async-done(((bf16[128,8,512]{2,0,1:T(8,128)(2,1)}), bf16[128,8,512]{2,0,1:T(8,128)(2,1)S(1)}, u32[]{:S(2)}, u32[]{:S(2)}) %all-to-all-start) | async-done | bytes 1048608 | tf_op jit(solution)/shard_map/all_to_all | solution.py:229
  317.3 8.7 %shard_map.54 = f32[32,128,128]{2,1,0:T(8,128)S(1)} custom-call(s32[32]{0:T(128)S(1)} %dynamic_slice.52.cols_ref, bf16[1024,4096]{1,0:T(8,128)(2,1)} %all-gather.2.cloned.1.call-done.h_ref, bf16[1024,512]{1,0:T(8,128)(2,1)S(1)} %bitcast.56), custom_call_target="tpu_custom_call" | custom-call | flops 1073741824 | bytes 11534336 | tf_op jit(solution)/shard_map/pallas_call | solution.py:158
  326.2 2.8 collective-permute-start.6
  329.2 2.4 collective-permute-done.6
  331.6 3.9 %collective-permute-start.7 = (f32[256,128]{1,0:T(8,128)S(1)}, f32[256,128]{1,0:T(8,128)S(1)}, u32[]{:S(2)}, u32[]{:S(2)}) collective-permute-start(f32[256,128]{1,0:T(8,128)S(1)} %bitcast_add_fusion.13), channel_id=1, source_target_pairs={{0,1},{1,2},{2,3},{3,4},{4,5},{5,6},{6,7},{7,0},{8,9},{9,10},{10,1... | collective-permute-start | bytes 393224 | tf_op jit(solution)/shard_map/ppermute | solution.py:186
  335.6 3.5 collective-permute-done.7
  339.2 3.8 collective-permute-start.8
  343.2 2.7 collective-permute-done.8
  346.0 3.8 collective-permute-start.9
  352.3 3.7 collective-permute-start.10
  358.6 3.7 collective-permute-start.11
  364.9 3.7 collective-permute-start.12
  371.1 3.9 %collective-permute-done.19 = f32[256,128]{1,0:T(8,128)S(1)} collective-permute-done((f32[256,128]{1,0:T(8,128)S(1)}, f32[256,128]{1,0:T(8,128)S(1)}, u32[]{:S(2)}, u32[]{:S(2)}) %collective-permute-start.19) | collective-permute-done | bytes 131104 | tf_op jit(solution)/shard_map/ppermute | solution.py:187
  (70 shorter events, 29.6 us)
Async XLA Ops:
  6.5 310.8 %all-gather.2.cloned.1.call-start = ((), (), s32[]{:S(2)}) async-start(), calls=%async_computation.1 | async-start | bytes 9437184 | tf_op jit(solution)/shard_map/all_gather | solution.py:232
  9.0 27.9 %copy-start.1 = (bf16[128,4096]{1,0:T(8,128)(2,1)S(1)}, bf16[128,4096]{1,0:T(8,128)(2,1)}, u32[]{:S(2)}) copy-start(bf16[128,4096]{1,0:T(8,128)(2,1)} %param.4) | copy-start | bytes 3145732
  19.1 17.8 %collective-permute-start = (bf16[128,4096]{1,0:T(8,128)(2,1)}, bf16[128,4096]{1,0:T(8,128)(2,1)S(1)}, u32[]{:S(2)}, u32[]{:S(2)}) collective-permute-start(bf16[128,4096]{1,0:T(8,128)(2,1)} %get-tuple-element.19), channel_id=1, source_target_pairs={{0,64},{64,128},{128,192},{1,65},{65,129},{129,193},{2,66},{66,130... | collective-permute-start | bytes 3145736 | tf_op jit(solution)/shard_map/ppermute | solution.py:20
  48.1 17.8 %collective-permute-start.1 = (bf16[128,4096]{1,0:T(8,128)(2,1)}, bf16[128,4096]{1,0:T(8,128)(2,1)S(1)}, u32[]{:S(2)}, u32[]{:S(2)}) collective-permute-start(bf16[128,4096]{1,0:T(8,128)(2,1)} %get-tuple-element.20), channel_id=1, source_target_pairs={{0,64},{64,128},{128,192},{1,65},{65,129},{129,193},{2,66},{66,130... | collective-permute-start | bytes 3145736 | tf_op jit(solution)/shard_map/ppermute | solution.py:20
  67.0 28.1 %copy-start.2 = (bf16[128,4096]{1,0:T(8,128)(2,1)S(1)}, bf16[128,4096]{1,0:T(8,128)(2,1)}, u32[]{:S(2)}) copy-start(bf16[128,4096]{1,0:T(8,128)(2,1)} %broadcast_select_fusion.2.h_ref) | copy-start | bytes 3145732
  77.2 17.9 %collective-permute-start.2 = (bf16[128,4096]{1,0:T(8,128)(2,1)}, bf16[128,4096]{1,0:T(8,128)(2,1)}, u32[]{:S(2)}, u32[]{:S(2)}) collective-permute-start(bf16[128,4096]{1,0:T(8,128)(2,1)} %get-tuple-element.21), channel_id=1, source_target_pairs={{0,64},{64,128},{128,192},{1,65},{65,129},{129,193},{2,66},{66,130... | collective-permute-start | bytes 3145736 | tf_op jit(solution)/shard_map/ppermute | solution.py:20
  79.1 19.1 %copy-start = (bf16[128,4096]{1,0:T(8,128)(2,1)S(1)}, bf16[128,4096]{1,0:T(8,128)(2,1)}, u32[]{:S(2)}) copy-start(bf16[128,4096]{1,0:T(8,128)(2,1)} %param.5) | copy-start | bytes 3145732
  99.3 10.1 %copy-start.3 = (f32[128,4096]{1,0:T(8,128)S(1)}, f32[128,4096]{1,0:T(8,128)}, u32[]{:S(2)}) copy-start(f32[128,4096]{1,0:T(8,128)} %get-tuple-element.25) | copy-start | bytes 6291460
  125.5 37.0 %collective-permute-start.3 = (bf16[128,4096]{1,0:T(8,128)(2,1)}, bf16[128,4096]{1,0:T(8,128)(2,1)S(1)}, u32[]{:S(2)}, u32[]{:S(2)}) collective-permute-start(bf16[128,4096]{1,0:T(8,128)(2,1)} %get-tuple-element.26), channel_id=1, source_target_pairs={{64,0},{128,64},{192,128},{65,1},{129,65},{193,129},{66,2},{130,66... | collective-permute-start | bytes 3145736 | tf_op jit(solution)/shard_map/ppermute | solution.py:20
  176.0 40.3 %collective-permute-start.4 = (bf16[128,4096]{1,0:T(8,128)(2,1)}, bf16[128,4096]{1,0:T(8,128)(2,1)S(1)}, u32[]{:S(2)}, u32[]{:S(2)}) collective-permute-start(bf16[128,4096]{1,0:T(8,128)(2,1)} %get-tuple-element.27), channel_id=1, source_target_pairs={{64,0},{128,64},{192,128},{65,1},{129,65},{193,129},{66,2},{130,66... | collective-permute-start | bytes 3145736 | tf_op jit(solution)/shard_map/ppermute | solution.py:20
  229.9 45.7 %collective-permute-start.5 = (bf16[128,4096]{1,0:T(8,128)(2,1)}, bf16[128,4096]{1,0:T(8,128)(2,1)S(1)}, u32[]{:S(2)}, u32[]{:S(2)}) collective-permute-start(bf16[128,4096]{1,0:T(8,128)(2,1)} %get-tuple-element.28), channel_id=1, source_target_pairs={{64,0},{128,64},{192,128},{65,1},{129,65},{193,129},{66,2},{130,66... | collective-permute-start | bytes 3145736 | tf_op jit(solution)/shard_map/ppermute | solution.py:20
  276.7 12.7 %copy-start.4 = (bf16[128,4096]{1,0:T(8,128)(2,1)S(1)}, bf16[128,4096]{1,0:T(8,128)(2,1)}, u32[]{:S(2)}) copy-start(bf16[128,4096]{1,0:T(8,128)(2,1)} %get-tuple-element.32) | copy-start | bytes 3145732
  276.7 12.7 %copy-start.5 = (bf16[128,4096]{1,0:T(8,128)(2,1)S(1)}, bf16[128,4096]{1,0:T(8,128)(2,1)}, u32[]{:S(2)}) copy-start(bf16[128,4096]{1,0:T(8,128)(2,1)} %get-tuple-element.31) | copy-start | bytes 3145732
  276.7 12.7 %copy-start.6 = (bf16[128,4096]{1,0:T(8,128)(2,1)S(1)}, bf16[128,4096]{1,0:T(8,128)(2,1)}, u32[]{:S(2)}) copy-start(bf16[128,4096]{1,0:T(8,128)(2,1)} %get-tuple-element.30) | copy-start | bytes 3145732
  289.6 6.2 %copy-start.7 = (s32[256]{0:T(256)S(1)}, s32[256]{0:T(256)}, u32[]{:S(2)}) copy-start(s32[256]{0:T(256)} %reshape_squeeze.3.cols_ref) | copy-start | bytes 3076
  290.7 26.6 %all-to-all-start = ((bf16[128,8,512]{2,0,1:T(8,128)(2,1)}), bf16[128,8,512]{2,0,1:T(8,128)(2,1)S(1)}, u32[]{:S(2)}, u32[]{:S(2)}) async-start(bf16[128,8,512]{2,0,1:T(8,128)(2,1)} %bitcast.54), calls=%async_computation | async-start | bytes 2097152 | tf_op jit(solution)/shard_map/all_to_all | solution.py:229
  326.2 5.4 %collective-permute-start.6 = (f32[256,128]{1,0:T(8,128)S(1)}, f32[256,128]{1,0:T(8,128)S(1)}, u32[]{:S(2)}, u32[]{:S(2)}) collective-permute-start(f32[256,128]{1,0:T(8,128)S(1)} %dynamic-slice_bitcast_fusion.1), channel_id=1, source_target_pairs={{0,1},{1,2},{2,3},{3,4},{4,5},{5,6},{6,7},{7,0},{8,9},{9,10},{10,1... | collective-permute-start | bytes 393224 | tf_op jit(solution)/shard_map/ppermute | solution.py:186
  329.1 6.4 %collective-permute-start.13 = (f32[256,128]{1,0:T(8,128)S(1)}, f32[256,128]{1,0:T(8,128)S(1)}, u32[]{:S(2)}, u32[]{:S(2)}) collective-permute-start(f32[256,128]{1,0:T(8,128)S(1)} %dynamic-slice_bitcast_fusion), channel_id=1, source_target_pairs={{0,7},{1,0},{2,1},{3,2},{4,3},{5,4},{6,5},{7,6},{8,15},{9,8},{10,9... | collective-permute-start | bytes 393224 | tf_op jit(solution)/shard_map/ppermute | solution.py:187
  331.6 7.5 %collective-permute-start.7 = (f32[256,128]{1,0:T(8,128)S(1)}, f32[256,128]{1,0:T(8,128)S(1)}, u32[]{:S(2)}, u32[]{:S(2)}) collective-permute-start(f32[256,128]{1,0:T(8,128)S(1)} %bitcast_add_fusion.13), channel_id=1, source_target_pairs={{0,1},{1,2},{2,3},{3,4},{4,5},{5,6},{6,7},{7,0},{8,9},{9,10},{10,1... | collective-permute-start | bytes 393224 | tf_op jit(solution)/shard_map/ppermute | solution.py:186
  335.5 7.6 %collective-permute-start.14 = (f32[256,128]{1,0:T(8,128)S(1)}, f32[256,128]{1,0:T(8,128)S(1)}, u32[]{:S(2)}, u32[]{:S(2)}) collective-permute-start(f32[256,128]{1,0:T(8,128)S(1)} %bitcast_add_fusion.6), channel_id=1, source_target_pairs={{0,7},{1,0},{2,1},{3,2},{4,3},{5,4},{6,5},{7,6},{8,15},{9,8},{10,9... | collective-permute-start | bytes 393224 | tf_op jit(solution)/shard_map/ppermute | solution.py:187
  339.2 6.8 %collective-permute-start.8 = (f32[256,128]{1,0:T(8,128)S(1)}, f32[256,128]{1,0:T(8,128)S(1)}, u32[]{:S(2)}, u32[]{:S(2)}) collective-permute-start(f32[256,128]{1,0:T(8,128)S(1)} %bitcast_add_fusion.12), channel_id=1, source_target_pairs={{0,1},{1,2},{2,3},{3,4},{4,5},{5,6},{6,7},{7,0},{8,9},{9,10},{10,1... | collective-permute-start | bytes 393224 | tf_op jit(solution)/shard_map/ppermute | solution.py:186
  343.1 6.8 %collective-permute-start.15 = (f32[256,128]{1,0:T(8,128)S(1)}, f32[256,128]{1,0:T(8,128)S(1)}, u32[]{:S(2)}, u32[]{:S(2)}) collective-permute-start(f32[256,128]{1,0:T(8,128)S(1)} %bitcast_add_fusion.5), channel_id=1, source_target_pairs={{0,7},{1,0},{2,1},{3,2},{4,3},{5,4},{6,5},{7,6},{8,15},{9,8},{10,9... | collective-permute-start | bytes 393224 | tf_op jit(solution)/shard_map/ppermute | solution.py:187
  346.0 6.3 %collective-permute-start.9 = (f32[256,128]{1,0:T(8,128)S(1)}, f32[256,128]{1,0:T(8,128)S(1)}, u32[]{:S(2)}, u32[]{:S(2)}) collective-permute-start(f32[256,128]{1,0:T(8,128)S(1)} %bitcast_add_fusion.11), channel_id=1, source_target_pairs={{0,1},{1,2},{2,3},{3,4},{4,5},{5,6},{6,7},{7,0},{8,9},{9,10},{10,1... | collective-permute-start | bytes 393224 | tf_op jit(solution)/shard_map/ppermute | solution.py:186
  350.0 6.3 %collective-permute-start.16 = (f32[256,128]{1,0:T(8,128)S(1)}, f32[256,128]{1,0:T(8,128)S(1)}, u32[]{:S(2)}, u32[]{:S(2)}) collective-permute-start(f32[256,128]{1,0:T(8,128)S(1)} %bitcast_add_fusion.4), channel_id=1, source_target_pairs={{0,7},{1,0},{2,1},{3,2},{4,3},{5,4},{6,5},{7,6},{8,15},{9,8},{10,9... | collective-permute-start | bytes 393224 | tf_op jit(solution)/shard_map/ppermute | solution.py:187
  352.3 6.3 %collective-permute-start.10 = (f32[256,128]{1,0:T(8,128)S(1)}, f32[256,128]{1,0:T(8,128)S(1)}, u32[]{:S(2)}, u32[]{:S(2)}) collective-permute-start(f32[256,128]{1,0:T(8,128)S(1)} %bitcast_add_fusion.10), channel_id=1, source_target_pairs={{0,1},{1,2},{2,3},{3,4},{4,5},{5,6},{6,7},{7,0},{8,9},{9,10},{10,1... | collective-permute-start | bytes 393224 | tf_op jit(solution)/shard_map/ppermute | solution.py:186
  356.2 6.3 %collective-permute-start.17 = (f32[256,128]{1,0:T(8,128)S(1)}, f32[256,128]{1,0:T(8,128)S(1)}, u32[]{:S(2)}, u32[]{:S(2)}) collective-permute-start(f32[256,128]{1,0:T(8,128)S(1)} %bitcast_add_fusion.3), channel_id=1, source_target_pairs={{0,7},{1,0},{2,1},{3,2},{4,3},{5,4},{6,5},{7,6},{8,15},{9,8},{10,9... | collective-permute-start | bytes 393224 | tf_op jit(solution)/shard_map/ppermute | solution.py:187
  358.6 6.3 %collective-permute-start.11 = (f32[256,128]{1,0:T(8,128)S(1)}, f32[256,128]{1,0:T(8,128)S(1)}, u32[]{:S(2)}, u32[]{:S(2)}) collective-permute-start(f32[256,128]{1,0:T(8,128)S(1)} %bitcast_add_fusion.9), channel_id=1, source_target_pairs={{0,1},{1,2},{2,3},{3,4},{4,5},{5,6},{6,7},{7,0},{8,9},{9,10},{10,1... | collective-permute-start | bytes 393224 | tf_op jit(solution)/shard_map/ppermute | solution.py:186
  362.5 6.3 %collective-permute-start.18 = (f32[256,128]{1,0:T(8,128)S(1)}, f32[256,128]{1,0:T(8,128)S(1)}, u32[]{:S(2)}, u32[]{:S(2)}) collective-permute-start(f32[256,128]{1,0:T(8,128)S(1)} %bitcast_add_fusion.2), channel_id=1, source_target_pairs={{0,7},{1,0},{2,1},{3,2},{4,3},{5,4},{6,5},{7,6},{8,15},{9,8},{10,9... | collective-permute-start | bytes 393224 | tf_op jit(solution)/shard_map/ppermute | solution.py:187
  364.9 6.3 %collective-permute-start.12 = (f32[256,128]{1,0:T(8,128)S(1)}, f32[256,128]{1,0:T(8,128)S(1)}, u32[]{:S(2)}, u32[]{:S(2)}) collective-permute-start(f32[256,128]{1,0:T(8,128)S(1)} %bitcast_add_fusion.8), channel_id=1, source_target_pairs={{0,1},{1,2},{2,3},{3,4},{4,5},{5,6},{6,7},{7,0},{8,9},{9,10},{10,1... | collective-permute-start | bytes 393224 | tf_op jit(solution)/shard_map/ppermute | solution.py:186
  368.8 6.3 %collective-permute-start.19 = (f32[256,128]{1,0:T(8,128)S(1)}, f32[256,128]{1,0:T(8,128)S(1)}, u32[]{:S(2)}, u32[]{:S(2)}) collective-permute-start(f32[256,128]{1,0:T(8,128)S(1)} %bitcast_add_fusion.1), channel_id=1, source_target_pairs={{0,7},{1,0},{2,1},{3,2},{4,3},{5,4},{6,5},{7,6},{8,15},{9,8},{10,9... | collective-permute-start | bytes 393224 | tf_op jit(solution)/shard_map/ppermute | solution.py:187
Sparse Core Ops, SparseCore 0:
  98.3 216.9 all-gather.1

commit v5 on v4

--- a/solution.py
+++ b/solution.py
@@ -221,20 +221,22 @@
     all_inputs = stash_x
     all_grads = stash_g
     ny, nx, nz = DP_SIZES
-    members = ny * nx
+    members = ny
     group_pairs = num_blocks * per_block // members
     group_j = num_blocks // members
-    member = lax.axis_index("y") * nx + lax.axis_index("xlo")
+    member = lax.axis_index("y")
     grads_here = all_grads.reshape(all_rows, members, group_j * edge_size)
     grads_group = lax.all_to_all(
-        grads_here, ("y", "xlo"), split_axis=1, concat_axis=0, tiled=True
-    ).reshape(members * all_rows, group_j, edge_size)
-    inputs_group = lax.all_gather(all_inputs, ("y", "xlo"), axis=0, tiled=True)
+        grads_here, "y", split_axis=1, concat_axis=0, tiled=True
+    ).reshape(members * all_rows, group_j * edge_size)
+    inputs_group = lax.all_gather(all_inputs, "y", axis=0, tiled=True)
     cols_here = lax.dynamic_slice_in_dim(flat_cols, member * group_pairs, group_pairs)
-    grads_flat = grads_group.reshape(members * all_rows, group_j * edge_size)
-    partial = group_grads(cols_here, inputs_group, grads_flat, group_pairs, group_pairs // nz)
-    partial = partial.reshape(nz, group_pairs // nz * edge_size, edge_size)
-    own_share = ring_reduce_scatter(partial, "z", nz)
+    partial = group_grads(cols_here, inputs_group, grads_group, group_pairs, 8)
+    halves = partial.reshape(nx, group_pairs // nx * edge_size, edge_size)
+    side = lax.axis_index("xlo")
+    got = lax.ppermute(lax.dynamic_index_in_dim(halves, 1 - side, 0, False), "xlo", [(0, 1), (1, 0)])
+    kept = lax.dynamic_index_in_dim(halves, side, 0, False) + got
+    own_share = ring_reduce_scatter(kept.reshape(nz, -1, edge_size), "z", nz)
     summed = own_share.astype(jnp.bfloat16)
     return summed[None]
 

time: 384 us -> 337 us (0.88)
  the two profiles are of different devices: /device:TPU:100 before, /device:TPU:2 now
where the time goes in v5:
time: 337 us; the launch traced here: 331 us
  waiting for transfers between devices  126 us (37%)
  Pallas kernels  99.8 us (30%)
  starting transfers between devices  69.4 us (21%)
  other arithmetic  16.7 us (5%)
  between operations  13.7 us (4%)
  local copies, waits for them, and re-layouts  5.36 us (2%)
    ppermute x6, waiting for transfers between devices, from_behind(): return lax.ppermute(block, axis, route)  58.7 us
    pallas_call x4, Pallas kernels, layer_backward(): pl.pallas_call(backward_kernel, grid_spec=grid, out_shape=[jax.ShapeDtype...  50.2 us
    pallas_call x4, Pallas kernels, layer_forward(): pl.pallas_call(forward_kernel, grid_spec=grid, out_shape=[jax.ShapeDtypeS...  40.4 us
    ppermute x1, waiting for transfers between devices, body(): lax.ppermute(lax.dynamic_index_in_dim(halves, 1 - side, 0, False), 'xlo',...  37.5 us
    ppermute x6, starting transfers between devices, from_behind(): return lax.ppermute(block, axis, route)  34.8 us
    ppermute x7, starting transfers between devices, ring_reduce_scatter(): got_w = lax.ppermute(send_w, axis, ccw)  26.5 us
    ppermute x7, waiting for transfers between devices, ring_reduce_scatter(): got_e = lax.ppermute(send_e, axis, cw)  18.5 us
    all_to_all x1, waiting for transfers between devices, body(): lax.all_to_all(grads_here, 'y', split_axis=1, concat_axis=0, tiled=True)  10.8 us
  transfers between devices with their start and end apart: 23, of which 17 were waited for; matrix products, arithmetic and copies ran while one was open for 2% of the time, Pallas kernels for 11%

profile of v5, /device:TPU:2, one launch (start us, length us, event | category | flops | bytes accessed | tf_op | source)
XLA Modules:
  0.0 330.5 jit_solution(1954754460907756605)
XLA Ops:
  10.2 10.2 %shard_map.46 = (f32[128,4096]{1,0:T(8,128)}, bf16[128,4096]{1,0:T(8,128)(2,1)}) custom-call(s32[256]{0:T(256)} %reshape_squeeze.3.cols_ref, bf16[128,4096]{1,0:T(8,128)(2,1)} %broadcast_select_fusion.3.h_ref, bf16[32,8,128,128]{3,2,1,0:T(8,128)(2,1)} %bitcast.63), custom_call_target="tpu_custom_call" | custom-call | flops 1073741824 | bytes 12582912 | tf_op jit(solution)/shard_map/pallas_call | solution.py:85
  21.7 2.4 collective-permute-done
  25.3 9.9 %shard_map.47 = (f32[128,4096]{1,0:T(8,128)}, bf16[128,4096]{1,0:T(8,128)(2,1)}) custom-call(s32[256]{0:T(256)} %reshape_squeeze.3.cols_ref, bf16[128,4096]{1,0:T(8,128)(2,1)} %broadcast_select_fusion.2.h_ref, bf16[32,8,128,128]{3,2,1,0:T(8,128)(2,1)} %bitcast.64), custom_call_target="tpu_custom_call" | custom-call | flops 1073741824 | bytes 12582912 | tf_op jit(solution)/shard_map/pallas_call | solution.py:85
  35.2 13.2 %collective-permute-start.1 = (bf16[128,4096]{1,0:T(8,128)(2,1)}, bf16[128,4096]{1,0:T(8,128)(2,1)S(1)}, u32[]{:S(2)}, u32[]{:S(2)}) collective-permute-start(bf16[128,4096]{1,0:T(8,128)(2,1)} %get-tuple-element.20), channel_id=1, source_target_pairs={{0,64},{64,128},{128,192},{1,65},{65,129},{129,193},{2,66},{66,130... | collective-permute-start | bytes 3145736 | tf_op jit(solution)/shard_map/ppermute | solution.py:20
  51.9 10.1 %shard_map.48 = (f32[128,4096]{1,0:T(8,128)}, bf16[128,4096]{1,0:T(8,128)(2,1)}) custom-call(s32[256]{0:T(256)} %reshape_squeeze.3.cols_ref, bf16[128,4096]{1,0:T(8,128)(2,1)} %broadcast_select_fusion.1.h_ref, bf16[32,8,128,128]{3,2,1,0:T(8,128)(2,1)} %bitcast.65), custom_call_target="tpu_custom_call" | custom-call | flops 1073741824 | bytes 12582912 | tf_op jit(solution)/shard_map/pallas_call | solution.py:85
  62.0 16.4 %collective-permute-start.2 = (bf16[128,4096]{1,0:T(8,128)(2,1)}, bf16[128,4096]{1,0:T(8,128)(2,1)}, u32[]{:S(2)}, u32[]{:S(2)}) collective-permute-start(bf16[128,4096]{1,0:T(8,128)(2,1)} %get-tuple-element.21), channel_id=1, source_target_pairs={{0,64},{64,128},{128,192},{1,65},{65,129},{129,193},{2,66},{66,130... | collective-permute-start | bytes 3145736 | tf_op jit(solution)/shard_map/ppermute | solution.py:20
  81.8 10.1 %shard_map.49 = (f32[128,4096]{1,0:T(8,128)}, bf16[128,4096]{1,0:T(8,128)(2,1)}) custom-call(s32[256]{0:T(256)} %reshape_squeeze.3.cols_ref, bf16[128,4096]{1,0:T(8,128)(2,1)} %get-tuple-element.34.h_ref, bf16[32,8,128,128]{3,2,1,0:T(8,128)(2,1)} %bitcast.66), custom_call_target="tpu_custom_call" | custom-call | flops 1073741824 | bytes 12582912 | tf_op jit(solution)/shard_map/pallas_call | solution.py:85
  93.9 12.5 %shard_map.50 = (bf16[128,4096]{1,0:T(8,128)(2,1)}, bf16[128,4096]{1,0:T(8,128)(2,1)}) custom-call(s32[256]{0:T(256)} %reshape_squeeze.3.cols_ref, bf16[128,4096]{1,0:T(8,128)(2,1)} %broadcast_select_fusion.7.up_ref, f32[128,4096]{1,0:T(8,128)} %select_select_fusion.z_ref, bf16[32,8,128,128]{3,2,1,0:T(8,128)(2,1)} %bitcast.67), custom_call_target="tpu_custom_call" | custom-call | flops 1073741824 | bytes 13631488 | tf_op jit(solution)/shard_map/pallas_call | solution.py:117
  107.7 19.1 %collective-permute-done.3 = bf16[128,4096]{1,0:T(8,128)(2,1)S(1)} collective-permute-done((bf16[128,4096]{1,0:T(8,128)(2,1)}, bf16[128,4096]{1,0:T(8,128)(2,1)S(1)}, u32[]{:S(2)}, u32[]{:S(2)}) %collective-permute-start.3) | collective-permute-done | bytes 1048608 | tf_op jit(solution)/shard_map/ppermute | solution.py:20
  127.9 12.4 %shard_map.51 = (bf16[128,4096]{1,0:T(8,128)(2,1)}, bf16[128,4096]{1,0:T(8,128)(2,1)}) custom-call(s32[256]{0:T(256)} %reshape_squeeze.3.cols_ref, bf16[128,4096]{1,0:T(8,128)(2,1)} %broadcast_select_fusion.6.up_ref, f32[128,4096]{1,0:T(8,128)} %select_select_fusion.z_ref, bf16[32,8,128,128]{3,2,1,0:T(8,128)(2,1)} %bitcast.68), custom_call_target="tpu_custom_call" | custom-call | flops 1073741824 | bytes 13631488 | tf_op jit(solution)/shard_map/pallas_call | solution.py:117
  141.6 17.4 %collective-permute-done.4 = bf16[128,4096]{1,0:T(8,128)(2,1)S(1)} collective-permute-done((bf16[128,4096]{1,0:T(8,128)(2,1)}, bf16[128,4096]{1,0:T(8,128)(2,1)S(1)}, u32[]{:S(2)}, u32[]{:S(2)}) %collective-permute-start.4) | collective-permute-done | bytes 1048608 | tf_op jit(solution)/shard_map/ppermute | solution.py:20
  160.1 12.6 %shard_map.52 = (bf16[128,4096]{1,0:T(8,128)(2,1)}, bf16[128,4096]{1,0:T(8,128)(2,1)}) custom-call(s32[256]{0:T(256)} %reshape_squeeze.3.cols_ref, bf16[128,4096]{1,0:T(8,128)(2,1)} %broadcast_select_fusion.5.up_ref, f32[128,4096]{1,0:T(8,128)} %select_select_fusion.z_ref, bf16[32,8,128,128]{3,2,1,0:T(8,128)(2,1)} %bitcast.69), custom_call_target="tpu_custom_call" | custom-call | flops 1073741824 | bytes 13631488 | tf_op jit(solution)/shard_map/pallas_call | solution.py:117
  174.0 16.8 %collective-permute-done.5 = bf16[128,4096]{1,0:T(8,128)(2,1)S(1)} collective-permute-done((bf16[128,4096]{1,0:T(8,128)(2,1)}, bf16[128,4096]{1,0:T(8,128)(2,1)S(1)}, u32[]{:S(2)}, u32[]{:S(2)}) %collective-permute-start.5) | collective-permute-done | bytes 1048608 | tf_op jit(solution)/shard_map/ppermute | solution.py:20
  191.9 12.7 %shard_map.53 = (bf16[128,4096]{1,0:T(8,128)(2,1)}, bf16[128,4096]{1,0:T(8,128)(2,1)}) custom-call(s32[256]{0:T(256)} %reshape_squeeze.3.cols_ref, bf16[128,4096]{1,0:T(8,128)(2,1)} %broadcast_select_fusion.4.up_ref, f32[128,4096]{1,0:T(8,128)} %select_select_fusion.z_ref, bf16[32,8,128,128]{3,2,1,0:T(8,128)(2,1)} %bitcast.70), custom_call_target="tpu_custom_call" | custom-call | flops 1073741824 | bytes 13631488 | tf_op jit(solution)/shard_map/pallas_call | solution.py:117
  207.1 4.3 %all-to-all-start = ((bf16[128,4,1024]{2,0,1:T(8,128)(2,1)}), bf16[128,4,1024]{2,0,1:T(8,128)(2,1)S(1)}, u32[]{:S(2)}, u32[]{:S(2)}) async-start(bf16[128,4,1024]{2,0,1:T(8,128)(2,1)} %bitcast.59), calls=%async_computation | async-start | bytes 2097152 | tf_op jit(solution)/shard_map/all_to_all | solution.py:229
  211.5 10.8 %all-to-all-done = bf16[128,4,1024]{2,0,1:T(8,128)(2,1)S(1)} async-done(((bf16[128,4,1024]{2,0,1:T(8,128)(2,1)}), bf16[128,4,1024]{2,0,1:T(8,128)(2,1)S(1)}, u32[]{:S(2)}, u32[]{:S(2)}) %all-to-all-start) | async-done | bytes 1048608 | tf_op jit(solution)/shard_map/all_to_all | solution.py:229
  222.4 9.2 %shard_map.54 = f32[64,128,128]{2,1,0:T(8,128)S(1)} custom-call(s32[64]{0:T(128)S(1)} %dynamic_slice.59.cols_ref, bf16[512,4096]{1,0:T(8,128)(2,1)} %all-gather.2.cloned.1.call-done.h_ref, bf16[512,1024]{1,0:T(8,128)(2,1)S(1)} %bitcast.62), custom_call_target="tpu_custom_call" | custom-call | flops 1073741824 | bytes 9437184 | tf_op jit(solution)/shard_map/pallas_call | solution.py:158
  235.4 37.5 %collective-permute-done.6 = f32[4096,128]{1,0:T(8,128)S(1)} collective-permute-done((f32[4096,128]{1,0:T(8,128)}, f32[4096,128]{1,0:T(8,128)S(1)}, u32[]{:S(2)}, u32[]{:S(2)}) %collective-permute-start.6) | collective-permute-done | bytes 2097184 | tf_op jit(solution)/shard_map/ppermute | solution.py:237
  276.9 4.2 %collective-permute-start.14 = (f32[256,128]{1,0:T(8,128)S(1)}, f32[256,128]{1,0:T(8,128)S(1)}, u32[]{:S(2)}, u32[]{:S(2)}) collective-permute-start(f32[256,128]{1,0:T(8,128)S(1)} %dynamic-slice_bitcast_fusion.1), channel_id=1, source_target_pairs={{0,7},{1,0},{2,1},{3,2},{4,3},{5,4},{6,5},{7,6},{8,15},{9,8},{10,9... | collective-permute-start | bytes 393224 | tf_op jit(solution)/shard_map/ppermute | solution.py:187
  281.2 2.4 collective-permute-done.7
  283.8 3.7 %collective-permute-start.15 = (f32[256,128]{1,0:T(8,128)S(1)}, f32[256,128]{1,0:T(8,128)S(1)}, u32[]{:S(2)}, u32[]{:S(2)}) collective-permute-start(f32[256,128]{1,0:T(8,128)S(1)} %bitcast_add_fusion.7), channel_id=1, source_target_pairs={{0,7},{1,0},{2,1},{3,2},{4,3},{5,4},{6,5},{7,6},{8,15},{9,8},{10,9... | collective-permute-start | bytes 393224 | tf_op jit(solution)/shard_map/ppermute | solution.py:187
  287.5 2.4 collective-permute-done.8
  290.0 3.7 %collective-permute-start.16 = (f32[256,128]{1,0:T(8,128)S(1)}, f32[256,128]{1,0:T(8,128)S(1)}, u32[]{:S(2)}, u32[]{:S(2)}) collective-permute-start(f32[256,128]{1,0:T(8,128)S(1)} %bitcast_add_fusion.6), channel_id=1, source_target_pairs={{0,7},{1,0},{2,1},{3,2},{4,3},{5,4},{6,5},{7,6},{8,15},{9,8},{10,9... | collective-permute-start | bytes 393224 | tf_op jit(solution)/shard_map/ppermute | solution.py:187
  293.7 2.4 collective-permute-done.9
  296.3 3.7 %collective-permute-start.17 = (f32[256,128]{1,0:T(8,128)S(1)}, f32[256,128]{1,0:T(8,128)S(1)}, u32[]{:S(2)}, u32[]{:S(2)}) collective-permute-start(f32[256,128]{1,0:T(8,128)S(1)} %bitcast_add_fusion.5), channel_id=1, source_target_pairs={{0,7},{1,0},{2,1},{3,2},{4,3},{5,4},{6,5},{7,6},{8,15},{9,8},{10,9... | collective-permute-start | bytes 393224 | tf_op jit(solution)/shard_map/ppermute | solution.py:187
  300.0 3.3 %collective-permute-done.10 = f32[256,128]{1,0:T(8,128)S(1)} collective-permute-done((f32[256,128]{1,0:T(8,128)S(1)}, f32[256,128]{1,0:T(8,128)S(1)}, u32[]{:S(2)}, u32[]{:S(2)}) %collective-permute-start.10) | collective-permute-done | bytes 131104 | tf_op jit(solution)/shard_map/ppermute | solution.py:186
  303.6 3.8 %collective-permute-start.18 = (f32[256,128]{1,0:T(8,128)S(1)}, f32[256,128]{1,0:T(8,128)S(1)}, u32[]{:S(2)}, u32[]{:S(2)}) collective-permute-start(f32[256,128]{1,0:T(8,128)S(1)} %bitcast_add_fusion.4), channel_id=1, source_target_pairs={{0,7},{1,0},{2,1},{3,2},{4,3},{5,4},{6,5},{7,6},{8,15},{9,8},{10,9... | collective-permute-start | bytes 393224 | tf_op jit(solution)/shard_map/ppermute | solution.py:187
  307.4 3.0 collective-permute-done.11
  310.5 3.7 %collective-permute-start.19 = (f32[256,128]{1,0:T(8,128)S(1)}, f32[256,128]{1,0:T(8,128)S(1)}, u32[]{:S(2)}, u32[]{:S(2)}) collective-permute-start(f32[256,128]{1,0:T(8,128)S(1)} %bitcast_add_fusion.3), channel_id=1, source_target_pairs={{0,7},{1,0},{2,1},{3,2},{4,3},{5,4},{6,5},{7,6},{8,15},{9,8},{10,9... | collective-permute-start | bytes 393224 | tf_op jit(solution)/shard_map/ppermute | solution.py:187
  314.2 2.4 collective-permute-done.12
  316.8 3.7 %collective-permute-start.20 = (f32[256,128]{1,0:T(8,128)S(1)}, f32[256,128]{1,0:T(8,128)S(1)}, u32[]{:S(2)}, u32[]{:S(2)}) collective-permute-start(f32[256,128]{1,0:T(8,128)S(1)} %bitcast_add_fusion.2), channel_id=1, source_target_pairs={{0,7},{1,0},{2,1},{3,2},{4,3},{5,4},{6,5},{7,6},{8,15},{9,8},{10,9... | collective-permute-start | bytes 393224 | tf_op jit(solution)/shard_map/ppermute | solution.py:187
  320.5 2.4 collective-permute-done.13
  (78 shorter events, 34.2 us)
Async XLA Ops:
  6.5 215.8 %all-gather.2.cloned.1.call-start = ((), (), s32[]{:S(2)}) async-start(), calls=%async_computation.1 | async-start | bytes 5242880 | tf_op jit(solution)/shard_map/all_gather | solution.py:232
  10.2 13.9 %copy-start.2 = (bf16[128,4096]{1,0:T(8,128)(2,1)S(1)}, bf16[128,4096]{1,0:T(8,128)(2,1)}, u32[]{:S(2)}) copy-start(bf16[128,4096]{1,0:T(8,128)(2,1)} %param.4) | copy-start | bytes 3145732
  20.4 3.8 %collective-permute-start = (bf16[128,4096]{1,0:T(8,128)(2,1)}, bf16[128,4096]{1,0:T(8,128)(2,1)S(1)}, u32[]{:S(2)}, u32[]{:S(2)}) collective-permute-start(bf16[128,4096]{1,0:T(8,128)(2,1)} %get-tuple-element.19), channel_id=1, source_target_pairs={{0,64},{64,128},{128,192},{1,65},{65,129},{129,193},{2,66},{66,130... | collective-permute-start | bytes 3145736 | tf_op jit(solution)/shard_map/ppermute | solution.py:20
  35.2 15.6 %collective-permute-start.1 = (bf16[128,4096]{1,0:T(8,128)(2,1)}, bf16[128,4096]{1,0:T(8,128)(2,1)S(1)}, u32[]{:S(2)}, u32[]{:S(2)}) collective-permute-start(bf16[128,4096]{1,0:T(8,128)(2,1)} %get-tuple-element.20), channel_id=1, source_target_pairs={{0,64},{64,128},{128,192},{1,65},{65,129},{129,193},{2,66},{66,130... | collective-permute-start | bytes 3145736 | tf_op jit(solution)/shard_map/ppermute | solution.py:20
  51.9 26.6 %copy-start.1 = (bf16[128,4096]{1,0:T(8,128)(2,1)S(1)}, bf16[128,4096]{1,0:T(8,128)(2,1)}, u32[]{:S(2)}) copy-start(bf16[128,4096]{1,0:T(8,128)(2,1)} %param.5) | copy-start | bytes 3145732
  62.0 18.1 %copy-start.3 = (bf16[128,4096]{1,0:T(8,128)(2,1)S(1)}, bf16[128,4096]{1,0:T(8,128)(2,1)}, u32[]{:S(2)}) copy-start(bf16[128,4096]{1,0:T(8,128)(2,1)} %broadcast_select_fusion.2.h_ref) | copy-start | bytes 3145732
  62.0 18.1 %collective-permute-start.2 = (bf16[128,4096]{1,0:T(8,128)(2,1)}, bf16[128,4096]{1,0:T(8,128)(2,1)}, u32[]{:S(2)}, u32[]{:S(2)}) collective-permute-start(bf16[128,4096]{1,0:T(8,128)(2,1)} %get-tuple-element.21), channel_id=1, source_target_pairs={{0,64},{64,128},{128,192},{1,65},{65,129},{129,193},{2,66},{66,130... | collective-permute-start | bytes 3145736 | tf_op jit(solution)/shard_map/ppermute | solution.py:20
  81.8 10.1 %copy-start.5 = (f32[128,4096]{1,0:T(8,128)S(1)}, f32[128,4096]{1,0:T(8,128)}, u32[]{:S(2)}) copy-start(f32[128,4096]{1,0:T(8,128)} %get-tuple-element.25) | copy-start | bytes 6291460
  106.4 20.4 %collective-permute-start.3 = (bf16[128,4096]{1,0:T(8,128)(2,1)}, bf16[128,4096]{1,0:T(8,128)(2,1)S(1)}, u32[]{:S(2)}, u32[]{:S(2)}) collective-permute-start(bf16[128,4096]{1,0:T(8,128)(2,1)} %get-tuple-element.26), channel_id=1, source_target_pairs={{64,0},{128,64},{192,128},{65,1},{129,65},{193,129},{66,2},{130,66... | collective-permute-start | bytes 3145736 | tf_op jit(solution)/shard_map/ppermute | solution.py:20
  140.3 18.7 %collective-permute-start.4 = (bf16[128,4096]{1,0:T(8,128)(2,1)}, bf16[128,4096]{1,0:T(8,128)(2,1)S(1)}, u32[]{:S(2)}, u32[]{:S(2)}) collective-permute-start(bf16[128,4096]{1,0:T(8,128)(2,1)} %get-tuple-element.27), channel_id=1, source_target_pairs={{64,0},{128,64},{192,128},{65,1},{129,65},{193,129},{66,2},{130,66... | collective-permute-start | bytes 3145736 | tf_op jit(solution)/shard_map/ppermute | solution.py:20
  172.7 18.1 %collective-permute-start.5 = (bf16[128,4096]{1,0:T(8,128)(2,1)}, bf16[128,4096]{1,0:T(8,128)(2,1)S(1)}, u32[]{:S(2)}, u32[]{:S(2)}) collective-permute-start(bf16[128,4096]{1,0:T(8,128)(2,1)} %get-tuple-element.28), channel_id=1, source_target_pairs={{64,0},{128,64},{192,128},{65,1},{129,65},{193,129},{66,2},{130,66... | collective-permute-start | bytes 3145736 | tf_op jit(solution)/shard_map/ppermute | solution.py:20
  191.9 12.7 %copy-start.6 = (bf16[128,4096]{1,0:T(8,128)(2,1)S(1)}, bf16[128,4096]{1,0:T(8,128)(2,1)}, u32[]{:S(2)}) copy-start(bf16[128,4096]{1,0:T(8,128)(2,1)} %get-tuple-element.32) | copy-start | bytes 3145732
  191.9 12.7 %copy-start.7 = (bf16[128,4096]{1,0:T(8,128)(2,1)S(1)}, bf16[128,4096]{1,0:T(8,128)(2,1)}, u32[]{:S(2)}) copy-start(bf16[128,4096]{1,0:T(8,128)(2,1)} %get-tuple-element.31) | copy-start | bytes 3145732
  191.9 12.7 %copy-start.8 = (bf16[128,4096]{1,0:T(8,128)(2,1)S(1)}, bf16[128,4096]{1,0:T(8,128)(2,1)}, u32[]{:S(2)}) copy-start(bf16[128,4096]{1,0:T(8,128)(2,1)} %get-tuple-element.30) | copy-start | bytes 3145732
  206.1 5.4 %copy-start.9 = (s32[256]{0:T(256)S(1)}, s32[256]{0:T(256)}, u32[]{:S(2)}) copy-start(s32[256]{0:T(256)} %reshape_squeeze.3.cols_ref) | copy-start | bytes 3076
  207.1 15.2 %all-to-all-start = ((bf16[128,4,1024]{2,0,1:T(8,128)(2,1)}), bf16[128,4,1024]{2,0,1:T(8,128)(2,1)S(1)}, u32[]{:S(2)}, u32[]{:S(2)}) async-start(bf16[128,4,1024]{2,0,1:T(8,128)(2,1)} %bitcast.59), calls=%async_computation | async-start | bytes 2097152 | tf_op jit(solution)/shard_map/all_to_all | solution.py:229
  231.6 2.6 copy-start
  234.2 38.7 %collective-permute-start.6 = (f32[4096,128]{1,0:T(8,128)}, f32[4096,128]{1,0:T(8,128)S(1)}, u32[]{:S(2)}, u32[]{:S(2)}) collective-permute-start(f32[4096,128]{1,0:T(8,128)} %dynamic-slice_bitcast_fusion), channel_id=1, source_target_pairs={{0,8},{8,0},{1,9},{9,1},{2,10},{10,2},{3,11},{11,3},{4,12},{12,4},... | collective-permute-start | bytes 6291464 | tf_op jit(solution)/shard_map/ppermute | solution.py:237
  274.9 8.7 %collective-permute-start.7 = (f32[256,128]{1,0:T(8,128)S(1)}, f32[256,128]{1,0:T(8,128)S(1)}, u32[]{:S(2)}, u32[]{:S(2)}) collective-permute-start(f32[256,128]{1,0:T(8,128)S(1)} %dynamic-slice_bitcast_fusion.2), channel_id=1, source_target_pairs={{0,1},{1,2},{2,3},{3,4},{4,5},{5,6},{6,7},{7,0},{8,9},{9,10},{10,1... | collective-permute-start | bytes 393224 | tf_op jit(solution)/shard_map/ppermute | solution.py:186
  276.9 6.8 %collective-permute-start.14 = (f32[256,128]{1,0:T(8,128)S(1)}, f32[256,128]{1,0:T(8,128)S(1)}, u32[]{:S(2)}, u32[]{:S(2)}) collective-permute-start(f32[256,128]{1,0:T(8,128)S(1)} %dynamic-slice_bitcast_fusion.1), channel_id=1, source_target_pairs={{0,7},{1,0},{2,1},{3,2},{4,3},{5,4},{6,5},{7,6},{8,15},{9,8},{10,9... | collective-permute-start | bytes 393224 | tf_op jit(solution)/shard_map/ppermute | solution.py:187
  283.6 6.3 %collective-permute-start.8 = (f32[256,128]{1,0:T(8,128)S(1)}, f32[256,128]{1,0:T(8,128)S(1)}, u32[]{:S(2)}, u32[]{:S(2)}) collective-permute-start(f32[256,128]{1,0:T(8,128)S(1)} %bitcast_add_fusion.14), channel_id=1, source_target_pairs={{0,1},{1,2},{2,3},{3,4},{4,5},{5,6},{6,7},{7,0},{8,9},{9,10},{10,1... | collective-permute-start | bytes 393224 | tf_op jit(solution)/shard_map/ppermute | solution.py:186
  283.8 6.2 %collective-permute-start.15 = (f32[256,128]{1,0:T(8,128)S(1)}, f32[256,128]{1,0:T(8,128)S(1)}, u32[]{:S(2)}, u32[]{:S(2)}) collective-permute-start(f32[256,128]{1,0:T(8,128)S(1)} %bitcast_add_fusion.7), channel_id=1, source_target_pairs={{0,7},{1,0},{2,1},{3,2},{4,3},{5,4},{6,5},{7,6},{8,15},{9,8},{10,9... | collective-permute-start | bytes 393224 | tf_op jit(solution)/shard_map/ppermute | solution.py:187
  289.9 6.3 %collective-permute-start.9 = (f32[256,128]{1,0:T(8,128)S(1)}, f32[256,128]{1,0:T(8,128)S(1)}, u32[]{:S(2)}, u32[]{:S(2)}) collective-permute-start(f32[256,128]{1,0:T(8,128)S(1)} %bitcast_add_fusion.13), channel_id=1, source_target_pairs={{0,1},{1,2},{2,3},{3,4},{4,5},{5,6},{6,7},{7,0},{8,9},{9,10},{10,1... | collective-permute-start | bytes 393224 | tf_op jit(solution)/shard_map/ppermute | solution.py:186
  290.0 6.2 %collective-permute-start.16 = (f32[256,128]{1,0:T(8,128)S(1)}, f32[256,128]{1,0:T(8,128)S(1)}, u32[]{:S(2)}, u32[]{:S(2)}) collective-permute-start(f32[256,128]{1,0:T(8,128)S(1)} %bitcast_add_fusion.6), channel_id=1, source_target_pairs={{0,7},{1,0},{2,1},{3,2},{4,3},{5,4},{6,5},{7,6},{8,15},{9,8},{10,9... | collective-permute-start | bytes 393224 | tf_op jit(solution)/shard_map/ppermute | solution.py:187
  296.2 7.2 %collective-permute-start.10 = (f32[256,128]{1,0:T(8,128)S(1)}, f32[256,128]{1,0:T(8,128)S(1)}, u32[]{:S(2)}, u32[]{:S(2)}) collective-permute-start(f32[256,128]{1,0:T(8,128)S(1)} %bitcast_add_fusion.12), channel_id=1, source_target_pairs={{0,1},{1,2},{2,3},{3,4},{4,5},{5,6},{6,7},{7,0},{8,9},{9,10},{10,1... | collective-permute-start | bytes 393224 | tf_op jit(solution)/shard_map/ppermute | solution.py:186
  296.3 7.3 %collective-permute-start.17 = (f32[256,128]{1,0:T(8,128)S(1)}, f32[256,128]{1,0:T(8,128)S(1)}, u32[]{:S(2)}, u32[]{:S(2)}) collective-permute-start(f32[256,128]{1,0:T(8,128)S(1)} %bitcast_add_fusion.5), channel_id=1, source_target_pairs={{0,7},{1,0},{2,1},{3,2},{4,3},{5,4},{6,5},{7,6},{8,15},{9,8},{10,9... | collective-permute-start | bytes 393224 | tf_op jit(solution)/shard_map/ppermute | solution.py:187
  303.4 7.0 %collective-permute-start.11 = (f32[256,128]{1,0:T(8,128)S(1)}, f32[256,128]{1,0:T(8,128)S(1)}, u32[]{:S(2)}, u32[]{:S(2)}) collective-permute-start(f32[256,128]{1,0:T(8,128)S(1)} %bitcast_add_fusion.11), channel_id=1, source_target_pairs={{0,1},{1,2},{2,3},{3,4},{4,5},{5,6},{6,7},{7,0},{8,9},{9,10},{10,1... | collective-permute-start | bytes 393224 | tf_op jit(solution)/shard_map/ppermute | solution.py:186
  303.6 6.9 %collective-permute-start.18 = (f32[256,128]{1,0:T(8,128)S(1)}, f32[256,128]{1,0:T(8,128)S(1)}, u32[]{:S(2)}, u32[]{:S(2)}) collective-permute-start(f32[256,128]{1,0:T(8,128)S(1)} %bitcast_add_fusion.4), channel_id=1, source_target_pairs={{0,7},{1,0},{2,1},{3,2},{4,3},{5,4},{6,5},{7,6},{8,15},{9,8},{10,9... | collective-permute-start | bytes 393224 | tf_op jit(solution)/shard_map/ppermute | solution.py:187
  310.4 6.3 %collective-permute-start.12 = (f32[256,128]{1,0:T(8,128)S(1)}, f32[256,128]{1,0:T(8,128)S(1)}, u32[]{:S(2)}, u32[]{:S(2)}) collective-permute-start(f32[256,128]{1,0:T(8,128)S(1)} %bitcast_add_fusion.10), channel_id=1, source_target_pairs={{0,1},{1,2},{2,3},{3,4},{4,5},{5,6},{6,7},{7,0},{8,9},{9,10},{10,1... | collective-permute-start | bytes 393224 | tf_op jit(solution)/shard_map/ppermute | solution.py:186
  310.5 6.2 %collective-permute-start.19 = (f32[256,128]{1,0:T(8,128)S(1)}, f32[256,128]{1,0:T(8,128)S(1)}, u32[]{:S(2)}, u32[]{:S(2)}) collective-permute-start(f32[256,128]{1,0:T(8,128)S(1)} %bitcast_add_fusion.3), channel_id=1, source_target_pairs={{0,7},{1,0},{2,1},{3,2},{4,3},{5,4},{6,5},{7,6},{8,15},{9,8},{10,9... | collective-permute-start | bytes 393224 | tf_op jit(solution)/shard_map/ppermute | solution.py:187
  316.7 6.3 %collective-permute-start.13 = (f32[256,128]{1,0:T(8,128)S(1)}, f32[256,128]{1,0:T(8,128)S(1)}, u32[]{:S(2)}, u32[]{:S(2)}) collective-permute-start(f32[256,128]{1,0:T(8,128)S(1)} %bitcast_add_fusion.9), channel_id=1, source_target_pairs={{0,1},{1,2},{2,3},{3,4},{4,5},{5,6},{6,7},{7,0},{8,9},{9,10},{10,1... | collective-permute-start | bytes 393224 | tf_op jit(solution)/shard_map/ppermute | solution.py:186
  316.8 6.2 %collective-permute-start.20 = (f32[256,128]{1,0:T(8,128)S(1)}, f32[256,128]{1,0:T(8,128)S(1)}, u32[]{:S(2)}, u32[]{:S(2)}) collective-permute-start(f32[256,128]{1,0:T(8,128)S(1)} %bitcast_add_fusion.2), channel_id=1, source_target_pairs={{0,7},{1,0},{2,1},{3,2},{4,3},{5,4},{6,5},{7,6},{8,15},{9,8},{10,9... | collective-permute-start | bytes 393224 | tf_op jit(solution)/shard_map/ppermute | solution.py:187
  (1 other events, 1.6 us)
Sparse Core Ops, SparseCore 0:
  107.9 72.5 all-gather.1

commit v6 on v5

--- a/solution.py
+++ b/solution.py
@@ -26,12 +26,16 @@
     step = pl.program_id(0)
     for jj in range(w_ref.shape[0]):
         j = step * w_ref.shape[0] + jj
-        acc = None
-        for k in range(per_block):
-            c = cols_ref[j * per_block + k]
-            x = h_ref[:, pl.ds(pl.multiple_of(c * edge, edge), edge)]
-            part = jnp.dot(x, w_ref[jj, k], preferred_element_type=jnp.float32)
-            acc = part if acc is None else acc + part
+        picked = jnp.concatenate(
+            [
+                h_ref[:, pl.ds(pl.multiple_of(cols_ref[j * per_block + k] * edge, edge), edge)]
+                for k in range(per_block)
+            ],
+            axis=1,
+        )
+        acc = jnp.dot(
+            picked, w_ref[jj].reshape(per_block * edge, edge), preferred_element_type=jnp.float32
+        )
         z_ref[:, jj * edge:(jj + 1) * edge] = acc
         own = h_ref[:, pl.ds(pl.multiple_of(j * edge, edge), edge)].astype(jnp.float32)
         out_ref[:, jj * edge:(jj + 1) * edge] = (own + acc * jax.nn.sigmoid(acc)).astype(out_ref.dtype)
@@ -53,13 +57,16 @@
         s = jax.nn.sigmoid(z)
         g = (u * s * (1.0 + z * (1.0 - s))).astype(jnp.bfloat16)
         g_ref[:, jj * edge:(jj + 1) * edge] = g
+        spread = lax.dot_general(
+            g,
+            w_ref[jj].reshape(per_block * edge, edge),
+            (((1,), (1,)), ((), ())),
+            preferred_element_type=jnp.float32,
+        )
         for k in range(per_block):
             c = cols_ref[j * per_block + k]
-            contrib = lax.dot_general(
-                g, w_ref[jj, k], (((1,), (1,)), ((), ())), preferred_element_type=jnp.float32
-            )
             at = pl.ds(pl.multiple_of(c * edge, edge), edge)
-            back_ref[:, at] = back_ref[:, at] + contrib
+            back_ref[:, at] = back_ref[:, at] + spread[:, k * edge:(k + 1) * edge]
 
     @pl.when(step == pl.num_programs(0) - 1)
     def _():

time: 337 us -> 332 us (0.985)
  Pallas kernels: 99.8 us -> 95.4 us
    pallas_call x4, Pallas kernels: 50.2 us -> 45.9 us  [layer_backward(): pl.pallas_call(backward_kernel, grid_spec=grid, out_shape=[jax.ShapeDtype...]
where the time goes in v6:
time: 332 us; the launch traced here: 326 us
  waiting for transfers between devices  126 us (38%)
  Pallas kernels  95.4 us (29%)
  starting transfers between devices  69.4 us (21%)
  other arithmetic  16.7 us (5%)
  between operations  13.7 us (4%)
  local copies, waits for them, and re-layouts  5.36 us (2%)
    ppermute x6, waiting for transfers between devices, from_behind(): return lax.ppermute(block, axis, route)  58.6 us
    pallas_call x4, Pallas kernels, layer_backward(): pl.pallas_call(backward_kernel, grid_spec=grid, out_shape=[jax.ShapeDtype...  45.9 us
    pallas_call x4, Pallas kernels, layer_forward(): pl.pallas_call(forward_kernel, grid_spec=grid, out_shape=[jax.ShapeDtypeS...  40.3 us
    ppermute x1, waiting for transfers between devices, body(): lax.ppermute(lax.dynamic_index_in_dim(halves, 1 - side, 0, False), 'xlo',...  37.5 us
    ppermute x6, starting transfers between devices, from_behind(): return lax.ppermute(block, axis, route)  34.8 us
    ppermute x7, starting transfers between devices, ring_reduce_scatter(): got_w = lax.ppermute(send_w, axis, ccw)  26.5 us
    ppermute x7, waiting for transfers between devices, ring_reduce_scatter(): got_e = lax.ppermute(send_e, axis, cw)  18.5 us
    all_to_all x1, waiting for transfers between devices, body(): lax.all_to_all(grads_here, 'y', split_axis=1, concat_axis=0, tiled=True)  10.8 us
  transfers between devices with their start and end apart: 23, of which 17 were waited for; matrix products, arithmetic and copies ran while one was open for 2% of the time, Pallas kernels for 11%

profile of v6, /device:TPU:2, one launch (start us, length us, event | category | flops | bytes accessed | tf_op | source)
XLA Modules:
  0.0 326.1 jit_solution(10736618717161971603)
XLA Ops:
  10.2 10.1 %shard_map.46 = (f32[128,4096]{1,0:T(8,128)}, bf16[128,4096]{1,0:T(8,128)(2,1)}) custom-call(s32[256]{0:T(256)} %reshape_squeeze.3.cols_ref, bf16[128,4096]{1,0:T(8,128)(2,1)} %broadcast_select_fusion.3.h_ref, bf16[32,8,128,128]{3,2,1,0:T(8,128)(2,1)} %bitcast.63), custom_call_target="tpu_custom_call" | custom-call | flops 1073741824 | bytes 12582912 | tf_op jit(solution)/shard_map/pallas_call | solution.py:92
  21.7 2.4 collective-permute-done
  25.2 9.9 %shard_map.47 = (f32[128,4096]{1,0:T(8,128)}, bf16[128,4096]{1,0:T(8,128)(2,1)}) custom-call(s32[256]{0:T(256)} %reshape_squeeze.3.cols_ref, bf16[128,4096]{1,0:T(8,128)(2,1)} %broadcast_select_fusion.2.h_ref, bf16[32,8,128,128]{3,2,1,0:T(8,128)(2,1)} %bitcast.64), custom_call_target="tpu_custom_call" | custom-call | flops 1073741824 | bytes 12582912 | tf_op jit(solution)/shard_map/pallas_call | solution.py:92
  35.2 13.1 %collective-permute-start.1 = (bf16[128,4096]{1,0:T(8,128)(2,1)}, bf16[128,4096]{1,0:T(8,128)(2,1)S(1)}, u32[]{:S(2)}, u32[]{:S(2)}) collective-permute-start(bf16[128,4096]{1,0:T(8,128)(2,1)} %get-tuple-element.20), channel_id=1, source_target_pairs={{0,64},{64,128},{128,192},{1,65},{65,129},{129,193},{2,66},{66,130... | collective-permute-start | bytes 3145736 | tf_op jit(solution)/shard_map/ppermute | solution.py:20
  48.3 2.4 collective-permute-done.1
  51.8 10.1 %shard_map.48 = (f32[128,4096]{1,0:T(8,128)}, bf16[128,4096]{1,0:T(8,128)(2,1)}) custom-call(s32[256]{0:T(256)} %reshape_squeeze.3.cols_ref, bf16[128,4096]{1,0:T(8,128)(2,1)} %broadcast_select_fusion.1.h_ref, bf16[32,8,128,128]{3,2,1,0:T(8,128)(2,1)} %bitcast.65), custom_call_target="tpu_custom_call" | custom-call | flops 1073741824 | bytes 12582912 | tf_op jit(solution)/shard_map/pallas_call | solution.py:92
  61.9 16.4 %collective-permute-start.2 = (bf16[128,4096]{1,0:T(8,128)(2,1)}, bf16[128,4096]{1,0:T(8,128)(2,1)}, u32[]{:S(2)}, u32[]{:S(2)}) collective-permute-start(bf16[128,4096]{1,0:T(8,128)(2,1)} %get-tuple-element.21), channel_id=1, source_target_pairs={{0,64},{64,128},{128,192},{1,65},{65,129},{129,193},{2,66},{66,130... | collective-permute-start | bytes 3145736 | tf_op jit(solution)/shard_map/ppermute | solution.py:20
  81.6 10.1 %shard_map.49 = (f32[128,4096]{1,0:T(8,128)}, bf16[128,4096]{1,0:T(8,128)(2,1)}) custom-call(s32[256]{0:T(256)} %reshape_squeeze.3.cols_ref, bf16[128,4096]{1,0:T(8,128)(2,1)} %get-tuple-element.34.h_ref, bf16[32,8,128,128]{3,2,1,0:T(8,128)(2,1)} %bitcast.66), custom_call_target="tpu_custom_call" | custom-call | flops 1073741824 | bytes 12582912 | tf_op jit(solution)/shard_map/pallas_call | solution.py:92
  93.7 11.5 %shard_map.50 = (bf16[128,4096]{1,0:T(8,128)(2,1)}, bf16[128,4096]{1,0:T(8,128)(2,1)}) custom-call(s32[256]{0:T(256)} %reshape_squeeze.3.cols_ref, bf16[128,4096]{1,0:T(8,128)(2,1)} %broadcast_select_fusion.7.up_ref, f32[128,4096]{1,0:T(8,128)} %select_select_fusion.z_ref, bf16[32,8,128,128]{3,2,1,0:T(8,128)(2,1)} %bitcast.67), custom_call_target="tpu_custom_call" | custom-call | flops 1073741824 | bytes 13631488 | tf_op jit(solution)/shard_map/pallas_call | solution.py:124
  106.5 19.0 %collective-permute-done.3 = bf16[128,4096]{1,0:T(8,128)(2,1)S(1)} collective-permute-done((bf16[128,4096]{1,0:T(8,128)(2,1)}, bf16[128,4096]{1,0:T(8,128)(2,1)S(1)}, u32[]{:S(2)}, u32[]{:S(2)}) %collective-permute-start.3) | collective-permute-done | bytes 1048608 | tf_op jit(solution)/shard_map/ppermute | solution.py:20
  126.6 11.4 %shard_map.51 = (bf16[128,4096]{1,0:T(8,128)(2,1)}, bf16[128,4096]{1,0:T(8,128)(2,1)}) custom-call(s32[256]{0:T(256)} %reshape_squeeze.3.cols_ref, bf16[128,4096]{1,0:T(8,128)(2,1)} %broadcast_select_fusion.6.up_ref, f32[128,4096]{1,0:T(8,128)} %select_select_fusion.z_ref, bf16[32,8,128,128]{3,2,1,0:T(8,128)(2,1)} %bitcast.68), custom_call_target="tpu_custom_call" | custom-call | flops 1073741824 | bytes 13631488 | tf_op jit(solution)/shard_map/pallas_call | solution.py:124
  139.3 17.4 %collective-permute-done.4 = bf16[128,4096]{1,0:T(8,128)(2,1)S(1)} collective-permute-done((bf16[128,4096]{1,0:T(8,128)(2,1)}, bf16[128,4096]{1,0:T(8,128)(2,1)S(1)}, u32[]{:S(2)}, u32[]{:S(2)}) %collective-permute-start.4) | collective-permute-done | bytes 1048608 | tf_op jit(solution)/shard_map/ppermute | solution.py:20
  157.7 11.5 %shard_map.52 = (bf16[128,4096]{1,0:T(8,128)(2,1)}, bf16[128,4096]{1,0:T(8,128)(2,1)}) custom-call(s32[256]{0:T(256)} %reshape_squeeze.3.cols_ref, bf16[128,4096]{1,0:T(8,128)(2,1)} %broadcast_select_fusion.5.up_ref, f32[128,4096]{1,0:T(8,128)} %select_select_fusion.z_ref, bf16[32,8,128,128]{3,2,1,0:T(8,128)(2,1)} %bitcast.69), custom_call_target="tpu_custom_call" | custom-call | flops 1073741824 | bytes 13631488 | tf_op jit(solution)/shard_map/pallas_call | solution.py:124
  170.5 16.8 %collective-permute-done.5 = bf16[128,4096]{1,0:T(8,128)(2,1)S(1)} collective-permute-done((bf16[128,4096]{1,0:T(8,128)(2,1)}, bf16[128,4096]{1,0:T(8,128)(2,1)S(1)}, u32[]{:S(2)}, u32[]{:S(2)}) %collective-permute-start.5) | collective-permute-done | bytes 1048608 | tf_op jit(solution)/shard_map/ppermute | solution.py:20
  188.5 11.6 %shard_map.53 = (bf16[128,4096]{1,0:T(8,128)(2,1)}, bf16[128,4096]{1,0:T(8,128)(2,1)}) custom-call(s32[256]{0:T(256)} %reshape_squeeze.3.cols_ref, bf16[128,4096]{1,0:T(8,128)(2,1)} %broadcast_select_fusion.4.up_ref, f32[128,4096]{1,0:T(8,128)} %select_select_fusion.z_ref, bf16[32,8,128,128]{3,2,1,0:T(8,128)(2,1)} %bitcast.70), custom_call_target="tpu_custom_call" | custom-call | flops 1073741824 | bytes 13631488 | tf_op jit(solution)/shard_map/pallas_call | solution.py:124
  202.6 4.4 %all-to-all-start = ((bf16[128,4,1024]{2,0,1:T(8,128)(2,1)}), bf16[128,4,1024]{2,0,1:T(8,128)(2,1)S(1)}, u32[]{:S(2)}, u32[]{:S(2)}) async-start(bf16[128,4,1024]{2,0,1:T(8,128)(2,1)} %bitcast.59), calls=%async_computation | async-start | bytes 2097152 | tf_op jit(solution)/shard_map/all_to_all | solution.py:236
  207.1 10.8 %all-to-all-done = bf16[128,4,1024]{2,0,1:T(8,128)(2,1)S(1)} async-done(((bf16[128,4,1024]{2,0,1:T(8,128)(2,1)}), bf16[128,4,1024]{2,0,1:T(8,128)(2,1)S(1)}, u32[]{:S(2)}, u32[]{:S(2)}) %all-to-all-start) | async-done | bytes 1048608 | tf_op jit(solution)/shard_map/all_to_all | solution.py:236
  217.9 9.2 %shard_map.54 = f32[64,128,128]{2,1,0:T(8,128)S(1)} custom-call(s32[64]{0:T(128)S(1)} %dynamic_slice.59.cols_ref, bf16[512,4096]{1,0:T(8,128)(2,1)} %all-gather.2.cloned.1.call-done.h_ref, bf16[512,1024]{1,0:T(8,128)(2,1)S(1)} %bitcast.62), custom_call_target="tpu_custom_call" | custom-call | flops 1073741824 | bytes 9437184 | tf_op jit(solution)/shard_map/pallas_call | solution.py:165
  230.9 37.5 %collective-permute-done.6 = f32[4096,128]{1,0:T(8,128)S(1)} collective-permute-done((f32[4096,128]{1,0:T(8,128)}, f32[4096,128]{1,0:T(8,128)S(1)}, u32[]{:S(2)}, u32[]{:S(2)}) %collective-permute-start.6) | collective-permute-done | bytes 2097184 | tf_op jit(solution)/shard_map/ppermute | solution.py:244
  272.5 4.3 %collective-permute-start.14 = (f32[256,128]{1,0:T(8,128)S(1)}, f32[256,128]{1,0:T(8,128)S(1)}, u32[]{:S(2)}, u32[]{:S(2)}) collective-permute-start(f32[256,128]{1,0:T(8,128)S(1)} %dynamic-slice_bitcast_fusion.1), channel_id=1, source_target_pairs={{0,7},{1,0},{2,1},{3,2},{4,3},{5,4},{6,5},{7,6},{8,15},{9,8},{10,9... | collective-permute-start | bytes 393224 | tf_op jit(solution)/shard_map/ppermute | solution.py:194
  276.7 2.4 collective-permute-done.7
  279.3 3.7 %collective-permute-start.15 = (f32[256,128]{1,0:T(8,128)S(1)}, f32[256,128]{1,0:T(8,128)S(1)}, u32[]{:S(2)}, u32[]{:S(2)}) collective-permute-start(f32[256,128]{1,0:T(8,128)S(1)} %bitcast_add_fusion.7), channel_id=1, source_target_pairs={{0,7},{1,0},{2,1},{3,2},{4,3},{5,4},{6,5},{7,6},{8,15},{9,8},{10,9... | collective-permute-start | bytes 393224 | tf_op jit(solution)/shard_map/ppermute | solution.py:194
  283.0 2.4 collective-permute-done.8
  285.6 3.7 %collective-permute-start.16 = (f32[256,128]{1,0:T(8,128)S(1)}, f32[256,128]{1,0:T(8,128)S(1)}, u32[]{:S(2)}, u32[]{:S(2)}) collective-permute-start(f32[256,128]{1,0:T(8,128)S(1)} %bitcast_add_fusion.6), channel_id=1, source_target_pairs={{0,7},{1,0},{2,1},{3,2},{4,3},{5,4},{6,5},{7,6},{8,15},{9,8},{10,9... | collective-permute-start | bytes 393224 | tf_op jit(solution)/shard_map/ppermute | solution.py:194
  289.3 2.4 collective-permute-done.9
  291.9 3.7 %collective-permute-start.17 = (f32[256,128]{1,0:T(8,128)S(1)}, f32[256,128]{1,0:T(8,128)S(1)}, u32[]{:S(2)}, u32[]{:S(2)}) collective-permute-start(f32[256,128]{1,0:T(8,128)S(1)} %bitcast_add_fusion.5), channel_id=1, source_target_pairs={{0,7},{1,0},{2,1},{3,2},{4,3},{5,4},{6,5},{7,6},{8,15},{9,8},{10,9... | collective-permute-start | bytes 393224 | tf_op jit(solution)/shard_map/ppermute | solution.py:194
  295.5 3.4 %collective-permute-done.10 = f32[256,128]{1,0:T(8,128)S(1)} collective-permute-done((f32[256,128]{1,0:T(8,128)S(1)}, f32[256,128]{1,0:T(8,128)S(1)}, u32[]{:S(2)}, u32[]{:S(2)}) %collective-permute-start.10) | collective-permute-done | bytes 131104 | tf_op jit(solution)/shard_map/ppermute | solution.py:193
  299.2 3.8 %collective-permute-start.18 = (f32[256,128]{1,0:T(8,128)S(1)}, f32[256,128]{1,0:T(8,128)S(1)}, u32[]{:S(2)}, u32[]{:S(2)}) collective-permute-start(f32[256,128]{1,0:T(8,128)S(1)} %bitcast_add_fusion.4), channel_id=1, source_target_pairs={{0,7},{1,0},{2,1},{3,2},{4,3},{5,4},{6,5},{7,6},{8,15},{9,8},{10,9... | collective-permute-start | bytes 393224 | tf_op jit(solution)/shard_map/ppermute | solution.py:194
  303.0 3.0 collective-permute-done.11
  306.1 3.7 %collective-permute-start.19 = (f32[256,128]{1,0:T(8,128)S(1)}, f32[256,128]{1,0:T(8,128)S(1)}, u32[]{:S(2)}, u32[]{:S(2)}) collective-permute-start(f32[256,128]{1,0:T(8,128)S(1)} %bitcast_add_fusion.3), channel_id=1, source_target_pairs={{0,7},{1,0},{2,1},{3,2},{4,3},{5,4},{6,5},{7,6},{8,15},{9,8},{10,9... | collective-permute-start | bytes 393224 | tf_op jit(solution)/shard_map/ppermute | solution.py:194
  312.3 3.7 %collective-permute-start.20 = (f32[256,128]{1,0:T(8,128)S(1)}, f32[256,128]{1,0:T(8,128)S(1)}, u32[]{:S(2)}, u32[]{:S(2)}) collective-permute-start(f32[256,128]{1,0:T(8,128)S(1)} %bitcast_add_fusion.2), channel_id=1, source_target_pairs={{0,7},{1,0},{2,1},{3,2},{4,3},{5,4},{6,5},{7,6},{8,15},{9,8},{10,9... | collective-permute-start | bytes 393224 | tf_op jit(solution)/shard_map/ppermute | solution.py:194
  316.1 2.4 collective-permute-done.13
  (78 shorter events, 34.1 us)
Async XLA Ops:
  6.5 211.3 %all-gather.2.cloned.1.call-start = ((), (), s32[]{:S(2)}) async-start(), calls=%async_computation.1 | async-start | bytes 5242880 | tf_op jit(solution)/shard_map/all_gather | solution.py:239
  10.2 13.9 %copy-start.2 = (bf16[128,4096]{1,0:T(8,128)(2,1)S(1)}, bf16[128,4096]{1,0:T(8,128)(2,1)}, u32[]{:S(2)}) copy-start(bf16[128,4096]{1,0:T(8,128)(2,1)} %param.4) | copy-start | bytes 3145732
  20.4 3.8 %collective-permute-start = (bf16[128,4096]{1,0:T(8,128)(2,1)}, bf16[128,4096]{1,0:T(8,128)(2,1)S(1)}, u32[]{:S(2)}, u32[]{:S(2)}) collective-permute-start(bf16[128,4096]{1,0:T(8,128)(2,1)} %get-tuple-element.19), channel_id=1, source_target_pairs={{0,64},{64,128},{128,192},{1,65},{65,129},{129,193},{2,66},{66,130... | collective-permute-start | bytes 3145736 | tf_op jit(solution)/shard_map/ppermute | solution.py:20
  35.2 15.5 %collective-permute-start.1 = (bf16[128,4096]{1,0:T(8,128)(2,1)}, bf16[128,4096]{1,0:T(8,128)(2,1)S(1)}, u32[]{:S(2)}, u32[]{:S(2)}) collective-permute-start(bf16[128,4096]{1,0:T(8,128)(2,1)} %get-tuple-element.20), channel_id=1, source_target_pairs={{0,64},{64,128},{128,192},{1,65},{65,129},{129,193},{2,66},{66,130... | collective-permute-start | bytes 3145736 | tf_op jit(solution)/shard_map/ppermute | solution.py:20
  51.8 26.5 %copy-start.1 = (bf16[128,4096]{1,0:T(8,128)(2,1)S(1)}, bf16[128,4096]{1,0:T(8,128)(2,1)}, u32[]{:S(2)}) copy-start(bf16[128,4096]{1,0:T(8,128)(2,1)} %param.5) | copy-start | bytes 3145732
  61.9 18.1 %copy-start.3 = (bf16[128,4096]{1,0:T(8,128)(2,1)S(1)}, bf16[128,4096]{1,0:T(8,128)(2,1)}, u32[]{:S(2)}) copy-start(bf16[128,4096]{1,0:T(8,128)(2,1)} %broadcast_select_fusion.2.h_ref) | copy-start | bytes 3145732
  61.9 18.1 %collective-permute-start.2 = (bf16[128,4096]{1,0:T(8,128)(2,1)}, bf16[128,4096]{1,0:T(8,128)(2,1)}, u32[]{:S(2)}, u32[]{:S(2)}) collective-permute-start(bf16[128,4096]{1,0:T(8,128)(2,1)} %get-tuple-element.21), channel_id=1, source_target_pairs={{0,64},{64,128},{128,192},{1,65},{65,129},{129,193},{2,66},{66,130... | collective-permute-start | bytes 3145736 | tf_op jit(solution)/shard_map/ppermute | solution.py:20
  81.6 10.1 %copy-start.5 = (f32[128,4096]{1,0:T(8,128)S(1)}, f32[128,4096]{1,0:T(8,128)}, u32[]{:S(2)}) copy-start(f32[128,4096]{1,0:T(8,128)} %get-tuple-element.25) | copy-start | bytes 6291460
  105.2 20.3 %collective-permute-start.3 = (bf16[128,4096]{1,0:T(8,128)(2,1)}, bf16[128,4096]{1,0:T(8,128)(2,1)S(1)}, u32[]{:S(2)}, u32[]{:S(2)}) collective-permute-start(bf16[128,4096]{1,0:T(8,128)(2,1)} %get-tuple-element.26), channel_id=1, source_target_pairs={{64,0},{128,64},{192,128},{65,1},{129,65},{193,129},{66,2},{130,66... | collective-permute-start | bytes 3145736 | tf_op jit(solution)/shard_map/ppermute | solution.py:20
  138.0 18.7 %collective-permute-start.4 = (bf16[128,4096]{1,0:T(8,128)(2,1)}, bf16[128,4096]{1,0:T(8,128)(2,1)S(1)}, u32[]{:S(2)}, u32[]{:S(2)}) collective-permute-start(bf16[128,4096]{1,0:T(8,128)(2,1)} %get-tuple-element.27), channel_id=1, source_target_pairs={{64,0},{128,64},{192,128},{65,1},{129,65},{193,129},{66,2},{130,66... | collective-permute-start | bytes 3145736 | tf_op jit(solution)/shard_map/ppermute | solution.py:20
  169.2 18.1 %collective-permute-start.5 = (bf16[128,4096]{1,0:T(8,128)(2,1)}, bf16[128,4096]{1,0:T(8,128)(2,1)S(1)}, u32[]{:S(2)}, u32[]{:S(2)}) collective-permute-start(bf16[128,4096]{1,0:T(8,128)(2,1)} %get-tuple-element.28), channel_id=1, source_target_pairs={{64,0},{128,64},{192,128},{65,1},{129,65},{193,129},{66,2},{130,66... | collective-permute-start | bytes 3145736 | tf_op jit(solution)/shard_map/ppermute | solution.py:20
  188.5 11.6 %copy-start.6 = (bf16[128,4096]{1,0:T(8,128)(2,1)S(1)}, bf16[128,4096]{1,0:T(8,128)(2,1)}, u32[]{:S(2)}) copy-start(bf16[128,4096]{1,0:T(8,128)(2,1)} %get-tuple-element.32) | copy-start | bytes 3145732
  188.5 11.6 %copy-start.7 = (bf16[128,4096]{1,0:T(8,128)(2,1)S(1)}, bf16[128,4096]{1,0:T(8,128)(2,1)}, u32[]{:S(2)}) copy-start(bf16[128,4096]{1,0:T(8,128)(2,1)} %get-tuple-element.31) | copy-start | bytes 3145732
  188.5 11.6 %copy-start.8 = (bf16[128,4096]{1,0:T(8,128)(2,1)S(1)}, bf16[128,4096]{1,0:T(8,128)(2,1)}, u32[]{:S(2)}) copy-start(bf16[128,4096]{1,0:T(8,128)(2,1)} %get-tuple-element.30) | copy-start | bytes 3145732
  201.5 5.4 %copy-start.9 = (s32[256]{0:T(256)S(1)}, s32[256]{0:T(256)}, u32[]{:S(2)}) copy-start(s32[256]{0:T(256)} %reshape_squeeze.3.cols_ref) | copy-start | bytes 3076
  202.6 15.3 %all-to-all-start = ((bf16[128,4,1024]{2,0,1:T(8,128)(2,1)}), bf16[128,4,1024]{2,0,1:T(8,128)(2,1)S(1)}, u32[]{:S(2)}, u32[]{:S(2)}) async-start(bf16[128,4,1024]{2,0,1:T(8,128)(2,1)} %bitcast.59), calls=%async_computation | async-start | bytes 2097152 | tf_op jit(solution)/shard_map/all_to_all | solution.py:236
  227.1 2.6 copy-start
  229.7 38.8 %collective-permute-start.6 = (f32[4096,128]{1,0:T(8,128)}, f32[4096,128]{1,0:T(8,128)S(1)}, u32[]{:S(2)}, u32[]{:S(2)}) collective-permute-start(f32[4096,128]{1,0:T(8,128)} %dynamic-slice_bitcast_fusion), channel_id=1, source_target_pairs={{0,8},{8,0},{1,9},{9,1},{2,10},{10,2},{3,11},{11,3},{4,12},{12,4},... | collective-permute-start | bytes 6291464 | tf_op jit(solution)/shard_map/ppermute | solution.py:244
  270.4 8.7 %collective-permute-start.7 = (f32[256,128]{1,0:T(8,128)S(1)}, f32[256,128]{1,0:T(8,128)S(1)}, u32[]{:S(2)}, u32[]{:S(2)}) collective-permute-start(f32[256,128]{1,0:T(8,128)S(1)} %dynamic-slice_bitcast_fusion.2), channel_id=1, source_target_pairs={{0,1},{1,2},{2,3},{3,4},{4,5},{5,6},{6,7},{7,0},{8,9},{9,10},{10,1... | collective-permute-start | bytes 393224 | tf_op jit(solution)/shard_map/ppermute | solution.py:193
  272.5 6.8 %collective-permute-start.14 = (f32[256,128]{1,0:T(8,128)S(1)}, f32[256,128]{1,0:T(8,128)S(1)}, u32[]{:S(2)}, u32[]{:S(2)}) collective-permute-start(f32[256,128]{1,0:T(8,128)S(1)} %dynamic-slice_bitcast_fusion.1), channel_id=1, source_target_pairs={{0,7},{1,0},{2,1},{3,2},{4,3},{5,4},{6,5},{7,6},{8,15},{9,8},{10,9... | collective-permute-start | bytes 393224 | tf_op jit(solution)/shard_map/ppermute | solution.py:194
  279.2 6.3 %collective-permute-start.8 = (f32[256,128]{1,0:T(8,128)S(1)}, f32[256,128]{1,0:T(8,128)S(1)}, u32[]{:S(2)}, u32[]{:S(2)}) collective-permute-start(f32[256,128]{1,0:T(8,128)S(1)} %bitcast_add_fusion.14), channel_id=1, source_target_pairs={{0,1},{1,2},{2,3},{3,4},{4,5},{5,6},{6,7},{7,0},{8,9},{9,10},{10,1... | collective-permute-start | bytes 393224 | tf_op jit(solution)/shard_map/ppermute | solution.py:193
  279.3 6.2 %collective-permute-start.15 = (f32[256,128]{1,0:T(8,128)S(1)}, f32[256,128]{1,0:T(8,128)S(1)}, u32[]{:S(2)}, u32[]{:S(2)}) collective-permute-start(f32[256,128]{1,0:T(8,128)S(1)} %bitcast_add_fusion.7), channel_id=1, source_target_pairs={{0,7},{1,0},{2,1},{3,2},{4,3},{5,4},{6,5},{7,6},{8,15},{9,8},{10,9... | collective-permute-start | bytes 393224 | tf_op jit(solution)/shard_map/ppermute | solution.py:194
  285.4 6.3 %collective-permute-start.9 = (f32[256,128]{1,0:T(8,128)S(1)}, f32[256,128]{1,0:T(8,128)S(1)}, u32[]{:S(2)}, u32[]{:S(2)}) collective-permute-start(f32[256,128]{1,0:T(8,128)S(1)} %bitcast_add_fusion.13), channel_id=1, source_target_pairs={{0,1},{1,2},{2,3},{3,4},{4,5},{5,6},{6,7},{7,0},{8,9},{9,10},{10,1... | collective-permute-start | bytes 393224 | tf_op jit(solution)/shard_map/ppermute | solution.py:193
  285.6 6.2 %collective-permute-start.16 = (f32[256,128]{1,0:T(8,128)S(1)}, f32[256,128]{1,0:T(8,128)S(1)}, u32[]{:S(2)}, u32[]{:S(2)}) collective-permute-start(f32[256,128]{1,0:T(8,128)S(1)} %bitcast_add_fusion.6), channel_id=1, source_target_pairs={{0,7},{1,0},{2,1},{3,2},{4,3},{5,4},{6,5},{7,6},{8,15},{9,8},{10,9... | collective-permute-start | bytes 393224 | tf_op jit(solution)/shard_map/ppermute | solution.py:194
  291.7 7.2 %collective-permute-start.10 = (f32[256,128]{1,0:T(8,128)S(1)}, f32[256,128]{1,0:T(8,128)S(1)}, u32[]{:S(2)}, u32[]{:S(2)}) collective-permute-start(f32[256,128]{1,0:T(8,128)S(1)} %bitcast_add_fusion.12), channel_id=1, source_target_pairs={{0,1},{1,2},{2,3},{3,4},{4,5},{5,6},{6,7},{7,0},{8,9},{9,10},{10,1... | collective-permute-start | bytes 393224 | tf_op jit(solution)/shard_map/ppermute | solution.py:193
  291.9 7.3 %collective-permute-start.17 = (f32[256,128]{1,0:T(8,128)S(1)}, f32[256,128]{1,0:T(8,128)S(1)}, u32[]{:S(2)}, u32[]{:S(2)}) collective-permute-start(f32[256,128]{1,0:T(8,128)S(1)} %bitcast_add_fusion.5), channel_id=1, source_target_pairs={{0,7},{1,0},{2,1},{3,2},{4,3},{5,4},{6,5},{7,6},{8,15},{9,8},{10,9... | collective-permute-start | bytes 393224 | tf_op jit(solution)/shard_map/ppermute | solution.py:194
  299.0 7.0 %collective-permute-start.11 = (f32[256,128]{1,0:T(8,128)S(1)}, f32[256,128]{1,0:T(8,128)S(1)}, u32[]{:S(2)}, u32[]{:S(2)}) collective-permute-start(f32[256,128]{1,0:T(8,128)S(1)} %bitcast_add_fusion.11), channel_id=1, source_target_pairs={{0,1},{1,2},{2,3},{3,4},{4,5},{5,6},{6,7},{7,0},{8,9},{9,10},{10,1... | collective-permute-start | bytes 393224 | tf_op jit(solution)/shard_map/ppermute | solution.py:193
  299.2 6.8 %collective-permute-start.18 = (f32[256,128]{1,0:T(8,128)S(1)}, f32[256,128]{1,0:T(8,128)S(1)}, u32[]{:S(2)}, u32[]{:S(2)}) collective-permute-start(f32[256,128]{1,0:T(8,128)S(1)} %bitcast_add_fusion.4), channel_id=1, source_target_pairs={{0,7},{1,0},{2,1},{3,2},{4,3},{5,4},{6,5},{7,6},{8,15},{9,8},{10,9... | collective-permute-start | bytes 393224 | tf_op jit(solution)/shard_map/ppermute | solution.py:194
  305.9 6.3 %collective-permute-start.12 = (f32[256,128]{1,0:T(8,128)S(1)}, f32[256,128]{1,0:T(8,128)S(1)}, u32[]{:S(2)}, u32[]{:S(2)}) collective-permute-start(f32[256,128]{1,0:T(8,128)S(1)} %bitcast_add_fusion.10), channel_id=1, source_target_pairs={{0,1},{1,2},{2,3},{3,4},{4,5},{5,6},{6,7},{7,0},{8,9},{9,10},{10,1... | collective-permute-start | bytes 393224 | tf_op jit(solution)/shard_map/ppermute | solution.py:193
  306.1 6.2 %collective-permute-start.19 = (f32[256,128]{1,0:T(8,128)S(1)}, f32[256,128]{1,0:T(8,128)S(1)}, u32[]{:S(2)}, u32[]{:S(2)}) collective-permute-start(f32[256,128]{1,0:T(8,128)S(1)} %bitcast_add_fusion.3), channel_id=1, source_target_pairs={{0,7},{1,0},{2,1},{3,2},{4,3},{5,4},{6,5},{7,6},{8,15},{9,8},{10,9... | collective-permute-start | bytes 393224 | tf_op jit(solution)/shard_map/ppermute | solution.py:194
  312.2 6.3 %collective-permute-start.13 = (f32[256,128]{1,0:T(8,128)S(1)}, f32[256,128]{1,0:T(8,128)S(1)}, u32[]{:S(2)}, u32[]{:S(2)}) collective-permute-start(f32[256,128]{1,0:T(8,128)S(1)} %bitcast_add_fusion.9), channel_id=1, source_target_pairs={{0,1},{1,2},{2,3},{3,4},{4,5},{5,6},{6,7},{7,0},{8,9},{9,10},{10,1... | collective-permute-start | bytes 393224 | tf_op jit(solution)/shard_map/ppermute | solution.py:193
  312.3 6.2 %collective-permute-start.20 = (f32[256,128]{1,0:T(8,128)S(1)}, f32[256,128]{1,0:T(8,128)S(1)}, u32[]{:S(2)}, u32[]{:S(2)}) collective-permute-start(f32[256,128]{1,0:T(8,128)S(1)} %bitcast_add_fusion.2), channel_id=1, source_target_pairs={{0,7},{1,0},{2,1},{3,2},{4,3},{5,4},{6,5},{7,6},{8,15},{9,8},{10,9... | collective-permute-start | bytes 393224 | tf_op jit(solution)/shard_map/ppermute | solution.py:194
  (1 other events, 1.6 us)
Sparse Core Ops, SparseCore 0:
  106.7 72.4 all-gather.1

commit v7 on v6

--- a/solution.py
+++ b/solution.py
@@ -205,26 +205,39 @@
     all_rows, layer_width = inputs.shape
     flat_cols = block_cols[0].reshape(-1)
 
-    stash_x = jnp.zeros((all_rows, layer_width), jnp.bfloat16)
-    stash_z = jnp.zeros((all_rows, layer_width), jnp.float32)
-    arrived = jnp.zeros((all_rows, layer_width), jnp.bfloat16)
+    def hop(block, src, dst):
+        return lax.ppermute(block, "segment", [(src, dst)])
+
+    zeros_x = jnp.zeros((all_rows, layer_width), jnp.bfloat16)
+    zeros_z = jnp.zeros((all_rows, layer_width), jnp.float32)
+    stash_x = inputs
+    stash_z = zeros_z
+    current = inputs
     for step_now in range(segments):
         active = segment_index == step_now
-        current = jnp.where(segment_index == 0, inputs, arrived)
-        preact, result = layer_forward(flat_cols, current, weight)
-        stash_x = jnp.where(active, current, stash_x)
-        stash_z = jnp.where(active, preact, stash_z)
+        held = current
+        stash_z, result = lax.cond(
+            active,
+            lambda: layer_forward(flat_cols, held, weight),
+            lambda: (stash_z, zeros_x),
+        )
+        if step_now > 0:
+            stash_x = jnp.where(active, current, stash_x)
         if step_now + 1 < segments:
-            arrived = from_behind(result, "segment", 1)
-    stash_g = jnp.zeros((all_rows, layer_width), jnp.bfloat16)
-    incoming = jnp.zeros((all_rows, layer_width), jnp.bfloat16)
+            current = hop(result, step_now, step_now + 1)
+    stash_g = zeros_x
+    upstream = cotangent
     for step_now in range(segments):
-        active = segment_index == segments - 1 - step_now
-        upstream = jnp.where(segment_index == segments - 1, cotangent, incoming)
-        grad_pre, passed = layer_backward(flat_cols, upstream, stash_z, weight)
-        stash_g = jnp.where(active, grad_pre, stash_g)
+        owner = segments - 1 - step_now
+        active = segment_index == owner
+        held = upstream
+        stash_g, passed = lax.cond(
+            active,
+            lambda: layer_backward(flat_cols, held, stash_z, weight),
+            lambda: (stash_g, zeros_x),
+        )
         if step_now + 1 < segments:
-            incoming = from_behind(passed, "segment", -1)
+            upstream = hop(passed, owner, owner - 1)
     all_inputs = stash_x
     all_grads = stash_g
     ny, nx, nz = DP_SIZES

time: 332 us -> 263 us (0.79); the launches traced: 326 us -> 262 us
  Pallas kernels: 95.4 us -> 28.7 us
  waiting for transfers between devices: 126 us -> 163 us
  starting transfers between devices: 69.4 us -> 40.4 us
  other arithmetic: 16.7 us -> 3.93 us
  local copies, waits for them, and re-layouts: 5.36 us -> 12.2 us
    ppermute x6, waiting for transfers between devices: 58.6 us -> 98.4 us  [hop(): return lax.ppermute(block, 'segment', [(src, dst)])]
    pallas_call x4 -> x1, Pallas kernels: 45.9 us -> 10.8 us  [layer_backward(): pl.pallas_call(backward_kernel, grid_spec=grid, out_shape=[jax.ShapeDtype...]
    pallas_call x4 -> x1, Pallas kernels: 40.3 us -> 8.62 us  [layer_forward(): pl.pallas_call(forward_kernel, grid_spec=grid, out_shape=[jax.ShapeDtypeS...]
    ppermute x6, starting transfers between devices: 34.8 us -> 7.38 us  [hop(): return lax.ppermute(block, 'segment', [(src, dst)])]
    select_n x9 -> x0, other arithmetic: 12.3 us -> none  [the longest x3 4.48 us: body(): current = jnp.where(segment_index == 0, inputs, arrived)]
    broadcast_in_dim x0 -> x6, local copies, waits for them, and re-layouts: none -> 5.51 us  [body(): zeros_x = jnp.zeros((all_rows, layer_width), jnp.bfloat16)]
    ppermute x1, waiting for transfers between devices: 37.5 us -> 33.4 us  [body(): lax.ppermute(lax.dynamic_index_in_dim(halves, 1 - side, 0, False), 'xlo',...]
  transfers between devices with their start and end apart: 23 -> 23, of which waited for: 17 -> 12; matrix products, arithmetic and copies ran while one was open for 2% -> 2% of each run, Pallas kernels for 11% -> 4%
where the time goes in v7:
time: 263 us; the launch traced here: 262 us
  waiting for transfers between devices  163 us (62%)
  starting transfers between devices  40.4 us (15%)
  Pallas kernels  28.7 us (11%)
  between operations  13.7 us (5%)
  local copies, waits for them, and re-layouts  12.2 us (5%)
  other arithmetic  3.93 us (1%)
    ppermute x6, waiting for transfers between devices, hop(): return lax.ppermute(block, 'segment', [(src, dst)])  98.4 us
    ppermute x1, waiting for transfers between devices, body(): lax.ppermute(lax.dynamic_index_in_dim(halves, 1 - side, 0, False), 'xlo',...  33.4 us
    ppermute x7, starting transfers between devices, ring_reduce_scatter(): got_w = lax.ppermute(send_w, axis, ccw)  25.2 us
    ppermute x7, waiting for transfers between devices, ring_reduce_scatter(): got_e = lax.ppermute(send_e, axis, cw)  20 us
    pallas_call x1, Pallas kernels, layer_backward(): pl.pallas_call(backward_kernel, grid_spec=grid, out_shape=[jax.ShapeDtype...  10.8 us
    all_to_all x1, waiting for transfers between devices, body(): lax.all_to_all(grads_here, 'y', split_axis=1, concat_axis=0, tiled=True)  10.8 us
    pallas_call x1, Pallas kernels, group_grads(): pl.pallas_call(grad_kernel, grid_spec=grid, out_shape=jax.ShapeDtypeStruc...  9.21 us
    pallas_call x1, Pallas kernels, layer_forward(): pl.pallas_call(forward_kernel, grid_spec=grid, out_shape=[jax.ShapeDtypeS...  8.62 us
  transfers between devices with their start and end apart: 23, of which 12 were waited for; matrix products, arithmetic and copies ran while one was open for 2% of the time, Pallas kernels for 4%

profile of v7, /device:TPU:2, one launch (start us, length us, event | category | flops | bytes accessed | tf_op | source)
XLA Modules:
  0.0 261.9 jit_solution(16460672584035061522)
XLA Ops:
  7.4 8.6 %conditional.8 = (bf16[128,4096]{1,0:T(8,128)(2,1)S(1)}, f32[128,4096]{1,0:T(8,128)S(1)}) conditional(s32[]{:T(128)} %convert_element_type.26, () %tuple.69, (s32[256]{0:T(256)S(1)}, bf16[128,4096]{1,0:T(8,128)(2,1)}, bf16[32,8,128,128]{3,2,1,0:T(8,128)(2,1)}) %tuple.106), branch_computations={%region_0.0_spmd, %region_1.0_spmd} | conditional | flops 1073741824 | bytes 12582928 | solution.py:219
  7.4 8.6 %branch_1_fun.8 = (f32[128,4096]{1,0:T(8,128)S(1)}, bf16[128,4096]{1,0:T(8,128)(2,1)S(1)}) custom-call(s32[256]{0:T(256)S(1)} %get-tuple-element.79.cols_ref, bf16[128,4096]{1,0:T(8,128)(2,1)} %get-tuple-element.80.h_ref, bf16[32,8,128,128]{3,2,1,0:T(8,128)(2,1)} %get-tuple-element.81.w_ref), custom_call_target="tpu_custom_call" | custom-call | flops 1073741824 | bytes 12582912 | tf_op jit(solution)/shard_map/cond/branch_1_fun/pallas_call | solution.py:92
  16.0 2.3 collective-permute-start
  18.3 1.4 collective-permute-done
  23.6 1.6 collective-permute-start.2
  26.5 1.2 conditional.12
  31.4 1.3 collective-permute-start.5
  32.7 97.0 %collective-permute-done.5 = bf16[128,4096]{1,0:T(8,128)(2,1)S(1)} collective-permute-done((bf16[128,4096]{1,0:T(8,128)(2,1)}, bf16[128,4096]{1,0:T(8,128)(2,1)S(1)}, u32[]{:S(2)}, u32[]{:S(2)}) %collective-permute-start.5) | collective-permute-done | bytes 1048608 | tf_op jit(solution)/shard_map/ppermute | solution.py:209
  129.7 11.8 %conditional.15 = (bf16[128,4096]{1,0:T(8,128)(2,1)S(1)}) conditional(s32[]{:T(128)} %convert_element_type.26, bf16[128,4096]{1,0:T(8,128)(2,1)S(1)} %get-tuple-element.135, (s32[256]{0:T(256)S(1)}, bf16[128,4096]{1,0:T(8,128)(2,1)S(1)}, f32[128,4096]{1,0:T(8,128)S(1)}, bf16[32,8,128,128]{3,2,1,0:T(8,128)(2,1)}) %tuple.113), branch_computations={%region_14.15_spmd, %region_15.16_spmd} | conditional | flops 1073741824 | bytes 17825828 | solution.py:234
  130.7 10.8 %branch_1_fun.15 = (bf16[128,4096]{1,0:T(8,128)(2,1)S(1)}, bf16[128,4096]{1,0:T(8,128)(2,1)}) custom-call(s32[256]{0:T(256)S(1)} %get-tuple-element.108.cols_ref, bf16[128,4096]{1,0:T(8,128)(2,1)} %copy-done.5, f32[128,4096]{1,0:T(8,128)S(1)} %get-tuple-element.110.z_ref, bf16[32,8,128,128]{3,2,1,0:T(8,128)(2,1)} %get-tuple-element.111.w_ref), custom_call_target="tpu_custom_call" | custom-call | flops 1073741824 | bytes 13631488 | tf_op jit(solution)/shard_map/cond/branch_1_fun/pallas_call | solution.py:124
  142.6 4.1 %all-to-all-start = ((bf16[128,4,1024]{2,0,1:T(8,128)(2,1)}), bf16[128,4,1024]{2,0,1:T(8,128)(2,1)S(1)}, u32[]{:S(2)}, u32[]{:S(2)}) async-start(bf16[128,4,1024]{2,0,1:T(8,128)(2,1)} %bitcast.59), calls=%async_computation | async-start | bytes 2097152 | tf_op jit(solution)/shard_map/all_to_all | solution.py:249
  146.7 10.8 %all-to-all-done = bf16[128,4,1024]{2,0,1:T(8,128)(2,1)S(1)} async-done(((bf16[128,4,1024]{2,0,1:T(8,128)(2,1)}), bf16[128,4,1024]{2,0,1:T(8,128)(2,1)S(1)}, u32[]{:S(2)}, u32[]{:S(2)}) %all-to-all-start) | async-done | bytes 1048608 | tf_op jit(solution)/shard_map/all_to_all | solution.py:249
  157.5 9.2 %shard_map.47 = f32[64,128,128]{2,1,0:T(8,128)S(1)} custom-call(s32[64]{0:T(128)S(1)} %dynamic_slice.59.cols_ref, bf16[512,4096]{1,0:T(8,128)(2,1)} %all-gather.2.cloned.1.call-done.h_ref, bf16[512,1024]{1,0:T(8,128)(2,1)S(1)} %bitcast.62), custom_call_target="tpu_custom_call" | custom-call | flops 1073741824 | bytes 9437184 | tf_op jit(solution)/shard_map/pallas_call | solution.py:165
  166.8 1.6 dynamic-slice_bitcast_fusion
  169.4 1.2 collective-permute-start.6
  170.6 33.4 %collective-permute-done.6 = f32[4096,128]{1,0:T(8,128)S(1)} collective-permute-done((f32[4096,128]{1,0:T(8,128)}, f32[4096,128]{1,0:T(8,128)S(1)}, u32[]{:S(2)}, u32[]{:S(2)}) %collective-permute-start.6) | collective-permute-done | bytes 2097184 | tf_op jit(solution)/shard_map/ppermute | solution.py:257
  204.0 1.8 bitcast_add_fusion
  206.0 1.9 collective-permute-start.7
  207.9 4.4 %collective-permute-start.14 = (f32[256,128]{1,0:T(8,128)S(1)}, f32[256,128]{1,0:T(8,128)S(1)}, u32[]{:S(2)}, u32[]{:S(2)}) collective-permute-start(f32[256,128]{1,0:T(8,128)S(1)} %dynamic-slice_bitcast_fusion.1), channel_id=1, source_target_pairs={{0,7},{1,0},{2,1},{3,2},{4,3},{5,4},{6,5},{7,6},{8,15},{9,8},{10,9... | collective-permute-start | bytes 393224 | tf_op jit(solution)/shard_map/ppermute | solution.py:194
  212.2 3.2 %collective-permute-done.7 = f32[256,128]{1,0:T(8,128)S(1)} collective-permute-done((f32[256,128]{1,0:T(8,128)S(1)}, f32[256,128]{1,0:T(8,128)S(1)}, u32[]{:S(2)}, u32[]{:S(2)}) %collective-permute-start.7) | collective-permute-done | bytes 131104 | tf_op jit(solution)/shard_map/ppermute | solution.py:193
  215.9 3.8 %collective-permute-start.15 = (f32[256,128]{1,0:T(8,128)S(1)}, f32[256,128]{1,0:T(8,128)S(1)}, u32[]{:S(2)}, u32[]{:S(2)}) collective-permute-start(f32[256,128]{1,0:T(8,128)S(1)} %bitcast_add_fusion.7), channel_id=1, source_target_pairs={{0,7},{1,0},{2,1},{3,2},{4,3},{5,4},{6,5},{7,6},{8,15},{9,8},{10,9... | collective-permute-start | bytes 393224 | tf_op jit(solution)/shard_map/ppermute | solution.py:194
  219.6 3.2 %collective-permute-done.8 = f32[256,128]{1,0:T(8,128)S(1)} collective-permute-done((f32[256,128]{1,0:T(8,128)S(1)}, f32[256,128]{1,0:T(8,128)S(1)}, u32[]{:S(2)}, u32[]{:S(2)}) %collective-permute-start.8) | collective-permute-done | bytes 131104 | tf_op jit(solution)/shard_map/ppermute | solution.py:193
  222.9 3.5 %collective-permute-start.16 = (f32[256,128]{1,0:T(8,128)S(1)}, f32[256,128]{1,0:T(8,128)S(1)}, u32[]{:S(2)}, u32[]{:S(2)}) collective-permute-start(f32[256,128]{1,0:T(8,128)S(1)} %bitcast_add_fusion.6), channel_id=1, source_target_pairs={{0,7},{1,0},{2,1},{3,2},{4,3},{5,4},{6,5},{7,6},{8,15},{9,8},{10,9... | collective-permute-start | bytes 393224 | tf_op jit(solution)/shard_map/ppermute | solution.py:194
  226.4 2.7 %collective-permute-done.9 = f32[256,128]{1,0:T(8,128)S(1)} collective-permute-done((f32[256,128]{1,0:T(8,128)S(1)}, f32[256,128]{1,0:T(8,128)S(1)}, u32[]{:S(2)}, u32[]{:S(2)}) %collective-permute-start.9) | collective-permute-done | bytes 131104 | tf_op jit(solution)/shard_map/ppermute | solution.py:193
  229.3 3.4 %collective-permute-start.17 = (f32[256,128]{1,0:T(8,128)S(1)}, f32[256,128]{1,0:T(8,128)S(1)}, u32[]{:S(2)}, u32[]{:S(2)}) collective-permute-start(f32[256,128]{1,0:T(8,128)S(1)} %bitcast_add_fusion.5), channel_id=1, source_target_pairs={{0,7},{1,0},{2,1},{3,2},{4,3},{5,4},{6,5},{7,6},{8,15},{9,8},{10,9... | collective-permute-start | bytes 393224 | tf_op jit(solution)/shard_map/ppermute | solution.py:194
  232.7 2.7 %collective-permute-done.10 = f32[256,128]{1,0:T(8,128)S(1)} collective-permute-done((f32[256,128]{1,0:T(8,128)S(1)}, f32[256,128]{1,0:T(8,128)S(1)}, u32[]{:S(2)}, u32[]{:S(2)}) %collective-permute-start.10) | collective-permute-done | bytes 131104 | tf_op jit(solution)/shard_map/ppermute | solution.py:193
  235.6 3.4 %collective-permute-start.18 = (f32[256,128]{1,0:T(8,128)S(1)}, f32[256,128]{1,0:T(8,128)S(1)}, u32[]{:S(2)}, u32[]{:S(2)}) collective-permute-start(f32[256,128]{1,0:T(8,128)S(1)} %bitcast_add_fusion.4), channel_id=1, source_target_pairs={{0,7},{1,0},{2,1},{3,2},{4,3},{5,4},{6,5},{7,6},{8,15},{9,8},{10,9... | collective-permute-start | bytes 393224 | tf_op jit(solution)/shard_map/ppermute | solution.py:194
  239.0 2.7 %collective-permute-done.11 = f32[256,128]{1,0:T(8,128)S(1)} collective-permute-done((f32[256,128]{1,0:T(8,128)S(1)}, f32[256,128]{1,0:T(8,128)S(1)}, u32[]{:S(2)}, u32[]{:S(2)}) %collective-permute-start.11) | collective-permute-done | bytes 131104 | tf_op jit(solution)/shard_map/ppermute | solution.py:193
  241.9 3.4 %collective-permute-start.19 = (f32[256,128]{1,0:T(8,128)S(1)}, f32[256,128]{1,0:T(8,128)S(1)}, u32[]{:S(2)}, u32[]{:S(2)}) collective-permute-start(f32[256,128]{1,0:T(8,128)S(1)} %bitcast_add_fusion.3), channel_id=1, source_target_pairs={{0,7},{1,0},{2,1},{3,2},{4,3},{5,4},{6,5},{7,6},{8,15},{9,8},{10,9... | collective-permute-start | bytes 393224 | tf_op jit(solution)/shard_map/ppermute | solution.py:194
  245.3 2.7 %collective-permute-done.12 = f32[256,128]{1,0:T(8,128)S(1)} collective-permute-done((f32[256,128]{1,0:T(8,128)S(1)}, f32[256,128]{1,0:T(8,128)S(1)}, u32[]{:S(2)}, u32[]{:S(2)}) %collective-permute-start.12) | collective-permute-done | bytes 131104 | tf_op jit(solution)/shard_map/ppermute | solution.py:193
  248.1 3.4 %collective-permute-start.20 = (f32[256,128]{1,0:T(8,128)S(1)}, f32[256,128]{1,0:T(8,128)S(1)}, u32[]{:S(2)}, u32[]{:S(2)}) collective-permute-start(f32[256,128]{1,0:T(8,128)S(1)} %bitcast_add_fusion.2), channel_id=1, source_target_pairs={{0,7},{1,0},{2,1},{3,2},{4,3},{5,4},{6,5},{7,6},{8,15},{9,8},{10,9... | collective-permute-start | bytes 393224 | tf_op jit(solution)/shard_map/ppermute | solution.py:194
  251.5 2.7 %collective-permute-done.13 = f32[256,128]{1,0:T(8,128)S(1)} collective-permute-done((f32[256,128]{1,0:T(8,128)S(1)}, f32[256,128]{1,0:T(8,128)S(1)}, u32[]{:S(2)}, u32[]{:S(2)}) %collective-permute-start.13) | collective-permute-done | bytes 131104 | tf_op jit(solution)/shard_map/ppermute | solution.py:193
  (65 shorter events, 20.1 us)
Async XLA Ops:
  6.5 151.0 %all-gather.2.cloned.1.call-start = ((), (), s32[]{:S(2)}) async-start(), calls=%async_computation.1 | async-start | bytes 5242880 | tf_op jit(solution)/shard_map/all_gather | solution.py:252
  16.0 3.7 %collective-permute-start = (bf16[128,4096]{1,0:T(8,128)(2,1)S(1)}, bf16[128,4096]{1,0:T(8,128)(2,1)}, u32[]{:S(2)}, u32[]{:S(2)}) collective-permute-start(bf16[128,4096]{1,0:T(8,128)(2,1)S(1)} %get-tuple-element.126), channel_id=1, source_target_pairs={{0,64},{1,65},{2,66},{3,67},{4,68},{5,69},{6,70},{7,71},{8,72},{9,... | collective-permute-start | bytes 3145736 | tf_op jit(solution)/shard_map/ppermute | solution.py:209
  20.8 0.7 collective-permute-start.1
  21.6 1.0 copy-start.2
  22.5 2.7 %copy-start.1 = (bf16[128,4096]{1,0:T(8,128)(2,1)S(1)}, bf16[128,4096]{1,0:T(8,128)(2,1)}, u32[]{:S(2)}) copy-start(bf16[128,4096]{1,0:T(8,128)(2,1)} %param.20) | copy-start | bytes 3145732
  23.6 1.6 collective-permute-start.2
  27.7 0.7 collective-permute-start.3
  29.6 0.7 collective-permute-start.4
  31.4 98.3 %collective-permute-start.5 = (bf16[128,4096]{1,0:T(8,128)(2,1)}, bf16[128,4096]{1,0:T(8,128)(2,1)S(1)}, u32[]{:S(2)}, u32[]{:S(2)}) collective-permute-start(bf16[128,4096]{1,0:T(8,128)(2,1)} %get-tuple-element.136), channel_id=1, source_target_pairs={{64,0},{65,1},{66,2},{67,3},{68,4},{69,5},{70,6},{71,7},{72,8},{73... | collective-permute-start | bytes 3145736 | tf_op jit(solution)/shard_map/ppermute | solution.py:209
  129.7 1.0 copy-start.5
  142.6 14.9 %all-to-all-start = ((bf16[128,4,1024]{2,0,1:T(8,128)(2,1)}), bf16[128,4,1024]{2,0,1:T(8,128)(2,1)S(1)}, u32[]{:S(2)}, u32[]{:S(2)}) async-start(bf16[128,4,1024]{2,0,1:T(8,128)(2,1)} %bitcast.59), calls=%async_computation | async-start | bytes 2097152 | tf_op jit(solution)/shard_map/all_to_all | solution.py:249
  166.8 2.6 copy-start
  169.4 34.6 %collective-permute-start.6 = (f32[4096,128]{1,0:T(8,128)}, f32[4096,128]{1,0:T(8,128)S(1)}, u32[]{:S(2)}, u32[]{:S(2)}) collective-permute-start(f32[4096,128]{1,0:T(8,128)} %dynamic-slice_bitcast_fusion), channel_id=1, source_target_pairs={{0,8},{8,0},{1,9},{9,1},{2,10},{10,2},{3,11},{11,3},{4,12},{12,4},... | collective-permute-start | bytes 6291464 | tf_op jit(solution)/shard_map/ppermute | solution.py:257
  206.0 9.4 %collective-permute-start.7 = (f32[256,128]{1,0:T(8,128)S(1)}, f32[256,128]{1,0:T(8,128)S(1)}, u32[]{:S(2)}, u32[]{:S(2)}) collective-permute-start(f32[256,128]{1,0:T(8,128)S(1)} %dynamic-slice_bitcast_fusion.2), channel_id=1, source_target_pairs={{0,1},{1,2},{2,3},{3,4},{4,5},{5,6},{6,7},{7,0},{8,9},{9,10},{10,1... | collective-permute-start | bytes 393224 | tf_op jit(solution)/shard_map/ppermute | solution.py:193
  207.9 8.0 %collective-permute-start.14 = (f32[256,128]{1,0:T(8,128)S(1)}, f32[256,128]{1,0:T(8,128)S(1)}, u32[]{:S(2)}, u32[]{:S(2)}) collective-permute-start(f32[256,128]{1,0:T(8,128)S(1)} %dynamic-slice_bitcast_fusion.1), channel_id=1, source_target_pairs={{0,7},{1,0},{2,1},{3,2},{4,3},{5,4},{6,5},{7,6},{8,15},{9,8},{10,9... | collective-permute-start | bytes 393224 | tf_op jit(solution)/shard_map/ppermute | solution.py:194
  215.5 7.3 %collective-permute-start.8 = (f32[256,128]{1,0:T(8,128)S(1)}, f32[256,128]{1,0:T(8,128)S(1)}, u32[]{:S(2)}, u32[]{:S(2)}) collective-permute-start(f32[256,128]{1,0:T(8,128)S(1)} %bitcast_add_fusion.14), channel_id=1, source_target_pairs={{0,1},{1,2},{2,3},{3,4},{4,5},{5,6},{6,7},{7,0},{8,9},{9,10},{10,1... | collective-permute-start | bytes 393224 | tf_op jit(solution)/shard_map/ppermute | solution.py:193
  215.9 7.0 %collective-permute-start.15 = (f32[256,128]{1,0:T(8,128)S(1)}, f32[256,128]{1,0:T(8,128)S(1)}, u32[]{:S(2)}, u32[]{:S(2)}) collective-permute-start(f32[256,128]{1,0:T(8,128)S(1)} %bitcast_add_fusion.7), channel_id=1, source_target_pairs={{0,7},{1,0},{2,1},{3,2},{4,3},{5,4},{6,5},{7,6},{8,15},{9,8},{10,9... | collective-permute-start | bytes 393224 | tf_op jit(solution)/shard_map/ppermute | solution.py:194
  222.8 6.4 %collective-permute-start.9 = (f32[256,128]{1,0:T(8,128)S(1)}, f32[256,128]{1,0:T(8,128)S(1)}, u32[]{:S(2)}, u32[]{:S(2)}) collective-permute-start(f32[256,128]{1,0:T(8,128)S(1)} %bitcast_add_fusion.13), channel_id=1, source_target_pairs={{0,1},{1,2},{2,3},{3,4},{4,5},{5,6},{6,7},{7,0},{8,9},{9,10},{10,1... | collective-permute-start | bytes 393224 | tf_op jit(solution)/shard_map/ppermute | solution.py:193
  222.9 6.4 %collective-permute-start.16 = (f32[256,128]{1,0:T(8,128)S(1)}, f32[256,128]{1,0:T(8,128)S(1)}, u32[]{:S(2)}, u32[]{:S(2)}) collective-permute-start(f32[256,128]{1,0:T(8,128)S(1)} %bitcast_add_fusion.6), channel_id=1, source_target_pairs={{0,7},{1,0},{2,1},{3,2},{4,3},{5,4},{6,5},{7,6},{8,15},{9,8},{10,9... | collective-permute-start | bytes 393224 | tf_op jit(solution)/shard_map/ppermute | solution.py:194
  229.2 6.3 %collective-permute-start.10 = (f32[256,128]{1,0:T(8,128)S(1)}, f32[256,128]{1,0:T(8,128)S(1)}, u32[]{:S(2)}, u32[]{:S(2)}) collective-permute-start(f32[256,128]{1,0:T(8,128)S(1)} %bitcast_add_fusion.12), channel_id=1, source_target_pairs={{0,1},{1,2},{2,3},{3,4},{4,5},{5,6},{6,7},{7,0},{8,9},{9,10},{10,1... | collective-permute-start | bytes 393224 | tf_op jit(solution)/shard_map/ppermute | solution.py:193
  229.3 6.2 %collective-permute-start.17 = (f32[256,128]{1,0:T(8,128)S(1)}, f32[256,128]{1,0:T(8,128)S(1)}, u32[]{:S(2)}, u32[]{:S(2)}) collective-permute-start(f32[256,128]{1,0:T(8,128)S(1)} %bitcast_add_fusion.5), channel_id=1, source_target_pairs={{0,7},{1,0},{2,1},{3,2},{4,3},{5,4},{6,5},{7,6},{8,15},{9,8},{10,9... | collective-permute-start | bytes 393224 | tf_op jit(solution)/shard_map/ppermute | solution.py:194
  235.5 6.3 %collective-permute-start.11 = (f32[256,128]{1,0:T(8,128)S(1)}, f32[256,128]{1,0:T(8,128)S(1)}, u32[]{:S(2)}, u32[]{:S(2)}) collective-permute-start(f32[256,128]{1,0:T(8,128)S(1)} %bitcast_add_fusion.11), channel_id=1, source_target_pairs={{0,1},{1,2},{2,3},{3,4},{4,5},{5,6},{6,7},{7,0},{8,9},{9,10},{10,1... | collective-permute-start | bytes 393224 | tf_op jit(solution)/shard_map/ppermute | solution.py:193
  235.6 6.2 %collective-permute-start.18 = (f32[256,128]{1,0:T(8,128)S(1)}, f32[256,128]{1,0:T(8,128)S(1)}, u32[]{:S(2)}, u32[]{:S(2)}) collective-permute-start(f32[256,128]{1,0:T(8,128)S(1)} %bitcast_add_fusion.4), channel_id=1, source_target_pairs={{0,7},{1,0},{2,1},{3,2},{4,3},{5,4},{6,5},{7,6},{8,15},{9,8},{10,9... | collective-permute-start | bytes 393224 | tf_op jit(solution)/shard_map/ppermute | solution.py:194
  241.7 6.3 %collective-permute-start.12 = (f32[256,128]{1,0:T(8,128)S(1)}, f32[256,128]{1,0:T(8,128)S(1)}, u32[]{:S(2)}, u32[]{:S(2)}) collective-permute-start(f32[256,128]{1,0:T(8,128)S(1)} %bitcast_add_fusion.10), channel_id=1, source_target_pairs={{0,1},{1,2},{2,3},{3,4},{4,5},{5,6},{6,7},{7,0},{8,9},{9,10},{10,1... | collective-permute-start | bytes 393224 | tf_op jit(solution)/shard_map/ppermute | solution.py:193
  241.9 6.2 %collective-permute-start.19 = (f32[256,128]{1,0:T(8,128)S(1)}, f32[256,128]{1,0:T(8,128)S(1)}, u32[]{:S(2)}, u32[]{:S(2)}) collective-permute-start(f32[256,128]{1,0:T(8,128)S(1)} %bitcast_add_fusion.3), channel_id=1, source_target_pairs={{0,7},{1,0},{2,1},{3,2},{4,3},{5,4},{6,5},{7,6},{8,15},{9,8},{10,9... | collective-permute-start | bytes 393224 | tf_op jit(solution)/shard_map/ppermute | solution.py:194
  248.0 6.3 %collective-permute-start.13 = (f32[256,128]{1,0:T(8,128)S(1)}, f32[256,128]{1,0:T(8,128)S(1)}, u32[]{:S(2)}, u32[]{:S(2)}) collective-permute-start(f32[256,128]{1,0:T(8,128)S(1)} %bitcast_add_fusion.9), channel_id=1, source_target_pairs={{0,1},{1,2},{2,3},{3,4},{4,5},{5,6},{6,7},{7,0},{8,9},{9,10},{10,1... | collective-permute-start | bytes 393224 | tf_op jit(solution)/shard_map/ppermute | solution.py:193
  248.1 6.2 %collective-permute-start.20 = (f32[256,128]{1,0:T(8,128)S(1)}, f32[256,128]{1,0:T(8,128)S(1)}, u32[]{:S(2)}, u32[]{:S(2)}) collective-permute-start(f32[256,128]{1,0:T(8,128)S(1)} %bitcast_add_fusion.2), channel_id=1, source_target_pairs={{0,7},{1,0},{2,1},{3,2},{4,3},{5,4},{6,5},{7,6},{8,15},{9,8},{10,9... | collective-permute-start | bytes 393224 | tf_op jit(solution)/shard_map/ppermute | solution.py:194
Sparse Core Ops, SparseCore 0:
  26.6 88.3 all-gather.1

commit v8 on v7

--- a/solution.py
+++ b/solution.py
@@ -205,8 +205,13 @@
     all_rows, layer_width = inputs.shape
     flat_cols = block_cols[0].reshape(-1)
 
+    sides = DP_SIZES[1]
+    middle = segments // 2
+
     def hop(block, src, dst):
-        return lax.ppermute(block, "segment", [(src, dst)])
+        flip = (src < middle) != (dst < middle)
+        route = [(src * sides + x, dst * sides + (sides - 1 - x if flip else x)) for x in range(sides)]
+        return lax.ppermute(block, ("segment", "xlo"), route)
 
     zeros_x = jnp.zeros((all_rows, layer_width), jnp.bfloat16)
     zeros_z = jnp.zeros((all_rows, layer_width), jnp.float32)
@@ -226,7 +231,10 @@
         if step_now + 1 < segments:
             current = hop(result, step_now, step_now + 1)
     stash_g = zeros_x
-    upstream = cotangent
+    last = segments - 1
+    upstream = lax.ppermute(
+        cotangent, ("segment", "xlo"), [(last * sides + x, last * sides + sides - 1 - x) for x in range(sides)]
+    )
     for step_now in range(segments):
         owner = segments - 1 - step_now
         active = segment_index == owner
@@ -241,22 +249,18 @@
     all_inputs = stash_x
     all_grads = stash_g
     ny, nx, nz = DP_SIZES
-    members = ny
+    members = ny * nx
     group_pairs = num_blocks * per_block // members
     group_j = num_blocks // members
-    member = lax.axis_index("y")
+    member = lax.axis_index("y") * nx + lax.axis_index("xlo")
     grads_here = all_grads.reshape(all_rows, members, group_j * edge_size)
     grads_group = lax.all_to_all(
-        grads_here, "y", split_axis=1, concat_axis=0, tiled=True
+        grads_here, ("y", "xlo"), split_axis=1, concat_axis=0, tiled=True
     ).reshape(members * all_rows, group_j * edge_size)
-    inputs_group = lax.all_gather(all_inputs, "y", axis=0, tiled=True)
+    inputs_group = lax.all_gather(all_inputs, ("y", "xlo"), axis=0, tiled=True)
     cols_here = lax.dynamic_slice_in_dim(flat_cols, member * group_pairs, group_pairs)
-    partial = group_grads(cols_here, inputs_group, grads_group, group_pairs, 8)
-    halves = partial.reshape(nx, group_pairs // nx * edge_size, edge_size)
-    side = lax.axis_index("xlo")
-    got = lax.ppermute(lax.dynamic_index_in_dim(halves, 1 - side, 0, False), "xlo", [(0, 1), (1, 0)])
-    kept = lax.dynamic_index_in_dim(halves, side, 0, False) + got
-    own_share = ring_reduce_scatter(kept.reshape(nz, -1, edge_size), "z", nz)
+    partial = group_grads(cols_here, inputs_group, grads_group, group_pairs, group_pairs // nz)
+    own_share = ring_reduce_scatter(partial.reshape(nz, -1, edge_size), "z", nz)
     summed = own_share.astype(jnp.bfloat16)
     return summed[None]
 

time: 263 us -> 314 us (1.19); the launches traced: 262 us -> 309 us
  waiting for transfers between devices: 163 us -> 216 us
    all_gather x1, waiting for transfers between devices: 0.01 us -> 66 us  [body(): inputs_group = lax.all_gather(all_inputs, ('y', 'xlo'), axis=0, tiled=True)]
    ppermute x7, waiting for transfers between devices: 132 us -> 109 us  [the longest x6 109 us: hop(): return lax.ppermute(block, ('segment', 'xlo'), route)]
    all_to_all x1, waiting for transfers between devices: 10.8 us -> 20.1 us  [body(): lax.all_to_all(grads_here, ('y', 'xlo'), split_axis=1, concat_axis=0, til...]
  transfers between devices with their start and end apart: 23 -> 23, of which waited for: 12 -> 11; matrix products, arithmetic and copies ran while one was open for 2% -> 2% of each run, Pallas kernels for 4% -> 3%
where the time goes in v8:
time: 314 us; the launch traced here: 309 us
  waiting for transfers between devices  216 us (69%)
  starting transfers between devices  39.4 us (13%)
  Pallas kernels  28.1 us (9%)
  between operations  13.7 us (4%)
  local copies, waits for them, and re-layouts  9.64 us (3%)
    ppermute x6, waiting for transfers between devices, hop(): return lax.ppermute(block, ('segment', 'xlo'), route)  109 us
    all_gather x1, waiting for transfers between devices, body(): inputs_group = lax.all_gather(all_inputs, ('y', 'xlo'), axis=0, tiled=True)  66 us
    ppermute x7, starting transfers between devices, ring_reduce_scatter(): got_w = lax.ppermute(send_w, axis, ccw)  23 us
    ppermute x7, waiting for transfers between devices, ring_reduce_scatter(): got_e = lax.ppermute(send_e, axis, cw)  21.2 us
    all_to_all x1, waiting for transfers between devices, body(): lax.all_to_all(grads_here, ('y', 'xlo'), split_axis=1, concat_axis=0, til...  20.1 us
    pallas_call x1, Pallas kernels, layer_backward(): pl.pallas_call(backward_kernel, grid_spec=grid, out_shape=[jax.ShapeDtype...  10.8 us
    pallas_call x1, Pallas kernels, group_grads(): pl.pallas_call(grad_kernel, grid_spec=grid, out_shape=jax.ShapeDtypeStruc...  8.71 us
    pallas_call x1, Pallas kernels, layer_forward(): pl.pallas_call(forward_kernel, grid_spec=grid, out_shape=[jax.ShapeDtypeS...  8.61 us
  transfers between devices with their start and end apart: 23, of which 11 were waited for; matrix products, arithmetic and copies ran while one was open for 2% of the time, Pallas kernels for 3%

profile of v8, /device:TPU:2, one launch (start us, length us, event | category | flops | bytes accessed | tf_op | source)
XLA Modules:
  0.0 309.0 jit_solution(12621426533273823463)
XLA Ops:
  7.4 8.6 %conditional.8 = (bf16[128,4096]{1,0:T(8,128)(2,1)S(1)}, f32[128,4096]{1,0:T(8,128)S(1)}) conditional(s32[]{:T(128)} %convert_element_type.26, () %tuple.69, (s32[256]{0:T(256)S(1)}, bf16[128,4096]{1,0:T(8,128)(2,1)}, bf16[32,8,128,128]{3,2,1,0:T(8,128)(2,1)}) %tuple.106), branch_computations={%region_0.0_spmd, %region_1.0_spmd} | conditional | flops 1073741824 | bytes 12582928 | solution.py:224
  7.4 8.6 %branch_1_fun.8 = (f32[128,4096]{1,0:T(8,128)S(1)}, bf16[128,4096]{1,0:T(8,128)(2,1)S(1)}) custom-call(s32[256]{0:T(256)S(1)} %get-tuple-element.79.cols_ref, bf16[128,4096]{1,0:T(8,128)(2,1)} %get-tuple-element.80.h_ref, bf16[32,8,128,128]{3,2,1,0:T(8,128)(2,1)} %get-tuple-element.81.w_ref), custom_call_target="tpu_custom_call" | custom-call | flops 1073741824 | bytes 12582912 | tf_op jit(solution)/shard_map/cond/branch_1_fun/pallas_call | solution.py:92
  16.0 2.3 collective-permute-start
  18.3 1.4 collective-permute-done
  22.5 1.1 conditional.10
  22.5 1.1 broadcast_in_dim.18
  23.6 1.6 collective-permute-start.2
  25.3 1.2 select_select_fusion
  27.2 1.2 conditional.12
  32.1 1.3 collective-permute-start.6
  33.4 107.3 %collective-permute-done.6 = bf16[128,4096]{1,0:T(8,128)(2,1)S(1)} collective-permute-done((bf16[128,4096]{1,0:T(8,128)(2,1)}, bf16[128,4096]{1,0:T(8,128)(2,1)S(1)}, u32[]{:S(2)}, u32[]{:S(2)}) %collective-permute-start.6) | collective-permute-done | bytes 1048608 | tf_op jit(solution)/shard_map/ppermute | solution.py:214
  140.7 11.7 %conditional.15 = (bf16[128,4096]{1,0:T(8,128)(2,1)S(1)}) conditional(s32[]{:T(128)} %convert_element_type.26, bf16[128,4096]{1,0:T(8,128)(2,1)S(1)} %get-tuple-element.135, (s32[256]{0:T(256)S(1)}, bf16[128,4096]{1,0:T(8,128)(2,1)S(1)}, f32[128,4096]{1,0:T(8,128)S(1)}, bf16[32,8,128,128]{3,2,1,0:T(8,128)(2,1)}) %tuple.113), branch_computations={%region_14.15_spmd, %region_15.16_spmd} | conditional | flops 1073741824 | bytes 17825828 | solution.py:242
  141.7 10.8 %branch_1_fun.15 = (bf16[128,4096]{1,0:T(8,128)(2,1)S(1)}, bf16[128,4096]{1,0:T(8,128)(2,1)}) custom-call(s32[256]{0:T(256)S(1)} %get-tuple-element.108.cols_ref, bf16[128,4096]{1,0:T(8,128)(2,1)} %copy-done.5, f32[128,4096]{1,0:T(8,128)S(1)} %get-tuple-element.110.z_ref, bf16[32,8,128,128]{3,2,1,0:T(8,128)(2,1)} %get-tuple-element.111.w_ref), custom_call_target="tpu_custom_call" | custom-call | flops 1073741824 | bytes 13631488 | tf_op jit(solution)/shard_map/cond/branch_1_fun/pallas_call | solution.py:124
  153.5 6.1 %all-to-all-start = ((bf16[128,8,512]{2,0,1:T(8,128)(2,1)}), bf16[128,8,512]{2,0,1:T(8,128)(2,1)S(1)}, u32[]{:S(2)}, u32[]{:S(2)}) async-start(bf16[128,8,512]{2,0,1:T(8,128)(2,1)} %bitcast.54), calls=%async_computation | async-start | bytes 2097152 | tf_op jit(solution)/shard_map/all_to_all | solution.py:257
  159.7 20.1 %all-to-all-done = bf16[128,8,512]{2,0,1:T(8,128)(2,1)S(1)} async-done(((bf16[128,8,512]{2,0,1:T(8,128)(2,1)}), bf16[128,8,512]{2,0,1:T(8,128)(2,1)S(1)}, u32[]{:S(2)}, u32[]{:S(2)}) %all-to-all-start) | async-done | bytes 1048608 | tf_op jit(solution)/shard_map/all_to_all | solution.py:257
  179.8 66.0 %all-gather.2.cloned.1.call-done.h_ref = bf16[1024,4096]{1,0:T(8,128)(2,1)} async-done(((bf16[128,4096]{1,0:T(8,128)(2,1)}), bf16[1024,4096]{1,0:T(8,128)(2,1)}) %all-gather.2.cloned.1.call-update) | async-done | bytes 8388624 | tf_op jit(solution)/shard_map/all_gather | solution.py:260
  245.7 8.7 %shard_map.46 = f32[32,128,128]{2,1,0:T(8,128)S(1)} custom-call(s32[32]{0:T(128)S(1)} %dynamic_slice.52.cols_ref, bf16[1024,4096]{1,0:T(8,128)(2,1)} %all-gather.2.cloned.1.call-done.h_ref, bf16[1024,512]{1,0:T(8,128)(2,1)S(1)} %bitcast.56), custom_call_target="tpu_custom_call" | custom-call | flops 1073741824 | bytes 11534336 | tf_op jit(solution)/shard_map/pallas_call | solution.py:165
  254.7 1.7 collective-permute-start.7
  256.4 2.0 collective-permute-start.14
  258.4 3.2 %collective-permute-done.7 = f32[256,128]{1,0:T(8,128)S(1)} collective-permute-done((f32[256,128]{1,0:T(8,128)S(1)}, f32[256,128]{1,0:T(8,128)S(1)}, u32[]{:S(2)}, u32[]{:S(2)}) %collective-permute-start.7) | collective-permute-done | bytes 131104 | tf_op jit(solution)/shard_map/ppermute | solution.py:193
  261.7 3.5 %collective-permute-start.15 = (f32[256,128]{1,0:T(8,128)S(1)}, f32[256,128]{1,0:T(8,128)S(1)}, u32[]{:S(2)}, u32[]{:S(2)}) collective-permute-start(f32[256,128]{1,0:T(8,128)S(1)} %bitcast_add_fusion.6), channel_id=1, source_target_pairs={{0,7},{1,0},{2,1},{3,2},{4,3},{5,4},{6,5},{7,6},{8,15},{9,8},{10,9... | collective-permute-start | bytes 393224 | tf_op jit(solution)/shard_map/ppermute | solution.py:194
  265.2 2.7 collective-permute-done.8
  268.0 3.5 %collective-permute-start.16 = (f32[256,128]{1,0:T(8,128)S(1)}, f32[256,128]{1,0:T(8,128)S(1)}, u32[]{:S(2)}, u32[]{:S(2)}) collective-permute-start(f32[256,128]{1,0:T(8,128)S(1)} %bitcast_add_fusion.5), channel_id=1, source_target_pairs={{0,7},{1,0},{2,1},{3,2},{4,3},{5,4},{6,5},{7,6},{8,15},{9,8},{10,9... | collective-permute-start | bytes 393224 | tf_op jit(solution)/shard_map/ppermute | solution.py:194
  271.5 2.7 collective-permute-done.9
  274.3 3.5 %collective-permute-start.17 = (f32[256,128]{1,0:T(8,128)S(1)}, f32[256,128]{1,0:T(8,128)S(1)}, u32[]{:S(2)}, u32[]{:S(2)}) collective-permute-start(f32[256,128]{1,0:T(8,128)S(1)} %bitcast_add_fusion.4), channel_id=1, source_target_pairs={{0,7},{1,0},{2,1},{3,2},{4,3},{5,4},{6,5},{7,6},{8,15},{9,8},{10,9... | collective-permute-start | bytes 393224 | tf_op jit(solution)/shard_map/ppermute | solution.py:194
  277.7 2.9 collective-permute-done.10
  280.8 3.8 %collective-permute-start.18 = (f32[256,128]{1,0:T(8,128)S(1)}, f32[256,128]{1,0:T(8,128)S(1)}, u32[]{:S(2)}, u32[]{:S(2)}) collective-permute-start(f32[256,128]{1,0:T(8,128)S(1)} %bitcast_add_fusion.3), channel_id=1, source_target_pairs={{0,7},{1,0},{2,1},{3,2},{4,3},{5,4},{6,5},{7,6},{8,15},{9,8},{10,9... | collective-permute-start | bytes 393224 | tf_op jit(solution)/shard_map/ppermute | solution.py:194
  284.6 3.7 %collective-permute-done.11 = f32[256,128]{1,0:T(8,128)S(1)} collective-permute-done((f32[256,128]{1,0:T(8,128)S(1)}, f32[256,128]{1,0:T(8,128)S(1)}, u32[]{:S(2)}, u32[]{:S(2)}) %collective-permute-start.11) | collective-permute-done | bytes 131104 | tf_op jit(solution)/shard_map/ppermute | solution.py:193
  288.5 3.5 %collective-permute-start.19 = (f32[256,128]{1,0:T(8,128)S(1)}, f32[256,128]{1,0:T(8,128)S(1)}, u32[]{:S(2)}, u32[]{:S(2)}) collective-permute-start(f32[256,128]{1,0:T(8,128)S(1)} %bitcast_add_fusion.2), channel_id=1, source_target_pairs={{0,7},{1,0},{2,1},{3,2},{4,3},{5,4},{6,5},{7,6},{8,15},{9,8},{10,9... | collective-permute-start | bytes 393224 | tf_op jit(solution)/shard_map/ppermute | solution.py:194
  291.9 3.2 %collective-permute-done.12 = f32[256,128]{1,0:T(8,128)S(1)} collective-permute-done((f32[256,128]{1,0:T(8,128)S(1)}, f32[256,128]{1,0:T(8,128)S(1)}, u32[]{:S(2)}, u32[]{:S(2)}) %collective-permute-start.12) | collective-permute-done | bytes 131104 | tf_op jit(solution)/shard_map/ppermute | solution.py:193
  295.3 3.3 %collective-permute-start.20 = (f32[256,128]{1,0:T(8,128)S(1)}, f32[256,128]{1,0:T(8,128)S(1)}, u32[]{:S(2)}, u32[]{:S(2)}) collective-permute-start(f32[256,128]{1,0:T(8,128)S(1)} %bitcast_add_fusion.1), channel_id=1, source_target_pairs={{0,7},{1,0},{2,1},{3,2},{4,3},{5,4},{6,5},{7,6},{8,15},{9,8},{10,9... | collective-permute-start | bytes 393224 | tf_op jit(solution)/shard_map/ppermute | solution.py:194
  298.6 2.8 collective-permute-done.13
  (61 shorter events, 16.2 us)
Async XLA Ops:
  6.5 239.2 %all-gather.2.cloned.1.call-start = ((), (), s32[]{:S(2)}) async-start(), calls=%async_computation.1 | async-start | bytes 9437184 | tf_op jit(solution)/shard_map/all_gather | solution.py:260
  16.0 3.7 %collective-permute-start = (bf16[128,4096]{1,0:T(8,128)(2,1)S(1)}, bf16[128,4096]{1,0:T(8,128)(2,1)}, u32[]{:S(2)}, u32[]{:S(2)}) collective-permute-start(bf16[128,4096]{1,0:T(8,128)(2,1)S(1)} %get-tuple-element.126), channel_id=1, source_target_pairs={{0,64},{8,72},{1,65},{9,73},{2,66},{10,74},{3,67},{11,75},{4,68},{... | collective-permute-start | bytes 3145736 | tf_op jit(solution)/shard_map/ppermute | solution.py:214
  20.8 0.7 collective-permute-start.1
  21.6 1.0 copy-start.1
  22.5 2.7 copy-start
  23.6 1.6 collective-permute-start.2
  26.4 0.8 collective-permute-start.3
  28.4 0.7 collective-permute-start.4
  30.2 0.7 collective-permute-start.5
  32.1 108.6 %collective-permute-start.6 = (bf16[128,4096]{1,0:T(8,128)(2,1)}, bf16[128,4096]{1,0:T(8,128)(2,1)S(1)}, u32[]{:S(2)}, u32[]{:S(2)}) collective-permute-start(bf16[128,4096]{1,0:T(8,128)(2,1)} %get-tuple-element.136), channel_id=1, source_target_pairs={{64,0},{72,8},{65,1},{73,9},{66,2},{74,10},{67,3},{75,11},{68,4},{... | collective-permute-start | bytes 3145736 | tf_op jit(solution)/shard_map/ppermute | solution.py:214
  140.7 1.0 copy-start.5
  153.5 26.3 %all-to-all-start = ((bf16[128,8,512]{2,0,1:T(8,128)(2,1)}), bf16[128,8,512]{2,0,1:T(8,128)(2,1)S(1)}, u32[]{:S(2)}, u32[]{:S(2)}) async-start(bf16[128,8,512]{2,0,1:T(8,128)(2,1)} %bitcast.54), calls=%async_computation | async-start | bytes 2097152 | tf_op jit(solution)/shard_map/all_to_all | solution.py:257
  254.7 6.9 %collective-permute-start.7 = (f32[256,128]{1,0:T(8,128)S(1)}, f32[256,128]{1,0:T(8,128)S(1)}, u32[]{:S(2)}, u32[]{:S(2)}) collective-permute-start(f32[256,128]{1,0:T(8,128)S(1)} %dynamic-slice_bitcast_fusion.1), channel_id=1, source_target_pairs={{0,1},{1,2},{2,3},{3,4},{4,5},{5,6},{6,7},{7,0},{8,9},{9,10},{10,1... | collective-permute-start | bytes 393224 | tf_op jit(solution)/shard_map/ppermute | solution.py:193
  256.4 5.3 %collective-permute-start.14 = (f32[256,128]{1,0:T(8,128)S(1)}, f32[256,128]{1,0:T(8,128)S(1)}, u32[]{:S(2)}, u32[]{:S(2)}) collective-permute-start(f32[256,128]{1,0:T(8,128)S(1)} %dynamic-slice_bitcast_fusion), channel_id=1, source_target_pairs={{0,7},{1,0},{2,1},{3,2},{4,3},{5,4},{6,5},{7,6},{8,15},{9,8},{10,9... | collective-permute-start | bytes 393224 | tf_op jit(solution)/shard_map/ppermute | solution.py:194
  261.6 6.3 %collective-permute-start.8 = (f32[256,128]{1,0:T(8,128)S(1)}, f32[256,128]{1,0:T(8,128)S(1)}, u32[]{:S(2)}, u32[]{:S(2)}) collective-permute-start(f32[256,128]{1,0:T(8,128)S(1)} %bitcast_add_fusion.13), channel_id=1, source_target_pairs={{0,1},{1,2},{2,3},{3,4},{4,5},{5,6},{6,7},{7,0},{8,9},{9,10},{10,1... | collective-permute-start | bytes 393224 | tf_op jit(solution)/shard_map/ppermute | solution.py:193
  261.7 6.2 %collective-permute-start.15 = (f32[256,128]{1,0:T(8,128)S(1)}, f32[256,128]{1,0:T(8,128)S(1)}, u32[]{:S(2)}, u32[]{:S(2)}) collective-permute-start(f32[256,128]{1,0:T(8,128)S(1)} %bitcast_add_fusion.6), channel_id=1, source_target_pairs={{0,7},{1,0},{2,1},{3,2},{4,3},{5,4},{6,5},{7,6},{8,15},{9,8},{10,9... | collective-permute-start | bytes 393224 | tf_op jit(solution)/shard_map/ppermute | solution.py:194
  267.9 6.3 %collective-permute-start.9 = (f32[256,128]{1,0:T(8,128)S(1)}, f32[256,128]{1,0:T(8,128)S(1)}, u32[]{:S(2)}, u32[]{:S(2)}) collective-permute-start(f32[256,128]{1,0:T(8,128)S(1)} %bitcast_add_fusion.12), channel_id=1, source_target_pairs={{0,1},{1,2},{2,3},{3,4},{4,5},{5,6},{6,7},{7,0},{8,9},{9,10},{10,1... | collective-permute-start | bytes 393224 | tf_op jit(solution)/shard_map/ppermute | solution.py:193
  268.0 6.2 %collective-permute-start.16 = (f32[256,128]{1,0:T(8,128)S(1)}, f32[256,128]{1,0:T(8,128)S(1)}, u32[]{:S(2)}, u32[]{:S(2)}) collective-permute-start(f32[256,128]{1,0:T(8,128)S(1)} %bitcast_add_fusion.5), channel_id=1, source_target_pairs={{0,7},{1,0},{2,1},{3,2},{4,3},{5,4},{6,5},{7,6},{8,15},{9,8},{10,9... | collective-permute-start | bytes 393224 | tf_op jit(solution)/shard_map/ppermute | solution.py:194
  274.1 6.5 %collective-permute-start.10 = (f32[256,128]{1,0:T(8,128)S(1)}, f32[256,128]{1,0:T(8,128)S(1)}, u32[]{:S(2)}, u32[]{:S(2)}) collective-permute-start(f32[256,128]{1,0:T(8,128)S(1)} %bitcast_add_fusion.11), channel_id=1, source_target_pairs={{0,1},{1,2},{2,3},{3,4},{4,5},{5,6},{6,7},{7,0},{8,9},{9,10},{10,1... | collective-permute-start | bytes 393224 | tf_op jit(solution)/shard_map/ppermute | solution.py:193
  274.3 6.5 %collective-permute-start.17 = (f32[256,128]{1,0:T(8,128)S(1)}, f32[256,128]{1,0:T(8,128)S(1)}, u32[]{:S(2)}, u32[]{:S(2)}) collective-permute-start(f32[256,128]{1,0:T(8,128)S(1)} %bitcast_add_fusion.4), channel_id=1, source_target_pairs={{0,7},{1,0},{2,1},{3,2},{4,3},{5,4},{6,5},{7,6},{8,15},{9,8},{10,9... | collective-permute-start | bytes 393224 | tf_op jit(solution)/shard_map/ppermute | solution.py:194
  280.7 7.6 %collective-permute-start.11 = (f32[256,128]{1,0:T(8,128)S(1)}, f32[256,128]{1,0:T(8,128)S(1)}, u32[]{:S(2)}, u32[]{:S(2)}) collective-permute-start(f32[256,128]{1,0:T(8,128)S(1)} %bitcast_add_fusion.10), channel_id=1, source_target_pairs={{0,1},{1,2},{2,3},{3,4},{4,5},{5,6},{6,7},{7,0},{8,9},{9,10},{10,1... | collective-permute-start | bytes 393224 | tf_op jit(solution)/shard_map/ppermute | solution.py:193
  280.8 7.6 %collective-permute-start.18 = (f32[256,128]{1,0:T(8,128)S(1)}, f32[256,128]{1,0:T(8,128)S(1)}, u32[]{:S(2)}, u32[]{:S(2)}) collective-permute-start(f32[256,128]{1,0:T(8,128)S(1)} %bitcast_add_fusion.3), channel_id=1, source_target_pairs={{0,7},{1,0},{2,1},{3,2},{4,3},{5,4},{6,5},{7,6},{8,15},{9,8},{10,9... | collective-permute-start | bytes 393224 | tf_op jit(solution)/shard_map/ppermute | solution.py:194
  288.3 6.8 %collective-permute-start.12 = (f32[256,128]{1,0:T(8,128)S(1)}, f32[256,128]{1,0:T(8,128)S(1)}, u32[]{:S(2)}, u32[]{:S(2)}) collective-permute-start(f32[256,128]{1,0:T(8,128)S(1)} %bitcast_add_fusion.9), channel_id=1, source_target_pairs={{0,1},{1,2},{2,3},{3,4},{4,5},{5,6},{6,7},{7,0},{8,9},{9,10},{10,1... | collective-permute-start | bytes 393224 | tf_op jit(solution)/shard_map/ppermute | solution.py:193
  288.5 6.8 %collective-permute-start.19 = (f32[256,128]{1,0:T(8,128)S(1)}, f32[256,128]{1,0:T(8,128)S(1)}, u32[]{:S(2)}, u32[]{:S(2)}) collective-permute-start(f32[256,128]{1,0:T(8,128)S(1)} %bitcast_add_fusion.2), channel_id=1, source_target_pairs={{0,7},{1,0},{2,1},{3,2},{4,3},{5,4},{6,5},{7,6},{8,15},{9,8},{10,9... | collective-permute-start | bytes 393224 | tf_op jit(solution)/shard_map/ppermute | solution.py:194
  295.2 6.3 %collective-permute-start.13 = (f32[256,128]{1,0:T(8,128)S(1)}, f32[256,128]{1,0:T(8,128)S(1)}, u32[]{:S(2)}, u32[]{:S(2)}) collective-permute-start(f32[256,128]{1,0:T(8,128)S(1)} %bitcast_add_fusion.8), channel_id=1, source_target_pairs={{0,1},{1,2},{2,3},{3,4},{4,5},{5,6},{6,7},{7,0},{8,9},{9,10},{10,1... | collective-permute-start | bytes 393224 | tf_op jit(solution)/shard_map/ppermute | solution.py:193
  295.3 6.2 %collective-permute-start.20 = (f32[256,128]{1,0:T(8,128)S(1)}, f32[256,128]{1,0:T(8,128)S(1)}, u32[]{:S(2)}, u32[]{:S(2)}) collective-permute-start(f32[256,128]{1,0:T(8,128)S(1)} %bitcast_add_fusion.1), channel_id=1, source_target_pairs={{0,7},{1,0},{2,1},{3,2},{4,3},{5,4},{6,5},{7,6},{8,15},{9,8},{10,9... | collective-permute-start | bytes 393224 | tf_op jit(solution)/shard_map/ppermute | solution.py:194
Sparse Core Ops, SparseCore 0:
  26.6 219.1 all-gather.1

commit v9 on v7

--- a/solution.py
+++ b/solution.py
@@ -10,7 +10,7 @@
 
 DP_AXES = ("y", "xlo", "z")
 DP_SIZES = (4, 2, 8)
-JB = 4
+JB = 8
 PER_BLOCK = 8
 
 

time: 263 us -> 253 us (0.962)
  waiting for transfers between devices: 163 us -> 157 us
  Pallas kernels: 28.7 us -> 25.5 us
    ppermute x6, waiting for transfers between devices: 98.4 us -> 90.3 us  [hop(): return lax.ppermute(block, 'segment', [(src, dst)])]
where the time goes in v9:
time: 253 us
  waiting for transfers between devices  157 us (62%)
  starting transfers between devices  40.3 us (16%)
  Pallas kernels  25.5 us (10%)
  between operations  13.7 us (5%)
  local copies, waits for them, and re-layouts  12.2 us (5%)
  other arithmetic  3.93 us (2%)
    ppermute x6, waiting for transfers between devices, hop(): return lax.ppermute(block, 'segment', [(src, dst)])  90.3 us
    ppermute x1, waiting for transfers between devices, body(): lax.ppermute(lax.dynamic_index_in_dim(halves, 1 - side, 0, False), 'xlo',...  34.9 us
    ppermute x7, starting transfers between devices, ring_reduce_scatter(): got_w = lax.ppermute(send_w, axis, ccw)  24.9 us
    ppermute x7, waiting for transfers between devices, ring_reduce_scatter(): got_e = lax.ppermute(send_e, axis, cw)  20.7 us
    all_to_all x1, waiting for transfers between devices, body(): lax.all_to_all(grads_here, 'y', split_axis=1, concat_axis=0, tiled=True)  10.8 us
    pallas_call x1, Pallas kernels, layer_backward(): pl.pallas_call(backward_kernel, grid_spec=grid, out_shape=[jax.ShapeDtype...  9.37 us
    pallas_call x1, Pallas kernels, group_grads(): pl.pallas_call(grad_kernel, grid_spec=grid, out_shape=jax.ShapeDtypeStruc...  9.21 us
    ppermute x6, starting transfers between devices, hop(): return lax.ppermute(block, 'segment', [(src, dst)])  7.38 us
  transfers between devices with their start and end apart: 23, of which 12 were waited for; matrix products, arithmetic and copies ran while one was open for 2% of the time, Pallas kernels for 4%

profile of v9, /device:TPU:2, one launch (start us, length us, event | category | flops | bytes accessed | tf_op | source)
XLA Modules:
  0.0 252.6 jit_solution(5068469373302031400)
XLA Ops:
  7.4 6.9 %conditional.8 = (bf16[128,4096]{1,0:T(8,128)(2,1)S(1)}, f32[128,4096]{1,0:T(8,128)S(1)}) conditional(s32[]{:T(128)} %convert_element_type.26, () %tuple.69, (s32[256]{0:T(256)S(1)}, bf16[128,4096]{1,0:T(8,128)(2,1)}, bf16[32,8,128,128]{3,2,1,0:T(8,128)(2,1)}) %tuple.106), branch_computations={%region_0.0_spmd, %region_1.0_spmd} | conditional | flops 1073741824 | bytes 12582928 | solution.py:219
  7.4 6.9 %branch_1_fun.8 = (f32[128,4096]{1,0:T(8,128)S(1)}, bf16[128,4096]{1,0:T(8,128)(2,1)S(1)}) custom-call(s32[256]{0:T(256)S(1)} %get-tuple-element.79.cols_ref, bf16[128,4096]{1,0:T(8,128)(2,1)} %get-tuple-element.80.h_ref, bf16[32,8,128,128]{3,2,1,0:T(8,128)(2,1)} %get-tuple-element.81.w_ref), custom_call_target="tpu_custom_call" | custom-call | flops 1073741824 | bytes 12582912 | tf_op jit(solution)/shard_map/cond/branch_1_fun/pallas_call | solution.py:92
  14.3 2.3 collective-permute-start
  16.6 1.4 collective-permute-done
  21.9 1.6 collective-permute-start.2
  23.6 1.2 select_select_fusion
  24.8 1.2 conditional.12
  29.7 1.3 collective-permute-start.5
  31.0 88.9 %collective-permute-done.5 = bf16[128,4096]{1,0:T(8,128)(2,1)S(1)} collective-permute-done((bf16[128,4096]{1,0:T(8,128)(2,1)}, bf16[128,4096]{1,0:T(8,128)(2,1)S(1)}, u32[]{:S(2)}, u32[]{:S(2)}) %collective-permute-start.5) | collective-permute-done | bytes 1048608 | tf_op jit(solution)/shard_map/ppermute | solution.py:209
  119.9 10.3 %conditional.15 = (bf16[128,4096]{1,0:T(8,128)(2,1)S(1)}) conditional(s32[]{:T(128)} %convert_element_type.26, bf16[128,4096]{1,0:T(8,128)(2,1)S(1)} %get-tuple-element.135, (s32[256]{0:T(256)S(1)}, bf16[128,4096]{1,0:T(8,128)(2,1)S(1)}, f32[128,4096]{1,0:T(8,128)S(1)}, bf16[32,8,128,128]{3,2,1,0:T(8,128)(2,1)}) %tuple.113), branch_computations={%region_14.15_spmd, %region_15.16_spmd} | conditional | flops 1073741824 | bytes 17825828 | solution.py:234
  120.8 9.4 %branch_1_fun.15 = (bf16[128,4096]{1,0:T(8,128)(2,1)S(1)}, bf16[128,4096]{1,0:T(8,128)(2,1)}) custom-call(s32[256]{0:T(256)S(1)} %get-tuple-element.108.cols_ref, bf16[128,4096]{1,0:T(8,128)(2,1)} %copy-done.5, f32[128,4096]{1,0:T(8,128)S(1)} %get-tuple-element.110.z_ref, bf16[32,8,128,128]{3,2,1,0:T(8,128)(2,1)} %get-tuple-element.111.w_ref), custom_call_target="tpu_custom_call" | custom-call | flops 1073741824 | bytes 13631488 | tf_op jit(solution)/shard_map/cond/branch_1_fun/pallas_call | solution.py:124
  131.3 4.3 %all-to-all-start = ((bf16[128,4,1024]{2,0,1:T(8,128)(2,1)}), bf16[128,4,1024]{2,0,1:T(8,128)(2,1)S(1)}, u32[]{:S(2)}, u32[]{:S(2)}) async-start(bf16[128,4,1024]{2,0,1:T(8,128)(2,1)} %bitcast.59), calls=%async_computation | async-start | bytes 2097152 | tf_op jit(solution)/shard_map/all_to_all | solution.py:249
  135.6 10.8 %all-to-all-done = bf16[128,4,1024]{2,0,1:T(8,128)(2,1)S(1)} async-done(((bf16[128,4,1024]{2,0,1:T(8,128)(2,1)}), bf16[128,4,1024]{2,0,1:T(8,128)(2,1)S(1)}, u32[]{:S(2)}, u32[]{:S(2)}) %all-to-all-start) | async-done | bytes 1048608 | tf_op jit(solution)/shard_map/all_to_all | solution.py:249
  146.5 9.2 %shard_map.47 = f32[64,128,128]{2,1,0:T(8,128)S(1)} custom-call(s32[64]{0:T(128)S(1)} %dynamic_slice.59.cols_ref, bf16[512,4096]{1,0:T(8,128)(2,1)} %all-gather.2.cloned.1.call-done.h_ref, bf16[512,1024]{1,0:T(8,128)(2,1)S(1)} %bitcast.62), custom_call_target="tpu_custom_call" | custom-call | flops 1073741824 | bytes 9437184 | tf_op jit(solution)/shard_map/pallas_call | solution.py:165
  155.7 1.6 dynamic-slice_bitcast_fusion
  159.5 34.9 %collective-permute-done.6 = f32[4096,128]{1,0:T(8,128)S(1)} collective-permute-done((f32[4096,128]{1,0:T(8,128)}, f32[4096,128]{1,0:T(8,128)S(1)}, u32[]{:S(2)}, u32[]{:S(2)}) %collective-permute-start.6) | collective-permute-done | bytes 2097184 | tf_op jit(solution)/shard_map/ppermute | solution.py:257
  194.4 1.8 bitcast_add_fusion
  196.4 2.1 collective-permute-start.7
  198.5 4.2 %collective-permute-start.14 = (f32[256,128]{1,0:T(8,128)S(1)}, f32[256,128]{1,0:T(8,128)S(1)}, u32[]{:S(2)}, u32[]{:S(2)}) collective-permute-start(f32[256,128]{1,0:T(8,128)S(1)} %dynamic-slice_bitcast_fusion.1), channel_id=1, source_target_pairs={{0,7},{1,0},{2,1},{3,2},{4,3},{5,4},{6,5},{7,6},{8,15},{9,8},{10,9... | collective-permute-start | bytes 393224 | tf_op jit(solution)/shard_map/ppermute | solution.py:194
  202.7 2.6 %collective-permute-done.7 = f32[256,128]{1,0:T(8,128)S(1)} collective-permute-done((f32[256,128]{1,0:T(8,128)S(1)}, f32[256,128]{1,0:T(8,128)S(1)}, u32[]{:S(2)}, u32[]{:S(2)}) %collective-permute-start.7) | collective-permute-done | bytes 131104 | tf_op jit(solution)/shard_map/ppermute | solution.py:193
  205.5 3.5 %collective-permute-start.15 = (f32[256,128]{1,0:T(8,128)S(1)}, f32[256,128]{1,0:T(8,128)S(1)}, u32[]{:S(2)}, u32[]{:S(2)}) collective-permute-start(f32[256,128]{1,0:T(8,128)S(1)} %bitcast_add_fusion.7), channel_id=1, source_target_pairs={{0,7},{1,0},{2,1},{3,2},{4,3},{5,4},{6,5},{7,6},{8,15},{9,8},{10,9... | collective-permute-start | bytes 393224 | tf_op jit(solution)/shard_map/ppermute | solution.py:194
  209.0 3.0 %collective-permute-done.8 = f32[256,128]{1,0:T(8,128)S(1)} collective-permute-done((f32[256,128]{1,0:T(8,128)S(1)}, f32[256,128]{1,0:T(8,128)S(1)}, u32[]{:S(2)}, u32[]{:S(2)}) %collective-permute-start.8) | collective-permute-done | bytes 131104 | tf_op jit(solution)/shard_map/ppermute | solution.py:193
  212.2 3.8 %collective-permute-start.16 = (f32[256,128]{1,0:T(8,128)S(1)}, f32[256,128]{1,0:T(8,128)S(1)}, u32[]{:S(2)}, u32[]{:S(2)}) collective-permute-start(f32[256,128]{1,0:T(8,128)S(1)} %bitcast_add_fusion.6), channel_id=1, source_target_pairs={{0,7},{1,0},{2,1},{3,2},{4,3},{5,4},{6,5},{7,6},{8,15},{9,8},{10,9... | collective-permute-start | bytes 393224 | tf_op jit(solution)/shard_map/ppermute | solution.py:194
  216.0 3.5 %collective-permute-done.9 = f32[256,128]{1,0:T(8,128)S(1)} collective-permute-done((f32[256,128]{1,0:T(8,128)S(1)}, f32[256,128]{1,0:T(8,128)S(1)}, u32[]{:S(2)}, u32[]{:S(2)}) %collective-permute-start.9) | collective-permute-done | bytes 131104 | tf_op jit(solution)/shard_map/ppermute | solution.py:193
  219.7 3.5 %collective-permute-start.17 = (f32[256,128]{1,0:T(8,128)S(1)}, f32[256,128]{1,0:T(8,128)S(1)}, u32[]{:S(2)}, u32[]{:S(2)}) collective-permute-start(f32[256,128]{1,0:T(8,128)S(1)} %bitcast_add_fusion.5), channel_id=1, source_target_pairs={{0,7},{1,0},{2,1},{3,2},{4,3},{5,4},{6,5},{7,6},{8,15},{9,8},{10,9... | collective-permute-start | bytes 393224 | tf_op jit(solution)/shard_map/ppermute | solution.py:194
  223.2 3.0 %collective-permute-done.10 = f32[256,128]{1,0:T(8,128)S(1)} collective-permute-done((f32[256,128]{1,0:T(8,128)S(1)}, f32[256,128]{1,0:T(8,128)S(1)}, u32[]{:S(2)}, u32[]{:S(2)}) %collective-permute-start.10) | collective-permute-done | bytes 131104 | tf_op jit(solution)/shard_map/ppermute | solution.py:193
  226.3 3.3 %collective-permute-start.18 = (f32[256,128]{1,0:T(8,128)S(1)}, f32[256,128]{1,0:T(8,128)S(1)}, u32[]{:S(2)}, u32[]{:S(2)}) collective-permute-start(f32[256,128]{1,0:T(8,128)S(1)} %bitcast_add_fusion.4), channel_id=1, source_target_pairs={{0,7},{1,0},{2,1},{3,2},{4,3},{5,4},{6,5},{7,6},{8,15},{9,8},{10,9... | collective-permute-start | bytes 393224 | tf_op jit(solution)/shard_map/ppermute | solution.py:194
  229.6 2.8 %collective-permute-done.11 = f32[256,128]{1,0:T(8,128)S(1)} collective-permute-done((f32[256,128]{1,0:T(8,128)S(1)}, f32[256,128]{1,0:T(8,128)S(1)}, u32[]{:S(2)}, u32[]{:S(2)}) %collective-permute-start.11) | collective-permute-done | bytes 131104 | tf_op jit(solution)/shard_map/ppermute | solution.py:193
  232.6 3.3 %collective-permute-start.19 = (f32[256,128]{1,0:T(8,128)S(1)}, f32[256,128]{1,0:T(8,128)S(1)}, u32[]{:S(2)}, u32[]{:S(2)}) collective-permute-start(f32[256,128]{1,0:T(8,128)S(1)} %bitcast_add_fusion.3), channel_id=1, source_target_pairs={{0,7},{1,0},{2,1},{3,2},{4,3},{5,4},{6,5},{7,6},{8,15},{9,8},{10,9... | collective-permute-start | bytes 393224 | tf_op jit(solution)/shard_map/ppermute | solution.py:194
  235.9 2.8 %collective-permute-done.12 = f32[256,128]{1,0:T(8,128)S(1)} collective-permute-done((f32[256,128]{1,0:T(8,128)S(1)}, f32[256,128]{1,0:T(8,128)S(1)}, u32[]{:S(2)}, u32[]{:S(2)}) %collective-permute-start.12) | collective-permute-done | bytes 131104 | tf_op jit(solution)/shard_map/ppermute | solution.py:193
  238.9 3.3 %collective-permute-start.20 = (f32[256,128]{1,0:T(8,128)S(1)}, f32[256,128]{1,0:T(8,128)S(1)}, u32[]{:S(2)}, u32[]{:S(2)}) collective-permute-start(f32[256,128]{1,0:T(8,128)S(1)} %bitcast_add_fusion.2), channel_id=1, source_target_pairs={{0,7},{1,0},{2,1},{3,2},{4,3},{5,4},{6,5},{7,6},{8,15},{9,8},{10,9... | collective-permute-start | bytes 393224 | tf_op jit(solution)/shard_map/ppermute | solution.py:194
  242.2 2.8 %collective-permute-done.13 = f32[256,128]{1,0:T(8,128)S(1)} collective-permute-done((f32[256,128]{1,0:T(8,128)S(1)}, f32[256,128]{1,0:T(8,128)S(1)}, u32[]{:S(2)}, u32[]{:S(2)}) %collective-permute-start.13) | collective-permute-done | bytes 131104 | tf_op jit(solution)/shard_map/ppermute | solution.py:193
  (65 shorter events, 19.9 us)
Async XLA Ops:
  6.5 139.9 %all-gather.2.cloned.1.call-start = ((), (), s32[]{:S(2)}) async-start(), calls=%async_computation.1 | async-start | bytes 5242880 | tf_op jit(solution)/shard_map/all_gather | solution.py:252
  14.3 3.7 %collective-permute-start = (bf16[128,4096]{1,0:T(8,128)(2,1)S(1)}, bf16[128,4096]{1,0:T(8,128)(2,1)}, u32[]{:S(2)}, u32[]{:S(2)}) collective-permute-start(bf16[128,4096]{1,0:T(8,128)(2,1)S(1)} %get-tuple-element.126), channel_id=1, source_target_pairs={{0,64},{1,65},{2,66},{3,67},{4,68},{5,69},{6,70},{7,71},{8,72},{9,... | collective-permute-start | bytes 3145736 | tf_op jit(solution)/shard_map/ppermute | solution.py:209
  19.1 0.7 collective-permute-start.1
  19.9 1.0 copy-start.2
  20.8 2.7 %copy-start.1 = (bf16[128,4096]{1,0:T(8,128)(2,1)S(1)}, bf16[128,4096]{1,0:T(8,128)(2,1)}, u32[]{:S(2)}) copy-start(bf16[128,4096]{1,0:T(8,128)(2,1)} %param.20) | copy-start | bytes 3145732
  21.9 1.6 collective-permute-start.2
  26.0 0.7 collective-permute-start.3
  27.9 0.7 collective-permute-start.4
  29.7 90.2 %collective-permute-start.5 = (bf16[128,4096]{1,0:T(8,128)(2,1)}, bf16[128,4096]{1,0:T(8,128)(2,1)S(1)}, u32[]{:S(2)}, u32[]{:S(2)}) collective-permute-start(bf16[128,4096]{1,0:T(8,128)(2,1)} %get-tuple-element.136), channel_id=1, source_target_pairs={{64,0},{65,1},{66,2},{67,3},{68,4},{69,5},{70,6},{71,7},{72,8},{73... | collective-permute-start | bytes 3145736 | tf_op jit(solution)/shard_map/ppermute | solution.py:209
  119.9 1.0 copy-start.5
  131.3 15.2 %all-to-all-start = ((bf16[128,4,1024]{2,0,1:T(8,128)(2,1)}), bf16[128,4,1024]{2,0,1:T(8,128)(2,1)S(1)}, u32[]{:S(2)}, u32[]{:S(2)}) async-start(bf16[128,4,1024]{2,0,1:T(8,128)(2,1)} %bitcast.59), calls=%async_computation | async-start | bytes 2097152 | tf_op jit(solution)/shard_map/all_to_all | solution.py:249
  155.7 2.6 %copy-start = (f32[64,128,128]{2,1,0:T(8,128)}, f32[64,128,128]{2,1,0:T(8,128)S(1)}, u32[]{:S(2)}) copy-start(f32[64,128,128]{2,1,0:T(8,128)S(1)} %shard_map.47) | copy-start | bytes 12582916
  158.3 36.1 %collective-permute-start.6 = (f32[4096,128]{1,0:T(8,128)}, f32[4096,128]{1,0:T(8,128)S(1)}, u32[]{:S(2)}, u32[]{:S(2)}) collective-permute-start(f32[4096,128]{1,0:T(8,128)} %dynamic-slice_bitcast_fusion), channel_id=1, source_target_pairs={{0,8},{8,0},{1,9},{9,1},{2,10},{10,2},{3,11},{11,3},{4,12},{12,4},... | collective-permute-start | bytes 6291464 | tf_op jit(solution)/shard_map/ppermute | solution.py:257
  196.4 8.9 %collective-permute-start.7 = (f32[256,128]{1,0:T(8,128)S(1)}, f32[256,128]{1,0:T(8,128)S(1)}, u32[]{:S(2)}, u32[]{:S(2)}) collective-permute-start(f32[256,128]{1,0:T(8,128)S(1)} %dynamic-slice_bitcast_fusion.2), channel_id=1, source_target_pairs={{0,1},{1,2},{2,3},{3,4},{4,5},{5,6},{6,7},{7,0},{8,9},{9,10},{10,1... | collective-permute-start | bytes 393224 | tf_op jit(solution)/shard_map/ppermute | solution.py:193
  198.5 6.9 %collective-permute-start.14 = (f32[256,128]{1,0:T(8,128)S(1)}, f32[256,128]{1,0:T(8,128)S(1)}, u32[]{:S(2)}, u32[]{:S(2)}) collective-permute-start(f32[256,128]{1,0:T(8,128)S(1)} %dynamic-slice_bitcast_fusion.1), channel_id=1, source_target_pairs={{0,7},{1,0},{2,1},{3,2},{4,3},{5,4},{6,5},{7,6},{8,15},{9,8},{10,9... | collective-permute-start | bytes 393224 | tf_op jit(solution)/shard_map/ppermute | solution.py:194
  205.3 6.7 %collective-permute-start.8 = (f32[256,128]{1,0:T(8,128)S(1)}, f32[256,128]{1,0:T(8,128)S(1)}, u32[]{:S(2)}, u32[]{:S(2)}) collective-permute-start(f32[256,128]{1,0:T(8,128)S(1)} %bitcast_add_fusion.14), channel_id=1, source_target_pairs={{0,1},{1,2},{2,3},{3,4},{4,5},{5,6},{6,7},{7,0},{8,9},{9,10},{10,1... | collective-permute-start | bytes 393224 | tf_op jit(solution)/shard_map/ppermute | solution.py:193
  205.5 6.7 %collective-permute-start.15 = (f32[256,128]{1,0:T(8,128)S(1)}, f32[256,128]{1,0:T(8,128)S(1)}, u32[]{:S(2)}, u32[]{:S(2)}) collective-permute-start(f32[256,128]{1,0:T(8,128)S(1)} %bitcast_add_fusion.7), channel_id=1, source_target_pairs={{0,7},{1,0},{2,1},{3,2},{4,3},{5,4},{6,5},{7,6},{8,15},{9,8},{10,9... | collective-permute-start | bytes 393224 | tf_op jit(solution)/shard_map/ppermute | solution.py:194
  212.0 7.5 %collective-permute-start.9 = (f32[256,128]{1,0:T(8,128)S(1)}, f32[256,128]{1,0:T(8,128)S(1)}, u32[]{:S(2)}, u32[]{:S(2)}) collective-permute-start(f32[256,128]{1,0:T(8,128)S(1)} %bitcast_add_fusion.13), channel_id=1, source_target_pairs={{0,1},{1,2},{2,3},{3,4},{4,5},{5,6},{6,7},{7,0},{8,9},{9,10},{10,1... | collective-permute-start | bytes 393224 | tf_op jit(solution)/shard_map/ppermute | solution.py:193
  212.2 7.4 %collective-permute-start.16 = (f32[256,128]{1,0:T(8,128)S(1)}, f32[256,128]{1,0:T(8,128)S(1)}, u32[]{:S(2)}, u32[]{:S(2)}) collective-permute-start(f32[256,128]{1,0:T(8,128)S(1)} %bitcast_add_fusion.6), channel_id=1, source_target_pairs={{0,7},{1,0},{2,1},{3,2},{4,3},{5,4},{6,5},{7,6},{8,15},{9,8},{10,9... | collective-permute-start | bytes 393224 | tf_op jit(solution)/shard_map/ppermute | solution.py:194
  219.5 6.6 %collective-permute-start.10 = (f32[256,128]{1,0:T(8,128)S(1)}, f32[256,128]{1,0:T(8,128)S(1)}, u32[]{:S(2)}, u32[]{:S(2)}) collective-permute-start(f32[256,128]{1,0:T(8,128)S(1)} %bitcast_add_fusion.12), channel_id=1, source_target_pairs={{0,1},{1,2},{2,3},{3,4},{4,5},{5,6},{6,7},{7,0},{8,9},{9,10},{10,1... | collective-permute-start | bytes 393224 | tf_op jit(solution)/shard_map/ppermute | solution.py:193
  219.7 6.6 %collective-permute-start.17 = (f32[256,128]{1,0:T(8,128)S(1)}, f32[256,128]{1,0:T(8,128)S(1)}, u32[]{:S(2)}, u32[]{:S(2)}) collective-permute-start(f32[256,128]{1,0:T(8,128)S(1)} %bitcast_add_fusion.5), channel_id=1, source_target_pairs={{0,7},{1,0},{2,1},{3,2},{4,3},{5,4},{6,5},{7,6},{8,15},{9,8},{10,9... | collective-permute-start | bytes 393224 | tf_op jit(solution)/shard_map/ppermute | solution.py:194
  226.2 6.3 %collective-permute-start.11 = (f32[256,128]{1,0:T(8,128)S(1)}, f32[256,128]{1,0:T(8,128)S(1)}, u32[]{:S(2)}, u32[]{:S(2)}) collective-permute-start(f32[256,128]{1,0:T(8,128)S(1)} %bitcast_add_fusion.11), channel_id=1, source_target_pairs={{0,1},{1,2},{2,3},{3,4},{4,5},{5,6},{6,7},{7,0},{8,9},{9,10},{10,1... | collective-permute-start | bytes 393224 | tf_op jit(solution)/shard_map/ppermute | solution.py:193
  226.3 6.2 %collective-permute-start.18 = (f32[256,128]{1,0:T(8,128)S(1)}, f32[256,128]{1,0:T(8,128)S(1)}, u32[]{:S(2)}, u32[]{:S(2)}) collective-permute-start(f32[256,128]{1,0:T(8,128)S(1)} %bitcast_add_fusion.4), channel_id=1, source_target_pairs={{0,7},{1,0},{2,1},{3,2},{4,3},{5,4},{6,5},{7,6},{8,15},{9,8},{10,9... | collective-permute-start | bytes 393224 | tf_op jit(solution)/shard_map/ppermute | solution.py:194
  232.5 6.3 %collective-permute-start.12 = (f32[256,128]{1,0:T(8,128)S(1)}, f32[256,128]{1,0:T(8,128)S(1)}, u32[]{:S(2)}, u32[]{:S(2)}) collective-permute-start(f32[256,128]{1,0:T(8,128)S(1)} %bitcast_add_fusion.10), channel_id=1, source_target_pairs={{0,1},{1,2},{2,3},{3,4},{4,5},{5,6},{6,7},{7,0},{8,9},{9,10},{10,1... | collective-permute-start | bytes 393224 | tf_op jit(solution)/shard_map/ppermute | solution.py:193
  232.6 6.2 %collective-permute-start.19 = (f32[256,128]{1,0:T(8,128)S(1)}, f32[256,128]{1,0:T(8,128)S(1)}, u32[]{:S(2)}, u32[]{:S(2)}) collective-permute-start(f32[256,128]{1,0:T(8,128)S(1)} %bitcast_add_fusion.3), channel_id=1, source_target_pairs={{0,7},{1,0},{2,1},{3,2},{4,3},{5,4},{6,5},{7,6},{8,15},{9,8},{10,9... | collective-permute-start | bytes 393224 | tf_op jit(solution)/shard_map/ppermute | solution.py:194
  238.7 6.3 %collective-permute-start.13 = (f32[256,128]{1,0:T(8,128)S(1)}, f32[256,128]{1,0:T(8,128)S(1)}, u32[]{:S(2)}, u32[]{:S(2)}) collective-permute-start(f32[256,128]{1,0:T(8,128)S(1)} %bitcast_add_fusion.9), channel_id=1, source_target_pairs={{0,1},{1,2},{2,3},{3,4},{4,5},{5,6},{6,7},{7,0},{8,9},{9,10},{10,1... | collective-permute-start | bytes 393224 | tf_op jit(solution)/shard_map/ppermute | solution.py:193
  238.9 6.2 %collective-permute-start.20 = (f32[256,128]{1,0:T(8,128)S(1)}, f32[256,128]{1,0:T(8,128)S(1)}, u32[]{:S(2)}, u32[]{:S(2)}) collective-permute-start(f32[256,128]{1,0:T(8,128)S(1)} %bitcast_add_fusion.2), channel_id=1, source_target_pairs={{0,7},{1,0},{2,1},{3,2},{4,3},{5,4},{6,5},{7,6},{8,15},{9,8},{10,9... | collective-permute-start | bytes 393224 | tf_op jit(solution)/shard_map/ppermute | solution.py:194
Sparse Core Ops, SparseCore 0:
  24.9 86.0 all-gather.1

commit v10 on v9

--- a/solution.py
+++ b/solution.py
@@ -135,7 +135,7 @@
     )(cols, upstream, preact, weight)
 
 
-def grad_kernel(cols_ref, h_ref, g_ref, out_ref):
+def grad_kernel(cols_ref, j_ref, h_ref, g_ref, out_ref):
     edge = out_ref.shape[-1]
     per_step = out_ref.shape[0]
     step = pl.program_id(0)
@@ -143,24 +143,24 @@
         q = step * per_step + qq
         c = cols_ref[q]
         x = h_ref[:, pl.ds(pl.multiple_of(c * edge, edge), edge)]
-        j = q // PER_BLOCK
+        j = j_ref[q]
         g = g_ref[:, pl.ds(pl.multiple_of(j * edge, edge), edge)]
         out_ref[qq] = lax.dot_general(
             x, g, (((0,), (0,)), ((), ())), preferred_element_type=jnp.float32
         )
 
 
-def group_grads(cols, inputs_group, grads_group, pairs, per_step):
+def group_grads(cols, j_index, inputs_group, grads_group, pairs, per_step):
     rows, width = inputs_group.shape
     edge = 128
     grid = pltpu.PrefetchScalarGridSpec(
-        num_scalar_prefetch=1,
+        num_scalar_prefetch=2,
         grid=(pairs // per_step,),
         in_specs=[
-            pl.BlockSpec((rows, width), lambda i, c: (0, 0)),
-            pl.BlockSpec(grads_group.shape, lambda i, c: (0, 0)),
-        ],
-        out_specs=pl.BlockSpec((per_step, edge, edge), lambda i, c: (i, 0, 0)),
+            pl.BlockSpec((rows, width), lambda i, c, j: (0, 0)),
+            pl.BlockSpec(grads_group.shape, lambda i, c, j: (0, 0)),
+        ],
+        out_specs=pl.BlockSpec((per_step, edge, edge), lambda i, c, j: (i, 0, 0)),
     )
     return pl.pallas_call(
         grad_kernel,
@@ -174,7 +174,7 @@
             transcendentals=0,
             bytes_accessed=inputs_group.size * 2 + grads_group.size * 2 + pairs * edge * edge * 4,
         ),
-    )(cols, inputs_group, grads_group)
+    )(cols, j_index, inputs_group, grads_group)
 
 
 def ring_reduce_scatter(chunks, axis, n):
@@ -251,12 +251,14 @@
     ).reshape(members * all_rows, group_j * edge_size)
     inputs_group = lax.all_gather(all_inputs, "y", axis=0, tiled=True)
     cols_here = lax.dynamic_slice_in_dim(flat_cols, member * group_pairs, group_pairs)
-    partial = group_grads(cols_here, inputs_group, grads_group, group_pairs, 8)
-    halves = partial.reshape(nx, group_pairs // nx * edge_size, edge_size)
+    order = np.arange(group_pairs).reshape(nx, nz, -1).transpose(1, 0, 2).reshape(-1)
+    j_index = jnp.asarray(order // per_block, jnp.int32)
+    partial = group_grads(cols_here[order], j_index, inputs_group, grads_group, group_pairs, 8)
+    reduced = ring_reduce_scatter(partial.reshape(nz, -1, edge_size), "z", nz)
+    halves = reduced.reshape(nx, -1, edge_size)
     side = lax.axis_index("xlo")
     got = lax.ppermute(lax.dynamic_index_in_dim(halves, 1 - side, 0, False), "xlo", [(0, 1), (1, 0)])
-    kept = lax.dynamic_index_in_dim(halves, side, 0, False) + got
-    own_share = ring_reduce_scatter(kept.reshape(nz, -1, edge_size), "z", nz)
+    own_share = lax.dynamic_index_in_dim(halves, side, 0, False) + got
     summed = own_share.astype(jnp.bfloat16)
     return summed[None]
 

time: 253 us -> 243 us (0.960)
  waiting for transfers between devices: 157 us -> 142 us
  other arithmetic: 3.93 us -> 8.99 us
    ppermute x1, waiting for transfers between devices: 34.9 us -> 6.15 us  [body(): lax.ppermute(lax.dynamic_index_in_dim(halves, 1 - side, 0, False), 'xlo',...]
    ppermute x7, waiting for transfers between devices: 20.7 us -> 35.6 us  [ring_reduce_scatter(): got_e = lax.ppermute(send_e, axis, cw)]
    add x6, other arithmetic: 0.1 us -> 5.87 us  [ring_reduce_scatter(): send_e = got_e + send_e]
  transfers between devices with their start and end apart: 23 -> 23, of which waited for: 12 -> 11; matrix products, arithmetic and copies ran while one was open for 2% -> 5% of each run, Pallas kernels for 4% -> 4%
where the time goes in v10:
time: 243 us; the launch traced here: 242 us
  waiting for transfers between devices  142 us (58%)
  starting transfers between devices  39.9 us (16%)
  Pallas kernels  25.6 us (11%)
  between operations  13.7 us (6%)
  local copies, waits for them, and re-layouts  12 us (5%)
  other arithmetic  8.99 us (4%)
    ppermute x6, waiting for transfers between devices, hop(): return lax.ppermute(block, 'segment', [(src, dst)])  90.3 us
    ppermute x7, waiting for transfers between devices, ring_reduce_scatter(): got_e = lax.ppermute(send_e, axis, cw)  35.6 us
    ppermute x7, starting transfers between devices, ring_reduce_scatter(): got_w = lax.ppermute(send_w, axis, ccw)  25.3 us
    all_to_all x1, waiting for transfers between devices, body(): lax.all_to_all(grads_here, 'y', split_axis=1, concat_axis=0, tiled=True)  10 us
    pallas_call x1, Pallas kernels, group_grads(): pl.pallas_call(grad_kernel, grid_spec=grid, out_shape=jax.ShapeDtypeStruc...  9.42 us
    pallas_call x1, Pallas kernels, layer_backward(): pl.pallas_call(backward_kernel, grid_spec=grid, out_shape=[jax.ShapeDtype...  9.27 us
    ppermute x6, starting transfers between devices, hop(): return lax.ppermute(block, 'segment', [(src, dst)])  7.41 us
    pallas_call x1, Pallas kernels, layer_forward(): pl.pallas_call(forward_kernel, grid_spec=grid, out_shape=[jax.ShapeDtypeS...  6.89 us
  transfers between devices with their start and end apart: 23, of which 11 were waited for; matrix products, arithmetic and copies ran while one was open for 5% of the time, Pallas kernels for 4%

profile of v10, /device:TPU:2, one launch (start us, length us, event | category | flops | bytes accessed | tf_op | source)
XLA Modules:
  0.0 242.3 jit_solution(575663524752494212)
XLA Ops:
  7.4 6.9 %conditional.8 = (bf16[128,4096]{1,0:T(8,128)(2,1)S(1)}, f32[128,4096]{1,0:T(8,128)S(1)}) conditional(s32[]{:T(128)} %convert_element_type.21, () %tuple.69, (s32[256]{0:T(256)S(1)}, bf16[128,4096]{1,0:T(8,128)(2,1)}, bf16[32,8,128,128]{3,2,1,0:T(8,128)(2,1)}) %tuple.106), branch_computations={%region_0.0_spmd, %region_1.0_spmd} | conditional | flops 1073741824 | bytes 12582928 | solution.py:219
  7.4 6.9 %branch_1_fun.8 = (f32[128,4096]{1,0:T(8,128)S(1)}, bf16[128,4096]{1,0:T(8,128)(2,1)S(1)}) custom-call(s32[256]{0:T(256)S(1)} %get-tuple-element.79.cols_ref, bf16[128,4096]{1,0:T(8,128)(2,1)} %get-tuple-element.80.h_ref, bf16[32,8,128,128]{3,2,1,0:T(8,128)(2,1)} %get-tuple-element.81.w_ref), custom_call_target="tpu_custom_call" | custom-call | flops 1073741824 | bytes 12582912 | tf_op jit(solution)/shard_map/cond/branch_1_fun/pallas_call | solution.py:92
  14.3 2.3 collective-permute-start
  16.6 1.4 collective-permute-done
  21.9 1.6 collective-permute-start.2
  23.5 1.2 select_select_fusion
  24.8 1.2 conditional.12
  26.7 1.1 conditional.13
  29.7 1.3 collective-permute-start.5
  31.0 88.9 %collective-permute-done.5 = bf16[128,4096]{1,0:T(8,128)(2,1)S(1)} collective-permute-done((bf16[128,4096]{1,0:T(8,128)(2,1)}, bf16[128,4096]{1,0:T(8,128)(2,1)S(1)}, u32[]{:S(2)}, u32[]{:S(2)}) %collective-permute-start.5) | collective-permute-done | bytes 1048608 | tf_op jit(solution)/shard_map/ppermute | solution.py:209
  119.9 10.3 %conditional.15 = (bf16[128,4096]{1,0:T(8,128)(2,1)S(1)}) conditional(s32[]{:T(128)} %convert_element_type.21, bf16[128,4096]{1,0:T(8,128)(2,1)S(1)} %get-tuple-element.135, (s32[256]{0:T(256)S(1)}, bf16[128,4096]{1,0:T(8,128)(2,1)S(1)}, f32[128,4096]{1,0:T(8,128)S(1)}, bf16[32,8,128,128]{3,2,1,0:T(8,128)(2,1)}) %tuple.113), branch_computations={%region_14.15_spmd, %region_15.16_spmd} | conditional | flops 1073741824 | bytes 17825828 | solution.py:234
  120.9 9.3 %branch_1_fun.15 = (bf16[128,4096]{1,0:T(8,128)(2,1)S(1)}, bf16[128,4096]{1,0:T(8,128)(2,1)}) custom-call(s32[256]{0:T(256)S(1)} %get-tuple-element.108.cols_ref, bf16[128,4096]{1,0:T(8,128)(2,1)} %copy-done.6, f32[128,4096]{1,0:T(8,128)S(1)} %get-tuple-element.110.z_ref, bf16[32,8,128,128]{3,2,1,0:T(8,128)(2,1)} %get-tuple-element.111.w_ref), custom_call_target="tpu_custom_call" | custom-call | flops 1073741824 | bytes 13631488 | tf_op jit(solution)/shard_map/cond/branch_1_fun/pallas_call | solution.py:124
  131.2 4.3 %all-to-all-start = ((bf16[128,4,1024]{2,0,1:T(8,128)(2,1)}), bf16[128,4,1024]{2,0,1:T(8,128)(2,1)S(1)}, u32[]{:S(2)}, u32[]{:S(2)}) async-start(bf16[128,4,1024]{2,0,1:T(8,128)(2,1)} %bitcast.53), calls=%async_computation | async-start | bytes 2097152 | tf_op jit(solution)/shard_map/all_to_all | solution.py:249
  136.4 10.0 %all-to-all-done = bf16[128,4,1024]{2,0,1:T(8,128)(2,1)S(1)} async-done(((bf16[128,4,1024]{2,0,1:T(8,128)(2,1)}), bf16[128,4,1024]{2,0,1:T(8,128)(2,1)S(1)}, u32[]{:S(2)}, u32[]{:S(2)}) %all-to-all-start) | async-done | bytes 1048608 | tf_op jit(solution)/shard_map/all_to_all | solution.py:249
  146.4 9.4 %shard_map.74 = f32[64,128,128]{2,1,0:T(8,128)S(1)} custom-call(s32[64]{0:T(128)S(1)} %gather_fusion, s32[64]{0:T(128)S(1)} %copy-done, bf16[512,4096]{1,0:T(8,128)(2,1)} %all-gather.2.cloned.1.call-done.h_ref, bf16[512,1024]{1,0:T(8,128)(2,1)S(1)} %bitcast.55), custom_call_target="tpu_custom_call" | custom-call | flops 1073741824 | bytes 9437184 | tf_op jit(solution)/shard_map/pallas_call | solution.py:165
  156.2 1.3 copy-done.1
  157.5 2.1 collective-permute-start.6
  159.6 4.0 %collective-permute-start.13 = (f32[512,128]{1,0:T(8,128)S(1)}, f32[512,128]{1,0:T(8,128)S(1)}, u32[]{:S(2)}, u32[]{:S(2)}) collective-permute-start(f32[512,128]{1,0:T(8,128)S(1)} %dynamic-slice_bitcast_fusion.1), channel_id=1, source_target_pairs={{0,7},{1,0},{2,1},{3,2},{4,3},{5,4},{6,5},{7,6},{8,15},{9,8},{10,9... | collective-permute-start | bytes 786440 | tf_op jit(solution)/shard_map/ppermute | solution.py:194
  163.6 4.2 %collective-permute-done.6 = f32[512,128]{1,0:T(8,128)S(1)} collective-permute-done((f32[512,128]{1,0:T(8,128)S(1)}, f32[512,128]{1,0:T(8,128)S(1)}, u32[]{:S(2)}, u32[]{:S(2)}) %collective-permute-start.6) | collective-permute-done | bytes 262176 | tf_op jit(solution)/shard_map/ppermute | solution.py:193
  169.0 4.9 %collective-permute-start.14 = (f32[512,128]{1,0:T(8,128)S(1)}, f32[512,128]{1,0:T(8,128)S(1)}, u32[]{:S(2)}, u32[]{:S(2)}) collective-permute-start(f32[512,128]{1,0:T(8,128)S(1)} %bitcast_add_fusion.7), channel_id=1, source_target_pairs={{0,7},{1,0},{2,1},{3,2},{4,3},{5,4},{6,5},{7,6},{8,15},{9,8},{10,9... | collective-permute-start | bytes 786440 | tf_op jit(solution)/shard_map/ppermute | solution.py:194
  173.8 6.9 %collective-permute-done.7 = f32[512,128]{1,0:T(8,128)S(1)} collective-permute-done((f32[512,128]{1,0:T(8,128)S(1)}, f32[512,128]{1,0:T(8,128)S(1)}, u32[]{:S(2)}, u32[]{:S(2)}) %collective-permute-start.7) | collective-permute-done | bytes 262176 | tf_op jit(solution)/shard_map/ppermute | solution.py:193
  181.9 3.3 %collective-permute-start.15 = (f32[512,128]{1,0:T(8,128)S(1)}, f32[512,128]{1,0:T(8,128)S(1)}, u32[]{:S(2)}, u32[]{:S(2)}) collective-permute-start(f32[512,128]{1,0:T(8,128)S(1)} %bitcast_add_fusion.6), channel_id=1, source_target_pairs={{0,7},{1,0},{2,1},{3,2},{4,3},{5,4},{6,5},{7,6},{8,15},{9,8},{10,9... | collective-permute-start | bytes 786440 | tf_op jit(solution)/shard_map/ppermute | solution.py:194
  185.2 6.2 %collective-permute-done.8 = f32[512,128]{1,0:T(8,128)S(1)} collective-permute-done((f32[512,128]{1,0:T(8,128)S(1)}, f32[512,128]{1,0:T(8,128)S(1)}, u32[]{:S(2)}, u32[]{:S(2)}) %collective-permute-start.8) | collective-permute-done | bytes 262176 | tf_op jit(solution)/shard_map/ppermute | solution.py:193
  192.5 3.3 %collective-permute-start.16 = (f32[512,128]{1,0:T(8,128)S(1)}, f32[512,128]{1,0:T(8,128)S(1)}, u32[]{:S(2)}, u32[]{:S(2)}) collective-permute-start(f32[512,128]{1,0:T(8,128)S(1)} %bitcast_add_fusion.5), channel_id=1, source_target_pairs={{0,7},{1,0},{2,1},{3,2},{4,3},{5,4},{6,5},{7,6},{8,15},{9,8},{10,9... | collective-permute-start | bytes 786440 | tf_op jit(solution)/shard_map/ppermute | solution.py:194
  195.8 5.4 %collective-permute-done.9 = f32[512,128]{1,0:T(8,128)S(1)} collective-permute-done((f32[512,128]{1,0:T(8,128)S(1)}, f32[512,128]{1,0:T(8,128)S(1)}, u32[]{:S(2)}, u32[]{:S(2)}) %collective-permute-start.9) | collective-permute-done | bytes 262176 | tf_op jit(solution)/shard_map/ppermute | solution.py:193
  202.2 3.3 %collective-permute-start.17 = (f32[512,128]{1,0:T(8,128)S(1)}, f32[512,128]{1,0:T(8,128)S(1)}, u32[]{:S(2)}, u32[]{:S(2)}) collective-permute-start(f32[512,128]{1,0:T(8,128)S(1)} %bitcast_add_fusion.4), channel_id=1, source_target_pairs={{0,7},{1,0},{2,1},{3,2},{4,3},{5,4},{6,5},{7,6},{8,15},{9,8},{10,9... | collective-permute-start | bytes 786440 | tf_op jit(solution)/shard_map/ppermute | solution.py:194
  205.5 4.4 %collective-permute-done.10 = f32[512,128]{1,0:T(8,128)S(1)} collective-permute-done((f32[512,128]{1,0:T(8,128)S(1)}, f32[512,128]{1,0:T(8,128)S(1)}, u32[]{:S(2)}, u32[]{:S(2)}) %collective-permute-start.10) | collective-permute-done | bytes 262176 | tf_op jit(solution)/shard_map/ppermute | solution.py:193
  211.1 3.3 %collective-permute-start.18 = (f32[512,128]{1,0:T(8,128)S(1)}, f32[512,128]{1,0:T(8,128)S(1)}, u32[]{:S(2)}, u32[]{:S(2)}) collective-permute-start(f32[512,128]{1,0:T(8,128)S(1)} %bitcast_add_fusion.3), channel_id=1, source_target_pairs={{0,7},{1,0},{2,1},{3,2},{4,3},{5,4},{6,5},{7,6},{8,15},{9,8},{10,9... | collective-permute-start | bytes 786440 | tf_op jit(solution)/shard_map/ppermute | solution.py:194
  214.4 4.2 %collective-permute-done.11 = f32[512,128]{1,0:T(8,128)S(1)} collective-permute-done((f32[512,128]{1,0:T(8,128)S(1)}, f32[512,128]{1,0:T(8,128)S(1)}, u32[]{:S(2)}, u32[]{:S(2)}) %collective-permute-start.11) | collective-permute-done | bytes 262176 | tf_op jit(solution)/shard_map/ppermute | solution.py:193
  219.7 3.3 %collective-permute-start.19 = (f32[512,128]{1,0:T(8,128)S(1)}, f32[512,128]{1,0:T(8,128)S(1)}, u32[]{:S(2)}, u32[]{:S(2)}) collective-permute-start(f32[512,128]{1,0:T(8,128)S(1)} %bitcast_add_fusion.2), channel_id=1, source_target_pairs={{0,7},{1,0},{2,1},{3,2},{4,3},{5,4},{6,5},{7,6},{8,15},{9,8},{10,9... | collective-permute-start | bytes 786440 | tf_op jit(solution)/shard_map/ppermute | solution.py:194
  223.0 4.2 %collective-permute-done.12 = f32[512,128]{1,0:T(8,128)S(1)} collective-permute-done((f32[512,128]{1,0:T(8,128)S(1)}, f32[512,128]{1,0:T(8,128)S(1)}, u32[]{:S(2)}, u32[]{:S(2)}) %collective-permute-start.12) | collective-permute-done | bytes 262176 | tf_op jit(solution)/shard_map/ppermute | solution.py:193
  228.7 6.1 %collective-permute-done.20 = f32[512,128]{1,0:T(8,128)S(1)} collective-permute-done((f32[512,128]{1,0:T(8,128)S(1)}, f32[512,128]{1,0:T(8,128)S(1)}, u32[]{:S(2)}, u32[]{:S(2)}) %collective-permute-start.20) | collective-permute-done | bytes 262176 | tf_op jit(solution)/shard_map/ppermute | solution.py:260
  (71 shorter events, 24.8 us)
Async XLA Ops:
  6.5 139.9 %all-gather.2.cloned.1.call-start = ((), (), s32[]{:S(2)}) async-start(), calls=%async_computation.1 | async-start | bytes 5242880 | tf_op jit(solution)/shard_map/all_gather | solution.py:252
  14.3 3.7 %collective-permute-start = (bf16[128,4096]{1,0:T(8,128)(2,1)S(1)}, bf16[128,4096]{1,0:T(8,128)(2,1)}, u32[]{:S(2)}, u32[]{:S(2)}) collective-permute-start(bf16[128,4096]{1,0:T(8,128)(2,1)S(1)} %get-tuple-element.126), channel_id=1, source_target_pairs={{0,64},{1,65},{2,66},{3,67},{4,68},{5,69},{6,70},{7,71},{8,72},{9,... | collective-permute-start | bytes 3145736 | tf_op jit(solution)/shard_map/ppermute | solution.py:209
  19.1 0.7 collective-permute-start.1
  19.8 1.0 copy-start.3
  20.8 2.7 %copy-start.2 = (bf16[128,4096]{1,0:T(8,128)(2,1)S(1)}, bf16[128,4096]{1,0:T(8,128)(2,1)}, u32[]{:S(2)}) copy-start(bf16[128,4096]{1,0:T(8,128)(2,1)} %param.23) | copy-start | bytes 3145732
  21.9 1.6 collective-permute-start.2
  26.0 0.7 collective-permute-start.3
  27.8 0.7 collective-permute-start.4
  29.7 90.2 %collective-permute-start.5 = (bf16[128,4096]{1,0:T(8,128)(2,1)}, bf16[128,4096]{1,0:T(8,128)(2,1)S(1)}, u32[]{:S(2)}, u32[]{:S(2)}) collective-permute-start(bf16[128,4096]{1,0:T(8,128)(2,1)} %get-tuple-element.136), channel_id=1, source_target_pairs={{64,0},{65,1},{66,2},{67,3},{68,4},{69,5},{70,6},{71,7},{72,8},{73... | collective-permute-start | bytes 3145736 | tf_op jit(solution)/shard_map/ppermute | solution.py:209
  119.9 1.0 copy-start.6
  130.1 5.5 %copy-start.7 = (s32[64]{0:T(128)S(1)}, s32[64]{0:T(128)}, u32[]{:S(2)}) copy-start(s32[64]{0:T(128)} %constant.199) | copy-start | bytes 772
  130.1 16.3 %copy-start = (s32[64]{0:T(128)S(1)}, s32[64]{0:T(128)}, u32[]{:S(2)}) copy-start(s32[64]{0:T(128)} %constant.193.clone.j_ref) | copy-start | bytes 772
  131.2 15.2 %all-to-all-start = ((bf16[128,4,1024]{2,0,1:T(8,128)(2,1)}), bf16[128,4,1024]{2,0,1:T(8,128)(2,1)S(1)}, u32[]{:S(2)}, u32[]{:S(2)}) async-start(bf16[128,4,1024]{2,0,1:T(8,128)(2,1)} %bitcast.53), calls=%async_computation | async-start | bytes 2097152 | tf_op jit(solution)/shard_map/all_to_all | solution.py:249
  156.2 1.3 copy-start.1
  157.5 10.3 %collective-permute-start.6 = (f32[512,128]{1,0:T(8,128)S(1)}, f32[512,128]{1,0:T(8,128)S(1)}, u32[]{:S(2)}, u32[]{:S(2)}) collective-permute-start(f32[512,128]{1,0:T(8,128)S(1)} %dynamic-slice_bitcast_fusion.2), channel_id=1, source_target_pairs={{0,1},{1,2},{2,3},{3,4},{4,5},{5,6},{6,7},{7,0},{8,9},{9,10},{10,1... | collective-permute-start | bytes 786440 | tf_op jit(solution)/shard_map/ppermute | solution.py:193
  159.6 9.3 %collective-permute-start.13 = (f32[512,128]{1,0:T(8,128)S(1)}, f32[512,128]{1,0:T(8,128)S(1)}, u32[]{:S(2)}, u32[]{:S(2)}) collective-permute-start(f32[512,128]{1,0:T(8,128)S(1)} %dynamic-slice_bitcast_fusion.1), channel_id=1, source_target_pairs={{0,7},{1,0},{2,1},{3,2},{4,3},{5,4},{6,5},{7,6},{8,15},{9,8},{10,9... | collective-permute-start | bytes 786440 | tf_op jit(solution)/shard_map/ppermute | solution.py:194
  168.8 11.9 %collective-permute-start.7 = (f32[512,128]{1,0:T(8,128)S(1)}, f32[512,128]{1,0:T(8,128)S(1)}, u32[]{:S(2)}, u32[]{:S(2)}) collective-permute-start(f32[512,128]{1,0:T(8,128)S(1)} %bitcast_add_fusion.14), channel_id=1, source_target_pairs={{0,1},{1,2},{2,3},{3,4},{4,5},{5,6},{6,7},{7,0},{8,9},{9,10},{10,1... | collective-permute-start | bytes 786440 | tf_op jit(solution)/shard_map/ppermute | solution.py:193
  169.0 12.8 %collective-permute-start.14 = (f32[512,128]{1,0:T(8,128)S(1)}, f32[512,128]{1,0:T(8,128)S(1)}, u32[]{:S(2)}, u32[]{:S(2)}) collective-permute-start(f32[512,128]{1,0:T(8,128)S(1)} %bitcast_add_fusion.7), channel_id=1, source_target_pairs={{0,7},{1,0},{2,1},{3,2},{4,3},{5,4},{6,5},{7,6},{8,15},{9,8},{10,9... | collective-permute-start | bytes 786440 | tf_op jit(solution)/shard_map/ppermute | solution.py:194
  181.7 9.6 %collective-permute-start.8 = (f32[512,128]{1,0:T(8,128)S(1)}, f32[512,128]{1,0:T(8,128)S(1)}, u32[]{:S(2)}, u32[]{:S(2)}) collective-permute-start(f32[512,128]{1,0:T(8,128)S(1)} %bitcast_add_fusion.13), channel_id=1, source_target_pairs={{0,1},{1,2},{2,3},{3,4},{4,5},{5,6},{6,7},{7,0},{8,9},{9,10},{10,1... | collective-permute-start | bytes 786440 | tf_op jit(solution)/shard_map/ppermute | solution.py:193
  181.9 10.5 %collective-permute-start.15 = (f32[512,128]{1,0:T(8,128)S(1)}, f32[512,128]{1,0:T(8,128)S(1)}, u32[]{:S(2)}, u32[]{:S(2)}) collective-permute-start(f32[512,128]{1,0:T(8,128)S(1)} %bitcast_add_fusion.6), channel_id=1, source_target_pairs={{0,7},{1,0},{2,1},{3,2},{4,3},{5,4},{6,5},{7,6},{8,15},{9,8},{10,9... | collective-permute-start | bytes 786440 | tf_op jit(solution)/shard_map/ppermute | solution.py:194
  192.3 8.8 %collective-permute-start.9 = (f32[512,128]{1,0:T(8,128)S(1)}, f32[512,128]{1,0:T(8,128)S(1)}, u32[]{:S(2)}, u32[]{:S(2)}) collective-permute-start(f32[512,128]{1,0:T(8,128)S(1)} %bitcast_add_fusion.12), channel_id=1, source_target_pairs={{0,1},{1,2},{2,3},{3,4},{4,5},{5,6},{6,7},{7,0},{8,9},{9,10},{10,1... | collective-permute-start | bytes 786440 | tf_op jit(solution)/shard_map/ppermute | solution.py:193
  192.5 9.7 %collective-permute-start.16 = (f32[512,128]{1,0:T(8,128)S(1)}, f32[512,128]{1,0:T(8,128)S(1)}, u32[]{:S(2)}, u32[]{:S(2)}) collective-permute-start(f32[512,128]{1,0:T(8,128)S(1)} %bitcast_add_fusion.5), channel_id=1, source_target_pairs={{0,7},{1,0},{2,1},{3,2},{4,3},{5,4},{6,5},{7,6},{8,15},{9,8},{10,9... | collective-permute-start | bytes 786440 | tf_op jit(solution)/shard_map/ppermute | solution.py:194
  202.1 7.9 %collective-permute-start.10 = (f32[512,128]{1,0:T(8,128)S(1)}, f32[512,128]{1,0:T(8,128)S(1)}, u32[]{:S(2)}, u32[]{:S(2)}) collective-permute-start(f32[512,128]{1,0:T(8,128)S(1)} %bitcast_add_fusion.11), channel_id=1, source_target_pairs={{0,1},{1,2},{2,3},{3,4},{4,5},{5,6},{6,7},{7,0},{8,9},{9,10},{10,1... | collective-permute-start | bytes 786440 | tf_op jit(solution)/shard_map/ppermute | solution.py:193
  202.2 8.8 %collective-permute-start.17 = (f32[512,128]{1,0:T(8,128)S(1)}, f32[512,128]{1,0:T(8,128)S(1)}, u32[]{:S(2)}, u32[]{:S(2)}) collective-permute-start(f32[512,128]{1,0:T(8,128)S(1)} %bitcast_add_fusion.4), channel_id=1, source_target_pairs={{0,7},{1,0},{2,1},{3,2},{4,3},{5,4},{6,5},{7,6},{8,15},{9,8},{10,9... | collective-permute-start | bytes 786440 | tf_op jit(solution)/shard_map/ppermute | solution.py:194
  210.9 7.7 %collective-permute-start.11 = (f32[512,128]{1,0:T(8,128)S(1)}, f32[512,128]{1,0:T(8,128)S(1)}, u32[]{:S(2)}, u32[]{:S(2)}) collective-permute-start(f32[512,128]{1,0:T(8,128)S(1)} %bitcast_add_fusion.10), channel_id=1, source_target_pairs={{0,1},{1,2},{2,3},{3,4},{4,5},{5,6},{6,7},{7,0},{8,9},{9,10},{10,1... | collective-permute-start | bytes 786440 | tf_op jit(solution)/shard_map/ppermute | solution.py:193
  211.1 8.6 %collective-permute-start.18 = (f32[512,128]{1,0:T(8,128)S(1)}, f32[512,128]{1,0:T(8,128)S(1)}, u32[]{:S(2)}, u32[]{:S(2)}) collective-permute-start(f32[512,128]{1,0:T(8,128)S(1)} %bitcast_add_fusion.3), channel_id=1, source_target_pairs={{0,7},{1,0},{2,1},{3,2},{4,3},{5,4},{6,5},{7,6},{8,15},{9,8},{10,9... | collective-permute-start | bytes 786440 | tf_op jit(solution)/shard_map/ppermute | solution.py:194
  219.6 7.7 %collective-permute-start.12 = (f32[512,128]{1,0:T(8,128)S(1)}, f32[512,128]{1,0:T(8,128)S(1)}, u32[]{:S(2)}, u32[]{:S(2)}) collective-permute-start(f32[512,128]{1,0:T(8,128)S(1)} %bitcast_add_fusion.9), channel_id=1, source_target_pairs={{0,1},{1,2},{2,3},{3,4},{4,5},{5,6},{6,7},{7,0},{8,9},{9,10},{10,1... | collective-permute-start | bytes 786440 | tf_op jit(solution)/shard_map/ppermute | solution.py:193
  219.7 8.5 %collective-permute-start.19 = (f32[512,128]{1,0:T(8,128)S(1)}, f32[512,128]{1,0:T(8,128)S(1)}, u32[]{:S(2)}, u32[]{:S(2)}) collective-permute-start(f32[512,128]{1,0:T(8,128)S(1)} %bitcast_add_fusion.2), channel_id=1, source_target_pairs={{0,7},{1,0},{2,1},{3,2},{4,3},{5,4},{6,5},{7,6},{8,15},{9,8},{10,9... | collective-permute-start | bytes 786440 | tf_op jit(solution)/shard_map/ppermute | solution.py:194
  228.3 6.5 %collective-permute-start.20 = (f32[512,128]{1,0:T(8,128)S(1)}, f32[512,128]{1,0:T(8,128)S(1)}, u32[]{:S(2)}, u32[]{:S(2)}) collective-permute-start(f32[512,128]{1,0:T(8,128)S(1)} %dynamic-slice_bitcast_fusion), channel_id=1, source_target_pairs={{0,8},{8,0},{1,9},{9,1},{2,10},{10,2},{3,11},{11,3},{4,12},{12,4},... | collective-permute-start | bytes 786440 | tf_op jit(solution)/shard_map/ppermute | solution.py:260
Sparse Core Ops, SparseCore 0:
  24.9 86.0 all-gather.1

commit v11 on v10

--- a/solution.py
+++ b/solution.py
@@ -20,10 +20,10 @@
     return lax.ppermute(block, axis, route)
 
 
-def forward_kernel(cols_ref, h_ref, w_ref, z_ref, out_ref):
+def forward_kernel(first, cols_ref, h_ref, w_ref, z_ref, out_ref):
     edge = w_ref.shape[-1]
     per_block = w_ref.shape[1]
-    step = pl.program_id(0)
+    step = first + pl.program_id(0)
     for jj in range(w_ref.shape[0]):
         j = step * w_ref.shape[0] + jj
         picked = jnp.concatenate(
@@ -73,32 +73,35 @@
         new_ref[...] = (up_ref[...].astype(jnp.float32) + back_ref[...]).astype(new_ref.dtype)
 
 
-def layer_forward(cols, hidden, weight):
+def layer_forward(cols, hidden, weight, first, count):
     rows, width = hidden.shape
     num_blocks, per_block, edge, _ = weight.shape
     grid = pltpu.PrefetchScalarGridSpec(
         num_scalar_prefetch=1,
-        grid=(num_blocks // JB,),
+        grid=(count,),
         in_specs=[
             pl.BlockSpec((rows, width), lambda i, c: (0, 0)),
-            pl.BlockSpec((JB, per_block, edge, edge), lambda i, c: (i, 0, 0, 0)),
+            pl.BlockSpec((JB, per_block, edge, edge), lambda i, c: (first + i, 0, 0, 0)),
         ],
         out_specs=[
             pl.BlockSpec((rows, JB * edge), lambda i, c: (0, i)),
             pl.BlockSpec((rows, JB * edge), lambda i, c: (0, i)),
         ],
     )
-    flops = 2 * rows * num_blocks * per_block * edge * edge
+    flops = 2 * rows * count * JB * per_block * edge * edge
+    out_width = count * JB * edge
     return pl.pallas_call(
-        forward_kernel,
+        functools.partial(forward_kernel, first),
         grid_spec=grid,
         out_shape=[
-            jax.ShapeDtypeStruct((rows, width), jnp.float32),
-            jax.ShapeDtypeStruct((rows, width), hidden.dtype),
+            jax.ShapeDtypeStruct((rows, out_width), jnp.float32),
+            jax.ShapeDtypeStruct((rows, out_width), hidden.dtype),
         ],
         compiler_params=pltpu.CompilerParams(dimension_semantics=("arbitrary",)),
         cost_estimate=pl.CostEstimate(
-            flops=flops, transcendentals=rows * width, bytes_accessed=weight.size * 2 + rows * width * 8
+            flops=flops,
+            transcendentals=rows * out_width,
+            bytes_accessed=count * JB * per_block * edge * edge * 2 + rows * width * 2 + rows * out_width * 6,
         ),
     )(cols, hidden, weight)
 
@@ -209,22 +212,29 @@
         return lax.ppermute(block, "segment", [(src, dst)])
 
     zeros_x = jnp.zeros((all_rows, layer_width), jnp.bfloat16)
-    zeros_z = jnp.zeros((all_rows, layer_width), jnp.float32)
+    halves = num_blocks // JB // 2
+    zeros_half = jnp.zeros((all_rows, layer_width // 2), jnp.bfloat16)
+    stash_halves = [jnp.zeros((all_rows, layer_width // 2), jnp.float32)] * 2
     stash_x = inputs
-    stash_z = zeros_z
     current = inputs
     for step_now in range(segments):
         active = segment_index == step_now
         held = current
-        stash_z, result = lax.cond(
-            active,
-            lambda: layer_forward(flat_cols, held, weight),
-            lambda: (stash_z, zeros_x),
-        )
+        sent = []
+        for part in range(2):
+            kept = stash_halves[part]
+            stash_halves[part], result = lax.cond(
+                active,
+                lambda part=part: layer_forward(flat_cols, held, weight, part * halves, halves),
+                lambda kept=kept: (kept, zeros_half),
+            )
+            if step_now + 1 < segments:
+                sent.append(hop(result, step_now, step_now + 1))
         if step_now > 0:
             stash_x = jnp.where(active, current, stash_x)
-        if step_now + 1 < segments:
-            current = hop(result, step_now, step_now + 1)
+        if sent:
+            current = jnp.concatenate(sent, axis=1)
+    stash_z = jnp.concatenate(stash_halves, axis=1)
     stash_g = zeros_x
     upstream = cotangent
     for step_now in range(segments):

time: 243 us -> 251 us (1.033)
  waiting for transfers between devices: 142 us -> 137 us
  Pallas kernels: 25.6 us -> 29.3 us
  starting transfers between devices: 39.9 us -> 43.3 us
  other arithmetic: 8.99 us -> 11.6 us
    ppermute x6 -> x9, waiting for transfers between devices: 90.3 us -> 86.1 us  [hop(): return lax.ppermute(block, 'segment', [(src, dst)])]
    pallas_call x1 -> x2, Pallas kernels: 6.89 us -> 10.6 us  [layer_forward(): pl.pallas_call(functools.partial(forward_kernel, first), grid_spec=grid,...]
    ppermute x6 -> x9, starting transfers between devices: 7.41 us -> 10.4 us  [hop(): return lax.ppermute(block, 'segment', [(src, dst)])]
    broadcast_in_dim x6 -> x4, local copies, waits for them, and re-layouts: 5.53 us -> 3.43 us  [body(): zeros_x = jnp.zeros((all_rows, layer_width), jnp.bfloat16)]
  transfers between devices with their start and end apart: 23 -> 26, of which waited for: 11 -> 11; matrix products, arithmetic and copies ran while one was open for 5% -> 6% of each run, Pallas kernels for 4% -> 6%
where the time goes in v11:
time: 251 us; the launch traced here: 250 us
  waiting for transfers between devices  137 us (55%)
  starting transfers between devices  43.3 us (17%)
  Pallas kernels  29.3 us (12%)
  local copies, waits for them, and re-layouts  14.5 us (6%)
  between operations  13.8 us (5%)
  other arithmetic  11.6 us (5%)
    ppermute x9, waiting for transfers between devices, hop(): return lax.ppermute(block, 'segment', [(src, dst)])  86.1 us
    ppermute x7, waiting for transfers between devices, ring_reduce_scatter(): got_e = lax.ppermute(send_e, axis, cw)  35.4 us
    ppermute x7, starting transfers between devices, ring_reduce_scatter(): got_w = lax.ppermute(send_w, axis, ccw)  25.5 us
    pallas_call x2, Pallas kernels, layer_forward(): pl.pallas_call(functools.partial(forward_kernel, first), grid_spec=grid,...  10.6 us
    ppermute x9, starting transfers between devices, hop(): return lax.ppermute(block, 'segment', [(src, dst)])  10.4 us
    all_to_all x1, waiting for transfers between devices, body(): lax.all_to_all(grads_here, 'y', split_axis=1, concat_axis=0, tiled=True)  10 us
    pallas_call x1, Pallas kernels, group_grads(): pl.pallas_call(grad_kernel, grid_spec=grid, out_shape=jax.ShapeDtypeStruc...  9.42 us
    pallas_call x1, Pallas kernels, layer_backward(): pl.pallas_call(backward_kernel, grid_spec=grid, out_shape=[jax.ShapeDtype...  9.29 us
  transfers between devices with their start and end apart: 26, of which 11 were waited for; matrix products, arithmetic and copies ran while one was open for 6% of the time, Pallas kernels for 6%

profile of v11, /device:TPU:2, one launch (start us, length us, event | category | flops | bytes accessed | tf_op | source)
XLA Modules:
  0.0 250.1 jit_solution(10941379422452166942)
XLA Ops:
  7.4 5.7 %conditional.12 = (bf16[128,2048]{1,0:T(8,128)(2,1)S(1)}, f32[128,2048]{1,0:T(8,128)}) conditional(s32[]{:T(128)} %convert_element_type.12, () %tuple.101, (s32[256]{0:T(256)S(1)}, bf16[128,4096]{1,0:T(8,128)(2,1)}, bf16[32,8,128,128]{3,2,1,0:T(8,128)(2,1)}) %tuple.151), branch_computations={%region_0.0_spmd, %region_1.0_spmd} | conditional | flops 536870912 | bytes 6815760 | solution.py:226
  7.4 5.6 %branch_1_fun.12 = (f32[128,2048]{1,0:T(8,128)}, bf16[128,2048]{1,0:T(8,128)(2,1)S(1)}) custom-call(s32[256]{0:T(256)S(1)} %get-tuple-element.112.cols_ref, bf16[128,4096]{1,0:T(8,128)(2,1)} %get-tuple-element.113.h_ref, bf16[32,8,128,128]{3,2,1,0:T(8,128)(2,1)} %get-tuple-element.114.w_ref), custom_call_target="tpu_custom_call" | custom-call | flops 536870912 | bytes 6815744 | tf_op jit(solution)/shard_map/cond/branch_1_fun/pallas_call | solution.py:93
  14.4 5.0 %conditional.13 = (bf16[128,2048]{1,0:T(8,128)(2,1)S(1)}, f32[128,2048]{1,0:T(8,128)}) conditional(s32[]{:T(128)} %convert_element_type.12, () %tuple.103, (s32[256]{0:T(256)S(1)}, bf16[128,4096]{1,0:T(8,128)(2,1)}, bf16[32,8,128,128]{3,2,1,0:T(8,128)(2,1)}) %tuple.152), branch_computations={%region_2.0_spmd, %region_3.0_spmd} | conditional | flops 536870912 | bytes 6815760 | solution.py:226
  14.4 5.0 %branch_1_fun.13 = (f32[128,2048]{1,0:T(8,128)}, bf16[128,2048]{1,0:T(8,128)(2,1)S(1)}) custom-call(s32[256]{0:T(256)S(1)} %get-tuple-element.117.cols_ref, bf16[128,4096]{1,0:T(8,128)(2,1)} %get-tuple-element.118.h_ref, bf16[32,8,128,128]{3,2,1,0:T(8,128)(2,1)} %get-tuple-element.119.w_ref), custom_call_target="tpu_custom_call" | custom-call | flops 536870912 | bytes 6815744 | tf_op jit(solution)/shard_map/cond/branch_1_fun/pallas_call | solution.py:93
  20.8 1.4 collective-permute-done.1
  23.1 1.5 collective-permute-start.3
  25.8 1.5 collective-permute-start.4
  28.1 1.5 collective-permute-start.5
  31.8 2.4 select_select_fusion
  35.5 1.4 pad_maximum_fusion
  43.1 84.6 %collective-permute-done.8 = bf16[128,4096]{1,0:T(8,128)(2,1)S(1)} collective-permute-done((bf16[128,4096]{1,0:T(8,128)(2,1)}, bf16[128,4096]{1,0:T(8,128)(2,1)S(1)}, u32[]{:S(2)}, u32[]{:S(2)}) %collective-permute-start.8) | collective-permute-done | bytes 1048608 | tf_op jit(solution)/shard_map/ppermute | solution.py:212
  127.8 10.3 %conditional.23 = (bf16[128,4096]{1,0:T(8,128)(2,1)S(1)}) conditional(s32[]{:T(128)} %convert_element_type.12, bf16[128,4096]{1,0:T(8,128)(2,1)S(1)} %get-tuple-element.195, (s32[256]{0:T(256)S(1)}, bf16[128,4096]{1,0:T(8,128)(2,1)S(1)}, f32[128,4096]{1,0:T(8,128)S(1)}, bf16[32,8,128,128]{3,2,1,0:T(8,128)(2,1)}) %tuple.162), branch_computations={%region_22.23_spmd, %region_23.24_spmd} | conditional | flops 1073741824 | bytes 17825828 | solution.py:244
  128.8 9.3 %branch_1_fun.23 = (bf16[128,4096]{1,0:T(8,128)(2,1)S(1)}, bf16[128,4096]{1,0:T(8,128)(2,1)}) custom-call(s32[256]{0:T(256)S(1)} %get-tuple-element.156.cols_ref, bf16[128,4096]{1,0:T(8,128)(2,1)} %copy-done.5, f32[128,4096]{1,0:T(8,128)S(1)} %get-tuple-element.158.z_ref, bf16[32,8,128,128]{3,2,1,0:T(8,128)(2,1)} %get-tuple-element.159.w_ref), custom_call_target="tpu_custom_call" | custom-call | flops 1073741824 | bytes 13631488 | tf_op jit(solution)/shard_map/cond/branch_1_fun/pallas_call | solution.py:127
  139.1 4.3 %all-to-all-start = ((bf16[128,4,1024]{2,0,1:T(8,128)(2,1)}), bf16[128,4,1024]{2,0,1:T(8,128)(2,1)S(1)}, u32[]{:S(2)}, u32[]{:S(2)}) async-start(bf16[128,4,1024]{2,0,1:T(8,128)(2,1)} %bitcast.53), calls=%async_computation | async-start | bytes 2097152 | tf_op jit(solution)/shard_map/all_to_all | solution.py:259
  144.2 10.0 %all-to-all-done = bf16[128,4,1024]{2,0,1:T(8,128)(2,1)S(1)} async-done(((bf16[128,4,1024]{2,0,1:T(8,128)(2,1)}), bf16[128,4,1024]{2,0,1:T(8,128)(2,1)S(1)}, u32[]{:S(2)}, u32[]{:S(2)}) %all-to-all-start) | async-done | bytes 1048608 | tf_op jit(solution)/shard_map/all_to_all | solution.py:259
  154.3 9.4 %shard_map.74 = f32[64,128,128]{2,1,0:T(8,128)S(1)} custom-call(s32[64]{0:T(128)S(1)} %gather_fusion, s32[64]{0:T(128)S(1)} %copy-done, bf16[512,4096]{1,0:T(8,128)(2,1)} %all-gather.2.cloned.1.call-done.h_ref, bf16[512,1024]{1,0:T(8,128)(2,1)S(1)} %bitcast.55), custom_call_target="tpu_custom_call" | custom-call | flops 1073741824 | bytes 9437184 | tf_op jit(solution)/shard_map/pallas_call | solution.py:168
  165.4 1.9 collective-permute-start.9
  167.3 4.0 %collective-permute-start.16 = (f32[512,128]{1,0:T(8,128)S(1)}, f32[512,128]{1,0:T(8,128)S(1)}, u32[]{:S(2)}, u32[]{:S(2)}) collective-permute-start(f32[512,128]{1,0:T(8,128)S(1)} %dynamic-slice_bitcast_fusion.1), channel_id=1, source_target_pairs={{0,7},{1,0},{2,1},{3,2},{4,3},{5,4},{6,5},{7,6},{8,15},{9,8},{10,9... | collective-permute-start | bytes 786440 | tf_op jit(solution)/shard_map/ppermute | solution.py:197
  171.3 4.2 %collective-permute-done.9 = f32[512,128]{1,0:T(8,128)S(1)} collective-permute-done((f32[512,128]{1,0:T(8,128)S(1)}, f32[512,128]{1,0:T(8,128)S(1)}, u32[]{:S(2)}, u32[]{:S(2)}) %collective-permute-start.9) | collective-permute-done | bytes 262176 | tf_op jit(solution)/shard_map/ppermute | solution.py:196
  176.7 4.9 %collective-permute-start.17 = (f32[512,128]{1,0:T(8,128)S(1)}, f32[512,128]{1,0:T(8,128)S(1)}, u32[]{:S(2)}, u32[]{:S(2)}) collective-permute-start(f32[512,128]{1,0:T(8,128)S(1)} %bitcast_add_fusion.7), channel_id=1, source_target_pairs={{0,7},{1,0},{2,1},{3,2},{4,3},{5,4},{6,5},{7,6},{8,15},{9,8},{10,9... | collective-permute-start | bytes 786440 | tf_op jit(solution)/shard_map/ppermute | solution.py:197
  181.6 6.9 %collective-permute-done.10 = f32[512,128]{1,0:T(8,128)S(1)} collective-permute-done((f32[512,128]{1,0:T(8,128)S(1)}, f32[512,128]{1,0:T(8,128)S(1)}, u32[]{:S(2)}, u32[]{:S(2)}) %collective-permute-start.10) | collective-permute-done | bytes 262176 | tf_op jit(solution)/shard_map/ppermute | solution.py:196
  189.6 3.3 %collective-permute-start.18 = (f32[512,128]{1,0:T(8,128)S(1)}, f32[512,128]{1,0:T(8,128)S(1)}, u32[]{:S(2)}, u32[]{:S(2)}) collective-permute-start(f32[512,128]{1,0:T(8,128)S(1)} %bitcast_add_fusion.6), channel_id=1, source_target_pairs={{0,7},{1,0},{2,1},{3,2},{4,3},{5,4},{6,5},{7,6},{8,15},{9,8},{10,9... | collective-permute-start | bytes 786440 | tf_op jit(solution)/shard_map/ppermute | solution.py:197
  192.9 6.2 %collective-permute-done.11 = f32[512,128]{1,0:T(8,128)S(1)} collective-permute-done((f32[512,128]{1,0:T(8,128)S(1)}, f32[512,128]{1,0:T(8,128)S(1)}, u32[]{:S(2)}, u32[]{:S(2)}) %collective-permute-start.11) | collective-permute-done | bytes 262176 | tf_op jit(solution)/shard_map/ppermute | solution.py:196
  200.2 3.5 %collective-permute-start.19 = (f32[512,128]{1,0:T(8,128)S(1)}, f32[512,128]{1,0:T(8,128)S(1)}, u32[]{:S(2)}, u32[]{:S(2)}) collective-permute-start(f32[512,128]{1,0:T(8,128)S(1)} %bitcast_add_fusion.5), channel_id=1, source_target_pairs={{0,7},{1,0},{2,1},{3,2},{4,3},{5,4},{6,5},{7,6},{8,15},{9,8},{10,9... | collective-permute-start | bytes 786440 | tf_op jit(solution)/shard_map/ppermute | solution.py:197
  203.7 5.1 %collective-permute-done.12 = f32[512,128]{1,0:T(8,128)S(1)} collective-permute-done((f32[512,128]{1,0:T(8,128)S(1)}, f32[512,128]{1,0:T(8,128)S(1)}, u32[]{:S(2)}, u32[]{:S(2)}) %collective-permute-start.12) | collective-permute-done | bytes 262176 | tf_op jit(solution)/shard_map/ppermute | solution.py:196
  210.0 3.3 %collective-permute-start.20 = (f32[512,128]{1,0:T(8,128)S(1)}, f32[512,128]{1,0:T(8,128)S(1)}, u32[]{:S(2)}, u32[]{:S(2)}) collective-permute-start(f32[512,128]{1,0:T(8,128)S(1)} %bitcast_add_fusion.4), channel_id=1, source_target_pairs={{0,7},{1,0},{2,1},{3,2},{4,3},{5,4},{6,5},{7,6},{8,15},{9,8},{10,9... | collective-permute-start | bytes 786440 | tf_op jit(solution)/shard_map/ppermute | solution.py:197
  213.3 4.4 %collective-permute-done.13 = f32[512,128]{1,0:T(8,128)S(1)} collective-permute-done((f32[512,128]{1,0:T(8,128)S(1)}, f32[512,128]{1,0:T(8,128)S(1)}, u32[]{:S(2)}, u32[]{:S(2)}) %collective-permute-start.13) | collective-permute-done | bytes 262176 | tf_op jit(solution)/shard_map/ppermute | solution.py:196
  218.8 3.3 %collective-permute-start.21 = (f32[512,128]{1,0:T(8,128)S(1)}, f32[512,128]{1,0:T(8,128)S(1)}, u32[]{:S(2)}, u32[]{:S(2)}) collective-permute-start(f32[512,128]{1,0:T(8,128)S(1)} %bitcast_add_fusion.3), channel_id=1, source_target_pairs={{0,7},{1,0},{2,1},{3,2},{4,3},{5,4},{6,5},{7,6},{8,15},{9,8},{10,9... | collective-permute-start | bytes 786440 | tf_op jit(solution)/shard_map/ppermute | solution.py:197
  222.1 4.2 %collective-permute-done.14 = f32[512,128]{1,0:T(8,128)S(1)} collective-permute-done((f32[512,128]{1,0:T(8,128)S(1)}, f32[512,128]{1,0:T(8,128)S(1)}, u32[]{:S(2)}, u32[]{:S(2)}) %collective-permute-start.14) | collective-permute-done | bytes 262176 | tf_op jit(solution)/shard_map/ppermute | solution.py:196
  227.5 3.3 %collective-permute-start.22 = (f32[512,128]{1,0:T(8,128)S(1)}, f32[512,128]{1,0:T(8,128)S(1)}, u32[]{:S(2)}, u32[]{:S(2)}) collective-permute-start(f32[512,128]{1,0:T(8,128)S(1)} %bitcast_add_fusion.2), channel_id=1, source_target_pairs={{0,7},{1,0},{2,1},{3,2},{4,3},{5,4},{6,5},{7,6},{8,15},{9,8},{10,9... | collective-permute-start | bytes 786440 | tf_op jit(solution)/shard_map/ppermute | solution.py:197
  230.7 4.2 %collective-permute-done.15 = f32[512,128]{1,0:T(8,128)S(1)} collective-permute-done((f32[512,128]{1,0:T(8,128)S(1)}, f32[512,128]{1,0:T(8,128)S(1)}, u32[]{:S(2)}, u32[]{:S(2)}) %collective-permute-start.15) | collective-permute-done | bytes 262176 | tf_op jit(solution)/shard_map/ppermute | solution.py:196
  236.7 5.8 %collective-permute-done.23 = f32[512,128]{1,0:T(8,128)S(1)} collective-permute-done((f32[512,128]{1,0:T(8,128)S(1)}, f32[512,128]{1,0:T(8,128)S(1)}, u32[]{:S(2)}, u32[]{:S(2)}) %collective-permute-start.23) | collective-permute-done | bytes 262176 | tf_op jit(solution)/shard_map/ppermute | solution.py:270
  (89 shorter events, 34.1 us)
Async XLA Ops:
  6.5 147.7 %all-gather.2.cloned.1.call-start = ((), (), s32[]{:S(2)}) async-start(), calls=%async_computation.1 | async-start | bytes 5242880 | tf_op jit(solution)/shard_map/all_gather | solution.py:262
  13.0 7.7 %collective-permute-start = (bf16[128,2048]{1,0:T(8,128)(2,1)S(1)}, bf16[128,2048]{1,0:T(8,128)(2,1)S(1)}, u32[]{:S(2)}, u32[]{:S(2)}) collective-permute-start(bf16[128,2048]{1,0:T(8,128)(2,1)S(1)} %get-tuple-element.180), channel_id=1, source_target_pairs={{0,64},{1,65},{2,66},{3,67},{4,68},{5,69},{6,70},{7,71},{8,72},{9,... | collective-permute-start | bytes 1572872 | tf_op jit(solution)/shard_map/ppermute | solution.py:212
  19.4 2.8 %collective-permute-start.1 = (bf16[128,2048]{1,0:T(8,128)(2,1)S(1)}, bf16[128,2048]{1,0:T(8,128)(2,1)S(1)}, u32[]{:S(2)}, u32[]{:S(2)}) collective-permute-start(bf16[128,2048]{1,0:T(8,128)(2,1)S(1)} %get-tuple-element.181), channel_id=1, source_target_pairs={{0,64},{1,65},{2,66},{3,67},{4,68},{5,69},{6,70},{7,71},{8,72},{9,... | collective-permute-start | bytes 1572872 | tf_op jit(solution)/shard_map/ppermute | solution.py:212
  22.3 2.3 collective-permute-start.2
  23.1 1.5 collective-permute-start.3
  25.8 3.8 %collective-permute-start.4 = (bf16[128,2048]{1,0:T(8,128)(2,1)S(1)}, bf16[128,2048]{1,0:T(8,128)(2,1)}, u32[]{:S(2)}, u32[]{:S(2)}) collective-permute-start(bf16[128,2048]{1,0:T(8,128)(2,1)S(1)} %get-tuple-element.186), channel_id=1, source_target_pairs={{128,192},{129,193},{130,194},{131,195},{132,196},{133,197},{134,1... | collective-permute-start | bytes 1572872 | tf_op jit(solution)/shard_map/ppermute | solution.py:212
  28.1 2.5 %collective-permute-start.5 = (bf16[128,2048]{1,0:T(8,128)(2,1)}, bf16[128,2048]{1,0:T(8,128)(2,1)}, u32[]{:S(2)}, u32[]{:S(2)}) collective-permute-start(bf16[128,2048]{1,0:T(8,128)(2,1)} %get-tuple-element.188), channel_id=1, source_target_pairs={{128,192},{129,193},{130,194},{131,195},{132,196},{133,197},{134,1... | collective-permute-start | bytes 1572872 | tf_op jit(solution)/shard_map/ppermute | solution.py:212
  34.2 1.2 copy-start.2
  38.1 0.7 collective-permute-start.6
  40.0 0.7 collective-permute-start.7
  41.8 85.9 %collective-permute-start.8 = (bf16[128,4096]{1,0:T(8,128)(2,1)}, bf16[128,4096]{1,0:T(8,128)(2,1)S(1)}, u32[]{:S(2)}, u32[]{:S(2)}) collective-permute-start(bf16[128,4096]{1,0:T(8,128)(2,1)} %get-tuple-element.196), channel_id=1, source_target_pairs={{64,0},{65,1},{66,2},{67,3},{68,4},{69,5},{70,6},{71,7},{72,8},{73... | collective-permute-start | bytes 3145736 | tf_op jit(solution)/shard_map/ppermute | solution.py:212
  127.8 1.0 copy-start.5
  138.0 5.4 %copy-start.6 = (s32[64]{0:T(128)S(1)}, s32[64]{0:T(128)}, u32[]{:S(2)}) copy-start(s32[64]{0:T(128)} %constant.207) | copy-start | bytes 772
  138.0 16.2 %copy-start = (s32[64]{0:T(128)S(1)}, s32[64]{0:T(128)}, u32[]{:S(2)}) copy-start(s32[64]{0:T(128)} %constant.201.clone.j_ref) | copy-start | bytes 772
  139.1 15.1 %all-to-all-start = ((bf16[128,4,1024]{2,0,1:T(8,128)(2,1)}), bf16[128,4,1024]{2,0,1:T(8,128)(2,1)S(1)}, u32[]{:S(2)}, u32[]{:S(2)}) async-start(bf16[128,4,1024]{2,0,1:T(8,128)(2,1)} %bitcast.53), calls=%async_computation | async-start | bytes 2097152 | tf_op jit(solution)/shard_map/all_to_all | solution.py:259
  164.1 1.3 copy-start.1
  165.4 10.2 %collective-permute-start.9 = (f32[512,128]{1,0:T(8,128)S(1)}, f32[512,128]{1,0:T(8,128)S(1)}, u32[]{:S(2)}, u32[]{:S(2)}) collective-permute-start(f32[512,128]{1,0:T(8,128)S(1)} %dynamic-slice_bitcast_fusion.2), channel_id=1, source_target_pairs={{0,1},{1,2},{2,3},{3,4},{4,5},{5,6},{6,7},{7,0},{8,9},{9,10},{10,1... | collective-permute-start | bytes 786440 | tf_op jit(solution)/shard_map/ppermute | solution.py:196
  167.3 9.3 %collective-permute-start.16 = (f32[512,128]{1,0:T(8,128)S(1)}, f32[512,128]{1,0:T(8,128)S(1)}, u32[]{:S(2)}, u32[]{:S(2)}) collective-permute-start(f32[512,128]{1,0:T(8,128)S(1)} %dynamic-slice_bitcast_fusion.1), channel_id=1, source_target_pairs={{0,7},{1,0},{2,1},{3,2},{4,3},{5,4},{6,5},{7,6},{8,15},{9,8},{10,9... | collective-permute-start | bytes 786440 | tf_op jit(solution)/shard_map/ppermute | solution.py:197
  176.5 11.9 %collective-permute-start.10 = (f32[512,128]{1,0:T(8,128)S(1)}, f32[512,128]{1,0:T(8,128)S(1)}, u32[]{:S(2)}, u32[]{:S(2)}) collective-permute-start(f32[512,128]{1,0:T(8,128)S(1)} %bitcast_add_fusion.14), channel_id=1, source_target_pairs={{0,1},{1,2},{2,3},{3,4},{4,5},{5,6},{6,7},{7,0},{8,9},{9,10},{10,1... | collective-permute-start | bytes 786440 | tf_op jit(solution)/shard_map/ppermute | solution.py:196
  176.7 12.9 %collective-permute-start.17 = (f32[512,128]{1,0:T(8,128)S(1)}, f32[512,128]{1,0:T(8,128)S(1)}, u32[]{:S(2)}, u32[]{:S(2)}) collective-permute-start(f32[512,128]{1,0:T(8,128)S(1)} %bitcast_add_fusion.7), channel_id=1, source_target_pairs={{0,7},{1,0},{2,1},{3,2},{4,3},{5,4},{6,5},{7,6},{8,15},{9,8},{10,9... | collective-permute-start | bytes 786440 | tf_op jit(solution)/shard_map/ppermute | solution.py:197
  189.5 9.6 %collective-permute-start.11 = (f32[512,128]{1,0:T(8,128)S(1)}, f32[512,128]{1,0:T(8,128)S(1)}, u32[]{:S(2)}, u32[]{:S(2)}) collective-permute-start(f32[512,128]{1,0:T(8,128)S(1)} %bitcast_add_fusion.13), channel_id=1, source_target_pairs={{0,1},{1,2},{2,3},{3,4},{4,5},{5,6},{6,7},{7,0},{8,9},{9,10},{10,1... | collective-permute-start | bytes 786440 | tf_op jit(solution)/shard_map/ppermute | solution.py:196
  189.6 10.5 %collective-permute-start.18 = (f32[512,128]{1,0:T(8,128)S(1)}, f32[512,128]{1,0:T(8,128)S(1)}, u32[]{:S(2)}, u32[]{:S(2)}) collective-permute-start(f32[512,128]{1,0:T(8,128)S(1)} %bitcast_add_fusion.6), channel_id=1, source_target_pairs={{0,7},{1,0},{2,1},{3,2},{4,3},{5,4},{6,5},{7,6},{8,15},{9,8},{10,9... | collective-permute-start | bytes 786440 | tf_op jit(solution)/shard_map/ppermute | solution.py:197
  200.1 8.8 %collective-permute-start.12 = (f32[512,128]{1,0:T(8,128)S(1)}, f32[512,128]{1,0:T(8,128)S(1)}, u32[]{:S(2)}, u32[]{:S(2)}) collective-permute-start(f32[512,128]{1,0:T(8,128)S(1)} %bitcast_add_fusion.12), channel_id=1, source_target_pairs={{0,1},{1,2},{2,3},{3,4},{4,5},{5,6},{6,7},{7,0},{8,9},{9,10},{10,1... | collective-permute-start | bytes 786440 | tf_op jit(solution)/shard_map/ppermute | solution.py:196
  200.2 9.7 %collective-permute-start.19 = (f32[512,128]{1,0:T(8,128)S(1)}, f32[512,128]{1,0:T(8,128)S(1)}, u32[]{:S(2)}, u32[]{:S(2)}) collective-permute-start(f32[512,128]{1,0:T(8,128)S(1)} %bitcast_add_fusion.5), channel_id=1, source_target_pairs={{0,7},{1,0},{2,1},{3,2},{4,3},{5,4},{6,5},{7,6},{8,15},{9,8},{10,9... | collective-permute-start | bytes 786440 | tf_op jit(solution)/shard_map/ppermute | solution.py:197
  209.8 7.9 %collective-permute-start.13 = (f32[512,128]{1,0:T(8,128)S(1)}, f32[512,128]{1,0:T(8,128)S(1)}, u32[]{:S(2)}, u32[]{:S(2)}) collective-permute-start(f32[512,128]{1,0:T(8,128)S(1)} %bitcast_add_fusion.11), channel_id=1, source_target_pairs={{0,1},{1,2},{2,3},{3,4},{4,5},{5,6},{6,7},{7,0},{8,9},{9,10},{10,1... | collective-permute-start | bytes 786440 | tf_op jit(solution)/shard_map/ppermute | solution.py:196
  210.0 8.8 %collective-permute-start.20 = (f32[512,128]{1,0:T(8,128)S(1)}, f32[512,128]{1,0:T(8,128)S(1)}, u32[]{:S(2)}, u32[]{:S(2)}) collective-permute-start(f32[512,128]{1,0:T(8,128)S(1)} %bitcast_add_fusion.4), channel_id=1, source_target_pairs={{0,7},{1,0},{2,1},{3,2},{4,3},{5,4},{6,5},{7,6},{8,15},{9,8},{10,9... | collective-permute-start | bytes 786440 | tf_op jit(solution)/shard_map/ppermute | solution.py:197
  218.7 7.7 %collective-permute-start.14 = (f32[512,128]{1,0:T(8,128)S(1)}, f32[512,128]{1,0:T(8,128)S(1)}, u32[]{:S(2)}, u32[]{:S(2)}) collective-permute-start(f32[512,128]{1,0:T(8,128)S(1)} %bitcast_add_fusion.10), channel_id=1, source_target_pairs={{0,1},{1,2},{2,3},{3,4},{4,5},{5,6},{6,7},{7,0},{8,9},{9,10},{10,1... | collective-permute-start | bytes 786440 | tf_op jit(solution)/shard_map/ppermute | solution.py:196
  218.8 8.6 %collective-permute-start.21 = (f32[512,128]{1,0:T(8,128)S(1)}, f32[512,128]{1,0:T(8,128)S(1)}, u32[]{:S(2)}, u32[]{:S(2)}) collective-permute-start(f32[512,128]{1,0:T(8,128)S(1)} %bitcast_add_fusion.3), channel_id=1, source_target_pairs={{0,7},{1,0},{2,1},{3,2},{4,3},{5,4},{6,5},{7,6},{8,15},{9,8},{10,9... | collective-permute-start | bytes 786440 | tf_op jit(solution)/shard_map/ppermute | solution.py:197
  227.3 7.7 %collective-permute-start.15 = (f32[512,128]{1,0:T(8,128)S(1)}, f32[512,128]{1,0:T(8,128)S(1)}, u32[]{:S(2)}, u32[]{:S(2)}) collective-permute-start(f32[512,128]{1,0:T(8,128)S(1)} %bitcast_add_fusion.9), channel_id=1, source_target_pairs={{0,1},{1,2},{2,3},{3,4},{4,5},{5,6},{6,7},{7,0},{8,9},{9,10},{10,1... | collective-permute-start | bytes 786440 | tf_op jit(solution)/shard_map/ppermute | solution.py:196
  227.5 8.5 %collective-permute-start.22 = (f32[512,128]{1,0:T(8,128)S(1)}, f32[512,128]{1,0:T(8,128)S(1)}, u32[]{:S(2)}, u32[]{:S(2)}) collective-permute-start(f32[512,128]{1,0:T(8,128)S(1)} %bitcast_add_fusion.2), channel_id=1, source_target_pairs={{0,7},{1,0},{2,1},{3,2},{4,3},{5,4},{6,5},{7,6},{8,15},{9,8},{10,9... | collective-permute-start | bytes 786440 | tf_op jit(solution)/shard_map/ppermute | solution.py:197
  236.1 6.5 %collective-permute-start.23 = (f32[512,128]{1,0:T(8,128)S(1)}, f32[512,128]{1,0:T(8,128)S(1)}, u32[]{:S(2)}, u32[]{:S(2)}) collective-permute-start(f32[512,128]{1,0:T(8,128)S(1)} %dynamic-slice_bitcast_fusion), channel_id=1, source_target_pairs={{0,8},{8,0},{1,9},{9,1},{2,10},{10,2},{3,11},{11,3},{4,12},{12,4},... | collective-permute-start | bytes 786440 | tf_op jit(solution)/shard_map/ppermute | solution.py:270
Sparse Core Ops, SparseCore 0:
  34.3 81.5 all-gather.1

commit v12 on v10

--- a/solution.py
+++ b/solution.py
@@ -246,14 +246,21 @@
     group_j = num_blocks // members
     member = lax.axis_index("y")
     grads_here = all_grads.reshape(all_rows, members, group_j * edge_size)
-    grads_group = lax.all_to_all(
-        grads_here, "y", split_axis=1, concat_axis=0, tiled=True
-    ).reshape(members * all_rows, group_j * edge_size)
+    pieces = [lax.dynamic_index_in_dim(grads_here, member, 1, False)]
+    for offset in range(1, members):
+        route = [(i, (i + offset) % members) for i in range(members)]
+        outgoing = lax.dynamic_index_in_dim(grads_here, (member + offset) % members, 1, False)
+        pieces.append(lax.ppermute(outgoing, "y", route))
+    by_offset = jnp.stack(pieces)
+    sender_offset = (member - jnp.arange(members, dtype=jnp.int32)) % members
+    grads_group = jnp.take(by_offset, sender_offset, axis=0).reshape(
+        members * all_rows, group_j * edge_size
+    )
     inputs_group = lax.all_gather(all_inputs, "y", axis=0, tiled=True)
     cols_here = lax.dynamic_slice_in_dim(flat_cols, member * group_pairs, group_pairs)
     order = np.arange(group_pairs).reshape(nx, nz, -1).transpose(1, 0, 2).reshape(-1)
     j_index = jnp.asarray(order // per_block, jnp.int32)
-    partial = group_grads(cols_here[order], j_index, inputs_group, grads_group, group_pairs, 8)
+    partial = group_grads(cols_here[order], j_index, inputs_group, grads_group, group_pairs, 16)
     reduced = ring_reduce_scatter(partial.reshape(nz, -1, edge_size), "z", nz)
     halves = reduced.reshape(nx, -1, edge_size)
     side = lax.axis_index("xlo")

time: 243 us -> 241 us (level)
  waiting for transfers between devices: 142 us -> 137 us
    all_to_all x1 -> x0, waiting for transfers between devices: 10 us -> none  [body(): lax.all_to_all(grads_here, 'y', split_axis=1, concat_axis=0, tiled=True)]
    ppermute x0 -> x3, starting transfers between devices: none -> 5.71 us  [body(): pieces.append(lax.ppermute(outgoing, 'y', route))]
    ppermute x0 -> x3, waiting for transfers between devices: none -> 4.79 us  [body(): pieces.append(lax.ppermute(outgoing, 'y', route))]
    all_to_all x1 -> x0, starting transfers between devices: 4.29 us -> none  [body(): lax.all_to_all(grads_here, 'y', split_axis=1, concat_axis=0, tiled=True)]
  transfers between devices with their start and end apart: 23 -> 25, of which waited for: 11 -> 12; matrix products, arithmetic and copies ran while one was open for 5% -> 7% of each run, Pallas kernels for 4% -> 4%
where the time goes in v12:
time: 241 us; the launch traced here: 240 us
  waiting for transfers between devices  137 us (57%)
  starting transfers between devices  41.4 us (17%)
  Pallas kernels  24.9 us (10%)
  local copies, waits for them, and re-layouts  13.9 us (6%)
  between operations  13.9 us (6%)
  other arithmetic  9.38 us (4%)
    ppermute x6, waiting for transfers between devices, hop(): return lax.ppermute(block, 'segment', [(src, dst)])  90.2 us
    ppermute x7, waiting for transfers between devices, ring_reduce_scatter(): got_e = lax.ppermute(send_e, axis, cw)  35.2 us
    ppermute x7, starting transfers between devices, ring_reduce_scatter(): got_w = lax.ppermute(send_w, axis, ccw)  25.5 us
    pallas_call x1, Pallas kernels, layer_backward(): pl.pallas_call(backward_kernel, grid_spec=grid, out_shape=[jax.ShapeDtype...  9.31 us
    pallas_call x1, Pallas kernels, group_grads(): pl.pallas_call(grad_kernel, grid_spec=grid, out_shape=jax.ShapeDtypeStruc...  8.72 us
    ppermute x6, starting transfers between devices, hop(): return lax.ppermute(block, 'segment', [(src, dst)])  7.4 us
    pallas_call x1, Pallas kernels, layer_forward(): pl.pallas_call(forward_kernel, grid_spec=grid, out_shape=[jax.ShapeDtypeS...  6.89 us
    ppermute x1, waiting for transfers between devices, body(): lax.ppermute(lax.dynamic_index_in_dim(halves, 1 - side, 0, False), 'xlo',...  6.27 us
  transfers between devices with their start and end apart: 25, of which 12 were waited for; matrix products, arithmetic and copies ran while one was open for 7% of the time, Pallas kernels for 4%

profile of v12, /device:TPU:2, one launch (start us, length us, event | category | flops | bytes accessed | tf_op | source)
XLA Modules:
  0.0 240.1 jit_solution(2490174689314591910)
XLA Ops:
  7.4 6.9 %conditional.8 = (bf16[128,4096]{1,0:T(8,128)(2,1)S(1)}, f32[128,4096]{1,0:T(8,128)S(1)}) conditional(s32[]{:T(128)} %convert_element_type.21, () %tuple.79, (s32[256]{0:T(256)S(1)}, bf16[128,4096]{1,0:T(8,128)(2,1)}, bf16[32,8,128,128]{3,2,1,0:T(8,128)(2,1)}) %tuple.125), branch_computations={%region_0.0_spmd, %region_1.0_spmd} | conditional | flops 1073741824 | bytes 12582928 | solution.py:219
  7.4 6.9 %branch_1_fun.8 = (f32[128,4096]{1,0:T(8,128)S(1)}, bf16[128,4096]{1,0:T(8,128)(2,1)S(1)}) custom-call(s32[256]{0:T(256)S(1)} %get-tuple-element.85.cols_ref, bf16[128,4096]{1,0:T(8,128)(2,1)} %get-tuple-element.86.h_ref, bf16[32,8,128,128]{3,2,1,0:T(8,128)(2,1)} %get-tuple-element.87.w_ref), custom_call_target="tpu_custom_call" | custom-call | flops 1073741824 | bytes 12582912 | tf_op jit(solution)/shard_map/cond/branch_1_fun/pallas_call | solution.py:92
  14.3 2.3 collective-permute-start
  16.6 1.4 collective-permute-done
  21.9 1.6 collective-permute-start.2
  24.8 1.2 conditional.12
  29.7 1.3 collective-permute-start.5
  31.1 88.8 %collective-permute-done.5 = bf16[128,4096]{1,0:T(8,128)(2,1)} collective-permute-done((bf16[128,4096]{1,0:T(8,128)(2,1)}, bf16[128,4096]{1,0:T(8,128)(2,1)}, u32[]{:S(2)}, u32[]{:S(2)}) %collective-permute-start.5) | collective-permute-done | bytes 1048608 | tf_op jit(solution)/shard_map/ppermute | solution.py:209
  119.9 9.3 %conditional.15 = (bf16[128,4096]{1,0:T(8,128)(2,1)S(1)}) conditional(s32[]{:T(128)} %convert_element_type.21, bf16[128,4096]{1,0:T(8,128)(2,1)S(1)} %get-tuple-element.141, (s32[256]{0:T(256)S(1)}, bf16[128,4096]{1,0:T(8,128)(2,1)}, f32[128,4096]{1,0:T(8,128)S(1)}, bf16[32,8,128,128]{3,2,1,0:T(8,128)(2,1)}) %tuple.132), branch_computations={%region_14.15_spmd, %region_15.16_spmd} | conditional | flops 1073741824 | bytes 13631496 | solution.py:234
  119.9 9.3 %branch_1_fun.15 = (bf16[128,4096]{1,0:T(8,128)(2,1)S(1)}, bf16[128,4096]{1,0:T(8,128)(2,1)}) custom-call(s32[256]{0:T(256)S(1)} %get-tuple-element.114.cols_ref, bf16[128,4096]{1,0:T(8,128)(2,1)} %get-tuple-element.115.up_ref, f32[128,4096]{1,0:T(8,128)S(1)} %get-tuple-element.116.z_ref, bf16[32,8,128,128]{3,2,1,0:T(8,128)(2,1)} %get-tuple-element.117.w_ref), custom_call_target="tpu_custom_call" | custom-call | flops 1073741824 | bytes 13631488 | tf_op jit(solution)/shard_map/cond/branch_1_fun/pallas_call | solution.py:124
  130.0 2.2 constant_dynamic-slice_fusion.3
  132.3 1.3 collective-permute-start.6
  133.7 3.4 %collective-permute-start.7 = (bf16[128,1024]{1,0:T(8,128)(2,1)S(1)}, bf16[128,1024]{1,0:T(8,128)(2,1)S(1)}, u32[]{:S(2)}, u32[]{:S(2)}) collective-permute-start(bf16[128,1024]{1,0:T(8,128)(2,1)S(1)} %bitcast.79), channel_id=1, source_target_pairs={{0,32},{16,48},{32,0},{48,16},{1,33},{17,49},{33,1},{49,17},{2,34}... | collective-permute-start | bytes 786440 | tf_op jit(solution)/shard_map/ppermute | solution.py:253
  139.9 4.1 %collective-permute-done.7 = bf16[128,1024]{1,0:T(8,128)(2,1)S(1)} collective-permute-done((bf16[128,1024]{1,0:T(8,128)(2,1)S(1)}, bf16[128,1024]{1,0:T(8,128)(2,1)S(1)}, u32[]{:S(2)}, u32[]{:S(2)}) %collective-permute-start.7) | collective-permute-done | bytes 262176 | tf_op jit(solution)/shard_map/ppermute | solution.py:253
  145.0 8.7 %shard_map.74 = f32[64,128,128]{2,1,0:T(8,128)S(1)} custom-call(s32[64]{0:T(128)S(1)} %gather_fusion, s32[64]{0:T(128)S(1)} %copy-done, bf16[512,4096]{1,0:T(8,128)(2,1)} %all-gather.2.cloned.1.call-done.h_ref, bf16[512,1024]{1,0:T(8,128)(2,1)S(1)} %bitcast_select_fusion.g_ref), custom_call_target="tpu_custom_call" | custom-call | flops 1073741824 | bytes 9437184 | tf_op jit(solution)/shard_map/pallas_call | solution.py:165
  154.1 1.3 copy-done.1
  155.5 2.1 collective-permute-start.9
  157.6 4.0 %collective-permute-start.16 = (f32[512,128]{1,0:T(8,128)S(1)}, f32[512,128]{1,0:T(8,128)S(1)}, u32[]{:S(2)}, u32[]{:S(2)}) collective-permute-start(f32[512,128]{1,0:T(8,128)S(1)} %dynamic-slice_bitcast_fusion.1), channel_id=1, source_target_pairs={{0,7},{1,0},{2,1},{3,2},{4,3},{5,4},{6,5},{7,6},{8,15},{9,8},{10,9... | collective-permute-start | bytes 786440 | tf_op jit(solution)/shard_map/ppermute | solution.py:194
  161.6 4.2 %collective-permute-done.9 = f32[512,128]{1,0:T(8,128)S(1)} collective-permute-done((f32[512,128]{1,0:T(8,128)S(1)}, f32[512,128]{1,0:T(8,128)S(1)}, u32[]{:S(2)}, u32[]{:S(2)}) %collective-permute-start.9) | collective-permute-done | bytes 262176 | tf_op jit(solution)/shard_map/ppermute | solution.py:193
  166.9 3.6 %collective-permute-start.17 = (f32[512,128]{1,0:T(8,128)S(1)}, f32[512,128]{1,0:T(8,128)S(1)}, u32[]{:S(2)}, u32[]{:S(2)}) collective-permute-start(f32[512,128]{1,0:T(8,128)S(1)} %bitcast_add_fusion.7), channel_id=1, source_target_pairs={{0,7},{1,0},{2,1},{3,2},{4,3},{5,4},{6,5},{7,6},{8,15},{9,8},{10,9... | collective-permute-start | bytes 786440 | tf_op jit(solution)/shard_map/ppermute | solution.py:194
  170.5 4.4 %collective-permute-done.10 = f32[512,128]{1,0:T(8,128)S(1)} collective-permute-done((f32[512,128]{1,0:T(8,128)S(1)}, f32[512,128]{1,0:T(8,128)S(1)}, u32[]{:S(2)}, u32[]{:S(2)}) %collective-permute-start.10) | collective-permute-done | bytes 262176 | tf_op jit(solution)/shard_map/ppermute | solution.py:193
  176.0 4.8 %collective-permute-start.18 = (f32[512,128]{1,0:T(8,128)S(1)}, f32[512,128]{1,0:T(8,128)S(1)}, u32[]{:S(2)}, u32[]{:S(2)}) collective-permute-start(f32[512,128]{1,0:T(8,128)S(1)} %bitcast_add_fusion.6), channel_id=1, source_target_pairs={{0,7},{1,0},{2,1},{3,2},{4,3},{5,4},{6,5},{7,6},{8,15},{9,8},{10,9... | collective-permute-start | bytes 786440 | tf_op jit(solution)/shard_map/ppermute | solution.py:194
  180.8 6.6 %collective-permute-done.11 = f32[512,128]{1,0:T(8,128)S(1)} collective-permute-done((f32[512,128]{1,0:T(8,128)S(1)}, f32[512,128]{1,0:T(8,128)S(1)}, u32[]{:S(2)}, u32[]{:S(2)}) %collective-permute-start.11) | collective-permute-done | bytes 262176 | tf_op jit(solution)/shard_map/ppermute | solution.py:193
  188.5 3.3 %collective-permute-start.19 = (f32[512,128]{1,0:T(8,128)S(1)}, f32[512,128]{1,0:T(8,128)S(1)}, u32[]{:S(2)}, u32[]{:S(2)}) collective-permute-start(f32[512,128]{1,0:T(8,128)S(1)} %bitcast_add_fusion.5), channel_id=1, source_target_pairs={{0,7},{1,0},{2,1},{3,2},{4,3},{5,4},{6,5},{7,6},{8,15},{9,8},{10,9... | collective-permute-start | bytes 786440 | tf_op jit(solution)/shard_map/ppermute | solution.py:194
  191.8 6.2 %collective-permute-done.12 = f32[512,128]{1,0:T(8,128)S(1)} collective-permute-done((f32[512,128]{1,0:T(8,128)S(1)}, f32[512,128]{1,0:T(8,128)S(1)}, u32[]{:S(2)}, u32[]{:S(2)}) %collective-permute-start.12) | collective-permute-done | bytes 262176 | tf_op jit(solution)/shard_map/ppermute | solution.py:193
  199.1 3.3 %collective-permute-start.20 = (f32[512,128]{1,0:T(8,128)S(1)}, f32[512,128]{1,0:T(8,128)S(1)}, u32[]{:S(2)}, u32[]{:S(2)}) collective-permute-start(f32[512,128]{1,0:T(8,128)S(1)} %bitcast_add_fusion.4), channel_id=1, source_target_pairs={{0,7},{1,0},{2,1},{3,2},{4,3},{5,4},{6,5},{7,6},{8,15},{9,8},{10,9... | collective-permute-start | bytes 786440 | tf_op jit(solution)/shard_map/ppermute | solution.py:194
  202.4 5.4 %collective-permute-done.13 = f32[512,128]{1,0:T(8,128)S(1)} collective-permute-done((f32[512,128]{1,0:T(8,128)S(1)}, f32[512,128]{1,0:T(8,128)S(1)}, u32[]{:S(2)}, u32[]{:S(2)}) %collective-permute-start.13) | collective-permute-done | bytes 262176 | tf_op jit(solution)/shard_map/ppermute | solution.py:193
  208.9 3.3 %collective-permute-start.21 = (f32[512,128]{1,0:T(8,128)S(1)}, f32[512,128]{1,0:T(8,128)S(1)}, u32[]{:S(2)}, u32[]{:S(2)}) collective-permute-start(f32[512,128]{1,0:T(8,128)S(1)} %bitcast_add_fusion.3), channel_id=1, source_target_pairs={{0,7},{1,0},{2,1},{3,2},{4,3},{5,4},{6,5},{7,6},{8,15},{9,8},{10,9... | collective-permute-start | bytes 786440 | tf_op jit(solution)/shard_map/ppermute | solution.py:194
  212.1 4.2 %collective-permute-done.14 = f32[512,128]{1,0:T(8,128)S(1)} collective-permute-done((f32[512,128]{1,0:T(8,128)S(1)}, f32[512,128]{1,0:T(8,128)S(1)}, u32[]{:S(2)}, u32[]{:S(2)}) %collective-permute-start.14) | collective-permute-done | bytes 262176 | tf_op jit(solution)/shard_map/ppermute | solution.py:193
  217.5 3.3 %collective-permute-start.22 = (f32[512,128]{1,0:T(8,128)S(1)}, f32[512,128]{1,0:T(8,128)S(1)}, u32[]{:S(2)}, u32[]{:S(2)}) collective-permute-start(f32[512,128]{1,0:T(8,128)S(1)} %bitcast_add_fusion.2), channel_id=1, source_target_pairs={{0,7},{1,0},{2,1},{3,2},{4,3},{5,4},{6,5},{7,6},{8,15},{9,8},{10,9... | collective-permute-start | bytes 786440 | tf_op jit(solution)/shard_map/ppermute | solution.py:194
  220.8 4.2 %collective-permute-done.15 = f32[512,128]{1,0:T(8,128)S(1)} collective-permute-done((f32[512,128]{1,0:T(8,128)S(1)}, f32[512,128]{1,0:T(8,128)S(1)}, u32[]{:S(2)}, u32[]{:S(2)}) %collective-permute-start.15) | collective-permute-done | bytes 262176 | tf_op jit(solution)/shard_map/ppermute | solution.py:193
  226.3 6.3 %collective-permute-done.23 = f32[512,128]{1,0:T(8,128)S(1)} collective-permute-done((f32[512,128]{1,0:T(8,128)S(1)}, f32[512,128]{1,0:T(8,128)S(1)}, u32[]{:S(2)}, u32[]{:S(2)}) %collective-permute-start.23) | collective-permute-done | bytes 262176 | tf_op jit(solution)/shard_map/ppermute | solution.py:267
  (85 shorter events, 28.8 us)
Async XLA Ops:
  6.5 138.5 %all-gather.2.cloned.1.call-start = ((), (), s32[]{:S(2)}) async-start(), calls=%async_computation | async-start | bytes 5242880 | tf_op jit(solution)/shard_map/all_gather | solution.py:259
  14.3 3.7 %collective-permute-start = (bf16[128,4096]{1,0:T(8,128)(2,1)S(1)}, bf16[128,4096]{1,0:T(8,128)(2,1)}, u32[]{:S(2)}, u32[]{:S(2)}) collective-permute-start(bf16[128,4096]{1,0:T(8,128)(2,1)S(1)} %get-tuple-element.132), channel_id=1, source_target_pairs={{0,64},{1,65},{2,66},{3,67},{4,68},{5,69},{6,70},{7,71},{8,72},{9,... | collective-permute-start | bytes 3145736 | tf_op jit(solution)/shard_map/ppermute | solution.py:209
  19.1 0.7 collective-permute-start.1
  19.8 1.0 copy-start.3
  20.8 2.7 %copy-start.2 = (bf16[128,4096]{1,0:T(8,128)(2,1)S(1)}, bf16[128,4096]{1,0:T(8,128)(2,1)}, u32[]{:S(2)}) copy-start(bf16[128,4096]{1,0:T(8,128)(2,1)} %param.23) | copy-start | bytes 3145732
  21.9 1.6 collective-permute-start.2
  26.0 0.7 collective-permute-start.3
  27.9 0.7 collective-permute-start.4
  28.6 2.5 %copy-start.6 = (s32[64]{0:T(128)S(1)}, s32[64]{0:T(128)}, u32[]{:S(2)}) copy-start(s32[64]{0:T(128)} %constant.247) | copy-start | bytes 772
  29.7 90.2 %collective-permute-start.5 = (bf16[128,4096]{1,0:T(8,128)(2,1)}, bf16[128,4096]{1,0:T(8,128)(2,1)}, u32[]{:S(2)}, u32[]{:S(2)}) collective-permute-start(bf16[128,4096]{1,0:T(8,128)(2,1)} %get-tuple-element.142), channel_id=1, source_target_pairs={{64,0},{65,1},{66,2},{67,3},{68,4},{69,5},{70,6},{71,7},{72,8},{73... | collective-permute-start | bytes 3145736 | tf_op jit(solution)/shard_map/ppermute | solution.py:209
  132.3 7.7 %collective-permute-start.6 = (bf16[128,1024]{1,0:T(8,128)(2,1)S(1)}, bf16[128,1024]{1,0:T(8,128)(2,1)S(1)}, u32[]{:S(2)}, u32[]{:S(2)}) collective-permute-start(bf16[128,1024]{1,0:T(8,128)(2,1)S(1)} %bitcast.78), channel_id=1, source_target_pairs={{0,16},{16,32},{32,48},{48,0},{1,17},{17,33},{33,49},{49,1},{2,18}... | collective-permute-start | bytes 786440 | tf_op jit(solution)/shard_map/ppermute | solution.py:253
  133.7 10.3 %collective-permute-start.7 = (bf16[128,1024]{1,0:T(8,128)(2,1)S(1)}, bf16[128,1024]{1,0:T(8,128)(2,1)S(1)}, u32[]{:S(2)}, u32[]{:S(2)}) collective-permute-start(bf16[128,1024]{1,0:T(8,128)(2,1)S(1)} %bitcast.79), channel_id=1, source_target_pairs={{0,32},{16,48},{32,0},{48,16},{1,33},{17,49},{33,1},{49,17},{2,34}... | collective-permute-start | bytes 786440 | tf_op jit(solution)/shard_map/ppermute | solution.py:253
  137.1 6.9 %collective-permute-start.8 = (bf16[128,1024]{1,0:T(8,128)(2,1)S(1)}, bf16[128,1024]{1,0:T(8,128)(2,1)S(1)}, u32[]{:S(2)}, u32[]{:S(2)}) collective-permute-start(bf16[128,1024]{1,0:T(8,128)(2,1)S(1)} %bitcast.80), channel_id=1, source_target_pairs={{0,48},{16,0},{32,16},{48,32},{1,49},{17,1},{33,17},{49,33},{2,50}... | collective-permute-start | bytes 786440 | tf_op jit(solution)/shard_map/ppermute | solution.py:253
  144.1 0.9 copy-start
  154.1 1.4 copy-start.1
  155.5 10.3 %collective-permute-start.9 = (f32[512,128]{1,0:T(8,128)S(1)}, f32[512,128]{1,0:T(8,128)S(1)}, u32[]{:S(2)}, u32[]{:S(2)}) collective-permute-start(f32[512,128]{1,0:T(8,128)S(1)} %dynamic-slice_bitcast_fusion.2), channel_id=1, source_target_pairs={{0,1},{1,2},{2,3},{3,4},{4,5},{5,6},{6,7},{7,0},{8,9},{9,10},{10,1... | collective-permute-start | bytes 786440 | tf_op jit(solution)/shard_map/ppermute | solution.py:193
  157.6 9.3 %collective-permute-start.16 = (f32[512,128]{1,0:T(8,128)S(1)}, f32[512,128]{1,0:T(8,128)S(1)}, u32[]{:S(2)}, u32[]{:S(2)}) collective-permute-start(f32[512,128]{1,0:T(8,128)S(1)} %dynamic-slice_bitcast_fusion.1), channel_id=1, source_target_pairs={{0,7},{1,0},{2,1},{3,2},{4,3},{5,4},{6,5},{7,6},{8,15},{9,8},{10,9... | collective-permute-start | bytes 786440 | tf_op jit(solution)/shard_map/ppermute | solution.py:194
  166.8 8.1 %collective-permute-start.10 = (f32[512,128]{1,0:T(8,128)S(1)}, f32[512,128]{1,0:T(8,128)S(1)}, u32[]{:S(2)}, u32[]{:S(2)}) collective-permute-start(f32[512,128]{1,0:T(8,128)S(1)} %bitcast_add_fusion.14), channel_id=1, source_target_pairs={{0,1},{1,2},{2,3},{3,4},{4,5},{5,6},{6,7},{7,0},{8,9},{9,10},{10,1... | collective-permute-start | bytes 786440 | tf_op jit(solution)/shard_map/ppermute | solution.py:193
  166.9 9.1 %collective-permute-start.17 = (f32[512,128]{1,0:T(8,128)S(1)}, f32[512,128]{1,0:T(8,128)S(1)}, u32[]{:S(2)}, u32[]{:S(2)}) collective-permute-start(f32[512,128]{1,0:T(8,128)S(1)} %bitcast_add_fusion.7), channel_id=1, source_target_pairs={{0,7},{1,0},{2,1},{3,2},{4,3},{5,4},{6,5},{7,6},{8,15},{9,8},{10,9... | collective-permute-start | bytes 786440 | tf_op jit(solution)/shard_map/ppermute | solution.py:194
  175.9 11.5 %collective-permute-start.11 = (f32[512,128]{1,0:T(8,128)S(1)}, f32[512,128]{1,0:T(8,128)S(1)}, u32[]{:S(2)}, u32[]{:S(2)}) collective-permute-start(f32[512,128]{1,0:T(8,128)S(1)} %bitcast_add_fusion.13), channel_id=1, source_target_pairs={{0,1},{1,2},{2,3},{3,4},{4,5},{5,6},{6,7},{7,0},{8,9},{9,10},{10,1... | collective-permute-start | bytes 786440 | tf_op jit(solution)/shard_map/ppermute | solution.py:193
  176.0 12.4 %collective-permute-start.18 = (f32[512,128]{1,0:T(8,128)S(1)}, f32[512,128]{1,0:T(8,128)S(1)}, u32[]{:S(2)}, u32[]{:S(2)}) collective-permute-start(f32[512,128]{1,0:T(8,128)S(1)} %bitcast_add_fusion.6), channel_id=1, source_target_pairs={{0,7},{1,0},{2,1},{3,2},{4,3},{5,4},{6,5},{7,6},{8,15},{9,8},{10,9... | collective-permute-start | bytes 786440 | tf_op jit(solution)/shard_map/ppermute | solution.py:194
  188.4 9.6 %collective-permute-start.12 = (f32[512,128]{1,0:T(8,128)S(1)}, f32[512,128]{1,0:T(8,128)S(1)}, u32[]{:S(2)}, u32[]{:S(2)}) collective-permute-start(f32[512,128]{1,0:T(8,128)S(1)} %bitcast_add_fusion.12), channel_id=1, source_target_pairs={{0,1},{1,2},{2,3},{3,4},{4,5},{5,6},{6,7},{7,0},{8,9},{9,10},{10,1... | collective-permute-start | bytes 786440 | tf_op jit(solution)/shard_map/ppermute | solution.py:193
  188.5 10.5 %collective-permute-start.19 = (f32[512,128]{1,0:T(8,128)S(1)}, f32[512,128]{1,0:T(8,128)S(1)}, u32[]{:S(2)}, u32[]{:S(2)}) collective-permute-start(f32[512,128]{1,0:T(8,128)S(1)} %bitcast_add_fusion.5), channel_id=1, source_target_pairs={{0,7},{1,0},{2,1},{3,2},{4,3},{5,4},{6,5},{7,6},{8,15},{9,8},{10,9... | collective-permute-start | bytes 786440 | tf_op jit(solution)/shard_map/ppermute | solution.py:194
  199.0 8.8 %collective-permute-start.13 = (f32[512,128]{1,0:T(8,128)S(1)}, f32[512,128]{1,0:T(8,128)S(1)}, u32[]{:S(2)}, u32[]{:S(2)}) collective-permute-start(f32[512,128]{1,0:T(8,128)S(1)} %bitcast_add_fusion.11), channel_id=1, source_target_pairs={{0,1},{1,2},{2,3},{3,4},{4,5},{5,6},{6,7},{7,0},{8,9},{9,10},{10,1... | collective-permute-start | bytes 786440 | tf_op jit(solution)/shard_map/ppermute | solution.py:193
  199.1 9.7 %collective-permute-start.20 = (f32[512,128]{1,0:T(8,128)S(1)}, f32[512,128]{1,0:T(8,128)S(1)}, u32[]{:S(2)}, u32[]{:S(2)}) collective-permute-start(f32[512,128]{1,0:T(8,128)S(1)} %bitcast_add_fusion.4), channel_id=1, source_target_pairs={{0,7},{1,0},{2,1},{3,2},{4,3},{5,4},{6,5},{7,6},{8,15},{9,8},{10,9... | collective-permute-start | bytes 786440 | tf_op jit(solution)/shard_map/ppermute | solution.py:194
  208.7 7.7 %collective-permute-start.14 = (f32[512,128]{1,0:T(8,128)S(1)}, f32[512,128]{1,0:T(8,128)S(1)}, u32[]{:S(2)}, u32[]{:S(2)}) collective-permute-start(f32[512,128]{1,0:T(8,128)S(1)} %bitcast_add_fusion.10), channel_id=1, source_target_pairs={{0,1},{1,2},{2,3},{3,4},{4,5},{5,6},{6,7},{7,0},{8,9},{9,10},{10,1... | collective-permute-start | bytes 786440 | tf_op jit(solution)/shard_map/ppermute | solution.py:193
  208.9 8.6 %collective-permute-start.21 = (f32[512,128]{1,0:T(8,128)S(1)}, f32[512,128]{1,0:T(8,128)S(1)}, u32[]{:S(2)}, u32[]{:S(2)}) collective-permute-start(f32[512,128]{1,0:T(8,128)S(1)} %bitcast_add_fusion.3), channel_id=1, source_target_pairs={{0,7},{1,0},{2,1},{3,2},{4,3},{5,4},{6,5},{7,6},{8,15},{9,8},{10,9... | collective-permute-start | bytes 786440 | tf_op jit(solution)/shard_map/ppermute | solution.py:194
  217.4 7.7 %collective-permute-start.15 = (f32[512,128]{1,0:T(8,128)S(1)}, f32[512,128]{1,0:T(8,128)S(1)}, u32[]{:S(2)}, u32[]{:S(2)}) collective-permute-start(f32[512,128]{1,0:T(8,128)S(1)} %bitcast_add_fusion.9), channel_id=1, source_target_pairs={{0,1},{1,2},{2,3},{3,4},{4,5},{5,6},{6,7},{7,0},{8,9},{9,10},{10,1... | collective-permute-start | bytes 786440 | tf_op jit(solution)/shard_map/ppermute | solution.py:193
  217.5 8.5 %collective-permute-start.22 = (f32[512,128]{1,0:T(8,128)S(1)}, f32[512,128]{1,0:T(8,128)S(1)}, u32[]{:S(2)}, u32[]{:S(2)}) collective-permute-start(f32[512,128]{1,0:T(8,128)S(1)} %bitcast_add_fusion.2), channel_id=1, source_target_pairs={{0,7},{1,0},{2,1},{3,2},{4,3},{5,4},{6,5},{7,6},{8,15},{9,8},{10,9... | collective-permute-start | bytes 786440 | tf_op jit(solution)/shard_map/ppermute | solution.py:194
  226.1 6.5 %collective-permute-start.23 = (f32[512,128]{1,0:T(8,128)S(1)}, f32[512,128]{1,0:T(8,128)S(1)}, u32[]{:S(2)}, u32[]{:S(2)}) collective-permute-start(f32[512,128]{1,0:T(8,128)S(1)} %dynamic-slice_bitcast_fusion), channel_id=1, source_target_pairs={{0,8},{8,0},{1,9},{9,1},{2,10},{10,2},{3,11},{11,3},{4,12},{12,4},... | collective-permute-start | bytes 786440 | tf_op jit(solution)/shard_map/ppermute | solution.py:267
Sparse Core Ops, SparseCore 0:
  24.9 86.0 all-gather.1

commit v13 on v12

--- a/solution.py
+++ b/solution.py
@@ -205,8 +205,13 @@
     all_rows, layer_width = inputs.shape
     flat_cols = block_cols[0].reshape(-1)
 
+    sides = DP_SIZES[1]
+    middle = segments // 2
+
     def hop(block, src, dst):
-        return lax.ppermute(block, "segment", [(src, dst)])
+        flip = (src < middle) != (dst < middle)
+        route = [(src * sides + x, dst * sides + (sides - 1 - x if flip else x)) for x in range(sides)]
+        return lax.ppermute(block, ("segment", "xlo"), route)
 
     zeros_x = jnp.zeros((all_rows, layer_width), jnp.bfloat16)
     zeros_z = jnp.zeros((all_rows, layer_width), jnp.float32)
@@ -226,7 +231,10 @@
         if step_now + 1 < segments:
             current = hop(result, step_now, step_now + 1)
     stash_g = zeros_x
-    upstream = cotangent
+    last = segments - 1
+    upstream = lax.ppermute(
+        cotangent, ("segment", "xlo"), [(last * sides + x, last * sides + sides - 1 - x) for x in range(sides)]
+    )
     for step_now in range(segments):
         owner = segments - 1 - step_now
         active = segment_index == owner

time: 241 us -> 250 us (1.037)
  waiting for transfers between devices: 137 us -> 142 us
    ppermute x6 -> x7, waiting for transfers between devices: 90.2 us -> 97.3 us  [the longest x6 97.3 us: hop(): return lax.ppermute(block, ('segment', 'xlo'), route)]
    ppermute x6 -> x7, starting transfers between devices: 7.4 us -> 8.15 us  [the longest x6 7.42 us: hop(): return lax.ppermute(block, ('segment', 'xlo'), route)]
  transfers between devices with their start and end apart: 25 -> 26, of which waited for: 12 -> 13; matrix products, arithmetic and copies ran while one was open for 7% -> 6% of each run, Pallas kernels for 4% -> 4%
where the time goes in v13:
time: 250 us; the launch traced here: 247 us
  waiting for transfers between devices  142 us (57%)
  starting transfers between devices  42.5 us (17%)
  Pallas kernels  24.9 us (10%)
  local copies, waits for them, and re-layouts  14 us (6%)
  between operations  13.9 us (6%)
  other arithmetic  9.39 us (4%)
    ppermute x6, waiting for transfers between devices, hop(): return lax.ppermute(block, ('segment', 'xlo'), route)  97.3 us
    ppermute x7, waiting for transfers between devices, ring_reduce_scatter(): got_e = lax.ppermute(send_e, axis, cw)  35.1 us
    ppermute x7, starting transfers between devices, ring_reduce_scatter(): got_w = lax.ppermute(send_w, axis, ccw)  26 us
    pallas_call x1, Pallas kernels, layer_backward(): pl.pallas_call(backward_kernel, grid_spec=grid, out_shape=[jax.ShapeDtype...  9.29 us
    pallas_call x1, Pallas kernels, group_grads(): pl.pallas_call(grad_kernel, grid_spec=grid, out_shape=jax.ShapeDtypeStruc...  8.72 us
    ppermute x6, starting transfers between devices, hop(): return lax.ppermute(block, ('segment', 'xlo'), route)  7.42 us
    pallas_call x1, Pallas kernels, layer_forward(): pl.pallas_call(forward_kernel, grid_spec=grid, out_shape=[jax.ShapeDtypeS...  6.91 us
    add x6, other arithmetic, ring_reduce_scatter(): send_e = got_e + send_e  5.87 us
  transfers between devices with their start and end apart: 26, of which 13 were waited for; matrix products, arithmetic and copies ran while one was open for 6% of the time, Pallas kernels for 4%

profile of v13, /device:TPU:2, one launch (start us, length us, event | category | flops | bytes accessed | tf_op | source)
XLA Modules:
  0.0 247.1 jit_solution(5185040051298671442)
XLA Ops:
  7.4 6.9 %conditional.8 = (bf16[128,4096]{1,0:T(8,128)(2,1)S(1)}, f32[128,4096]{1,0:T(8,128)S(1)}) conditional(s32[]{:T(128)} %convert_element_type.21, () %tuple.79, (s32[256]{0:T(256)S(1)}, bf16[128,4096]{1,0:T(8,128)(2,1)}, bf16[32,8,128,128]{3,2,1,0:T(8,128)(2,1)}) %tuple.125), branch_computations={%region_0.0_spmd, %region_1.0_spmd} | conditional | flops 1073741824 | bytes 12582928 | solution.py:224
  7.4 6.9 %branch_1_fun.8 = (f32[128,4096]{1,0:T(8,128)S(1)}, bf16[128,4096]{1,0:T(8,128)(2,1)S(1)}) custom-call(s32[256]{0:T(256)S(1)} %get-tuple-element.85.cols_ref, bf16[128,4096]{1,0:T(8,128)(2,1)} %get-tuple-element.86.h_ref, bf16[32,8,128,128]{3,2,1,0:T(8,128)(2,1)} %get-tuple-element.87.w_ref), custom_call_target="tpu_custom_call" | custom-call | flops 1073741824 | bytes 12582912 | tf_op jit(solution)/shard_map/cond/branch_1_fun/pallas_call | solution.py:92
  14.3 2.3 collective-permute-start
  16.7 1.4 collective-permute-done
  21.9 1.7 collective-permute-start.2
  30.5 1.3 collective-permute-start.6
  31.9 95.9 %collective-permute-done.6 = bf16[128,4096]{1,0:T(8,128)(2,1)} collective-permute-done((bf16[128,4096]{1,0:T(8,128)(2,1)}, bf16[128,4096]{1,0:T(8,128)(2,1)}, u32[]{:S(2)}, u32[]{:S(2)}) %collective-permute-start.6) | collective-permute-done | bytes 1048608 | tf_op jit(solution)/shard_map/ppermute | solution.py:214
  127.8 9.3 %conditional.15 = (bf16[128,4096]{1,0:T(8,128)(2,1)S(1)}) conditional(s32[]{:T(128)} %convert_element_type.21, bf16[128,4096]{1,0:T(8,128)(2,1)S(1)} %get-tuple-element.141, (s32[256]{0:T(256)S(1)}, bf16[128,4096]{1,0:T(8,128)(2,1)}, f32[128,4096]{1,0:T(8,128)S(1)}, bf16[32,8,128,128]{3,2,1,0:T(8,128)(2,1)}) %tuple.132), branch_computations={%region_14.15_spmd, %region_15.16_spmd} | conditional | flops 1073741824 | bytes 13631496 | solution.py:242
  127.8 9.3 %branch_1_fun.15 = (bf16[128,4096]{1,0:T(8,128)(2,1)S(1)}, bf16[128,4096]{1,0:T(8,128)(2,1)}) custom-call(s32[256]{0:T(256)S(1)} %get-tuple-element.114.cols_ref, bf16[128,4096]{1,0:T(8,128)(2,1)} %get-tuple-element.115.up_ref, f32[128,4096]{1,0:T(8,128)S(1)} %get-tuple-element.116.z_ref, bf16[32,8,128,128]{3,2,1,0:T(8,128)(2,1)} %get-tuple-element.117.w_ref), custom_call_target="tpu_custom_call" | custom-call | flops 1073741824 | bytes 13631488 | tf_op jit(solution)/shard_map/cond/branch_1_fun/pallas_call | solution.py:124
  137.8 2.2 constant_dynamic-slice_fusion.3
  140.8 2.9 %collective-permute-start.8 = (bf16[128,1024]{1,0:T(8,128)(2,1)S(1)}, bf16[128,1024]{1,0:T(8,128)(2,1)S(1)}, u32[]{:S(2)}, u32[]{:S(2)}) collective-permute-start(bf16[128,1024]{1,0:T(8,128)(2,1)S(1)} %bitcast.79), channel_id=1, source_target_pairs={{0,32},{16,48},{32,0},{48,16},{1,33},{17,49},{33,1},{49,17},{2,34}... | collective-permute-start | bytes 786440 | tf_op jit(solution)/shard_map/ppermute | solution.py:261
  143.8 1.5 collective-permute-start.9
  146.3 1.4 collective-permute-done.7
  147.8 2.9 %collective-permute-done.8 = bf16[128,1024]{1,0:T(8,128)(2,1)S(1)} collective-permute-done((bf16[128,1024]{1,0:T(8,128)(2,1)S(1)}, bf16[128,1024]{1,0:T(8,128)(2,1)S(1)}, u32[]{:S(2)}, u32[]{:S(2)}) %collective-permute-start.8) | collective-permute-done | bytes 262176 | tf_op jit(solution)/shard_map/ppermute | solution.py:261
  152.6 8.7 %shard_map.73 = f32[64,128,128]{2,1,0:T(8,128)S(1)} custom-call(s32[64]{0:T(128)S(1)} %gather_fusion, s32[64]{0:T(128)S(1)} %copy-done, bf16[512,4096]{1,0:T(8,128)(2,1)} %all-gather.2.cloned.1.call-done.h_ref, bf16[512,1024]{1,0:T(8,128)(2,1)S(1)} %bitcast_select_fusion.g_ref), custom_call_target="tpu_custom_call" | custom-call | flops 1073741824 | bytes 9437184 | tf_op jit(solution)/shard_map/pallas_call | solution.py:165
  161.7 1.4 copy-done.1
  164.1 4.5 %collective-permute-start.17 = (f32[512,128]{1,0:T(8,128)S(1)}, f32[512,128]{1,0:T(8,128)S(1)}, u32[]{:S(2)}, u32[]{:S(2)}) collective-permute-start(f32[512,128]{1,0:T(8,128)S(1)} %dynamic-slice_bitcast_fusion.1), channel_id=1, source_target_pairs={{0,7},{1,0},{2,1},{3,2},{4,3},{5,4},{6,5},{7,6},{8,15},{9,8},{10,9... | collective-permute-start | bytes 786440 | tf_op jit(solution)/shard_map/ppermute | solution.py:194
  168.7 4.2 %collective-permute-done.10 = f32[512,128]{1,0:T(8,128)S(1)} collective-permute-done((f32[512,128]{1,0:T(8,128)S(1)}, f32[512,128]{1,0:T(8,128)S(1)}, u32[]{:S(2)}, u32[]{:S(2)}) %collective-permute-start.10) | collective-permute-done | bytes 262176 | tf_op jit(solution)/shard_map/ppermute | solution.py:193
  174.0 3.6 %collective-permute-start.18 = (f32[512,128]{1,0:T(8,128)S(1)}, f32[512,128]{1,0:T(8,128)S(1)}, u32[]{:S(2)}, u32[]{:S(2)}) collective-permute-start(f32[512,128]{1,0:T(8,128)S(1)} %bitcast_add_fusion.7), channel_id=1, source_target_pairs={{0,7},{1,0},{2,1},{3,2},{4,3},{5,4},{6,5},{7,6},{8,15},{9,8},{10,9... | collective-permute-start | bytes 786440 | tf_op jit(solution)/shard_map/ppermute | solution.py:194
  177.6 4.4 %collective-permute-done.11 = f32[512,128]{1,0:T(8,128)S(1)} collective-permute-done((f32[512,128]{1,0:T(8,128)S(1)}, f32[512,128]{1,0:T(8,128)S(1)}, u32[]{:S(2)}, u32[]{:S(2)}) %collective-permute-start.11) | collective-permute-done | bytes 262176 | tf_op jit(solution)/shard_map/ppermute | solution.py:193
  183.1 4.8 %collective-permute-start.19 = (f32[512,128]{1,0:T(8,128)S(1)}, f32[512,128]{1,0:T(8,128)S(1)}, u32[]{:S(2)}, u32[]{:S(2)}) collective-permute-start(f32[512,128]{1,0:T(8,128)S(1)} %bitcast_add_fusion.6), channel_id=1, source_target_pairs={{0,7},{1,0},{2,1},{3,2},{4,3},{5,4},{6,5},{7,6},{8,15},{9,8},{10,9... | collective-permute-start | bytes 786440 | tf_op jit(solution)/shard_map/ppermute | solution.py:194
  187.8 6.5 %collective-permute-done.12 = f32[512,128]{1,0:T(8,128)S(1)} collective-permute-done((f32[512,128]{1,0:T(8,128)S(1)}, f32[512,128]{1,0:T(8,128)S(1)}, u32[]{:S(2)}, u32[]{:S(2)}) %collective-permute-start.12) | collective-permute-done | bytes 262176 | tf_op jit(solution)/shard_map/ppermute | solution.py:193
  195.5 3.3 %collective-permute-start.20 = (f32[512,128]{1,0:T(8,128)S(1)}, f32[512,128]{1,0:T(8,128)S(1)}, u32[]{:S(2)}, u32[]{:S(2)}) collective-permute-start(f32[512,128]{1,0:T(8,128)S(1)} %bitcast_add_fusion.5), channel_id=1, source_target_pairs={{0,7},{1,0},{2,1},{3,2},{4,3},{5,4},{6,5},{7,6},{8,15},{9,8},{10,9... | collective-permute-start | bytes 786440 | tf_op jit(solution)/shard_map/ppermute | solution.py:194
  198.8 6.2 %collective-permute-done.13 = f32[512,128]{1,0:T(8,128)S(1)} collective-permute-done((f32[512,128]{1,0:T(8,128)S(1)}, f32[512,128]{1,0:T(8,128)S(1)}, u32[]{:S(2)}, u32[]{:S(2)}) %collective-permute-start.13) | collective-permute-done | bytes 262176 | tf_op jit(solution)/shard_map/ppermute | solution.py:193
  206.1 3.3 %collective-permute-start.21 = (f32[512,128]{1,0:T(8,128)S(1)}, f32[512,128]{1,0:T(8,128)S(1)}, u32[]{:S(2)}, u32[]{:S(2)}) collective-permute-start(f32[512,128]{1,0:T(8,128)S(1)} %bitcast_add_fusion.4), channel_id=1, source_target_pairs={{0,7},{1,0},{2,1},{3,2},{4,3},{5,4},{6,5},{7,6},{8,15},{9,8},{10,9... | collective-permute-start | bytes 786440 | tf_op jit(solution)/shard_map/ppermute | solution.py:194
  209.4 5.4 %collective-permute-done.14 = f32[512,128]{1,0:T(8,128)S(1)} collective-permute-done((f32[512,128]{1,0:T(8,128)S(1)}, f32[512,128]{1,0:T(8,128)S(1)}, u32[]{:S(2)}, u32[]{:S(2)}) %collective-permute-start.14) | collective-permute-done | bytes 262176 | tf_op jit(solution)/shard_map/ppermute | solution.py:193
  215.9 3.3 %collective-permute-start.22 = (f32[512,128]{1,0:T(8,128)S(1)}, f32[512,128]{1,0:T(8,128)S(1)}, u32[]{:S(2)}, u32[]{:S(2)}) collective-permute-start(f32[512,128]{1,0:T(8,128)S(1)} %bitcast_add_fusion.3), channel_id=1, source_target_pairs={{0,7},{1,0},{2,1},{3,2},{4,3},{5,4},{6,5},{7,6},{8,15},{9,8},{10,9... | collective-permute-start | bytes 786440 | tf_op jit(solution)/shard_map/ppermute | solution.py:194
  219.2 4.2 %collective-permute-done.15 = f32[512,128]{1,0:T(8,128)S(1)} collective-permute-done((f32[512,128]{1,0:T(8,128)S(1)}, f32[512,128]{1,0:T(8,128)S(1)}, u32[]{:S(2)}, u32[]{:S(2)}) %collective-permute-start.15) | collective-permute-done | bytes 262176 | tf_op jit(solution)/shard_map/ppermute | solution.py:193
  224.5 3.3 %collective-permute-start.23 = (f32[512,128]{1,0:T(8,128)S(1)}, f32[512,128]{1,0:T(8,128)S(1)}, u32[]{:S(2)}, u32[]{:S(2)}) collective-permute-start(f32[512,128]{1,0:T(8,128)S(1)} %bitcast_add_fusion.2), channel_id=1, source_target_pairs={{0,7},{1,0},{2,1},{3,2},{4,3},{5,4},{6,5},{7,6},{8,15},{9,8},{10,9... | collective-permute-start | bytes 786440 | tf_op jit(solution)/shard_map/ppermute | solution.py:194
  227.8 4.2 %collective-permute-done.16 = f32[512,128]{1,0:T(8,128)S(1)} collective-permute-done((f32[512,128]{1,0:T(8,128)S(1)}, f32[512,128]{1,0:T(8,128)S(1)}, u32[]{:S(2)}, u32[]{:S(2)}) %collective-permute-start.16) | collective-permute-done | bytes 262176 | tf_op jit(solution)/shard_map/ppermute | solution.py:193
  233.1 1.8 collective-permute-start.24
  234.9 4.7 %collective-permute-done.24 = f32[512,128]{1,0:T(8,128)S(1)} collective-permute-done((f32[512,128]{1,0:T(8,128)S(1)}, f32[512,128]{1,0:T(8,128)S(1)}, u32[]{:S(2)}, u32[]{:S(2)}) %collective-permute-start.24) | collective-permute-done | bytes 262176 | tf_op jit(solution)/shard_map/ppermute | solution.py:275
  (87 shorter events, 31.4 us)
Async XLA Ops:
  6.5 146.1 %all-gather.2.cloned.1.call-start = ((), (), s32[]{:S(2)}) async-start(), calls=%async_computation | async-start | bytes 5242880 | tf_op jit(solution)/shard_map/all_gather | solution.py:267
  14.3 3.7 %collective-permute-start = (bf16[128,4096]{1,0:T(8,128)(2,1)S(1)}, bf16[128,4096]{1,0:T(8,128)(2,1)}, u32[]{:S(2)}, u32[]{:S(2)}) collective-permute-start(bf16[128,4096]{1,0:T(8,128)(2,1)S(1)} %get-tuple-element.132), channel_id=1, source_target_pairs={{0,64},{8,72},{1,65},{9,73},{2,66},{10,74},{3,67},{11,75},{4,68},{... | collective-permute-start | bytes 3145736 | tf_op jit(solution)/shard_map/ppermute | solution.py:214
  19.1 0.7 collective-permute-start.1
  19.9 1.0 copy-start.3
  20.9 2.7 %copy-start.2 = (bf16[128,4096]{1,0:T(8,128)(2,1)S(1)}, bf16[128,4096]{1,0:T(8,128)(2,1)}, u32[]{:S(2)}) copy-start(bf16[128,4096]{1,0:T(8,128)(2,1)} %param.23) | copy-start | bytes 3145732
  21.9 1.7 collective-permute-start.2
  24.8 0.8 collective-permute-start.3
  26.8 0.7 collective-permute-start.4
  28.6 0.7 collective-permute-start.5
  29.4 2.5 copy-start.7
  30.5 97.3 %collective-permute-start.6 = (bf16[128,4096]{1,0:T(8,128)(2,1)}, bf16[128,4096]{1,0:T(8,128)(2,1)}, u32[]{:S(2)}, u32[]{:S(2)}) collective-permute-start(bf16[128,4096]{1,0:T(8,128)(2,1)} %get-tuple-element.142), channel_id=1, source_target_pairs={{64,0},{72,8},{65,1},{73,9},{66,2},{74,10},{67,3},{75,11},{68,4},{... | collective-permute-start | bytes 3145736 | tf_op jit(solution)/shard_map/ppermute | solution.py:214
  140.1 7.7 %collective-permute-start.7 = (bf16[128,1024]{1,0:T(8,128)(2,1)S(1)}, bf16[128,1024]{1,0:T(8,128)(2,1)S(1)}, u32[]{:S(2)}, u32[]{:S(2)}) collective-permute-start(bf16[128,1024]{1,0:T(8,128)(2,1)S(1)} %bitcast.78), channel_id=1, source_target_pairs={{0,16},{16,32},{32,48},{48,0},{1,17},{17,33},{33,49},{49,1},{2,18}... | collective-permute-start | bytes 786440 | tf_op jit(solution)/shard_map/ppermute | solution.py:261
  140.8 9.9 %collective-permute-start.8 = (bf16[128,1024]{1,0:T(8,128)(2,1)S(1)}, bf16[128,1024]{1,0:T(8,128)(2,1)S(1)}, u32[]{:S(2)}, u32[]{:S(2)}) collective-permute-start(bf16[128,1024]{1,0:T(8,128)(2,1)S(1)} %bitcast.79), channel_id=1, source_target_pairs={{0,32},{16,48},{32,0},{48,16},{1,33},{17,49},{33,1},{49,17},{2,34}... | collective-permute-start | bytes 786440 | tf_op jit(solution)/shard_map/ppermute | solution.py:261
  143.8 7.8 %collective-permute-start.9 = (bf16[128,1024]{1,0:T(8,128)(2,1)S(1)}, bf16[128,1024]{1,0:T(8,128)(2,1)S(1)}, u32[]{:S(2)}, u32[]{:S(2)}) collective-permute-start(bf16[128,1024]{1,0:T(8,128)(2,1)S(1)} %bitcast.80), channel_id=1, source_target_pairs={{0,48},{16,0},{32,16},{48,32},{1,49},{17,1},{33,17},{49,33},{2,50}... | collective-permute-start | bytes 786440 | tf_op jit(solution)/shard_map/ppermute | solution.py:261
  151.7 0.9 copy-start
  161.7 1.4 copy-start.1
  163.1 9.8 %collective-permute-start.10 = (f32[512,128]{1,0:T(8,128)S(1)}, f32[512,128]{1,0:T(8,128)S(1)}, u32[]{:S(2)}, u32[]{:S(2)}) collective-permute-start(f32[512,128]{1,0:T(8,128)S(1)} %dynamic-slice_bitcast_fusion.2), channel_id=1, source_target_pairs={{0,1},{1,2},{2,3},{3,4},{4,5},{5,6},{6,7},{7,0},{8,9},{9,10},{10,1... | collective-permute-start | bytes 786440 | tf_op jit(solution)/shard_map/ppermute | solution.py:193
  164.1 9.8 %collective-permute-start.17 = (f32[512,128]{1,0:T(8,128)S(1)}, f32[512,128]{1,0:T(8,128)S(1)}, u32[]{:S(2)}, u32[]{:S(2)}) collective-permute-start(f32[512,128]{1,0:T(8,128)S(1)} %dynamic-slice_bitcast_fusion.1), channel_id=1, source_target_pairs={{0,7},{1,0},{2,1},{3,2},{4,3},{5,4},{6,5},{7,6},{8,15},{9,8},{10,9... | collective-permute-start | bytes 786440 | tf_op jit(solution)/shard_map/ppermute | solution.py:194
  173.9 8.1 %collective-permute-start.11 = (f32[512,128]{1,0:T(8,128)S(1)}, f32[512,128]{1,0:T(8,128)S(1)}, u32[]{:S(2)}, u32[]{:S(2)}) collective-permute-start(f32[512,128]{1,0:T(8,128)S(1)} %bitcast_add_fusion.14), channel_id=1, source_target_pairs={{0,1},{1,2},{2,3},{3,4},{4,5},{5,6},{6,7},{7,0},{8,9},{9,10},{10,1... | collective-permute-start | bytes 786440 | tf_op jit(solution)/shard_map/ppermute | solution.py:193
  174.0 9.0 %collective-permute-start.18 = (f32[512,128]{1,0:T(8,128)S(1)}, f32[512,128]{1,0:T(8,128)S(1)}, u32[]{:S(2)}, u32[]{:S(2)}) collective-permute-start(f32[512,128]{1,0:T(8,128)S(1)} %bitcast_add_fusion.7), channel_id=1, source_target_pairs={{0,7},{1,0},{2,1},{3,2},{4,3},{5,4},{6,5},{7,6},{8,15},{9,8},{10,9... | collective-permute-start | bytes 786440 | tf_op jit(solution)/shard_map/ppermute | solution.py:194
  182.9 11.5 %collective-permute-start.12 = (f32[512,128]{1,0:T(8,128)S(1)}, f32[512,128]{1,0:T(8,128)S(1)}, u32[]{:S(2)}, u32[]{:S(2)}) collective-permute-start(f32[512,128]{1,0:T(8,128)S(1)} %bitcast_add_fusion.13), channel_id=1, source_target_pairs={{0,1},{1,2},{2,3},{3,4},{4,5},{5,6},{6,7},{7,0},{8,9},{9,10},{10,1... | collective-permute-start | bytes 786440 | tf_op jit(solution)/shard_map/ppermute | solution.py:193
  183.1 12.4 %collective-permute-start.19 = (f32[512,128]{1,0:T(8,128)S(1)}, f32[512,128]{1,0:T(8,128)S(1)}, u32[]{:S(2)}, u32[]{:S(2)}) collective-permute-start(f32[512,128]{1,0:T(8,128)S(1)} %bitcast_add_fusion.6), channel_id=1, source_target_pairs={{0,7},{1,0},{2,1},{3,2},{4,3},{5,4},{6,5},{7,6},{8,15},{9,8},{10,9... | collective-permute-start | bytes 786440 | tf_op jit(solution)/shard_map/ppermute | solution.py:194
  195.4 9.6 %collective-permute-start.13 = (f32[512,128]{1,0:T(8,128)S(1)}, f32[512,128]{1,0:T(8,128)S(1)}, u32[]{:S(2)}, u32[]{:S(2)}) collective-permute-start(f32[512,128]{1,0:T(8,128)S(1)} %bitcast_add_fusion.12), channel_id=1, source_target_pairs={{0,1},{1,2},{2,3},{3,4},{4,5},{5,6},{6,7},{7,0},{8,9},{9,10},{10,1... | collective-permute-start | bytes 786440 | tf_op jit(solution)/shard_map/ppermute | solution.py:193
  195.5 10.5 %collective-permute-start.20 = (f32[512,128]{1,0:T(8,128)S(1)}, f32[512,128]{1,0:T(8,128)S(1)}, u32[]{:S(2)}, u32[]{:S(2)}) collective-permute-start(f32[512,128]{1,0:T(8,128)S(1)} %bitcast_add_fusion.5), channel_id=1, source_target_pairs={{0,7},{1,0},{2,1},{3,2},{4,3},{5,4},{6,5},{7,6},{8,15},{9,8},{10,9... | collective-permute-start | bytes 786440 | tf_op jit(solution)/shard_map/ppermute | solution.py:194
  206.0 8.8 %collective-permute-start.14 = (f32[512,128]{1,0:T(8,128)S(1)}, f32[512,128]{1,0:T(8,128)S(1)}, u32[]{:S(2)}, u32[]{:S(2)}) collective-permute-start(f32[512,128]{1,0:T(8,128)S(1)} %bitcast_add_fusion.11), channel_id=1, source_target_pairs={{0,1},{1,2},{2,3},{3,4},{4,5},{5,6},{6,7},{7,0},{8,9},{9,10},{10,1... | collective-permute-start | bytes 786440 | tf_op jit(solution)/shard_map/ppermute | solution.py:193
  206.1 9.7 %collective-permute-start.21 = (f32[512,128]{1,0:T(8,128)S(1)}, f32[512,128]{1,0:T(8,128)S(1)}, u32[]{:S(2)}, u32[]{:S(2)}) collective-permute-start(f32[512,128]{1,0:T(8,128)S(1)} %bitcast_add_fusion.4), channel_id=1, source_target_pairs={{0,7},{1,0},{2,1},{3,2},{4,3},{5,4},{6,5},{7,6},{8,15},{9,8},{10,9... | collective-permute-start | bytes 786440 | tf_op jit(solution)/shard_map/ppermute | solution.py:194
  215.7 7.7 %collective-permute-start.15 = (f32[512,128]{1,0:T(8,128)S(1)}, f32[512,128]{1,0:T(8,128)S(1)}, u32[]{:S(2)}, u32[]{:S(2)}) collective-permute-start(f32[512,128]{1,0:T(8,128)S(1)} %bitcast_add_fusion.10), channel_id=1, source_target_pairs={{0,1},{1,2},{2,3},{3,4},{4,5},{5,6},{6,7},{7,0},{8,9},{9,10},{10,1... | collective-permute-start | bytes 786440 | tf_op jit(solution)/shard_map/ppermute | solution.py:193
  215.9 8.6 %collective-permute-start.22 = (f32[512,128]{1,0:T(8,128)S(1)}, f32[512,128]{1,0:T(8,128)S(1)}, u32[]{:S(2)}, u32[]{:S(2)}) collective-permute-start(f32[512,128]{1,0:T(8,128)S(1)} %bitcast_add_fusion.3), channel_id=1, source_target_pairs={{0,7},{1,0},{2,1},{3,2},{4,3},{5,4},{6,5},{7,6},{8,15},{9,8},{10,9... | collective-permute-start | bytes 786440 | tf_op jit(solution)/shard_map/ppermute | solution.py:194
  224.4 7.7 %collective-permute-start.16 = (f32[512,128]{1,0:T(8,128)S(1)}, f32[512,128]{1,0:T(8,128)S(1)}, u32[]{:S(2)}, u32[]{:S(2)}) collective-permute-start(f32[512,128]{1,0:T(8,128)S(1)} %bitcast_add_fusion.9), channel_id=1, source_target_pairs={{0,1},{1,2},{2,3},{3,4},{4,5},{5,6},{6,7},{7,0},{8,9},{9,10},{10,1... | collective-permute-start | bytes 786440 | tf_op jit(solution)/shard_map/ppermute | solution.py:193
  224.5 8.5 %collective-permute-start.23 = (f32[512,128]{1,0:T(8,128)S(1)}, f32[512,128]{1,0:T(8,128)S(1)}, u32[]{:S(2)}, u32[]{:S(2)}) collective-permute-start(f32[512,128]{1,0:T(8,128)S(1)} %bitcast_add_fusion.2), channel_id=1, source_target_pairs={{0,7},{1,0},{2,1},{3,2},{4,3},{5,4},{6,5},{7,6},{8,15},{9,8},{10,9... | collective-permute-start | bytes 786440 | tf_op jit(solution)/shard_map/ppermute | solution.py:194
  233.1 6.5 %collective-permute-start.24 = (f32[512,128]{1,0:T(8,128)S(1)}, f32[512,128]{1,0:T(8,128)S(1)}, u32[]{:S(2)}, u32[]{:S(2)}) collective-permute-start(f32[512,128]{1,0:T(8,128)S(1)} %dynamic-slice_bitcast_fusion), channel_id=1, source_target_pairs={{0,8},{8,0},{1,9},{9,1},{2,10},{10,2},{3,11},{11,3},{4,12},{12,4},... | collective-permute-start | bytes 786440 | tf_op jit(solution)/shard_map/ppermute | solution.py:275
Sparse Core Ops, SparseCore 0:
  25.0 85.4 all-gather.1

commit v14 on v12

--- a/solution.py
+++ b/solution.py
@@ -10,7 +10,7 @@
 
 DP_AXES = ("y", "xlo", "z")
 DP_SIZES = (4, 2, 8)
-JB = 8
+JB = 16
 PER_BLOCK = 8
 
 

time: 241 us -> 254 us (1.054)
  starting transfers between devices: 41.4 us -> 51 us
    ppermute x3, starting transfers between devices: 5.71 us -> 16.1 us  [body(): pieces.append(lax.ppermute(outgoing, 'y', route))]
  transfers between devices with their start and end apart: 25 -> 25, of which waited for: 12 -> 11; matrix products, arithmetic and copies ran while one was open for 7% -> 6% of each run, Pallas kernels for 4% -> 4%
where the time goes in v14:
time: 254 us; the launch traced here: 251 us
  waiting for transfers between devices  137 us (54%)
  starting transfers between devices  51 us (20%)
  Pallas kernels  24.6 us (10%)
  between operations  14.1 us (6%)
  local copies, waits for them, and re-layouts  13.9 us (5%)
  other arithmetic  9.38 us (4%)
    ppermute x6, waiting for transfers between devices, hop(): return lax.ppermute(block, 'segment', [(src, dst)])  90.9 us
    ppermute x7, waiting for transfers between devices, ring_reduce_scatter(): got_e = lax.ppermute(send_e, axis, cw)  35.9 us
    ppermute x7, starting transfers between devices, ring_reduce_scatter(): got_w = lax.ppermute(send_w, axis, ccw)  24.7 us
    ppermute x3, starting transfers between devices, body(): pieces.append(lax.ppermute(outgoing, 'y', route))  16.1 us
    pallas_call x1, Pallas kernels, layer_backward(): pl.pallas_call(backward_kernel, grid_spec=grid, out_shape=[jax.ShapeDtype...  9.44 us
    pallas_call x1, Pallas kernels, group_grads(): pl.pallas_call(grad_kernel, grid_spec=grid, out_shape=jax.ShapeDtypeStruc...  8.72 us
    ppermute x6, starting transfers between devices, hop(): return lax.ppermute(block, 'segment', [(src, dst)])  7.42 us
    pallas_call x1, Pallas kernels, layer_forward(): pl.pallas_call(forward_kernel, grid_spec=grid, out_shape=[jax.ShapeDtypeS...  6.42 us
  transfers between devices with their start and end apart: 25, of which 11 were waited for; matrix products, arithmetic and copies ran while one was open for 6% of the time, Pallas kernels for 4%

profile of v14, /device:TPU:2, one launch (start us, length us, event | category | flops | bytes accessed | tf_op | source)
XLA Modules:
  0.0 250.6 jit_solution(2174055667547276160)
XLA Ops:
  7.4 6.4 %conditional.8 = (bf16[128,4096]{1,0:T(8,128)(2,1)S(1)}, f32[128,4096]{1,0:T(8,128)S(1)}) conditional(s32[]{:T(128)} %convert_element_type.21, () %tuple.79, (s32[256]{0:T(256)S(1)}, bf16[128,4096]{1,0:T(8,128)(2,1)}, bf16[32,8,128,128]{3,2,1,0:T(8,128)(2,1)}) %tuple.125), branch_computations={%region_0.0_spmd, %region_1.0_spmd} | conditional | flops 1073741824 | bytes 12582928 | solution.py:219
  7.4 6.4 %branch_1_fun.8 = (f32[128,4096]{1,0:T(8,128)S(1)}, bf16[128,4096]{1,0:T(8,128)(2,1)S(1)}) custom-call(s32[256]{0:T(256)S(1)} %get-tuple-element.85.cols_ref, bf16[128,4096]{1,0:T(8,128)(2,1)} %get-tuple-element.86.h_ref, bf16[32,8,128,128]{3,2,1,0:T(8,128)(2,1)} %get-tuple-element.87.w_ref), custom_call_target="tpu_custom_call" | custom-call | flops 1073741824 | bytes 12582912 | tf_op jit(solution)/shard_map/cond/branch_1_fun/pallas_call | solution.py:92
  13.8 2.3 collective-permute-start
  16.2 1.4 collective-permute-done
  21.4 1.6 collective-permute-start.2
  26.3 1.3 conditional.13
  30.9 89.5 %collective-permute-done.5 = bf16[128,4096]{1,0:T(8,128)(2,1)} collective-permute-done((bf16[128,4096]{1,0:T(8,128)(2,1)}, bf16[128,4096]{1,0:T(8,128)(2,1)}, u32[]{:S(2)}, u32[]{:S(2)}) %collective-permute-start.5) | collective-permute-done | bytes 1048608 | tf_op jit(solution)/shard_map/ppermute | solution.py:209
  120.3 9.4 %conditional.15 = (bf16[128,4096]{1,0:T(8,128)(2,1)S(1)}) conditional(s32[]{:T(128)} %convert_element_type.21, bf16[128,4096]{1,0:T(8,128)(2,1)S(1)} %get-tuple-element.141, (s32[256]{0:T(256)S(1)}, bf16[128,4096]{1,0:T(8,128)(2,1)}, f32[128,4096]{1,0:T(8,128)S(1)}, bf16[32,8,128,128]{3,2,1,0:T(8,128)(2,1)}) %tuple.132), branch_computations={%region_14.15_spmd, %region_15.16_spmd} | conditional | flops 1073741824 | bytes 13631496 | solution.py:234
  120.3 9.4 %branch_1_fun.15 = (bf16[128,4096]{1,0:T(8,128)(2,1)S(1)}, bf16[128,4096]{1,0:T(8,128)(2,1)}) custom-call(s32[256]{0:T(256)S(1)} %get-tuple-element.114.cols_ref, bf16[128,4096]{1,0:T(8,128)(2,1)} %get-tuple-element.115.up_ref, f32[128,4096]{1,0:T(8,128)S(1)} %get-tuple-element.116.z_ref, bf16[32,8,128,128]{3,2,1,0:T(8,128)(2,1)} %get-tuple-element.117.w_ref), custom_call_target="tpu_custom_call" | custom-call | flops 1073741824 | bytes 13631488 | tf_op jit(solution)/shard_map/cond/branch_1_fun/pallas_call | solution.py:124
  130.6 2.2 constant_dynamic-slice_fusion.3
  132.8 1.3 collective-permute-start.6
  134.2 3.4 %collective-permute-start.7 = (bf16[128,1024]{1,0:T(8,128)(2,1)S(1)}, bf16[128,1024]{1,0:T(8,128)(2,1)S(1)}, u32[]{:S(2)}, u32[]{:S(2)}) collective-permute-start(bf16[128,1024]{1,0:T(8,128)(2,1)S(1)} %bitcast.79), channel_id=1, source_target_pairs={{0,32},{16,48},{32,0},{48,16},{1,33},{17,49},{33,1},{49,17},{2,34}... | collective-permute-start | bytes 786440 | tf_op jit(solution)/shard_map/ppermute | solution.py:253
  137.7 11.4 %collective-permute-start.8 = (bf16[128,1024]{1,0:T(8,128)(2,1)S(1)}, bf16[128,1024]{1,0:T(8,128)(2,1)S(1)}, u32[]{:S(2)}, u32[]{:S(2)}) collective-permute-start(bf16[128,1024]{1,0:T(8,128)(2,1)S(1)} %bitcast.80), channel_id=1, source_target_pairs={{0,48},{16,0},{32,16},{48,32},{1,49},{17,1},{33,17},{49,33},{2,50}... | collective-permute-start | bytes 786440 | tf_op jit(solution)/shard_map/ppermute | solution.py:253
  150.2 4.3 %collective-permute-done.8 = bf16[128,1024]{1,0:T(8,128)(2,1)S(1)} collective-permute-done((bf16[128,1024]{1,0:T(8,128)(2,1)S(1)}, bf16[128,1024]{1,0:T(8,128)(2,1)S(1)}, u32[]{:S(2)}, u32[]{:S(2)}) %collective-permute-start.8) | collective-permute-done | bytes 262176 | tf_op jit(solution)/shard_map/ppermute | solution.py:253
  155.5 8.7 %shard_map.74 = f32[64,128,128]{2,1,0:T(8,128)S(1)} custom-call(s32[64]{0:T(128)S(1)} %gather_fusion, s32[64]{0:T(128)S(1)} %copy-done, bf16[512,4096]{1,0:T(8,128)(2,1)} %all-gather.2.cloned.1.call-done.h_ref, bf16[512,1024]{1,0:T(8,128)(2,1)S(1)} %bitcast_select_fusion.g_ref), custom_call_target="tpu_custom_call" | custom-call | flops 1073741824 | bytes 9437184 | tf_op jit(solution)/shard_map/pallas_call | solution.py:165
  164.6 1.3 copy-done.1
  166.0 2.0 collective-permute-start.9
  168.0 4.0 %collective-permute-start.16 = (f32[512,128]{1,0:T(8,128)S(1)}, f32[512,128]{1,0:T(8,128)S(1)}, u32[]{:S(2)}, u32[]{:S(2)}) collective-permute-start(f32[512,128]{1,0:T(8,128)S(1)} %dynamic-slice_bitcast_fusion.1), channel_id=1, source_target_pairs={{0,7},{1,0},{2,1},{3,2},{4,3},{5,4},{6,5},{7,6},{8,15},{9,8},{10,9... | collective-permute-start | bytes 786440 | tf_op jit(solution)/shard_map/ppermute | solution.py:194
  172.0 4.2 %collective-permute-done.9 = f32[512,128]{1,0:T(8,128)S(1)} collective-permute-done((f32[512,128]{1,0:T(8,128)S(1)}, f32[512,128]{1,0:T(8,128)S(1)}, u32[]{:S(2)}, u32[]{:S(2)}) %collective-permute-start.9) | collective-permute-done | bytes 262176 | tf_op jit(solution)/shard_map/ppermute | solution.py:193
  177.4 3.3 %collective-permute-start.17 = (f32[512,128]{1,0:T(8,128)S(1)}, f32[512,128]{1,0:T(8,128)S(1)}, u32[]{:S(2)}, u32[]{:S(2)}) collective-permute-start(f32[512,128]{1,0:T(8,128)S(1)} %bitcast_add_fusion.7), channel_id=1, source_target_pairs={{0,7},{1,0},{2,1},{3,2},{4,3},{5,4},{6,5},{7,6},{8,15},{9,8},{10,9... | collective-permute-start | bytes 786440 | tf_op jit(solution)/shard_map/ppermute | solution.py:194
  180.7 4.2 %collective-permute-done.10 = f32[512,128]{1,0:T(8,128)S(1)} collective-permute-done((f32[512,128]{1,0:T(8,128)S(1)}, f32[512,128]{1,0:T(8,128)S(1)}, u32[]{:S(2)}, u32[]{:S(2)}) %collective-permute-start.10) | collective-permute-done | bytes 262176 | tf_op jit(solution)/shard_map/ppermute | solution.py:193
  186.0 4.2 %collective-permute-start.18 = (f32[512,128]{1,0:T(8,128)S(1)}, f32[512,128]{1,0:T(8,128)S(1)}, u32[]{:S(2)}, u32[]{:S(2)}) collective-permute-start(f32[512,128]{1,0:T(8,128)S(1)} %bitcast_add_fusion.6), channel_id=1, source_target_pairs={{0,7},{1,0},{2,1},{3,2},{4,3},{5,4},{6,5},{7,6},{8,15},{9,8},{10,9... | collective-permute-start | bytes 786440 | tf_op jit(solution)/shard_map/ppermute | solution.py:194
  190.2 5.8 %collective-permute-done.11 = f32[512,128]{1,0:T(8,128)S(1)} collective-permute-done((f32[512,128]{1,0:T(8,128)S(1)}, f32[512,128]{1,0:T(8,128)S(1)}, u32[]{:S(2)}, u32[]{:S(2)}) %collective-permute-start.11) | collective-permute-done | bytes 262176 | tf_op jit(solution)/shard_map/ppermute | solution.py:193
  197.2 3.3 %collective-permute-start.19 = (f32[512,128]{1,0:T(8,128)S(1)}, f32[512,128]{1,0:T(8,128)S(1)}, u32[]{:S(2)}, u32[]{:S(2)}) collective-permute-start(f32[512,128]{1,0:T(8,128)S(1)} %bitcast_add_fusion.5), channel_id=1, source_target_pairs={{0,7},{1,0},{2,1},{3,2},{4,3},{5,4},{6,5},{7,6},{8,15},{9,8},{10,9... | collective-permute-start | bytes 786440 | tf_op jit(solution)/shard_map/ppermute | solution.py:194
  200.5 7.0 %collective-permute-done.12 = f32[512,128]{1,0:T(8,128)S(1)} collective-permute-done((f32[512,128]{1,0:T(8,128)S(1)}, f32[512,128]{1,0:T(8,128)S(1)}, u32[]{:S(2)}, u32[]{:S(2)}) %collective-permute-start.12) | collective-permute-done | bytes 262176 | tf_op jit(solution)/shard_map/ppermute | solution.py:193
  208.6 3.3 %collective-permute-start.20 = (f32[512,128]{1,0:T(8,128)S(1)}, f32[512,128]{1,0:T(8,128)S(1)}, u32[]{:S(2)}, u32[]{:S(2)}) collective-permute-start(f32[512,128]{1,0:T(8,128)S(1)} %bitcast_add_fusion.4), channel_id=1, source_target_pairs={{0,7},{1,0},{2,1},{3,2},{4,3},{5,4},{6,5},{7,6},{8,15},{9,8},{10,9... | collective-permute-start | bytes 786440 | tf_op jit(solution)/shard_map/ppermute | solution.py:194
  211.9 6.2 %collective-permute-done.13 = f32[512,128]{1,0:T(8,128)S(1)} collective-permute-done((f32[512,128]{1,0:T(8,128)S(1)}, f32[512,128]{1,0:T(8,128)S(1)}, u32[]{:S(2)}, u32[]{:S(2)}) %collective-permute-start.13) | collective-permute-done | bytes 262176 | tf_op jit(solution)/shard_map/ppermute | solution.py:193
  219.2 3.3 %collective-permute-start.21 = (f32[512,128]{1,0:T(8,128)S(1)}, f32[512,128]{1,0:T(8,128)S(1)}, u32[]{:S(2)}, u32[]{:S(2)}) collective-permute-start(f32[512,128]{1,0:T(8,128)S(1)} %bitcast_add_fusion.3), channel_id=1, source_target_pairs={{0,7},{1,0},{2,1},{3,2},{4,3},{5,4},{6,5},{7,6},{8,15},{9,8},{10,9... | collective-permute-start | bytes 786440 | tf_op jit(solution)/shard_map/ppermute | solution.py:194
  222.5 4.2 %collective-permute-done.14 = f32[512,128]{1,0:T(8,128)S(1)} collective-permute-done((f32[512,128]{1,0:T(8,128)S(1)}, f32[512,128]{1,0:T(8,128)S(1)}, u32[]{:S(2)}, u32[]{:S(2)}) %collective-permute-start.14) | collective-permute-done | bytes 262176 | tf_op jit(solution)/shard_map/ppermute | solution.py:193
  227.8 3.3 %collective-permute-start.22 = (f32[512,128]{1,0:T(8,128)S(1)}, f32[512,128]{1,0:T(8,128)S(1)}, u32[]{:S(2)}, u32[]{:S(2)}) collective-permute-start(f32[512,128]{1,0:T(8,128)S(1)} %bitcast_add_fusion.2), channel_id=1, source_target_pairs={{0,7},{1,0},{2,1},{3,2},{4,3},{5,4},{6,5},{7,6},{8,15},{9,8},{10,9... | collective-permute-start | bytes 786440 | tf_op jit(solution)/shard_map/ppermute | solution.py:194
  231.1 4.2 %collective-permute-done.15 = f32[512,128]{1,0:T(8,128)S(1)} collective-permute-done((f32[512,128]{1,0:T(8,128)S(1)}, f32[512,128]{1,0:T(8,128)S(1)}, u32[]{:S(2)}, u32[]{:S(2)}) %collective-permute-start.15) | collective-permute-done | bytes 262176 | tf_op jit(solution)/shard_map/ppermute | solution.py:193
  236.8 6.1 %collective-permute-done.23 = f32[512,128]{1,0:T(8,128)S(1)} collective-permute-done((f32[512,128]{1,0:T(8,128)S(1)}, f32[512,128]{1,0:T(8,128)S(1)}, u32[]{:S(2)}, u32[]{:S(2)}) %collective-permute-start.23) | collective-permute-done | bytes 262176 | tf_op jit(solution)/shard_map/ppermute | solution.py:267
  (85 shorter events, 28.6 us)
Async XLA Ops:
  6.5 149.0 %all-gather.2.cloned.1.call-start = ((), (), s32[]{:S(2)}) async-start(), calls=%async_computation | async-start | bytes 5242880 | tf_op jit(solution)/shard_map/all_gather | solution.py:259
  13.8 3.7 %collective-permute-start = (bf16[128,4096]{1,0:T(8,128)(2,1)S(1)}, bf16[128,4096]{1,0:T(8,128)(2,1)}, u32[]{:S(2)}, u32[]{:S(2)}) collective-permute-start(bf16[128,4096]{1,0:T(8,128)(2,1)S(1)} %get-tuple-element.132), channel_id=1, source_target_pairs={{0,64},{1,65},{2,66},{3,67},{4,68},{5,69},{6,70},{7,71},{8,72},{9,... | collective-permute-start | bytes 3145736 | tf_op jit(solution)/shard_map/ppermute | solution.py:209
  18.6 0.7 collective-permute-start.1
  19.4 1.0 copy-start.3
  20.4 2.7 %copy-start.2 = (bf16[128,4096]{1,0:T(8,128)(2,1)S(1)}, bf16[128,4096]{1,0:T(8,128)(2,1)}, u32[]{:S(2)}) copy-start(bf16[128,4096]{1,0:T(8,128)(2,1)} %param.23) | copy-start | bytes 3145732
  21.4 1.6 collective-permute-start.2
  25.6 0.7 collective-permute-start.3
  27.6 0.7 collective-permute-start.4
  28.4 2.5 copy-start.6
  29.5 90.9 %collective-permute-start.5 = (bf16[128,4096]{1,0:T(8,128)(2,1)}, bf16[128,4096]{1,0:T(8,128)(2,1)}, u32[]{:S(2)}, u32[]{:S(2)}) collective-permute-start(bf16[128,4096]{1,0:T(8,128)(2,1)} %get-tuple-element.142), channel_id=1, source_target_pairs={{64,0},{65,1},{66,2},{67,3},{68,4},{69,5},{70,6},{71,7},{72,8},{73... | collective-permute-start | bytes 3145736 | tf_op jit(solution)/shard_map/ppermute | solution.py:209
  132.8 17.3 %collective-permute-start.6 = (bf16[128,1024]{1,0:T(8,128)(2,1)S(1)}, bf16[128,1024]{1,0:T(8,128)(2,1)S(1)}, u32[]{:S(2)}, u32[]{:S(2)}) collective-permute-start(bf16[128,1024]{1,0:T(8,128)(2,1)S(1)} %bitcast.78), channel_id=1, source_target_pairs={{0,16},{16,32},{32,48},{48,0},{1,17},{17,33},{33,49},{49,1},{2,18}... | collective-permute-start | bytes 786440 | tf_op jit(solution)/shard_map/ppermute | solution.py:253
  134.2 15.9 %collective-permute-start.7 = (bf16[128,1024]{1,0:T(8,128)(2,1)S(1)}, bf16[128,1024]{1,0:T(8,128)(2,1)S(1)}, u32[]{:S(2)}, u32[]{:S(2)}) collective-permute-start(bf16[128,1024]{1,0:T(8,128)(2,1)S(1)} %bitcast.79), channel_id=1, source_target_pairs={{0,32},{16,48},{32,0},{48,16},{1,33},{17,49},{33,1},{49,17},{2,34}... | collective-permute-start | bytes 786440 | tf_op jit(solution)/shard_map/ppermute | solution.py:253
  137.7 16.8 %collective-permute-start.8 = (bf16[128,1024]{1,0:T(8,128)(2,1)S(1)}, bf16[128,1024]{1,0:T(8,128)(2,1)S(1)}, u32[]{:S(2)}, u32[]{:S(2)}) collective-permute-start(bf16[128,1024]{1,0:T(8,128)(2,1)S(1)} %bitcast.80), channel_id=1, source_target_pairs={{0,48},{16,0},{32,16},{48,32},{1,49},{17,1},{33,17},{49,33},{2,50}... | collective-permute-start | bytes 786440 | tf_op jit(solution)/shard_map/ppermute | solution.py:253
  154.6 0.9 copy-start
  164.6 1.4 copy-start.1
  166.0 10.2 %collective-permute-start.9 = (f32[512,128]{1,0:T(8,128)S(1)}, f32[512,128]{1,0:T(8,128)S(1)}, u32[]{:S(2)}, u32[]{:S(2)}) collective-permute-start(f32[512,128]{1,0:T(8,128)S(1)} %dynamic-slice_bitcast_fusion.2), channel_id=1, source_target_pairs={{0,1},{1,2},{2,3},{3,4},{4,5},{5,6},{6,7},{7,0},{8,9},{9,10},{10,1... | collective-permute-start | bytes 786440 | tf_op jit(solution)/shard_map/ppermute | solution.py:193
  168.0 9.3 %collective-permute-start.16 = (f32[512,128]{1,0:T(8,128)S(1)}, f32[512,128]{1,0:T(8,128)S(1)}, u32[]{:S(2)}, u32[]{:S(2)}) collective-permute-start(f32[512,128]{1,0:T(8,128)S(1)} %dynamic-slice_bitcast_fusion.1), channel_id=1, source_target_pairs={{0,7},{1,0},{2,1},{3,2},{4,3},{5,4},{6,5},{7,6},{8,15},{9,8},{10,9... | collective-permute-start | bytes 786440 | tf_op jit(solution)/shard_map/ppermute | solution.py:194
  177.2 7.7 %collective-permute-start.10 = (f32[512,128]{1,0:T(8,128)S(1)}, f32[512,128]{1,0:T(8,128)S(1)}, u32[]{:S(2)}, u32[]{:S(2)}) collective-permute-start(f32[512,128]{1,0:T(8,128)S(1)} %bitcast_add_fusion.14), channel_id=1, source_target_pairs={{0,1},{1,2},{2,3},{3,4},{4,5},{5,6},{6,7},{7,0},{8,9},{9,10},{10,1... | collective-permute-start | bytes 786440 | tf_op jit(solution)/shard_map/ppermute | solution.py:193
  177.4 8.6 %collective-permute-start.17 = (f32[512,128]{1,0:T(8,128)S(1)}, f32[512,128]{1,0:T(8,128)S(1)}, u32[]{:S(2)}, u32[]{:S(2)}) collective-permute-start(f32[512,128]{1,0:T(8,128)S(1)} %bitcast_add_fusion.7), channel_id=1, source_target_pairs={{0,7},{1,0},{2,1},{3,2},{4,3},{5,4},{6,5},{7,6},{8,15},{9,8},{10,9... | collective-permute-start | bytes 786440 | tf_op jit(solution)/shard_map/ppermute | solution.py:194
  185.9 10.2 %collective-permute-start.11 = (f32[512,128]{1,0:T(8,128)S(1)}, f32[512,128]{1,0:T(8,128)S(1)}, u32[]{:S(2)}, u32[]{:S(2)}) collective-permute-start(f32[512,128]{1,0:T(8,128)S(1)} %bitcast_add_fusion.13), channel_id=1, source_target_pairs={{0,1},{1,2},{2,3},{3,4},{4,5},{5,6},{6,7},{7,0},{8,9},{9,10},{10,1... | collective-permute-start | bytes 786440 | tf_op jit(solution)/shard_map/ppermute | solution.py:193
  186.0 11.1 %collective-permute-start.18 = (f32[512,128]{1,0:T(8,128)S(1)}, f32[512,128]{1,0:T(8,128)S(1)}, u32[]{:S(2)}, u32[]{:S(2)}) collective-permute-start(f32[512,128]{1,0:T(8,128)S(1)} %bitcast_add_fusion.6), channel_id=1, source_target_pairs={{0,7},{1,0},{2,1},{3,2},{4,3},{5,4},{6,5},{7,6},{8,15},{9,8},{10,9... | collective-permute-start | bytes 786440 | tf_op jit(solution)/shard_map/ppermute | solution.py:194
  197.0 10.4 %collective-permute-start.12 = (f32[512,128]{1,0:T(8,128)S(1)}, f32[512,128]{1,0:T(8,128)S(1)}, u32[]{:S(2)}, u32[]{:S(2)}) collective-permute-start(f32[512,128]{1,0:T(8,128)S(1)} %bitcast_add_fusion.12), channel_id=1, source_target_pairs={{0,1},{1,2},{2,3},{3,4},{4,5},{5,6},{6,7},{7,0},{8,9},{9,10},{10,1... | collective-permute-start | bytes 786440 | tf_op jit(solution)/shard_map/ppermute | solution.py:193
  197.2 11.4 %collective-permute-start.19 = (f32[512,128]{1,0:T(8,128)S(1)}, f32[512,128]{1,0:T(8,128)S(1)}, u32[]{:S(2)}, u32[]{:S(2)}) collective-permute-start(f32[512,128]{1,0:T(8,128)S(1)} %bitcast_add_fusion.5), channel_id=1, source_target_pairs={{0,7},{1,0},{2,1},{3,2},{4,3},{5,4},{6,5},{7,6},{8,15},{9,8},{10,9... | collective-permute-start | bytes 786440 | tf_op jit(solution)/shard_map/ppermute | solution.py:194
  208.4 9.6 %collective-permute-start.13 = (f32[512,128]{1,0:T(8,128)S(1)}, f32[512,128]{1,0:T(8,128)S(1)}, u32[]{:S(2)}, u32[]{:S(2)}) collective-permute-start(f32[512,128]{1,0:T(8,128)S(1)} %bitcast_add_fusion.11), channel_id=1, source_target_pairs={{0,1},{1,2},{2,3},{3,4},{4,5},{5,6},{6,7},{7,0},{8,9},{9,10},{10,1... | collective-permute-start | bytes 786440 | tf_op jit(solution)/shard_map/ppermute | solution.py:193
  208.6 10.5 %collective-permute-start.20 = (f32[512,128]{1,0:T(8,128)S(1)}, f32[512,128]{1,0:T(8,128)S(1)}, u32[]{:S(2)}, u32[]{:S(2)}) collective-permute-start(f32[512,128]{1,0:T(8,128)S(1)} %bitcast_add_fusion.4), channel_id=1, source_target_pairs={{0,7},{1,0},{2,1},{3,2},{4,3},{5,4},{6,5},{7,6},{8,15},{9,8},{10,9... | collective-permute-start | bytes 786440 | tf_op jit(solution)/shard_map/ppermute | solution.py:194
  219.0 7.7 %collective-permute-start.14 = (f32[512,128]{1,0:T(8,128)S(1)}, f32[512,128]{1,0:T(8,128)S(1)}, u32[]{:S(2)}, u32[]{:S(2)}) collective-permute-start(f32[512,128]{1,0:T(8,128)S(1)} %bitcast_add_fusion.10), channel_id=1, source_target_pairs={{0,1},{1,2},{2,3},{3,4},{4,5},{5,6},{6,7},{7,0},{8,9},{9,10},{10,1... | collective-permute-start | bytes 786440 | tf_op jit(solution)/shard_map/ppermute | solution.py:193
  219.2 8.6 %collective-permute-start.21 = (f32[512,128]{1,0:T(8,128)S(1)}, f32[512,128]{1,0:T(8,128)S(1)}, u32[]{:S(2)}, u32[]{:S(2)}) collective-permute-start(f32[512,128]{1,0:T(8,128)S(1)} %bitcast_add_fusion.3), channel_id=1, source_target_pairs={{0,7},{1,0},{2,1},{3,2},{4,3},{5,4},{6,5},{7,6},{8,15},{9,8},{10,9... | collective-permute-start | bytes 786440 | tf_op jit(solution)/shard_map/ppermute | solution.py:194
  227.7 7.7 %collective-permute-start.15 = (f32[512,128]{1,0:T(8,128)S(1)}, f32[512,128]{1,0:T(8,128)S(1)}, u32[]{:S(2)}, u32[]{:S(2)}) collective-permute-start(f32[512,128]{1,0:T(8,128)S(1)} %bitcast_add_fusion.9), channel_id=1, source_target_pairs={{0,1},{1,2},{2,3},{3,4},{4,5},{5,6},{6,7},{7,0},{8,9},{9,10},{10,1... | collective-permute-start | bytes 786440 | tf_op jit(solution)/shard_map/ppermute | solution.py:193
  227.8 8.5 %collective-permute-start.22 = (f32[512,128]{1,0:T(8,128)S(1)}, f32[512,128]{1,0:T(8,128)S(1)}, u32[]{:S(2)}, u32[]{:S(2)}) collective-permute-start(f32[512,128]{1,0:T(8,128)S(1)} %bitcast_add_fusion.2), channel_id=1, source_target_pairs={{0,7},{1,0},{2,1},{3,2},{4,3},{5,4},{6,5},{7,6},{8,15},{9,8},{10,9... | collective-permute-start | bytes 786440 | tf_op jit(solution)/shard_map/ppermute | solution.py:194
  236.5 6.5 %collective-permute-start.23 = (f32[512,128]{1,0:T(8,128)S(1)}, f32[512,128]{1,0:T(8,128)S(1)}, u32[]{:S(2)}, u32[]{:S(2)}) collective-permute-start(f32[512,128]{1,0:T(8,128)S(1)} %dynamic-slice_bitcast_fusion), channel_id=1, source_target_pairs={{0,8},{8,0},{1,9},{9,1},{2,10},{10,2},{3,11},{11,3},{4,12},{12,4},... | collective-permute-start | bytes 786440 | tf_op jit(solution)/shard_map/ppermute | solution.py:267
Sparse Core Ops, SparseCore 0:
  24.4 86.1 all-gather.1

commit v15 on v12

--- a/solution.py
+++ b/solution.py
@@ -179,22 +179,14 @@
 
 def ring_reduce_scatter(chunks, axis, n):
     i = lax.axis_index(axis)
-    half = chunks.shape[1] // 2
-    east, west = chunks[:, :half], chunks[:, half:]
     cw = [(k, (k + 1) % n) for k in range(n)]
-    ccw = [(k, (k - 1) % n) for k in range(n)]
-    got_e = got_w = None
+    got = None
     for s in range(n - 1):
-        send_e = lax.dynamic_index_in_dim(east, (i - s - 1) % n, 0, False)
-        send_w = lax.dynamic_index_in_dim(west, (i + s + 1) % n, 0, False)
-        if got_e is not None:
-            send_e = got_e + send_e
-            send_w = got_w + send_w
-        got_e = lax.ppermute(send_e, axis, cw)
-        got_w = lax.ppermute(send_w, axis, ccw)
-    own_e = lax.dynamic_index_in_dim(east, i, 0, False)
-    own_w = lax.dynamic_index_in_dim(west, i, 0, False)
-    return jnp.concatenate([got_e + own_e, got_w + own_w], 0)
+        send = lax.dynamic_index_in_dim(chunks, (i - s - 1) % n, 0, False)
+        if got is not None:
+            send = got + send
+        got = lax.ppermute(send, axis, cw)
+    return got + lax.dynamic_index_in_dim(chunks, i, 0, False)
 
 
 def body(inputs, cotangent, blocks, block_cols):

time: 241 us -> 271 us (1.12)
  waiting for transfers between devices: 137 us -> 191 us
  starting transfers between devices: 41.4 us -> 15.8 us
    ppermute x14 -> x7, waiting for transfers between devices: 35.2 us -> 90.2 us  [ring_reduce_scatter(): got = lax.ppermute(send, axis, cw)]
    ppermute x14 -> x7, starting transfers between devices: 28.1 us -> 2.55 us  [ring_reduce_scatter(): got = lax.ppermute(send, axis, cw)]
    add x14 -> x7, other arithmetic: 7.08 us -> 7.67 us  [the longest x6 6.57 us: ring_reduce_scatter(): send = got + send]
  transfers between devices with their start and end apart: 25 -> 18, of which waited for: 12 -> 12; matrix products, arithmetic and copies ran while one was open for 7% -> 3% of each run, Pallas kernels for 4% -> 3%
where the time goes in v15:
time: 271 us; the launch traced here: 270 us
  waiting for transfers between devices  191 us (70%)
  Pallas kernels  25 us (9%)
  starting transfers between devices  15.8 us (6%)
  local copies, waits for them, and re-layouts  14.2 us (5%)
  between operations  13.9 us (5%)
  other arithmetic  9.94 us (4%)
    ppermute x6, waiting for transfers between devices, hop(): return lax.ppermute(block, 'segment', [(src, dst)])  90.3 us
    ppermute x7, waiting for transfers between devices, ring_reduce_scatter(): got = lax.ppermute(send, axis, cw)  90.2 us
    pallas_call x1, Pallas kernels, layer_backward(): pl.pallas_call(backward_kernel, grid_spec=grid, out_shape=[jax.ShapeDtype...  9.32 us
    pallas_call x1, Pallas kernels, group_grads(): pl.pallas_call(grad_kernel, grid_spec=grid, out_shape=jax.ShapeDtypeStruc...  8.73 us
    ppermute x6, starting transfers between devices, hop(): return lax.ppermute(block, 'segment', [(src, dst)])  7.37 us
    pallas_call x1, Pallas kernels, layer_forward(): pl.pallas_call(forward_kernel, grid_spec=grid, out_shape=[jax.ShapeDtypeS...  6.91 us
    add x6, other arithmetic, ring_reduce_scatter(): send = got + send  6.57 us
    ppermute x1, waiting for transfers between devices, body(): lax.ppermute(lax.dynamic_index_in_dim(halves, 1 - side, 0, False), 'xlo',...  6.26 us
  transfers between devices with their start and end apart: 18, of which 12 were waited for; matrix products, arithmetic and copies ran while one was open for 3% of the time, Pallas kernels for 3%

profile of v15, /device:TPU:2, one launch (start us, length us, event | category | flops | bytes accessed | tf_op | source)
XLA Modules:
  0.0 270.4 jit_solution(18415375108165309738)
XLA Ops:
  7.4 6.9 %conditional.8 = (bf16[128,4096]{1,0:T(8,128)(2,1)S(1)}, f32[128,4096]{1,0:T(8,128)S(1)}) conditional(s32[]{:T(128)} %convert_element_type.21, () %tuple.79, (s32[256]{0:T(256)S(1)}, bf16[128,4096]{1,0:T(8,128)(2,1)}, bf16[32,8,128,128]{3,2,1,0:T(8,128)(2,1)}) %tuple.124), branch_computations={%region_0.0_spmd, %region_1.0_spmd} | conditional | flops 1073741824 | bytes 12582928 | solution.py:211
  7.4 6.9 %branch_1_fun.8 = (f32[128,4096]{1,0:T(8,128)S(1)}, bf16[128,4096]{1,0:T(8,128)(2,1)S(1)}) custom-call(s32[256]{0:T(256)S(1)} %get-tuple-element.85.cols_ref, bf16[128,4096]{1,0:T(8,128)(2,1)} %get-tuple-element.86.h_ref, bf16[32,8,128,128]{3,2,1,0:T(8,128)(2,1)} %get-tuple-element.87.w_ref), custom_call_target="tpu_custom_call" | custom-call | flops 1073741824 | bytes 12582912 | tf_op jit(solution)/shard_map/cond/branch_1_fun/pallas_call | solution.py:92
  14.3 2.3 collective-permute-start
  16.6 1.4 collective-permute-done
  21.9 1.6 collective-permute-start.2
  23.6 1.2 select_select_fusion
  24.8 1.2 conditional.12
  26.8 1.1 conditional.13
  28.6 1.1 conditional.14
  29.7 1.3 collective-permute-start.5
  31.1 88.8 %collective-permute-done.5 = bf16[128,4096]{1,0:T(8,128)(2,1)} collective-permute-done((bf16[128,4096]{1,0:T(8,128)(2,1)}, bf16[128,4096]{1,0:T(8,128)(2,1)}, u32[]{:S(2)}, u32[]{:S(2)}) %collective-permute-start.5) | collective-permute-done | bytes 1048608 | tf_op jit(solution)/shard_map/ppermute | solution.py:201
  120.0 9.3 %conditional.15 = (bf16[128,4096]{1,0:T(8,128)(2,1)S(1)}) conditional(s32[]{:T(128)} %convert_element_type.21, bf16[128,4096]{1,0:T(8,128)(2,1)S(1)} %get-tuple-element.141, (s32[256]{0:T(256)S(1)}, bf16[128,4096]{1,0:T(8,128)(2,1)}, f32[128,4096]{1,0:T(8,128)S(1)}, bf16[32,8,128,128]{3,2,1,0:T(8,128)(2,1)}) %tuple.131), branch_computations={%region_14.15_spmd, %region_15.16_spmd} | conditional | flops 1073741824 | bytes 13631496 | solution.py:226
  120.0 9.3 %branch_1_fun.15 = (bf16[128,4096]{1,0:T(8,128)(2,1)S(1)}, bf16[128,4096]{1,0:T(8,128)(2,1)}) custom-call(s32[256]{0:T(256)S(1)} %get-tuple-element.114.cols_ref, bf16[128,4096]{1,0:T(8,128)(2,1)} %get-tuple-element.115.up_ref, f32[128,4096]{1,0:T(8,128)S(1)} %get-tuple-element.116.z_ref, bf16[32,8,128,128]{3,2,1,0:T(8,128)(2,1)} %get-tuple-element.117.w_ref), custom_call_target="tpu_custom_call" | custom-call | flops 1073741824 | bytes 13631488 | tf_op jit(solution)/shard_map/cond/branch_1_fun/pallas_call | solution.py:124
  130.1 2.2 constant_dynamic-slice_fusion.3
  132.3 1.3 collective-permute-start.6
  133.7 3.4 %collective-permute-start.7 = (bf16[128,1024]{1,0:T(8,128)(2,1)S(1)}, bf16[128,1024]{1,0:T(8,128)(2,1)S(1)}, u32[]{:S(2)}, u32[]{:S(2)}) collective-permute-start(bf16[128,1024]{1,0:T(8,128)(2,1)S(1)} %bitcast.70), channel_id=1, source_target_pairs={{0,32},{16,48},{32,0},{48,16},{1,33},{17,49},{33,1},{49,17},{2,34}... | collective-permute-start | bytes 786440 | tf_op jit(solution)/shard_map/ppermute | solution.py:245
  140.0 4.1 %collective-permute-done.7 = bf16[128,1024]{1,0:T(8,128)(2,1)S(1)} collective-permute-done((bf16[128,1024]{1,0:T(8,128)(2,1)S(1)}, bf16[128,1024]{1,0:T(8,128)(2,1)S(1)}, u32[]{:S(2)}, u32[]{:S(2)}) %collective-permute-start.7) | collective-permute-done | bytes 262176 | tf_op jit(solution)/shard_map/ppermute | solution.py:245
  145.1 8.7 %shard_map.74 = f32[64,128,128]{2,1,0:T(8,128)S(1)} custom-call(s32[64]{0:T(128)S(1)} %gather_fusion, s32[64]{0:T(128)S(1)} %copy-done.1, bf16[512,4096]{1,0:T(8,128)(2,1)} %all-gather.2.cloned.1.call-done.h_ref, bf16[512,1024]{1,0:T(8,128)(2,1)S(1)} %bitcast_select_fusion.g_ref), custom_call_target="tpu_custom_call" | custom-call | flops 1073741824 | bytes 9437184 | tf_op jit(solution)/shard_map/pallas_call | solution.py:165
  153.8 2.0 copy-done
  155.8 2.0 collective-permute-start.9
  157.9 16.1 %collective-permute-done.9 = f32[1024,128]{1,0:T(8,128)S(1)} collective-permute-done((f32[1024,128]{1,0:T(8,128)S(1)}, f32[1024,128]{1,0:T(8,128)S(1)}, u32[]{:S(2)}, u32[]{:S(2)}) %collective-permute-start.9) | collective-permute-done | bytes 524320 | tf_op jit(solution)/shard_map/ppermute | solution.py:188
  173.9 1.1 bitcast_add_fusion.6
  175.1 14.6 %collective-permute-done.10 = f32[1024,128]{1,0:T(8,128)S(1)} collective-permute-done((f32[1024,128]{1,0:T(8,128)S(1)}, f32[1024,128]{1,0:T(8,128)S(1)}, u32[]{:S(2)}, u32[]{:S(2)}) %collective-permute-start.10) | collective-permute-done | bytes 524320 | tf_op jit(solution)/shard_map/ppermute | solution.py:188
  189.7 1.1 bitcast_add_fusion.5
  190.9 13.7 %collective-permute-done.11 = f32[1024,128]{1,0:T(8,128)S(1)} collective-permute-done((f32[1024,128]{1,0:T(8,128)S(1)}, f32[1024,128]{1,0:T(8,128)S(1)}, u32[]{:S(2)}, u32[]{:S(2)}) %collective-permute-start.11) | collective-permute-done | bytes 524320 | tf_op jit(solution)/shard_map/ppermute | solution.py:188
  204.6 1.1 bitcast_add_fusion.4
  205.8 12.7 %collective-permute-done.12 = f32[1024,128]{1,0:T(8,128)S(1)} collective-permute-done((f32[1024,128]{1,0:T(8,128)S(1)}, f32[1024,128]{1,0:T(8,128)S(1)}, u32[]{:S(2)}, u32[]{:S(2)}) %collective-permute-start.12) | collective-permute-done | bytes 524320 | tf_op jit(solution)/shard_map/ppermute | solution.py:188
  219.8 11.8 %collective-permute-done.13 = f32[1024,128]{1,0:T(8,128)S(1)} collective-permute-done((f32[1024,128]{1,0:T(8,128)S(1)}, f32[1024,128]{1,0:T(8,128)S(1)}, u32[]{:S(2)}, u32[]{:S(2)}) %collective-permute-start.13) | collective-permute-done | bytes 524320 | tf_op jit(solution)/shard_map/ppermute | solution.py:188
  231.6 1.1 bitcast_add_fusion.2
  232.8 10.9 %collective-permute-done.14 = f32[1024,128]{1,0:T(8,128)S(1)} collective-permute-done((f32[1024,128]{1,0:T(8,128)S(1)}, f32[1024,128]{1,0:T(8,128)S(1)}, u32[]{:S(2)}, u32[]{:S(2)}) %collective-permute-start.14) | collective-permute-done | bytes 524320 | tf_op jit(solution)/shard_map/ppermute | solution.py:188
  244.9 10.4 %collective-permute-done.15 = f32[1024,128]{1,0:T(8,128)S(1)} collective-permute-done((f32[1024,128]{1,0:T(8,128)S(1)}, f32[1024,128]{1,0:T(8,128)S(1)}, u32[]{:S(2)}, u32[]{:S(2)}) %collective-permute-start.15) | collective-permute-done | bytes 524320 | tf_op jit(solution)/shard_map/ppermute | solution.py:188
  256.6 6.3 %collective-permute-done.16 = f32[512,128]{1,0:T(8,128)S(1)} collective-permute-done((f32[512,128]{1,0:T(8,128)S(1)}, f32[512,128]{1,0:T(8,128)S(1)}, u32[]{:S(2)}, u32[]{:S(2)}) %collective-permute-start.16) | collective-permute-done | bytes 262176 | tf_op jit(solution)/shard_map/ppermute | solution.py:259
  (61 shorter events, 21.3 us)
Async XLA Ops:
  6.5 138.5 %all-gather.2.cloned.1.call-start = ((), (), s32[]{:S(2)}) async-start(), calls=%async_computation | async-start | bytes 5242880 | tf_op jit(solution)/shard_map/all_gather | solution.py:251
  14.3 3.7 %collective-permute-start = (bf16[128,4096]{1,0:T(8,128)(2,1)S(1)}, bf16[128,4096]{1,0:T(8,128)(2,1)}, u32[]{:S(2)}, u32[]{:S(2)}) collective-permute-start(bf16[128,4096]{1,0:T(8,128)(2,1)S(1)} %get-tuple-element.132), channel_id=1, source_target_pairs={{0,64},{1,65},{2,66},{3,67},{4,68},{5,69},{6,70},{7,71},{8,72},{9,... | collective-permute-start | bytes 3145736 | tf_op jit(solution)/shard_map/ppermute | solution.py:201
  19.1 0.7 collective-permute-start.1
  19.9 1.0 copy-start.3
  20.9 2.7 %copy-start.2 = (bf16[128,4096]{1,0:T(8,128)(2,1)S(1)}, bf16[128,4096]{1,0:T(8,128)(2,1)}, u32[]{:S(2)}) copy-start(bf16[128,4096]{1,0:T(8,128)(2,1)} %param.23) | copy-start | bytes 3145732
  21.9 1.6 collective-permute-start.2
  26.0 0.7 collective-permute-start.3
  27.9 0.7 collective-permute-start.4
  28.6 2.5 copy-start.6
  29.7 90.2 %collective-permute-start.5 = (bf16[128,4096]{1,0:T(8,128)(2,1)}, bf16[128,4096]{1,0:T(8,128)(2,1)}, u32[]{:S(2)}, u32[]{:S(2)}) collective-permute-start(bf16[128,4096]{1,0:T(8,128)(2,1)} %get-tuple-element.142), channel_id=1, source_target_pairs={{64,0},{65,1},{66,2},{67,3},{68,4},{69,5},{70,6},{71,7},{72,8},{73... | collective-permute-start | bytes 3145736 | tf_op jit(solution)/shard_map/ppermute | solution.py:201
  132.3 7.7 %collective-permute-start.6 = (bf16[128,1024]{1,0:T(8,128)(2,1)S(1)}, bf16[128,1024]{1,0:T(8,128)(2,1)S(1)}, u32[]{:S(2)}, u32[]{:S(2)}) collective-permute-start(bf16[128,1024]{1,0:T(8,128)(2,1)S(1)} %bitcast.69), channel_id=1, source_target_pairs={{0,16},{16,32},{32,48},{48,0},{1,17},{17,33},{33,49},{49,1},{2,18}... | collective-permute-start | bytes 786440 | tf_op jit(solution)/shard_map/ppermute | solution.py:245
  133.7 10.3 %collective-permute-start.7 = (bf16[128,1024]{1,0:T(8,128)(2,1)S(1)}, bf16[128,1024]{1,0:T(8,128)(2,1)S(1)}, u32[]{:S(2)}, u32[]{:S(2)}) collective-permute-start(bf16[128,1024]{1,0:T(8,128)(2,1)S(1)} %bitcast.70), channel_id=1, source_target_pairs={{0,32},{16,48},{32,0},{48,16},{1,33},{17,49},{33,1},{49,17},{2,34}... | collective-permute-start | bytes 786440 | tf_op jit(solution)/shard_map/ppermute | solution.py:245
  137.1 8.0 %copy-start.1 = (s32[64]{0:T(128)S(1)}, s32[64]{0:T(128)}, u32[]{:S(2)}) copy-start(s32[64]{0:T(128)} %constant.189.clone.j_ref) | copy-start | bytes 772
  137.2 6.9 %collective-permute-start.8 = (bf16[128,1024]{1,0:T(8,128)(2,1)S(1)}, bf16[128,1024]{1,0:T(8,128)(2,1)S(1)}, u32[]{:S(2)}, u32[]{:S(2)}) collective-permute-start(bf16[128,1024]{1,0:T(8,128)(2,1)S(1)} %bitcast.71), channel_id=1, source_target_pairs={{0,48},{16,0},{32,16},{48,32},{1,49},{17,1},{33,17},{49,33},{2,50}... | collective-permute-start | bytes 786440 | tf_op jit(solution)/shard_map/ppermute | solution.py:245
  153.8 2.0 copy-start
  155.8 18.1 %collective-permute-start.9 = (f32[1024,128]{1,0:T(8,128)S(1)}, f32[1024,128]{1,0:T(8,128)S(1)}, u32[]{:S(2)}, u32[]{:S(2)}) collective-permute-start(f32[1024,128]{1,0:T(8,128)S(1)} %dynamic-slice_bitcast_fusion), channel_id=1, source_target_pairs={{0,1},{1,2},{2,3},{3,4},{4,5},{5,6},{6,7},{7,0},{8,9},{9,10},{10,1... | collective-permute-start | bytes 1572872 | tf_op jit(solution)/shard_map/ppermute | solution.py:188
  175.0 14.7 %collective-permute-start.10 = (f32[1024,128]{1,0:T(8,128)S(1)}, f32[1024,128]{1,0:T(8,128)S(1)}, u32[]{:S(2)}, u32[]{:S(2)}) collective-permute-start(f32[1024,128]{1,0:T(8,128)S(1)} %bitcast_add_fusion.6), channel_id=1, source_target_pairs={{0,1},{1,2},{2,3},{3,4},{4,5},{5,6},{6,7},{7,0},{8,9},{9,10},{10,1... | collective-permute-start | bytes 1572872 | tf_op jit(solution)/shard_map/ppermute | solution.py:188
  190.8 13.8 %collective-permute-start.11 = (f32[1024,128]{1,0:T(8,128)S(1)}, f32[1024,128]{1,0:T(8,128)S(1)}, u32[]{:S(2)}, u32[]{:S(2)}) collective-permute-start(f32[1024,128]{1,0:T(8,128)S(1)} %bitcast_add_fusion.5), channel_id=1, source_target_pairs={{0,1},{1,2},{2,3},{3,4},{4,5},{5,6},{6,7},{7,0},{8,9},{9,10},{10,1... | collective-permute-start | bytes 1572872 | tf_op jit(solution)/shard_map/ppermute | solution.py:188
  205.7 12.9 %collective-permute-start.12 = (f32[1024,128]{1,0:T(8,128)S(1)}, f32[1024,128]{1,0:T(8,128)S(1)}, u32[]{:S(2)}, u32[]{:S(2)}) collective-permute-start(f32[1024,128]{1,0:T(8,128)S(1)} %bitcast_add_fusion.4), channel_id=1, source_target_pairs={{0,1},{1,2},{2,3},{3,4},{4,5},{5,6},{6,7},{7,0},{8,9},{9,10},{10,1... | collective-permute-start | bytes 1572872 | tf_op jit(solution)/shard_map/ppermute | solution.py:188
  219.6 11.9 %collective-permute-start.13 = (f32[1024,128]{1,0:T(8,128)S(1)}, f32[1024,128]{1,0:T(8,128)S(1)}, u32[]{:S(2)}, u32[]{:S(2)}) collective-permute-start(f32[1024,128]{1,0:T(8,128)S(1)} %bitcast_add_fusion.3), channel_id=1, source_target_pairs={{0,1},{1,2},{2,3},{3,4},{4,5},{5,6},{6,7},{7,0},{8,9},{9,10},{10,1... | collective-permute-start | bytes 1572872 | tf_op jit(solution)/shard_map/ppermute | solution.py:188
  232.7 11.0 %collective-permute-start.14 = (f32[1024,128]{1,0:T(8,128)S(1)}, f32[1024,128]{1,0:T(8,128)S(1)}, u32[]{:S(2)}, u32[]{:S(2)}) collective-permute-start(f32[1024,128]{1,0:T(8,128)S(1)} %bitcast_add_fusion.2), channel_id=1, source_target_pairs={{0,1},{1,2},{2,3},{3,4},{4,5},{5,6},{6,7},{7,0},{8,9},{9,10},{10,1... | collective-permute-start | bytes 1572872 | tf_op jit(solution)/shard_map/ppermute | solution.py:188
  244.8 10.5 %collective-permute-start.15 = (f32[1024,128]{1,0:T(8,128)S(1)}, f32[1024,128]{1,0:T(8,128)S(1)}, u32[]{:S(2)}, u32[]{:S(2)}) collective-permute-start(f32[1024,128]{1,0:T(8,128)S(1)} %bitcast_add_fusion.1), channel_id=1, source_target_pairs={{0,1},{1,2},{2,3},{3,4},{4,5},{5,6},{6,7},{7,0},{8,9},{9,10},{10,1... | collective-permute-start | bytes 1572872 | tf_op jit(solution)/shard_map/ppermute | solution.py:188
  256.4 6.5 %collective-permute-start.16 = (f32[512,128]{1,0:T(8,128)S(1)}, f32[512,128]{1,0:T(8,128)S(1)}, u32[]{:S(2)}, u32[]{:S(2)}) collective-permute-start(f32[512,128]{1,0:T(8,128)S(1)} %dynamic-slice_bitcast_fusion.1), channel_id=1, source_target_pairs={{0,8},{8,0},{1,9},{9,1},{2,10},{10,2},{3,11},{11,3},{4,12},{12,4},... | collective-permute-start | bytes 786440 | tf_op jit(solution)/shard_map/ppermute | solution.py:259
Sparse Core Ops, SparseCore 0:
  24.9 86.0 all-gather.1

commit v16 on v12

--- a/solution.py
+++ b/solution.py
@@ -260,7 +260,7 @@
     cols_here = lax.dynamic_slice_in_dim(flat_cols, member * group_pairs, group_pairs)
     order = np.arange(group_pairs).reshape(nx, nz, -1).transpose(1, 0, 2).reshape(-1)
     j_index = jnp.asarray(order // per_block, jnp.int32)
-    partial = group_grads(cols_here[order], j_index, inputs_group, grads_group, group_pairs, 16)
+    partial = group_grads(cols_here[order], j_index, inputs_group, grads_group, group_pairs, 32)
     reduced = ring_reduce_scatter(partial.reshape(nz, -1, edge_size), "z", nz)
     halves = reduced.reshape(nx, -1, edge_size)
     side = lax.axis_index("xlo")

time: 241 us -> 241 us (level)
  no operation moved by 1% of the time
where the time goes in v16:
time: 241 us; the launch traced here: 240 us
  waiting for transfers between devices  137 us (57%)
  starting transfers between devices  41.1 us (17%)
  Pallas kernels  24.5 us (10%)
  local copies, waits for them, and re-layouts  13.9 us (6%)
  between operations  13.9 us (6%)
  other arithmetic  9.38 us (4%)
    ppermute x6, waiting for transfers between devices, hop(): return lax.ppermute(block, 'segment', [(src, dst)])  90.4 us
    ppermute x7, waiting for transfers between devices, ring_reduce_scatter(): got_e = lax.ppermute(send_e, axis, cw)  35.3 us
    ppermute x7, starting transfers between devices, ring_reduce_scatter(): got_w = lax.ppermute(send_w, axis, ccw)  25 us
    pallas_call x1, Pallas kernels, layer_backward(): pl.pallas_call(backward_kernel, grid_spec=grid, out_shape=[jax.ShapeDtype...  9.28 us
    pallas_call x1, Pallas kernels, group_grads(): pl.pallas_call(grad_kernel, grid_spec=grid, out_shape=jax.ShapeDtypeStruc...  8.38 us
    ppermute x6, starting transfers between devices, hop(): return lax.ppermute(block, 'segment', [(src, dst)])  7.4 us
    pallas_call x1, Pallas kernels, layer_forward(): pl.pallas_call(forward_kernel, grid_spec=grid, out_shape=[jax.ShapeDtypeS...  6.88 us
    ppermute x1, waiting for transfers between devices, body(): lax.ppermute(lax.dynamic_index_in_dim(halves, 1 - side, 0, False), 'xlo',...  6.27 us
  transfers between devices with their start and end apart: 25, of which 12 were waited for; matrix products, arithmetic and copies ran while one was open for 7% of the time, Pallas kernels for 4%

profile of v16, /device:TPU:2, one launch (start us, length us, event | category | flops | bytes accessed | tf_op | source)
XLA Modules:
  0.0 239.7 jit_solution(7948903337783898556)
XLA Ops:
  7.4 6.9 %conditional.8 = (bf16[128,4096]{1,0:T(8,128)(2,1)S(1)}, f32[128,4096]{1,0:T(8,128)S(1)}) conditional(s32[]{:T(128)} %convert_element_type.21, () %tuple.79, (s32[256]{0:T(256)S(1)}, bf16[128,4096]{1,0:T(8,128)(2,1)}, bf16[32,8,128,128]{3,2,1,0:T(8,128)(2,1)}) %tuple.125), branch_computations={%region_0.0_spmd, %region_1.0_spmd} | conditional | flops 1073741824 | bytes 12582928 | solution.py:219
  7.4 6.9 %branch_1_fun.8 = (f32[128,4096]{1,0:T(8,128)S(1)}, bf16[128,4096]{1,0:T(8,128)(2,1)S(1)}) custom-call(s32[256]{0:T(256)S(1)} %get-tuple-element.85.cols_ref, bf16[128,4096]{1,0:T(8,128)(2,1)} %get-tuple-element.86.h_ref, bf16[32,8,128,128]{3,2,1,0:T(8,128)(2,1)} %get-tuple-element.87.w_ref), custom_call_target="tpu_custom_call" | custom-call | flops 1073741824 | bytes 12582912 | tf_op jit(solution)/shard_map/cond/branch_1_fun/pallas_call | solution.py:92
  14.3 2.3 collective-permute-start
  16.6 1.4 collective-permute-done
  21.9 1.6 collective-permute-start.2
  24.8 1.2 conditional.12
  29.7 1.3 collective-permute-start.5
  31.1 89.0 %collective-permute-done.5 = bf16[128,4096]{1,0:T(8,128)(2,1)} collective-permute-done((bf16[128,4096]{1,0:T(8,128)(2,1)}, bf16[128,4096]{1,0:T(8,128)(2,1)}, u32[]{:S(2)}, u32[]{:S(2)}) %collective-permute-start.5) | collective-permute-done | bytes 1048608 | tf_op jit(solution)/shard_map/ppermute | solution.py:209
  120.0 9.3 %conditional.15 = (bf16[128,4096]{1,0:T(8,128)(2,1)S(1)}) conditional(s32[]{:T(128)} %convert_element_type.21, bf16[128,4096]{1,0:T(8,128)(2,1)S(1)} %get-tuple-element.141, (s32[256]{0:T(256)S(1)}, bf16[128,4096]{1,0:T(8,128)(2,1)}, f32[128,4096]{1,0:T(8,128)S(1)}, bf16[32,8,128,128]{3,2,1,0:T(8,128)(2,1)}) %tuple.132), branch_computations={%region_14.15_spmd, %region_15.16_spmd} | conditional | flops 1073741824 | bytes 13631496 | solution.py:234
  120.0 9.3 %branch_1_fun.15 = (bf16[128,4096]{1,0:T(8,128)(2,1)S(1)}, bf16[128,4096]{1,0:T(8,128)(2,1)}) custom-call(s32[256]{0:T(256)S(1)} %get-tuple-element.114.cols_ref, bf16[128,4096]{1,0:T(8,128)(2,1)} %get-tuple-element.115.up_ref, f32[128,4096]{1,0:T(8,128)S(1)} %get-tuple-element.116.z_ref, bf16[32,8,128,128]{3,2,1,0:T(8,128)(2,1)} %get-tuple-element.117.w_ref), custom_call_target="tpu_custom_call" | custom-call | flops 1073741824 | bytes 13631488 | tf_op jit(solution)/shard_map/cond/branch_1_fun/pallas_call | solution.py:124
  130.1 2.2 constant_dynamic-slice_fusion.3
  132.4 1.3 collective-permute-start.6
  133.8 3.3 %collective-permute-start.7 = (bf16[128,1024]{1,0:T(8,128)(2,1)S(1)}, bf16[128,1024]{1,0:T(8,128)(2,1)S(1)}, u32[]{:S(2)}, u32[]{:S(2)}) collective-permute-start(bf16[128,1024]{1,0:T(8,128)(2,1)S(1)} %bitcast.79), channel_id=1, source_target_pairs={{0,32},{16,48},{32,0},{48,16},{1,33},{17,49},{33,1},{49,17},{2,34}... | collective-permute-start | bytes 786440 | tf_op jit(solution)/shard_map/ppermute | solution.py:253
  140.0 4.0 %collective-permute-done.7 = bf16[128,1024]{1,0:T(8,128)(2,1)S(1)} collective-permute-done((bf16[128,1024]{1,0:T(8,128)(2,1)S(1)}, bf16[128,1024]{1,0:T(8,128)(2,1)S(1)}, u32[]{:S(2)}, u32[]{:S(2)}) %collective-permute-start.7) | collective-permute-done | bytes 262176 | tf_op jit(solution)/shard_map/ppermute | solution.py:253
  145.1 8.4 %shard_map.74 = f32[64,128,128]{2,1,0:T(8,128)S(1)} custom-call(s32[64]{0:T(128)S(1)} %gather_fusion, s32[64]{0:T(128)S(1)} %copy-done, bf16[512,4096]{1,0:T(8,128)(2,1)} %all-gather.2.cloned.1.call-done.h_ref, bf16[512,1024]{1,0:T(8,128)(2,1)S(1)} %bitcast_select_fusion.g_ref), custom_call_target="tpu_custom_call" | custom-call | flops 1073741824 | bytes 9437184 | tf_op jit(solution)/shard_map/pallas_call | solution.py:165
  153.9 1.3 copy-done.1
  155.2 2.1 collective-permute-start.9
  157.4 4.0 %collective-permute-start.16 = (f32[512,128]{1,0:T(8,128)S(1)}, f32[512,128]{1,0:T(8,128)S(1)}, u32[]{:S(2)}, u32[]{:S(2)}) collective-permute-start(f32[512,128]{1,0:T(8,128)S(1)} %dynamic-slice_bitcast_fusion.1), channel_id=1, source_target_pairs={{0,7},{1,0},{2,1},{3,2},{4,3},{5,4},{6,5},{7,6},{8,15},{9,8},{10,9... | collective-permute-start | bytes 786440 | tf_op jit(solution)/shard_map/ppermute | solution.py:194
  161.3 4.2 %collective-permute-done.9 = f32[512,128]{1,0:T(8,128)S(1)} collective-permute-done((f32[512,128]{1,0:T(8,128)S(1)}, f32[512,128]{1,0:T(8,128)S(1)}, u32[]{:S(2)}, u32[]{:S(2)}) %collective-permute-start.9) | collective-permute-done | bytes 262176 | tf_op jit(solution)/shard_map/ppermute | solution.py:193
  166.7 3.3 %collective-permute-start.17 = (f32[512,128]{1,0:T(8,128)S(1)}, f32[512,128]{1,0:T(8,128)S(1)}, u32[]{:S(2)}, u32[]{:S(2)}) collective-permute-start(f32[512,128]{1,0:T(8,128)S(1)} %bitcast_add_fusion.7), channel_id=1, source_target_pairs={{0,7},{1,0},{2,1},{3,2},{4,3},{5,4},{6,5},{7,6},{8,15},{9,8},{10,9... | collective-permute-start | bytes 786440 | tf_op jit(solution)/shard_map/ppermute | solution.py:194
  170.0 4.2 %collective-permute-done.10 = f32[512,128]{1,0:T(8,128)S(1)} collective-permute-done((f32[512,128]{1,0:T(8,128)S(1)}, f32[512,128]{1,0:T(8,128)S(1)}, u32[]{:S(2)}, u32[]{:S(2)}) %collective-permute-start.10) | collective-permute-done | bytes 262176 | tf_op jit(solution)/shard_map/ppermute | solution.py:193
  175.5 4.5 %collective-permute-start.18 = (f32[512,128]{1,0:T(8,128)S(1)}, f32[512,128]{1,0:T(8,128)S(1)}, u32[]{:S(2)}, u32[]{:S(2)}) collective-permute-start(f32[512,128]{1,0:T(8,128)S(1)} %bitcast_add_fusion.6), channel_id=1, source_target_pairs={{0,7},{1,0},{2,1},{3,2},{4,3},{5,4},{6,5},{7,6},{8,15},{9,8},{10,9... | collective-permute-start | bytes 786440 | tf_op jit(solution)/shard_map/ppermute | solution.py:194
  180.1 6.6 %collective-permute-done.11 = f32[512,128]{1,0:T(8,128)S(1)} collective-permute-done((f32[512,128]{1,0:T(8,128)S(1)}, f32[512,128]{1,0:T(8,128)S(1)}, u32[]{:S(2)}, u32[]{:S(2)}) %collective-permute-start.11) | collective-permute-done | bytes 262176 | tf_op jit(solution)/shard_map/ppermute | solution.py:193
  187.8 3.3 %collective-permute-start.19 = (f32[512,128]{1,0:T(8,128)S(1)}, f32[512,128]{1,0:T(8,128)S(1)}, u32[]{:S(2)}, u32[]{:S(2)}) collective-permute-start(f32[512,128]{1,0:T(8,128)S(1)} %bitcast_add_fusion.5), channel_id=1, source_target_pairs={{0,7},{1,0},{2,1},{3,2},{4,3},{5,4},{6,5},{7,6},{8,15},{9,8},{10,9... | collective-permute-start | bytes 786440 | tf_op jit(solution)/shard_map/ppermute | solution.py:194
  191.1 6.3 %collective-permute-done.12 = f32[512,128]{1,0:T(8,128)S(1)} collective-permute-done((f32[512,128]{1,0:T(8,128)S(1)}, f32[512,128]{1,0:T(8,128)S(1)}, u32[]{:S(2)}, u32[]{:S(2)}) %collective-permute-start.12) | collective-permute-done | bytes 262176 | tf_op jit(solution)/shard_map/ppermute | solution.py:193
  198.5 3.3 %collective-permute-start.20 = (f32[512,128]{1,0:T(8,128)S(1)}, f32[512,128]{1,0:T(8,128)S(1)}, u32[]{:S(2)}, u32[]{:S(2)}) collective-permute-start(f32[512,128]{1,0:T(8,128)S(1)} %bitcast_add_fusion.4), channel_id=1, source_target_pairs={{0,7},{1,0},{2,1},{3,2},{4,3},{5,4},{6,5},{7,6},{8,15},{9,8},{10,9... | collective-permute-start | bytes 786440 | tf_op jit(solution)/shard_map/ppermute | solution.py:194
  201.8 5.5 %collective-permute-done.13 = f32[512,128]{1,0:T(8,128)S(1)} collective-permute-done((f32[512,128]{1,0:T(8,128)S(1)}, f32[512,128]{1,0:T(8,128)S(1)}, u32[]{:S(2)}, u32[]{:S(2)}) %collective-permute-start.13) | collective-permute-done | bytes 262176 | tf_op jit(solution)/shard_map/ppermute | solution.py:193
  208.4 3.3 %collective-permute-start.21 = (f32[512,128]{1,0:T(8,128)S(1)}, f32[512,128]{1,0:T(8,128)S(1)}, u32[]{:S(2)}, u32[]{:S(2)}) collective-permute-start(f32[512,128]{1,0:T(8,128)S(1)} %bitcast_add_fusion.3), channel_id=1, source_target_pairs={{0,7},{1,0},{2,1},{3,2},{4,3},{5,4},{6,5},{7,6},{8,15},{9,8},{10,9... | collective-permute-start | bytes 786440 | tf_op jit(solution)/shard_map/ppermute | solution.py:194
  211.7 4.2 %collective-permute-done.14 = f32[512,128]{1,0:T(8,128)S(1)} collective-permute-done((f32[512,128]{1,0:T(8,128)S(1)}, f32[512,128]{1,0:T(8,128)S(1)}, u32[]{:S(2)}, u32[]{:S(2)}) %collective-permute-start.14) | collective-permute-done | bytes 262176 | tf_op jit(solution)/shard_map/ppermute | solution.py:193
  217.0 3.3 %collective-permute-start.22 = (f32[512,128]{1,0:T(8,128)S(1)}, f32[512,128]{1,0:T(8,128)S(1)}, u32[]{:S(2)}, u32[]{:S(2)}) collective-permute-start(f32[512,128]{1,0:T(8,128)S(1)} %bitcast_add_fusion.2), channel_id=1, source_target_pairs={{0,7},{1,0},{2,1},{3,2},{4,3},{5,4},{6,5},{7,6},{8,15},{9,8},{10,9... | collective-permute-start | bytes 786440 | tf_op jit(solution)/shard_map/ppermute | solution.py:194
  220.3 4.2 %collective-permute-done.15 = f32[512,128]{1,0:T(8,128)S(1)} collective-permute-done((f32[512,128]{1,0:T(8,128)S(1)}, f32[512,128]{1,0:T(8,128)S(1)}, u32[]{:S(2)}, u32[]{:S(2)}) %collective-permute-start.15) | collective-permute-done | bytes 262176 | tf_op jit(solution)/shard_map/ppermute | solution.py:193
  225.9 6.3 %collective-permute-done.23 = f32[512,128]{1,0:T(8,128)S(1)} collective-permute-done((f32[512,128]{1,0:T(8,128)S(1)}, f32[512,128]{1,0:T(8,128)S(1)}, u32[]{:S(2)}, u32[]{:S(2)}) %collective-permute-start.23) | collective-permute-done | bytes 262176 | tf_op jit(solution)/shard_map/ppermute | solution.py:267
  (85 shorter events, 29.1 us)
Async XLA Ops:
  6.5 138.6 %all-gather.2.cloned.1.call-start = ((), (), s32[]{:S(2)}) async-start(), calls=%async_computation | async-start | bytes 5242880 | tf_op jit(solution)/shard_map/all_gather | solution.py:259
  14.3 3.7 %collective-permute-start = (bf16[128,4096]{1,0:T(8,128)(2,1)S(1)}, bf16[128,4096]{1,0:T(8,128)(2,1)}, u32[]{:S(2)}, u32[]{:S(2)}) collective-permute-start(bf16[128,4096]{1,0:T(8,128)(2,1)S(1)} %get-tuple-element.132), channel_id=1, source_target_pairs={{0,64},{1,65},{2,66},{3,67},{4,68},{5,69},{6,70},{7,71},{8,72},{9,... | collective-permute-start | bytes 3145736 | tf_op jit(solution)/shard_map/ppermute | solution.py:209
  19.1 0.7 collective-permute-start.1
  19.8 1.0 copy-start.3
  20.8 2.7 %copy-start.2 = (bf16[128,4096]{1,0:T(8,128)(2,1)S(1)}, bf16[128,4096]{1,0:T(8,128)(2,1)}, u32[]{:S(2)}) copy-start(bf16[128,4096]{1,0:T(8,128)(2,1)} %param.23) | copy-start | bytes 3145732
  21.9 1.6 collective-permute-start.2
  26.0 0.7 collective-permute-start.3
  27.8 0.7 collective-permute-start.4
  28.6 2.5 %copy-start.6 = (s32[64]{0:T(128)S(1)}, s32[64]{0:T(128)}, u32[]{:S(2)}) copy-start(s32[64]{0:T(128)} %constant.247) | copy-start | bytes 772
  29.7 90.4 %collective-permute-start.5 = (bf16[128,4096]{1,0:T(8,128)(2,1)}, bf16[128,4096]{1,0:T(8,128)(2,1)}, u32[]{:S(2)}, u32[]{:S(2)}) collective-permute-start(bf16[128,4096]{1,0:T(8,128)(2,1)} %get-tuple-element.142), channel_id=1, source_target_pairs={{64,0},{65,1},{66,2},{67,3},{68,4},{69,5},{70,6},{71,7},{72,8},{73... | collective-permute-start | bytes 3145736 | tf_op jit(solution)/shard_map/ppermute | solution.py:209
  132.4 7.7 %collective-permute-start.6 = (bf16[128,1024]{1,0:T(8,128)(2,1)S(1)}, bf16[128,1024]{1,0:T(8,128)(2,1)S(1)}, u32[]{:S(2)}, u32[]{:S(2)}) collective-permute-start(bf16[128,1024]{1,0:T(8,128)(2,1)S(1)} %bitcast.78), channel_id=1, source_target_pairs={{0,16},{16,32},{32,48},{48,0},{1,17},{17,33},{33,49},{49,1},{2,18}... | collective-permute-start | bytes 786440 | tf_op jit(solution)/shard_map/ppermute | solution.py:253
  133.8 10.3 %collective-permute-start.7 = (bf16[128,1024]{1,0:T(8,128)(2,1)S(1)}, bf16[128,1024]{1,0:T(8,128)(2,1)S(1)}, u32[]{:S(2)}, u32[]{:S(2)}) collective-permute-start(bf16[128,1024]{1,0:T(8,128)(2,1)S(1)} %bitcast.79), channel_id=1, source_target_pairs={{0,32},{16,48},{32,0},{48,16},{1,33},{17,49},{33,1},{49,17},{2,34}... | collective-permute-start | bytes 786440 | tf_op jit(solution)/shard_map/ppermute | solution.py:253
  137.2 6.9 %collective-permute-start.8 = (bf16[128,1024]{1,0:T(8,128)(2,1)S(1)}, bf16[128,1024]{1,0:T(8,128)(2,1)S(1)}, u32[]{:S(2)}, u32[]{:S(2)}) collective-permute-start(bf16[128,1024]{1,0:T(8,128)(2,1)S(1)} %bitcast.80), channel_id=1, source_target_pairs={{0,48},{16,0},{32,16},{48,32},{1,49},{17,1},{33,17},{49,33},{2,50}... | collective-permute-start | bytes 786440 | tf_op jit(solution)/shard_map/ppermute | solution.py:253
  144.2 0.9 copy-start
  153.9 1.4 copy-start.1
  155.2 10.3 %collective-permute-start.9 = (f32[512,128]{1,0:T(8,128)S(1)}, f32[512,128]{1,0:T(8,128)S(1)}, u32[]{:S(2)}, u32[]{:S(2)}) collective-permute-start(f32[512,128]{1,0:T(8,128)S(1)} %dynamic-slice_bitcast_fusion.2), channel_id=1, source_target_pairs={{0,1},{1,2},{2,3},{3,4},{4,5},{5,6},{6,7},{7,0},{8,9},{9,10},{10,1... | collective-permute-start | bytes 786440 | tf_op jit(solution)/shard_map/ppermute | solution.py:193
  157.4 9.3 %collective-permute-start.16 = (f32[512,128]{1,0:T(8,128)S(1)}, f32[512,128]{1,0:T(8,128)S(1)}, u32[]{:S(2)}, u32[]{:S(2)}) collective-permute-start(f32[512,128]{1,0:T(8,128)S(1)} %dynamic-slice_bitcast_fusion.1), channel_id=1, source_target_pairs={{0,7},{1,0},{2,1},{3,2},{4,3},{5,4},{6,5},{7,6},{8,15},{9,8},{10,9... | collective-permute-start | bytes 786440 | tf_op jit(solution)/shard_map/ppermute | solution.py:194
  166.5 7.7 %collective-permute-start.10 = (f32[512,128]{1,0:T(8,128)S(1)}, f32[512,128]{1,0:T(8,128)S(1)}, u32[]{:S(2)}, u32[]{:S(2)}) collective-permute-start(f32[512,128]{1,0:T(8,128)S(1)} %bitcast_add_fusion.14), channel_id=1, source_target_pairs={{0,1},{1,2},{2,3},{3,4},{4,5},{5,6},{6,7},{7,0},{8,9},{9,10},{10,1... | collective-permute-start | bytes 786440 | tf_op jit(solution)/shard_map/ppermute | solution.py:193
  166.7 8.8 %collective-permute-start.17 = (f32[512,128]{1,0:T(8,128)S(1)}, f32[512,128]{1,0:T(8,128)S(1)}, u32[]{:S(2)}, u32[]{:S(2)}) collective-permute-start(f32[512,128]{1,0:T(8,128)S(1)} %bitcast_add_fusion.7), channel_id=1, source_target_pairs={{0,7},{1,0},{2,1},{3,2},{4,3},{5,4},{6,5},{7,6},{8,15},{9,8},{10,9... | collective-permute-start | bytes 786440 | tf_op jit(solution)/shard_map/ppermute | solution.py:194
  175.2 11.5 %collective-permute-start.11 = (f32[512,128]{1,0:T(8,128)S(1)}, f32[512,128]{1,0:T(8,128)S(1)}, u32[]{:S(2)}, u32[]{:S(2)}) collective-permute-start(f32[512,128]{1,0:T(8,128)S(1)} %bitcast_add_fusion.13), channel_id=1, source_target_pairs={{0,1},{1,2},{2,3},{3,4},{4,5},{5,6},{6,7},{7,0},{8,9},{9,10},{10,1... | collective-permute-start | bytes 786440 | tf_op jit(solution)/shard_map/ppermute | solution.py:193
  175.5 12.2 %collective-permute-start.18 = (f32[512,128]{1,0:T(8,128)S(1)}, f32[512,128]{1,0:T(8,128)S(1)}, u32[]{:S(2)}, u32[]{:S(2)}) collective-permute-start(f32[512,128]{1,0:T(8,128)S(1)} %bitcast_add_fusion.6), channel_id=1, source_target_pairs={{0,7},{1,0},{2,1},{3,2},{4,3},{5,4},{6,5},{7,6},{8,15},{9,8},{10,9... | collective-permute-start | bytes 786440 | tf_op jit(solution)/shard_map/ppermute | solution.py:194
  187.7 9.7 %collective-permute-start.12 = (f32[512,128]{1,0:T(8,128)S(1)}, f32[512,128]{1,0:T(8,128)S(1)}, u32[]{:S(2)}, u32[]{:S(2)}) collective-permute-start(f32[512,128]{1,0:T(8,128)S(1)} %bitcast_add_fusion.12), channel_id=1, source_target_pairs={{0,1},{1,2},{2,3},{3,4},{4,5},{5,6},{6,7},{7,0},{8,9},{9,10},{10,1... | collective-permute-start | bytes 786440 | tf_op jit(solution)/shard_map/ppermute | solution.py:193
  187.8 10.6 %collective-permute-start.19 = (f32[512,128]{1,0:T(8,128)S(1)}, f32[512,128]{1,0:T(8,128)S(1)}, u32[]{:S(2)}, u32[]{:S(2)}) collective-permute-start(f32[512,128]{1,0:T(8,128)S(1)} %bitcast_add_fusion.5), channel_id=1, source_target_pairs={{0,7},{1,0},{2,1},{3,2},{4,3},{5,4},{6,5},{7,6},{8,15},{9,8},{10,9... | collective-permute-start | bytes 786440 | tf_op jit(solution)/shard_map/ppermute | solution.py:194
  198.4 8.9 %collective-permute-start.13 = (f32[512,128]{1,0:T(8,128)S(1)}, f32[512,128]{1,0:T(8,128)S(1)}, u32[]{:S(2)}, u32[]{:S(2)}) collective-permute-start(f32[512,128]{1,0:T(8,128)S(1)} %bitcast_add_fusion.11), channel_id=1, source_target_pairs={{0,1},{1,2},{2,3},{3,4},{4,5},{5,6},{6,7},{7,0},{8,9},{9,10},{10,1... | collective-permute-start | bytes 786440 | tf_op jit(solution)/shard_map/ppermute | solution.py:193
  198.5 9.8 %collective-permute-start.20 = (f32[512,128]{1,0:T(8,128)S(1)}, f32[512,128]{1,0:T(8,128)S(1)}, u32[]{:S(2)}, u32[]{:S(2)}) collective-permute-start(f32[512,128]{1,0:T(8,128)S(1)} %bitcast_add_fusion.4), channel_id=1, source_target_pairs={{0,7},{1,0},{2,1},{3,2},{4,3},{5,4},{6,5},{7,6},{8,15},{9,8},{10,9... | collective-permute-start | bytes 786440 | tf_op jit(solution)/shard_map/ppermute | solution.py:194
  208.3 7.7 %collective-permute-start.14 = (f32[512,128]{1,0:T(8,128)S(1)}, f32[512,128]{1,0:T(8,128)S(1)}, u32[]{:S(2)}, u32[]{:S(2)}) collective-permute-start(f32[512,128]{1,0:T(8,128)S(1)} %bitcast_add_fusion.10), channel_id=1, source_target_pairs={{0,1},{1,2},{2,3},{3,4},{4,5},{5,6},{6,7},{7,0},{8,9},{9,10},{10,1... | collective-permute-start | bytes 786440 | tf_op jit(solution)/shard_map/ppermute | solution.py:193
  208.4 8.6 %collective-permute-start.21 = (f32[512,128]{1,0:T(8,128)S(1)}, f32[512,128]{1,0:T(8,128)S(1)}, u32[]{:S(2)}, u32[]{:S(2)}) collective-permute-start(f32[512,128]{1,0:T(8,128)S(1)} %bitcast_add_fusion.3), channel_id=1, source_target_pairs={{0,7},{1,0},{2,1},{3,2},{4,3},{5,4},{6,5},{7,6},{8,15},{9,8},{10,9... | collective-permute-start | bytes 786440 | tf_op jit(solution)/shard_map/ppermute | solution.py:194
  216.9 7.7 %collective-permute-start.15 = (f32[512,128]{1,0:T(8,128)S(1)}, f32[512,128]{1,0:T(8,128)S(1)}, u32[]{:S(2)}, u32[]{:S(2)}) collective-permute-start(f32[512,128]{1,0:T(8,128)S(1)} %bitcast_add_fusion.9), channel_id=1, source_target_pairs={{0,1},{1,2},{2,3},{3,4},{4,5},{5,6},{6,7},{7,0},{8,9},{9,10},{10,1... | collective-permute-start | bytes 786440 | tf_op jit(solution)/shard_map/ppermute | solution.py:193
  217.0 8.5 %collective-permute-start.22 = (f32[512,128]{1,0:T(8,128)S(1)}, f32[512,128]{1,0:T(8,128)S(1)}, u32[]{:S(2)}, u32[]{:S(2)}) collective-permute-start(f32[512,128]{1,0:T(8,128)S(1)} %bitcast_add_fusion.2), channel_id=1, source_target_pairs={{0,7},{1,0},{2,1},{3,2},{4,3},{5,4},{6,5},{7,6},{8,15},{9,8},{10,9... | collective-permute-start | bytes 786440 | tf_op jit(solution)/shard_map/ppermute | solution.py:194
  225.7 6.5 %collective-permute-start.23 = (f32[512,128]{1,0:T(8,128)S(1)}, f32[512,128]{1,0:T(8,128)S(1)}, u32[]{:S(2)}, u32[]{:S(2)}) collective-permute-start(f32[512,128]{1,0:T(8,128)S(1)} %dynamic-slice_bitcast_fusion), channel_id=1, source_target_pairs={{0,8},{8,0},{1,9},{9,1},{2,10},{10,2},{3,11},{11,3},{4,12},{12,4},... | collective-permute-start | bytes 786440 | tf_op jit(solution)/shard_map/ppermute | solution.py:267
Sparse Core Ops, SparseCore 0:
  24.9 86.0 all-gather.1

commit v17 on v16

--- a/solution.py
+++ b/solution.py
@@ -260,7 +260,7 @@
     cols_here = lax.dynamic_slice_in_dim(flat_cols, member * group_pairs, group_pairs)
     order = np.arange(group_pairs).reshape(nx, nz, -1).transpose(1, 0, 2).reshape(-1)
     j_index = jnp.asarray(order // per_block, jnp.int32)
-    partial = group_grads(cols_here[order], j_index, inputs_group, grads_group, group_pairs, 32)
+    partial = group_grads(cols_here[order], j_index, inputs_group, grads_group, group_pairs, 64)
     reduced = ring_reduce_scatter(partial.reshape(nz, -1, edge_size), "z", nz)
     halves = reduced.reshape(nx, -1, edge_size)
     side = lax.axis_index("xlo")

time: 241 us -> 241 us (level)
  no operation moved by 1% of the time
where the time goes in v17:
time: 241 us; the launch traced here: 239 us
  waiting for transfers between devices  137 us (57%)
  starting transfers between devices  41.4 us (17%)
  Pallas kernels  24.3 us (10%)
  local copies, waits for them, and re-layouts  13.9 us (6%)
  between operations  13.9 us (6%)
  other arithmetic  9.38 us (4%)
    ppermute x6, waiting for transfers between devices, hop(): return lax.ppermute(block, 'segment', [(src, dst)])  90.3 us
    ppermute x7, waiting for transfers between devices, ring_reduce_scatter(): got_e = lax.ppermute(send_e, axis, cw)  35.1 us
    ppermute x7, starting transfers between devices, ring_reduce_scatter(): got_w = lax.ppermute(send_w, axis, ccw)  25.5 us
    pallas_call x1, Pallas kernels, layer_backward(): pl.pallas_call(backward_kernel, grid_spec=grid, out_shape=[jax.ShapeDtype...  9.29 us
    pallas_call x1, Pallas kernels, group_grads(): pl.pallas_call(grad_kernel, grid_spec=grid, out_shape=jax.ShapeDtypeStruc...  8.13 us
    ppermute x6, starting transfers between devices, hop(): return lax.ppermute(block, 'segment', [(src, dst)])  7.4 us
    pallas_call x1, Pallas kernels, layer_forward(): pl.pallas_call(forward_kernel, grid_spec=grid, out_shape=[jax.ShapeDtypeS...  6.88 us
    ppermute x1, waiting for transfers between devices, body(): lax.ppermute(lax.dynamic_index_in_dim(halves, 1 - side, 0, False), 'xlo',...  6.28 us
  transfers between devices with their start and end apart: 25, of which 12 were waited for; matrix products, arithmetic and copies ran while one was open for 7% of the time, Pallas kernels for 4%

profile of v17, /device:TPU:2, one launch (start us, length us, event | category | flops | bytes accessed | tf_op | source)
XLA Modules:
  0.0 239.5 jit_solution(3494342387929143638)
XLA Ops:
  7.4 6.9 %conditional.8 = (bf16[128,4096]{1,0:T(8,128)(2,1)S(1)}, f32[128,4096]{1,0:T(8,128)S(1)}) conditional(s32[]{:T(128)} %convert_element_type.21, () %tuple.79, (s32[256]{0:T(256)S(1)}, bf16[128,4096]{1,0:T(8,128)(2,1)}, bf16[32,8,128,128]{3,2,1,0:T(8,128)(2,1)}) %tuple.125), branch_computations={%region_0.0_spmd, %region_1.0_spmd} | conditional | flops 1073741824 | bytes 12582928 | solution.py:219
  7.4 6.9 %branch_1_fun.8 = (f32[128,4096]{1,0:T(8,128)S(1)}, bf16[128,4096]{1,0:T(8,128)(2,1)S(1)}) custom-call(s32[256]{0:T(256)S(1)} %get-tuple-element.85.cols_ref, bf16[128,4096]{1,0:T(8,128)(2,1)} %get-tuple-element.86.h_ref, bf16[32,8,128,128]{3,2,1,0:T(8,128)(2,1)} %get-tuple-element.87.w_ref), custom_call_target="tpu_custom_call" | custom-call | flops 1073741824 | bytes 12582912 | tf_op jit(solution)/shard_map/cond/branch_1_fun/pallas_call | solution.py:92
  14.3 2.3 collective-permute-start
  16.6 1.4 collective-permute-done
  21.9 1.6 collective-permute-start.2
  24.8 1.2 conditional.12
  29.7 1.3 collective-permute-start.5
  31.1 88.9 %collective-permute-done.5 = bf16[128,4096]{1,0:T(8,128)(2,1)} collective-permute-done((bf16[128,4096]{1,0:T(8,128)(2,1)}, bf16[128,4096]{1,0:T(8,128)(2,1)}, u32[]{:S(2)}, u32[]{:S(2)}) %collective-permute-start.5) | collective-permute-done | bytes 1048608 | tf_op jit(solution)/shard_map/ppermute | solution.py:209
  119.9 9.3 %conditional.15 = (bf16[128,4096]{1,0:T(8,128)(2,1)S(1)}) conditional(s32[]{:T(128)} %convert_element_type.21, bf16[128,4096]{1,0:T(8,128)(2,1)S(1)} %get-tuple-element.141, (s32[256]{0:T(256)S(1)}, bf16[128,4096]{1,0:T(8,128)(2,1)}, f32[128,4096]{1,0:T(8,128)S(1)}, bf16[32,8,128,128]{3,2,1,0:T(8,128)(2,1)}) %tuple.132), branch_computations={%region_14.15_spmd, %region_15.16_spmd} | conditional | flops 1073741824 | bytes 13631496 | solution.py:234
  119.9 9.3 %branch_1_fun.15 = (bf16[128,4096]{1,0:T(8,128)(2,1)S(1)}, bf16[128,4096]{1,0:T(8,128)(2,1)}) custom-call(s32[256]{0:T(256)S(1)} %get-tuple-element.114.cols_ref, bf16[128,4096]{1,0:T(8,128)(2,1)} %get-tuple-element.115.up_ref, f32[128,4096]{1,0:T(8,128)S(1)} %get-tuple-element.116.z_ref, bf16[32,8,128,128]{3,2,1,0:T(8,128)(2,1)} %get-tuple-element.117.w_ref), custom_call_target="tpu_custom_call" | custom-call | flops 1073741824 | bytes 13631488 | tf_op jit(solution)/shard_map/cond/branch_1_fun/pallas_call | solution.py:124
  130.0 2.2 constant_dynamic-slice_fusion.3
  132.3 1.3 collective-permute-start.6
  133.7 3.3 %collective-permute-start.7 = (bf16[128,1024]{1,0:T(8,128)(2,1)S(1)}, bf16[128,1024]{1,0:T(8,128)(2,1)S(1)}, u32[]{:S(2)}, u32[]{:S(2)}) collective-permute-start(bf16[128,1024]{1,0:T(8,128)(2,1)S(1)} %bitcast.79), channel_id=1, source_target_pairs={{0,32},{16,48},{32,0},{48,16},{1,33},{17,49},{33,1},{49,17},{2,34}... | collective-permute-start | bytes 786440 | tf_op jit(solution)/shard_map/ppermute | solution.py:253
  140.0 4.0 %collective-permute-done.7 = bf16[128,1024]{1,0:T(8,128)(2,1)S(1)} collective-permute-done((bf16[128,1024]{1,0:T(8,128)(2,1)S(1)}, bf16[128,1024]{1,0:T(8,128)(2,1)S(1)}, u32[]{:S(2)}, u32[]{:S(2)}) %collective-permute-start.7) | collective-permute-done | bytes 262176 | tf_op jit(solution)/shard_map/ppermute | solution.py:253
  145.0 8.1 %shard_map.74 = f32[64,128,128]{2,1,0:T(8,128)S(1)} custom-call(s32[64]{0:T(128)S(1)} %gather_fusion, s32[64]{0:T(128)S(1)} %copy-done, bf16[512,4096]{1,0:T(8,128)(2,1)} %all-gather.2.cloned.1.call-done.h_ref, bf16[512,1024]{1,0:T(8,128)(2,1)S(1)} %bitcast_select_fusion.g_ref), custom_call_target="tpu_custom_call" | custom-call | flops 1073741824 | bytes 9437184 | tf_op jit(solution)/shard_map/pallas_call | solution.py:165
  153.5 1.3 copy-done.1
  154.9 2.1 collective-permute-start.9
  157.0 4.3 %collective-permute-start.16 = (f32[512,128]{1,0:T(8,128)S(1)}, f32[512,128]{1,0:T(8,128)S(1)}, u32[]{:S(2)}, u32[]{:S(2)}) collective-permute-start(f32[512,128]{1,0:T(8,128)S(1)} %dynamic-slice_bitcast_fusion.1), channel_id=1, source_target_pairs={{0,7},{1,0},{2,1},{3,2},{4,3},{5,4},{6,5},{7,6},{8,15},{9,8},{10,9... | collective-permute-start | bytes 786440 | tf_op jit(solution)/shard_map/ppermute | solution.py:194
  161.2 4.0 %collective-permute-done.9 = f32[512,128]{1,0:T(8,128)S(1)} collective-permute-done((f32[512,128]{1,0:T(8,128)S(1)}, f32[512,128]{1,0:T(8,128)S(1)}, u32[]{:S(2)}, u32[]{:S(2)}) %collective-permute-start.9) | collective-permute-done | bytes 262176 | tf_op jit(solution)/shard_map/ppermute | solution.py:193
  166.3 3.6 %collective-permute-start.17 = (f32[512,128]{1,0:T(8,128)S(1)}, f32[512,128]{1,0:T(8,128)S(1)}, u32[]{:S(2)}, u32[]{:S(2)}) collective-permute-start(f32[512,128]{1,0:T(8,128)S(1)} %bitcast_add_fusion.7), channel_id=1, source_target_pairs={{0,7},{1,0},{2,1},{3,2},{4,3},{5,4},{6,5},{7,6},{8,15},{9,8},{10,9... | collective-permute-start | bytes 786440 | tf_op jit(solution)/shard_map/ppermute | solution.py:194
  169.9 4.4 %collective-permute-done.10 = f32[512,128]{1,0:T(8,128)S(1)} collective-permute-done((f32[512,128]{1,0:T(8,128)S(1)}, f32[512,128]{1,0:T(8,128)S(1)}, u32[]{:S(2)}, u32[]{:S(2)}) %collective-permute-start.10) | collective-permute-done | bytes 262176 | tf_op jit(solution)/shard_map/ppermute | solution.py:193
  175.4 4.6 %collective-permute-start.18 = (f32[512,128]{1,0:T(8,128)S(1)}, f32[512,128]{1,0:T(8,128)S(1)}, u32[]{:S(2)}, u32[]{:S(2)}) collective-permute-start(f32[512,128]{1,0:T(8,128)S(1)} %bitcast_add_fusion.6), channel_id=1, source_target_pairs={{0,7},{1,0},{2,1},{3,2},{4,3},{5,4},{6,5},{7,6},{8,15},{9,8},{10,9... | collective-permute-start | bytes 786440 | tf_op jit(solution)/shard_map/ppermute | solution.py:194
  180.0 6.8 %collective-permute-done.11 = f32[512,128]{1,0:T(8,128)S(1)} collective-permute-done((f32[512,128]{1,0:T(8,128)S(1)}, f32[512,128]{1,0:T(8,128)S(1)}, u32[]{:S(2)}, u32[]{:S(2)}) %collective-permute-start.11) | collective-permute-done | bytes 262176 | tf_op jit(solution)/shard_map/ppermute | solution.py:193
  187.9 3.3 %collective-permute-start.19 = (f32[512,128]{1,0:T(8,128)S(1)}, f32[512,128]{1,0:T(8,128)S(1)}, u32[]{:S(2)}, u32[]{:S(2)}) collective-permute-start(f32[512,128]{1,0:T(8,128)S(1)} %bitcast_add_fusion.5), channel_id=1, source_target_pairs={{0,7},{1,0},{2,1},{3,2},{4,3},{5,4},{6,5},{7,6},{8,15},{9,8},{10,9... | collective-permute-start | bytes 786440 | tf_op jit(solution)/shard_map/ppermute | solution.py:194
  191.2 6.2 %collective-permute-done.12 = f32[512,128]{1,0:T(8,128)S(1)} collective-permute-done((f32[512,128]{1,0:T(8,128)S(1)}, f32[512,128]{1,0:T(8,128)S(1)}, u32[]{:S(2)}, u32[]{:S(2)}) %collective-permute-start.12) | collective-permute-done | bytes 262176 | tf_op jit(solution)/shard_map/ppermute | solution.py:193
  198.5 3.3 %collective-permute-start.20 = (f32[512,128]{1,0:T(8,128)S(1)}, f32[512,128]{1,0:T(8,128)S(1)}, u32[]{:S(2)}, u32[]{:S(2)}) collective-permute-start(f32[512,128]{1,0:T(8,128)S(1)} %bitcast_add_fusion.4), channel_id=1, source_target_pairs={{0,7},{1,0},{2,1},{3,2},{4,3},{5,4},{6,5},{7,6},{8,15},{9,8},{10,9... | collective-permute-start | bytes 786440 | tf_op jit(solution)/shard_map/ppermute | solution.py:194
  201.8 5.4 %collective-permute-done.13 = f32[512,128]{1,0:T(8,128)S(1)} collective-permute-done((f32[512,128]{1,0:T(8,128)S(1)}, f32[512,128]{1,0:T(8,128)S(1)}, u32[]{:S(2)}, u32[]{:S(2)}) %collective-permute-start.13) | collective-permute-done | bytes 262176 | tf_op jit(solution)/shard_map/ppermute | solution.py:193
  208.2 3.3 %collective-permute-start.21 = (f32[512,128]{1,0:T(8,128)S(1)}, f32[512,128]{1,0:T(8,128)S(1)}, u32[]{:S(2)}, u32[]{:S(2)}) collective-permute-start(f32[512,128]{1,0:T(8,128)S(1)} %bitcast_add_fusion.3), channel_id=1, source_target_pairs={{0,7},{1,0},{2,1},{3,2},{4,3},{5,4},{6,5},{7,6},{8,15},{9,8},{10,9... | collective-permute-start | bytes 786440 | tf_op jit(solution)/shard_map/ppermute | solution.py:194
  211.5 4.2 %collective-permute-done.14 = f32[512,128]{1,0:T(8,128)S(1)} collective-permute-done((f32[512,128]{1,0:T(8,128)S(1)}, f32[512,128]{1,0:T(8,128)S(1)}, u32[]{:S(2)}, u32[]{:S(2)}) %collective-permute-start.14) | collective-permute-done | bytes 262176 | tf_op jit(solution)/shard_map/ppermute | solution.py:193
  216.9 3.3 %collective-permute-start.22 = (f32[512,128]{1,0:T(8,128)S(1)}, f32[512,128]{1,0:T(8,128)S(1)}, u32[]{:S(2)}, u32[]{:S(2)}) collective-permute-start(f32[512,128]{1,0:T(8,128)S(1)} %bitcast_add_fusion.2), channel_id=1, source_target_pairs={{0,7},{1,0},{2,1},{3,2},{4,3},{5,4},{6,5},{7,6},{8,15},{9,8},{10,9... | collective-permute-start | bytes 786440 | tf_op jit(solution)/shard_map/ppermute | solution.py:194
  220.2 4.2 %collective-permute-done.15 = f32[512,128]{1,0:T(8,128)S(1)} collective-permute-done((f32[512,128]{1,0:T(8,128)S(1)}, f32[512,128]{1,0:T(8,128)S(1)}, u32[]{:S(2)}, u32[]{:S(2)}) %collective-permute-start.15) | collective-permute-done | bytes 262176 | tf_op jit(solution)/shard_map/ppermute | solution.py:193
  225.7 6.3 %collective-permute-done.23 = f32[512,128]{1,0:T(8,128)S(1)} collective-permute-done((f32[512,128]{1,0:T(8,128)S(1)}, f32[512,128]{1,0:T(8,128)S(1)}, u32[]{:S(2)}, u32[]{:S(2)}) %collective-permute-start.23) | collective-permute-done | bytes 262176 | tf_op jit(solution)/shard_map/ppermute | solution.py:267
  (85 shorter events, 28.9 us)
Async XLA Ops:
  6.5 138.5 %all-gather.2.cloned.1.call-start = ((), (), s32[]{:S(2)}) async-start(), calls=%async_computation | async-start | bytes 5242880 | tf_op jit(solution)/shard_map/all_gather | solution.py:259
  14.3 3.7 %collective-permute-start = (bf16[128,4096]{1,0:T(8,128)(2,1)S(1)}, bf16[128,4096]{1,0:T(8,128)(2,1)}, u32[]{:S(2)}, u32[]{:S(2)}) collective-permute-start(bf16[128,4096]{1,0:T(8,128)(2,1)S(1)} %get-tuple-element.132), channel_id=1, source_target_pairs={{0,64},{1,65},{2,66},{3,67},{4,68},{5,69},{6,70},{7,71},{8,72},{9,... | collective-permute-start | bytes 3145736 | tf_op jit(solution)/shard_map/ppermute | solution.py:209
  19.1 0.7 collective-permute-start.1
  19.8 1.0 copy-start.3
  20.8 2.7 %copy-start.2 = (bf16[128,4096]{1,0:T(8,128)(2,1)S(1)}, bf16[128,4096]{1,0:T(8,128)(2,1)}, u32[]{:S(2)}) copy-start(bf16[128,4096]{1,0:T(8,128)(2,1)} %param.23) | copy-start | bytes 3145732
  21.9 1.6 collective-permute-start.2
  26.0 0.7 collective-permute-start.3
  27.8 0.7 collective-permute-start.4
  28.6 2.5 %copy-start.6 = (s32[64]{0:T(128)S(1)}, s32[64]{0:T(128)}, u32[]{:S(2)}) copy-start(s32[64]{0:T(128)} %constant.247) | copy-start | bytes 772
  29.7 90.3 %collective-permute-start.5 = (bf16[128,4096]{1,0:T(8,128)(2,1)}, bf16[128,4096]{1,0:T(8,128)(2,1)}, u32[]{:S(2)}, u32[]{:S(2)}) collective-permute-start(bf16[128,4096]{1,0:T(8,128)(2,1)} %get-tuple-element.142), channel_id=1, source_target_pairs={{64,0},{65,1},{66,2},{67,3},{68,4},{69,5},{70,6},{71,7},{72,8},{73... | collective-permute-start | bytes 3145736 | tf_op jit(solution)/shard_map/ppermute | solution.py:209
  132.3 7.7 %collective-permute-start.6 = (bf16[128,1024]{1,0:T(8,128)(2,1)S(1)}, bf16[128,1024]{1,0:T(8,128)(2,1)S(1)}, u32[]{:S(2)}, u32[]{:S(2)}) collective-permute-start(bf16[128,1024]{1,0:T(8,128)(2,1)S(1)} %bitcast.78), channel_id=1, source_target_pairs={{0,16},{16,32},{32,48},{48,0},{1,17},{17,33},{33,49},{49,1},{2,18}... | collective-permute-start | bytes 786440 | tf_op jit(solution)/shard_map/ppermute | solution.py:253
  133.7 10.3 %collective-permute-start.7 = (bf16[128,1024]{1,0:T(8,128)(2,1)S(1)}, bf16[128,1024]{1,0:T(8,128)(2,1)S(1)}, u32[]{:S(2)}, u32[]{:S(2)}) collective-permute-start(bf16[128,1024]{1,0:T(8,128)(2,1)S(1)} %bitcast.79), channel_id=1, source_target_pairs={{0,32},{16,48},{32,0},{48,16},{1,33},{17,49},{33,1},{49,17},{2,34}... | collective-permute-start | bytes 786440 | tf_op jit(solution)/shard_map/ppermute | solution.py:253
  137.1 6.9 %collective-permute-start.8 = (bf16[128,1024]{1,0:T(8,128)(2,1)S(1)}, bf16[128,1024]{1,0:T(8,128)(2,1)S(1)}, u32[]{:S(2)}, u32[]{:S(2)}) collective-permute-start(bf16[128,1024]{1,0:T(8,128)(2,1)S(1)} %bitcast.80), channel_id=1, source_target_pairs={{0,48},{16,0},{32,16},{48,32},{1,49},{17,1},{33,17},{49,33},{2,50}... | collective-permute-start | bytes 786440 | tf_op jit(solution)/shard_map/ppermute | solution.py:253
  144.1 0.9 copy-start
  153.5 1.4 copy-start.1
  154.9 10.3 %collective-permute-start.9 = (f32[512,128]{1,0:T(8,128)S(1)}, f32[512,128]{1,0:T(8,128)S(1)}, u32[]{:S(2)}, u32[]{:S(2)}) collective-permute-start(f32[512,128]{1,0:T(8,128)S(1)} %dynamic-slice_bitcast_fusion.2), channel_id=1, source_target_pairs={{0,1},{1,2},{2,3},{3,4},{4,5},{5,6},{6,7},{7,0},{8,9},{9,10},{10,1... | collective-permute-start | bytes 786440 | tf_op jit(solution)/shard_map/ppermute | solution.py:193
  157.0 9.3 %collective-permute-start.16 = (f32[512,128]{1,0:T(8,128)S(1)}, f32[512,128]{1,0:T(8,128)S(1)}, u32[]{:S(2)}, u32[]{:S(2)}) collective-permute-start(f32[512,128]{1,0:T(8,128)S(1)} %dynamic-slice_bitcast_fusion.1), channel_id=1, source_target_pairs={{0,7},{1,0},{2,1},{3,2},{4,3},{5,4},{6,5},{7,6},{8,15},{9,8},{10,9... | collective-permute-start | bytes 786440 | tf_op jit(solution)/shard_map/ppermute | solution.py:194
  166.2 8.1 %collective-permute-start.10 = (f32[512,128]{1,0:T(8,128)S(1)}, f32[512,128]{1,0:T(8,128)S(1)}, u32[]{:S(2)}, u32[]{:S(2)}) collective-permute-start(f32[512,128]{1,0:T(8,128)S(1)} %bitcast_add_fusion.14), channel_id=1, source_target_pairs={{0,1},{1,2},{2,3},{3,4},{4,5},{5,6},{6,7},{7,0},{8,9},{9,10},{10,1... | collective-permute-start | bytes 786440 | tf_op jit(solution)/shard_map/ppermute | solution.py:193
  166.3 9.0 %collective-permute-start.17 = (f32[512,128]{1,0:T(8,128)S(1)}, f32[512,128]{1,0:T(8,128)S(1)}, u32[]{:S(2)}, u32[]{:S(2)}) collective-permute-start(f32[512,128]{1,0:T(8,128)S(1)} %bitcast_add_fusion.7), channel_id=1, source_target_pairs={{0,7},{1,0},{2,1},{3,2},{4,3},{5,4},{6,5},{7,6},{8,15},{9,8},{10,9... | collective-permute-start | bytes 786440 | tf_op jit(solution)/shard_map/ppermute | solution.py:194
  175.3 11.5 %collective-permute-start.11 = (f32[512,128]{1,0:T(8,128)S(1)}, f32[512,128]{1,0:T(8,128)S(1)}, u32[]{:S(2)}, u32[]{:S(2)}) collective-permute-start(f32[512,128]{1,0:T(8,128)S(1)} %bitcast_add_fusion.13), channel_id=1, source_target_pairs={{0,1},{1,2},{2,3},{3,4},{4,5},{5,6},{6,7},{7,0},{8,9},{9,10},{10,1... | collective-permute-start | bytes 786440 | tf_op jit(solution)/shard_map/ppermute | solution.py:193
  175.4 12.4 %collective-permute-start.18 = (f32[512,128]{1,0:T(8,128)S(1)}, f32[512,128]{1,0:T(8,128)S(1)}, u32[]{:S(2)}, u32[]{:S(2)}) collective-permute-start(f32[512,128]{1,0:T(8,128)S(1)} %bitcast_add_fusion.6), channel_id=1, source_target_pairs={{0,7},{1,0},{2,1},{3,2},{4,3},{5,4},{6,5},{7,6},{8,15},{9,8},{10,9... | collective-permute-start | bytes 786440 | tf_op jit(solution)/shard_map/ppermute | solution.py:194
  187.7 9.6 %collective-permute-start.12 = (f32[512,128]{1,0:T(8,128)S(1)}, f32[512,128]{1,0:T(8,128)S(1)}, u32[]{:S(2)}, u32[]{:S(2)}) collective-permute-start(f32[512,128]{1,0:T(8,128)S(1)} %bitcast_add_fusion.12), channel_id=1, source_target_pairs={{0,1},{1,2},{2,3},{3,4},{4,5},{5,6},{6,7},{7,0},{8,9},{9,10},{10,1... | collective-permute-start | bytes 786440 | tf_op jit(solution)/shard_map/ppermute | solution.py:193
  187.9 10.5 %collective-permute-start.19 = (f32[512,128]{1,0:T(8,128)S(1)}, f32[512,128]{1,0:T(8,128)S(1)}, u32[]{:S(2)}, u32[]{:S(2)}) collective-permute-start(f32[512,128]{1,0:T(8,128)S(1)} %bitcast_add_fusion.5), channel_id=1, source_target_pairs={{0,7},{1,0},{2,1},{3,2},{4,3},{5,4},{6,5},{7,6},{8,15},{9,8},{10,9... | collective-permute-start | bytes 786440 | tf_op jit(solution)/shard_map/ppermute | solution.py:194
  198.3 8.8 %collective-permute-start.13 = (f32[512,128]{1,0:T(8,128)S(1)}, f32[512,128]{1,0:T(8,128)S(1)}, u32[]{:S(2)}, u32[]{:S(2)}) collective-permute-start(f32[512,128]{1,0:T(8,128)S(1)} %bitcast_add_fusion.11), channel_id=1, source_target_pairs={{0,1},{1,2},{2,3},{3,4},{4,5},{5,6},{6,7},{7,0},{8,9},{9,10},{10,1... | collective-permute-start | bytes 786440 | tf_op jit(solution)/shard_map/ppermute | solution.py:193
  198.5 9.7 %collective-permute-start.20 = (f32[512,128]{1,0:T(8,128)S(1)}, f32[512,128]{1,0:T(8,128)S(1)}, u32[]{:S(2)}, u32[]{:S(2)}) collective-permute-start(f32[512,128]{1,0:T(8,128)S(1)} %bitcast_add_fusion.4), channel_id=1, source_target_pairs={{0,7},{1,0},{2,1},{3,2},{4,3},{5,4},{6,5},{7,6},{8,15},{9,8},{10,9... | collective-permute-start | bytes 786440 | tf_op jit(solution)/shard_map/ppermute | solution.py:194
  208.1 7.7 %collective-permute-start.14 = (f32[512,128]{1,0:T(8,128)S(1)}, f32[512,128]{1,0:T(8,128)S(1)}, u32[]{:S(2)}, u32[]{:S(2)}) collective-permute-start(f32[512,128]{1,0:T(8,128)S(1)} %bitcast_add_fusion.10), channel_id=1, source_target_pairs={{0,1},{1,2},{2,3},{3,4},{4,5},{5,6},{6,7},{7,0},{8,9},{9,10},{10,1... | collective-permute-start | bytes 786440 | tf_op jit(solution)/shard_map/ppermute | solution.py:193
  208.2 8.6 %collective-permute-start.21 = (f32[512,128]{1,0:T(8,128)S(1)}, f32[512,128]{1,0:T(8,128)S(1)}, u32[]{:S(2)}, u32[]{:S(2)}) collective-permute-start(f32[512,128]{1,0:T(8,128)S(1)} %bitcast_add_fusion.3), channel_id=1, source_target_pairs={{0,7},{1,0},{2,1},{3,2},{4,3},{5,4},{6,5},{7,6},{8,15},{9,8},{10,9... | collective-permute-start | bytes 786440 | tf_op jit(solution)/shard_map/ppermute | solution.py:194
  216.7 7.7 %collective-permute-start.15 = (f32[512,128]{1,0:T(8,128)S(1)}, f32[512,128]{1,0:T(8,128)S(1)}, u32[]{:S(2)}, u32[]{:S(2)}) collective-permute-start(f32[512,128]{1,0:T(8,128)S(1)} %bitcast_add_fusion.9), channel_id=1, source_target_pairs={{0,1},{1,2},{2,3},{3,4},{4,5},{5,6},{6,7},{7,0},{8,9},{9,10},{10,1... | collective-permute-start | bytes 786440 | tf_op jit(solution)/shard_map/ppermute | solution.py:193
  216.9 8.5 %collective-permute-start.22 = (f32[512,128]{1,0:T(8,128)S(1)}, f32[512,128]{1,0:T(8,128)S(1)}, u32[]{:S(2)}, u32[]{:S(2)}) collective-permute-start(f32[512,128]{1,0:T(8,128)S(1)} %bitcast_add_fusion.2), channel_id=1, source_target_pairs={{0,7},{1,0},{2,1},{3,2},{4,3},{5,4},{6,5},{7,6},{8,15},{9,8},{10,9... | collective-permute-start | bytes 786440 | tf_op jit(solution)/shard_map/ppermute | solution.py:194
  225.5 6.5 %collective-permute-start.23 = (f32[512,128]{1,0:T(8,128)S(1)}, f32[512,128]{1,0:T(8,128)S(1)}, u32[]{:S(2)}, u32[]{:S(2)}) collective-permute-start(f32[512,128]{1,0:T(8,128)S(1)} %dynamic-slice_bitcast_fusion), channel_id=1, source_target_pairs={{0,8},{8,0},{1,9},{9,1},{2,10},{10,2},{3,11},{11,3},{4,12},{12,4},... | collective-permute-start | bytes 786440 | tf_op jit(solution)/shard_map/ppermute | solution.py:267
Sparse Core Ops, SparseCore 0:
  24.9 86.0 all-gather.1
